TPU v7x, 32 devices: a whole 2x2x4 slice. The times are simulated.
32 devices in a mesh: ctx: 32 (over z, y, x, core), tp: 1.
Axes of the slice: x: 2, y: 2, z: 4, core: 2. Of those that a mesh axis runs over, the one named last changes fastest.
Arguments:
- x_in: bfloat16 [8192, 8192], P('ctx', 'tp'), may hold values from -6 to 6
- gate_z: bfloat16 [8192, 8192], P('ctx', 'tp'), may hold values from -6 to 6
- bc_in: bfloat16 [8192, 256], P('ctx'), may hold values from -6 to 6
- dt_raw: float32 [128, 8192], P('tp', 'ctx'), may hold values from -2.5 to 2.5
- dt_bias: float32 [128], P('tp')
- a_rate: float32 [128], P('tp')
- skip_d: float32 [128], P('tp'), may hold values from 0.5 to 1.5
- conv_x_w: bfloat16 [4, 8192], P(None, 'tp'), may hold values from -3 to 3
- conv_x_b: bfloat16 [8192], P('tp'), may hold values from -3 to 3
- conv_bc_w: bfloat16 [4, 256], replicated, may hold values from -3 to 3
- conv_bc_b: bfloat16 [256], replicated, may hold values from -3 to 3
- norm_gain: bfloat16 [8192], P('tp'), may hold values from 0.5 to 1.5
- segment_ids: int32 [8192], P('ctx'), may hold values from 0 to 7, never falling along the last dimension, each value on 1 to 2048 neighbouring positions
Outputs:
- y_out: bfloat16 [8192, 8192], P('ctx', 'tp')
Inputs may be any that keep to these rules, and one draw needn't show every extreme that they name: `segment_ids`: segment numbers never fall along the tokens and every number is used; a file holds at most a quarter of 8192 tokens, and one holds exactly that many.
All inputs are finite; a program needn't handle non-finite values.
Results may differ from a plain program's by a relative error of at most 0.0034.
Values may be sent and summed in bfloat16 or wider, within the bound.
No kernel may reach another device: no remote copies, remote signals or barrier semaphores. Data moves between devices by JAX's collectives and lax.ppermute only.
A program may use at most 256 MiB of HBM per device.

v0:
```python
import jax
import jax.numpy as jnp
from jax import lax
from jax.sharding import PartitionSpec as P

HEAD_DIM = 64
STATE = 128
GROUP = 256
CONV = 4
INNER = 8192


epsilon = 1e-05


def carried_in(part, axis, combine, identity):
    place = lax.axis_index(axis)
    gathered = jax.tree.map(lambda a: lax.all_gather(a, axis), part)
    state = jax.tree.map(lambda a, e: jnp.zeros_like(a) + jnp.asarray(e, a.dtype), part, identity)

    def one(lap, state):
        return combine(
            state, jax.tree.map(lambda a: lax.dynamic_index_in_dim(a, lap, 0, False), gathered)
        )

    return lax.fori_loop(0, place, one, state)


def passed_along(value, axis, steps):
    count = lax.axis_size(axis)
    leading, last = (max(0, -steps), min(count, count - steps))
    return lax.ppermute(value, axis, [(source, source + steps) for source in range(leading, last)])


def causal_conv(rim_vals, values, rim_segment, segment, weight, offset_bias):
    extended = jnp.concatenate([rim_vals, values], axis=0)
    ext_segment = jnp.concatenate([rim_segment, segment], axis=0)
    length = values.shape[0]
    summed = jnp.zeros(values.shape, jnp.float32) + offset_bias.astype(jnp.float32)
    for offset in range(CONV):
        visible = (ext_segment[offset : offset + length] == segment).astype(jnp.float32)
        summed = (
            summed
            + weight[offset].astype(jnp.float32)
            * extended[offset : offset + length].astype(jnp.float32)
            * visible[:, None]
        )
    return jax.nn.silu(summed).astype(jnp.bfloat16)


def mixing_part(x_group, b_group, c_group, step_size, cum_decay, segment):
    places = jnp.arange(segment.shape[0])
    visible = jnp.logical_and(
        places[:, None] >= places[None, :], segment[:, None] == segment[None, :]
    )
    scores = jnp.einsum("in,jn->ij", c_group, b_group, preferred_element_type=jnp.float32)
    exponent = jnp.where(visible[None], cum_decay[:, :, None] - cum_decay[:, None, :], -jnp.inf)
    mixing = (scores[None] * jnp.exp(exponent) * step_size[:, None, :]).astype(jnp.bfloat16)
    return jnp.einsum("hij,jhp->ihp", mixing, x_group, preferred_element_type=jnp.float32)


def state_part(x_group, b_group, step_size, cum_decay, segment, seg_before):
    closing = cum_decay[:, -1:]
    tail_mask = (segment == segment[-1]).astype(jnp.float32)
    factor = jnp.exp(closing - cum_decay) * step_size * tail_mask[None]
    weighted = (b_group.astype(jnp.float32)[None] * factor[:, :, None]).astype(jnp.bfloat16)
    block_state = jnp.einsum("hjn,jhp->hpn", weighted, x_group, preferred_element_type=jnp.float32)
    transmit = jnp.exp(cum_decay[:, -1]) * (segment[-1] == seg_before).astype(jnp.float32)
    return (block_state, transmit)


def entry_part(c_group, entering, cum_decay, segment, seg_before):
    packed = entering.astype(jnp.bfloat16)
    reach = jnp.exp(cum_decay) * (segment == seg_before).astype(jnp.float32)[None]
    product = jnp.einsum("in,hpn->ihp", c_group, packed, preferred_element_type=jnp.float32)
    return product * jnp.transpose(reach)[:, :, None]


def link_pairs(earlier, later):
    return (earlier[0] * later[0], later[0][:, None, None] * earlier[1] + later[1])


def device_entry(dev_transmit, dev_state):
    identity = (jnp.ones_like(dev_transmit), jnp.zeros_like(dev_state))
    prefix = carried_in((dev_transmit, dev_state), "ctx", link_pairs, identity)
    return prefix[1]


def chain_states(block_states, transmits):

    def advance(carried, item):
        passing, state_now = carried
        transmit, block_state = item
        return (
            (passing * transmit, transmit[:, None, None] * state_now + block_state),
            (passing, state_now),
        )

    start = (jnp.ones_like(transmits[0]), jnp.zeros_like(block_states[0]))
    finals, befores = lax.scan(advance, start, (transmits, block_states))
    entering_dev = device_entry(finals[0], finals[1])
    return befores[0][:, :, None, None] * entering_dev[None] + befores[1]


def local(
    x_in,
    gate_z,
    bc_in,
    dt_raw,
    dt_bias,
    a_rate,
    skip_d,
    conv_x_w,
    conv_x_b,
    conv_bc_w,
    conv_bc_b,
    norm_gain,
    segment_ids,
):
    tok_rows = x_in.shape[0]
    channels = x_in.shape[1]
    head_count = dt_raw.shape[0]
    block_count = tok_rows // GROUP
    rim_rows = CONV - 1
    rim_x, rim_bc, rim_mark = passed_along(
        (
            x_in[tok_rows - rim_rows :],
            bc_in[tok_rows - rim_rows :],
            segment_ids[tok_rows - rim_rows :].astype(jnp.bfloat16),
        ),
        "ctx",
        1,
    )
    rim_segment = rim_mark.astype(jnp.int32)
    x_conv = causal_conv(rim_x, x_in, rim_segment, segment_ids, conv_x_w, conv_x_b)
    bc_conv = causal_conv(rim_bc, bc_in, rim_segment, segment_ids, conv_bc_w, conv_bc_b)
    step_size = jax.nn.softplus(dt_raw + dt_bias[:, None])
    log_decay = -step_size * a_rate[:, None]
    cum_decay = jnp.transpose(
        jnp.cumsum(log_decay.reshape(head_count, block_count, GROUP), axis=2), (1, 0, 2)
    )
    step_blocks = jnp.transpose(step_size.reshape(head_count, block_count, GROUP), (1, 0, 2))
    seg_blocks = segment_ids.reshape(block_count, GROUP)
    seg_before = jnp.concatenate([rim_segment[rim_rows - 1 :], seg_blocks[:-1, -1]])
    x_blocks = x_conv.reshape(block_count, GROUP, head_count, HEAD_DIM)
    b_blocks = bc_conv[:, :STATE].reshape(block_count, GROUP, STATE)
    c_blocks = bc_conv[:, STATE:].reshape(block_count, GROUP, STATE)
    everything = (x_blocks, b_blocks, c_blocks, step_blocks, cum_decay, seg_blocks, seg_before)

    def both_of(item):
        x_group, b_group, c_group, steps_here, decay_here, segment, before = item
        block_state, transmit = state_part(
            x_group, b_group, steps_here, decay_here, segment, before
        )
        return (
            mixing_part(x_group, b_group, c_group, steps_here, decay_here, segment),
            block_state,
            transmit,
        )

    y_intra, block_states, transmits = lax.map(both_of, everything)
    entering = chain_states(block_states, transmits)

    def enter_of(item):
        c_group, decay_here, segment, before, entering_here = item
        return entry_part(c_group, entering_here, decay_here, segment, before)

    y_state = lax.map(enter_of, (c_blocks, cum_decay, seg_blocks, seg_before, entering))
    y_blocks = y_intra + y_state
    x_heads = x_conv.reshape(tok_rows, head_count, HEAD_DIM).astype(jnp.float32)
    y_total = y_blocks.reshape(tok_rows, head_count, HEAD_DIM) + skip_d[None, :, None] * x_heads
    gated = y_total.reshape(tok_rows, channels) * jax.nn.silu(gate_z.astype(jnp.float32))
    local_sq = jnp.sum(gated * gated, axis=1)
    total_sq = lax.psum(local_sq, "tp")
    scale = lax.rsqrt(total_sq / INNER + epsilon)
    return (gated * scale[:, None] * norm_gain.astype(jnp.float32)).astype(jnp.bfloat16)


def solution(mesh):
    in_specs = (
        P("ctx", "tp"),
        P("ctx", "tp"),
        P("ctx", None),
        P("tp", "ctx"),
        P("tp"),
        P("tp"),
        P("tp"),
        P(None, "tp"),
        P("tp"),
        P(),
        P(),
        P("tp"),
        P("ctx"),
    )
    out_specs = P("ctx", "tp")
    return jax.shard_map(local, mesh=mesh, in_specs=in_specs, out_specs=out_specs, check_vma=False)
```

profile of v0, /device:TPU:31, one launch (start us, length us, event | category | flops | bytes accessed | tf_op | source)
XLA Modules:
  0.0 953.9 jit_solution(10036000999905133183)
XLA Ops:
  7.4 1.3 collective-permute-start.1
  9.6 1.3 collective-permute-start
  12.9 1.3 slice.114
  16.1 6.4 copy.37
  27.5 16.5 %multiply_convert_fusion.5 = bf16[256,8192]{0,1:T(8,128)(2,1)S(1)} fusion(bf16[256,8192]{0,1:T(8,128)(2,1)} %copy.37, bf16[3,8192]{0,1:T(8,128)(2,1)S(1)} %copy.36, f32[8192]{0:T(1024)S(1)} %bitcast.55, f32[256]{0:T(256)S(1)} %get-tuple-element.148, f32[8192]{0:T(1024)S(1)} %bitcast.56, f32[256]{0:T(256)S(1)} %get-tuple-element.149, f32[8192]{0:T(1024)S(1)} %bitcast.54, ...), kind=kLoop, calls=%fused_computation.24 | loop fusion | flops 60817408 | bytes 8604672 | tf_op jit(solution)/shard_map/convert_element_type | solution.py:48
  44.0 1.9 copy-done
  46.0 7.4 fusion.16
  53.6 6.4 copy.49
  60.4 38.1 %all-gather = f32[4096,1]{0,1:T(1,128)S(1)} all-gather(f32[128,1]{0,1:T(1,128)S(1)} %get-tuple-element.142), channel_id=2, replica_groups=mesh['ctx'=32,'tp'=1] {'ctx'}, dimensions={0}, use_global_device_ids=true | all-gather | bytes 16896 | tf_op jit(solution)/shard_map/all_gather | solution.py:18
  98.7 635.8 %all-gather.4.cloned.1.call-done = f32[4096,64,128]{2,1,0:T(8,128)} async-done(((f32[128,64,128]{2,1,0:T(8,128)}), f32[4096,64,128]{2,1,0:T(8,128)}) %all-gather.4.cloned.1.call-update) | async-done | bytes 134217744 | tf_op jit(solution)/shard_map/all_gather | solution.py:18
  734.6 2.5 broadcast.104
  737.1 183.3 %while.3 = (s32[]{:T(128)}, f32[128,64,128]{2,1,0:T(8,128)}, s32[]{:T(128)}, f32[32,128]{1,0:T(8,128)S(1)}, f32[32,128,64,128]{3,2,1,0:T(8,128)}, /*index=5*/s32[]{:T(128)}, s32[]{:T(128)}, s32[]{:T(128)}) while((s32[]{:T(128)}, f32[128,64,128]{2,1,0:T(8,128)}, s32[]{:T(128)}, f32[32,128]{1,0:T(8,128)S(1)}, f32[32,128,64,128]{3,2,1,0:T(8,128)}, ...), condition=%wide.region_3.4_spmd, body=%wide.region_2.3_spmd.sunk | while | flops 2097157 | bytes 12584575 | solution.py:26
  737.1 5.9 bitcast_add_fusion.6
  743.0 5.9 bitcast_add_fusion.6
  748.9 5.9 bitcast_add_fusion.6
  754.8 5.9 bitcast_add_fusion.6
  760.7 5.9 bitcast_add_fusion.6
  766.6 5.9 bitcast_add_fusion.6
  772.6 5.9 bitcast_add_fusion.6
  778.5 5.9 bitcast_add_fusion.6
  784.4 5.9 bitcast_add_fusion.6
  790.3 5.9 bitcast_add_fusion.6
  796.2 5.9 bitcast_add_fusion.6
  802.1 5.9 bitcast_add_fusion.6
  808.0 5.9 bitcast_add_fusion.6
  813.9 5.9 bitcast_add_fusion.6
  819.9 5.9 bitcast_add_fusion.6
  825.8 5.9 bitcast_add_fusion.6
  831.7 5.9 bitcast_add_fusion.6
  837.6 5.9 bitcast_add_fusion.6
  843.5 5.9 bitcast_add_fusion.6
  849.4 5.9 bitcast_add_fusion.6
  855.3 5.9 bitcast_add_fusion.6
  861.2 5.9 bitcast_add_fusion.6
  867.2 5.9 bitcast_add_fusion.6
  873.1 5.9 bitcast_add_fusion.6
  879.0 5.9 bitcast_add_fusion.6
  884.9 5.9 bitcast_add_fusion.6
  890.8 5.9 bitcast_add_fusion.6
  896.7 5.9 bitcast_add_fusion.6
  902.6 5.9 bitcast_add_fusion.6
  908.5 5.9 bitcast_add_fusion.6
  914.5 5.9 bitcast_add_fusion.6
  920.4 3.6 fusion.17
  924.0 9.4 bitcast_add_fusion.2
  933.4 4.7 multiply_reduce_fusion
  938.1 2.6 multiply_convert_fusion.4
  940.7 6.3 copy.50
  (94 shorter events, 10.3 us)
Async XLA Ops:
  6.5 16.8 %copy-start.7 = (s32[256]{0:T(256)S(1)}, s32[256]{0:T(256)}, u32[]{:S(2)}) copy-start(s32[256]{0:T(256)} %param.27) | copy-start | bytes 3076
  6.5 19.6 %copy-start.4 = (bf16[256,256]{1,0:T(8,128)(2,1)S(1)}, bf16[256,256]{1,0:T(8,128)(2,1)}, u32[]{:S(2)}) copy-start(bf16[256,256]{1,0:T(8,128)(2,1)} %param.17) | copy-start | bytes 393220
  6.5 16.0 %copy-start.3 = (bf16[4,8192]{1,0:T(4,128)(2,1)S(1)}, bf16[4,8192]{1,0:T(4,128)(2,1)}, u32[]{:S(2)}) copy-start(bf16[4,8192]{1,0:T(4,128)(2,1)} %param.22) | copy-start | bytes 196612
  6.5 16.1 %copy-start.5 = (bf16[8192]{0:T(1024)(128)(2,1)S(1)}, bf16[8192]{0:T(1024)(128)(2,1)}, u32[]{:S(2)}) copy-start(bf16[8192]{0:T(1024)(128)(2,1)} %param.23) | copy-start | bytes 49156
  6.5 16.1 %copy-start.8 = (bf16[4,256]{1,0:T(4,128)(2,1)S(1)}, bf16[4,256]{1,0:T(4,128)(2,1)}, u32[]{:S(2)}) copy-start(bf16[4,256]{1,0:T(4,128)(2,1)} %param.24) | copy-start | bytes 6148
  6.5 16.1 %copy-start.10 = (bf16[256]{0:T(256)(128)(2,1)S(1)}, bf16[256]{0:T(256)(128)(2,1)}, u32[]{:S(2)}) copy-start(bf16[256]{0:T(256)(128)(2,1)} %param.25) | copy-start | bytes 1540
  6.6 728.0 %all-gather.4.cloned.1.call-start = ((), (), s32[]{:S(2)}) async-start(), calls=%async_computation | async-start | bytes 138412032 | tf_op jit(solution)/shard_map/all_gather | solution.py:18
  7.4 15.3 %collective-permute-start.1 = (bf16[3]{0:T(256)(128)(2,1)S(1)}, bf16[3]{0:T(256)(128)(2,1)S(1)}, u32[]{:S(2)}, u32[]{:S(2)}) collective-permute-start(bf16[3]{0:T(256)(128)(2,1)S(1)} %slice.92), channel_id=1, source_target_pairs={{0,1},{1,2},{2,3},{3,4},{4,5},{5,6},{6,7},{7,8},{8,9},{9,10},{10,1... | collective-permute-start | bytes 26 | tf_op jit(solution)/shard_map/ppermute | solution.py:32
  9.6 16.8 %collective-permute-start = (bf16[3,8192]{1,0:T(4,128)(2,1)S(1)}, bf16[3,8192]{1,0:T(4,128)(2,1)S(1)}, u32[]{:S(2)}, u32[]{:S(2)}) collective-permute-start(bf16[3,8192]{1,0:T(4,128)(2,1)S(1)} %slice.90), channel_id=1, source_target_pairs={{0,1},{1,2},{2,3},{3,4},{4,5},{5,6},{6,7},{7,8},{8,9},{9,10},{10,1... | collective-permute-start | bytes 147464 | tf_op jit(solution)/shard_map/ppermute | solution.py:32
  11.6 14.5 %collective-permute-start.2 = (bf16[3,256]{1,0:T(4,128)(2,1)S(1)}, bf16[3,256]{1,0:T(4,128)(2,1)S(1)}, u32[]{:S(2)}, u32[]{:S(2)}) collective-permute-start(bf16[3,256]{1,0:T(4,128)(2,1)S(1)} %slice.102), channel_id=1, source_target_pairs={{0,1},{1,2},{2,3},{3,4},{4,5},{5,6},{6,7},{7,8},{8,9},{9,10},{10,1... | collective-permute-start | bytes 4616 | tf_op jit(solution)/shard_map/ppermute | solution.py:32
  44.0 2.0 copy-start
  53.4 6.5 copy-start.9
  53.4 6.7 copy-start.6
  920.4 3.6 copy-start.1
  924.0 9.5 copy-start.2
Sparse Core Ops, SparseCore 0:
  53.6 680.9 all-gather.3
where the time goes:
time: 955 us; the launch traced here: 954 us
  waiting for transfers between devices  636 us (67%)
  other arithmetic  211 us (22%)
  blocking collectives  38.1 us (4%)
  local copies, waits for them, and re-layouts  29.9 us (3%)
  matrix products  20.6 us (2%)
  between operations  14.9 us (2%)
    all_gather x1, waiting for transfers between devices, carried_in(): gathered = jax.tree.map(lambda a: lax.all_gather(a, axis), part)  636 us
    add x31, other arithmetic, link_pairs(): later[0][:, None, None] * earlier[1] + later[1]  183 us
    all_gather x1, blocking collectives, carried_in(): gathered = jax.tree.map(lambda a: lax.all_gather(a, axis), part)  38.1 us
  transfers between devices with their start and end apart: 4, of which 1 were waited for; matrix products, arithmetic and copies ran while one was open for 2% of the time, Pallas kernels for 0%

commit v1 on v0

--- a/solution.py
+++ b/solution.py
@@ -1,3 +1,5 @@
+import functools
+
 import jax
 import jax.numpy as jnp
 from jax import lax
@@ -11,19 +13,6 @@
 
 
 epsilon = 1e-05
-
-
-def carried_in(part, axis, combine, identity):
-    place = lax.axis_index(axis)
-    gathered = jax.tree.map(lambda a: lax.all_gather(a, axis), part)
-    state = jax.tree.map(lambda a, e: jnp.zeros_like(a) + jnp.asarray(e, a.dtype), part, identity)
-
-    def one(lap, state):
-        return combine(
-            state, jax.tree.map(lambda a: lax.dynamic_index_in_dim(a, lap, 0, False), gathered)
-        )
-
-    return lax.fori_loop(0, place, one, state)
 
 
 def passed_along(value, axis, steps):
@@ -76,17 +65,50 @@
     return product * jnp.transpose(reach)[:, :, None]
 
 
-def link_pairs(earlier, later):
-    return (earlier[0] * later[0], later[0][:, None, None] * earlier[1] + later[1])
-
-
-def device_entry(dev_transmit, dev_state):
-    identity = (jnp.ones_like(dev_transmit), jnp.zeros_like(dev_state))
-    prefix = carried_in((dev_transmit, dev_state), "ctx", link_pairs, identity)
-    return prefix[1]
-
-
-def chain_states(block_states, transmits):
+def shifted(value, axis, steps, count):
+    return lax.ppermute(value, axis, [(s, s + steps) for s in range(count - steps)])
+
+
+def scan_rounds(carry, axis, stride, span, count):
+    transmit, state = shifted(carry, axis, stride, count)
+    covered = 1
+    while covered < span - 1:
+        far_t, far_s = shifted((transmit, state), axis, stride * covered, count)
+        state = transmit[:, None, None] * far_s + state
+        transmit = transmit * far_t
+        covered *= 2
+    return state
+
+
+def device_entry(dev_transmit, dev_state, paired):
+    count = lax.axis_size("ctx")
+    if not paired:
+        return scan_rounds((dev_transmit, dev_state), "ctx", 1, count, count)
+    heads = dev_state.shape[0]
+    half = heads // 2
+    core = lax.axis_index("ctx") % 2
+    swap = [(s, s ^ 1) for s in range(count)]
+    own_lo = core * half
+    give = lax.dynamic_slice_in_dim(dev_state, half - own_lo, half, 0)
+    other_t, other_s = lax.ppermute((dev_transmit, give), "ctx", swap)
+    mine_s = lax.dynamic_slice_in_dim(dev_state, own_lo, half, 0)
+    mine_t = lax.dynamic_slice_in_dim(dev_transmit, own_lo, half, 0)
+    peer_t = lax.dynamic_slice_in_dim(other_t, own_lo, half, 0)
+    first = core == 0
+    chip_s = jnp.where(first, peer_t[:, None, None] * mine_s + other_s, mine_t[:, None, None] * other_s + mine_s)
+    chip_t = mine_t * peer_t
+    entering = scan_rounds((chip_t, chip_s), "ctx", 2, count // 2, count)
+    lead_t = jnp.where(first, mine_t, peer_t)
+    lead_s = jnp.where(first, mine_s, other_s)
+    second = lead_t[:, None, None] * entering + lead_s
+    back = lax.ppermute(jnp.where(first, second, entering), "ctx", swap)
+    mine = jnp.where(first, entering, second)
+    low = jnp.where(first, mine, back)
+    high = jnp.where(first, back, mine)
+    return jnp.concatenate([low, high], axis=0)
+
+
+def chain_states(block_states, transmits, paired):
 
     def advance(carried, item):
         passing, state_now = carried
@@ -98,11 +120,12 @@
 
     start = (jnp.ones_like(transmits[0]), jnp.zeros_like(block_states[0]))
     finals, befores = lax.scan(advance, start, (transmits, block_states))
-    entering_dev = device_entry(finals[0], finals[1])
+    entering_dev = device_entry(finals[0], finals[1], paired)
     return befores[0][:, :, None, None] * entering_dev[None] + befores[1]
 
 
 def local(
+    paired,
     x_in,
     gate_z,
     bc_in,
@@ -159,7 +182,7 @@
         )
 
     y_intra, block_states, transmits = lax.map(both_of, everything)
-    entering = chain_states(block_states, transmits)
+    entering = chain_states(block_states, transmits, paired)
 
     def enter_of(item):
         c_group, decay_here, segment, before, entering_here = item
@@ -176,6 +199,19 @@
     return (gated * scale[:, None] * norm_gain.astype(jnp.float32)).astype(jnp.bfloat16)
 
 
+def cores_paired(mesh):
+    row = mesh.devices[:, 0] if mesh.devices.ndim == 2 else mesh.devices.reshape(-1)
+    if len(row) % 2:
+        return False
+    try:
+        for lo, hi in zip(row[0::2], row[1::2]):
+            if tuple(lo.coords) != tuple(hi.coords) or lo.core_on_chip == hi.core_on_chip:
+                return False
+    except AttributeError:
+        return False
+    return True
+
+
 def solution(mesh):
     in_specs = (
         P("ctx", "tp"),
@@ -193,4 +229,5 @@
         P("ctx"),
     )
     out_specs = P("ctx", "tp")
-    return jax.shard_map(local, mesh=mesh, in_specs=in_specs, out_specs=out_specs, check_vma=False)
+    paired = cores_paired(mesh)
+    return jax.shard_map(functools.partial(local, paired), mesh=mesh, in_specs=in_specs, out_specs=out_specs, check_vma=False)

time: 955 us -> 396 us (0.41)
  the two profiles are of different devices: /device:TPU:31 before, /device:TPU:9 now
where the time goes in v1:
time: 396 us; the launch traced here: 394 us
  waiting for transfers between devices  269 us (68%)
  other arithmetic  39.4 us (10%)
  starting transfers between devices  34.2 us (9%)
  local copies, waits for them, and re-layouts  33.5 us (8%)
  matrix products  16.3 us (4%)
    ppermute x9, waiting for transfers between devices, shifted(): lax.ppermute(value, axis, [(s, s + steps) for s in range(count - steps)])  265 us
    ppermute x9, starting transfers between devices, shifted(): lax.ppermute(value, axis, [(s, s + steps) for s in range(count - steps)])  24.1 us
    convert_element_type x2, other arithmetic, causal_conv(): return jax.nn.silu(summed).astype(jnp.bfloat16)  16.9 us
    unnamed x49, local copies, waits for them, and re-layouts  16.4 us
    dot_general x1, matrix products, mixing_part(): jnp.einsum('hij,jhp->ihp', mixing, x_group, preferred_element_type=jnp.fl...  9.69 us
    ppermute x3, starting transfers between devices, passed_along(): lax.ppermute(value, axis, [(source, source + steps) for source in range(l...  9.08 us
  transfers between devices with their start and end apart: 15, of which 9 were waited for; matrix products, arithmetic and copies ran while one was open for 7% of the time, Pallas kernels for 0%

profile of v1, /device:TPU:9, one launch (start us, length us, event | category | flops | bytes accessed | tf_op | source)
XLA Modules:
  0.0 394.3 jit_solution(9083275494033210982)
XLA Ops:
  0.8 3.7 collective-permute-start.1
  4.4 0.9 slice.90
  5.4 1.9 collective-permute-start
  7.3 0.7 slice.102
  8.0 3.5 collective-permute-start.2
  11.5 1.3 slice.114
  12.8 1.0 copy.39
  13.8 0.8 negate_multiply_fusion
  14.8 6.4 %copy.37 = bf16[256,8192]{0,1:T(8,128)(2,1)} copy(bf16[256,8192]{1,0:T(8,128)(2,1)} %param.13) | data formatting | bytes 8388608 | tf_op args[0]
  23.3 1.3 compare_convert_fusion.4
  24.6 0.8 multiply_bitcast_fusion
  25.9 1.1 copy.36
  26.9 16.7 %multiply_convert_fusion.5 = bf16[256,8192]{0,1:T(8,128)(2,1)S(1)} fusion(bf16[256,8192]{0,1:T(8,128)(2,1)} %copy.37, bf16[3,8192]{0,1:T(8,128)(2,1)S(1)} %copy.36, f32[8192]{0:T(1024)S(1)} %bitcast.46, f32[256]{0:T(256)S(1)} %get-tuple-element.89, f32[8192]{0:T(1024)S(1)} %bitcast.47, f32[256]{0:T(256)S(1)} %get-tuple-element.90, f32[8192]{0:T(1024)S(1)} %bitcast.45, ...), kind=kLoop, calls=%fused_computation.22 | loop fusion | flops 60817408 | bytes 8604672 | tf_op jit(solution)/shard_map/convert_element_type | solution.py:37
  43.6 5.2 %fusion.16 = f32[128,64,128]{2,1,0:T(8,128)S(1)} fusion(bf16[256,128,64]{0,2,1:T(8,128)(2,1)S(1)} %bitcast.41, f32[128,256]{1,0:T(8,128)S(1)} %copy.45, f32[256,128]{1,0:T(8,128)S(1)} %slice_convert_fusion, f32[128]{0:T(128)S(1)} %get-tuple-element.73), kind=kOutput, calls=%fused_computation.30 | convolution fusion | flops 546308096 | bytes 8651264 | tf_op jit(solution)/shard_map/while/body/eval_jaxpr/hjn,jhp->hpn/dot_general | solution.py:56
  48.8 1.6 constant_dynamic-slice_fusion
  50.4 1.1 copy-done.5
  52.0 3.3 collective-permute-done.3
  55.8 2.8 add_select_fusion
  58.6 3.1 collective-permute-start.9
  61.7 47.7 %collective-permute-done.9 = f32[64,64,128]{2,1,0:T(8,128)S(1)} collective-permute-done((f32[64,64,128]{2,1,0:T(8,128)S(1)}, f32[64,64,128]{2,1,0:T(8,128)S(1)}, u32[]{:S(2)}, u32[]{:S(2)}) %collective-permute-start.9) | collective-permute-done | bytes 2097184 | tf_op jit(solution)/shard_map/ppermute | solution.py:69
  109.4 1.9 collective-permute-start.10
  111.3 3.4 collective-permute-start.4
  114.7 44.5 %collective-permute-done.4 = f32[64]{0:T(128)S(1)} collective-permute-done((f32[64]{0:T(128)S(1)}, f32[64]{0:T(128)S(1)}, u32[]{:S(2)}, u32[]{:S(2)}) %collective-permute-start.4) | collective-permute-done | bytes 288 | tf_op jit(solution)/shard_map/ppermute | solution.py:69
  159.5 1.9 collective-permute-start.11
  161.5 1.9 collective-permute-start.5
  163.4 42.4 %collective-permute-done.5 = f32[64]{0:T(128)S(1)} collective-permute-done((f32[64]{0:T(128)S(1)}, f32[64]{0:T(128)S(1)}, u32[]{:S(2)}, u32[]{:S(2)}) %collective-permute-start.5) | collective-permute-done | bytes 288 | tf_op jit(solution)/shard_map/ppermute | solution.py:69
  205.8 1.7 collective-permute-done.11
  207.8 3.5 collective-permute-start.12
  211.3 1.9 collective-permute-start.6
  213.2 39.9 %collective-permute-done.6 = f32[64]{0:T(128)S(1)} collective-permute-done((f32[64]{0:T(128)S(1)}, f32[64]{0:T(128)S(1)}, u32[]{:S(2)}, u32[]{:S(2)}) %collective-permute-start.6) | collective-permute-done | bytes 288 | tf_op jit(solution)/shard_map/ppermute | solution.py:69
  253.1 1.1 collective-permute-done.12
  254.5 4.3 %collective-permute-start.13 = (f32[64,64,128]{2,1,0:T(8,128)S(1)}, f32[64,64,128]{2,1,0:T(8,128)S(1)}, u32[]{:S(2)}, u32[]{:S(2)}) collective-permute-start(f32[64,64,128]{2,1,0:T(8,128)S(1)} %multiply_add_fusion.1), channel_id=1, source_target_pairs={{0,16},{1,17},{2,18},{3,19},{4,20},{5,21},{6,22},{7,23},{8,24},{9,... | collective-permute-start | bytes 6291464 | tf_op jit(solution)/shard_map/ppermute | solution.py:69
  258.9 2.1 collective-permute-start.7
  261.0 87.9 %collective-permute-done.7 = f32[64]{0:T(128)S(1)} collective-permute-done((f32[64]{0:T(128)S(1)}, f32[64]{0:T(128)S(1)}, u32[]{:S(2)}, u32[]{:S(2)}) %collective-permute-start.7) | collective-permute-done | bytes 288 | tf_op jit(solution)/shard_map/ppermute | solution.py:69
  349.5 1.8 fusion.21
  351.7 0.8 copy.44
  352.5 6.4 %copy.49 = bf16[256,8192]{0,1:T(8,128)(2,1)} copy(bf16[256,8192]{1,0:T(8,128)(2,1)} %param.14) | data formatting | bytes 8388608 | tf_op args[1]
  358.9 1.4 mul.480
  360.2 1.5 mul.481
  362.4 1.5 fusion.23
  363.9 0.8 copy.42
  364.9 3.6 select_convert_fusion.1
  368.7 1.3 fusion.17
  370.0 0.9 copy-done.3
  370.9 9.7 %bitcast_add_fusion.1 = f32[256,128,64]{0,2,1:T(8,128)S(1)} fusion(f32[256,128,64]{0,2,1:T(8,128)S(1)} %fusion.17, f32[256,128]{0,1:T(8,128)S(1)} %copy.47, bf16[256,128,64]{0,2,1:T(8,128)(2,1)S(1)} %bitcast.42, f32[128,256]{1,0:T(8,128)S(1)} %copy-done.13, f32[128,256]{1,0:T(8,128)S(1)} %copy-done.14, f32[256,256]{1,0:T(8,128)S(1)} %fusion.29, ...), kind=kOutput, calls=%fused_computation.17 | convolution fusion | flops 1119879168 | bytes 21692416 | tf_op jit(solution)/shard_map/while/body/eval_jaxpr/hij,jhp->ihp/dot_general | solution.py:48
  380.7 4.7 %multiply_reduce_fusion = (f32[256]{0:T(256)S(1)}, f32[256,8192]{0,1:T(8,128)S(1)}) fusion(bf16[256,8192]{0,1:T(8,128)(2,1)S(1)} %copy-done.4, bf16[256,8192]{0,1:T(8,128)(2,1)S(1)} %copy-done.3, f32[8192]{0:T(1024)S(1)} %copy-done.11, f32[256,128,64]{0,2,1:T(8,128)S(1)} %bitcast_add_fusion.1), kind=kLoop, calls=%fused_computation.19 | loop fusion | flops 23068416 | bytes 25199616 | tf_op jit(solution)/shard_map/reduce_sum | solution.py:196
  385.4 2.6 multiply_convert_fusion.4
  388.0 6.3 %copy.50 = bf16[256,8192]{1,0:T(8,128)(2,1)} copy(bf16[256,8192]{0,1:T(8,128)(2,1)} %multiply_convert_fusion.4) | data formatting | bytes 8388608 | tf_op jit(solution)/shard_map/convert_element_type | solution.py:199
  (87 shorter events, 6.3 us)
Async XLA Ops:
  0.8 20.7 %collective-permute-start.1 = (bf16[3]{0:T(256)(128)(2,1)S(1)}, bf16[3]{0:T(256)(128)(2,1)S(1)}, u32[]{:S(2)}, u32[]{:S(2)}) collective-permute-start(bf16[3]{0:T(256)(128)(2,1)S(1)} %slice.92), channel_id=1, source_target_pairs={{0,1},{1,2},{2,3},{3,4},{4,5},{5,6},{6,7},{7,8},{8,9},{9,10},{10,1... | collective-permute-start | bytes 26 | tf_op jit(solution)/shard_map/ppermute | solution.py:21
  5.4 20.5 %collective-permute-start = (bf16[3,8192]{1,0:T(4,128)(2,1)S(1)}, bf16[3,8192]{1,0:T(4,128)(2,1)S(1)}, u32[]{:S(2)}, u32[]{:S(2)}) collective-permute-start(bf16[3,8192]{1,0:T(4,128)(2,1)S(1)} %slice.90), channel_id=1, source_target_pairs={{0,1},{1,2},{2,3},{3,4},{4,5},{5,6},{6,7},{7,8},{8,9},{9,10},{10,1... | collective-permute-start | bytes 147464 | tf_op jit(solution)/shard_map/ppermute | solution.py:21
  8.0 17.6 %collective-permute-start.2 = (bf16[3,256]{1,0:T(4,128)(2,1)S(1)}, bf16[3,256]{1,0:T(4,128)(2,1)S(1)}, u32[]{:S(2)}, u32[]{:S(2)}) collective-permute-start(bf16[3,256]{1,0:T(4,128)(2,1)S(1)} %slice.102), channel_id=1, source_target_pairs={{0,1},{1,2},{2,3},{3,4},{4,5},{5,6},{6,7},{7,8},{8,9},{9,10},{10,1... | collective-permute-start | bytes 4616 | tf_op jit(solution)/shard_map/ppermute | solution.py:21
  14.7 6.6 %copy-start.9 = (bf16[4,8192]{1,0:T(4,128)(2,1)S(1)}, bf16[4,8192]{1,0:T(4,128)(2,1)}, u32[]{:S(2)}) copy-start(bf16[4,8192]{1,0:T(4,128)(2,1)} %param.20) | copy-start | bytes 196612
  14.7 6.6 %copy-start.16 = (bf16[8192]{0:T(1024)(128)(2,1)S(1)}, bf16[8192]{0:T(1024)(128)(2,1)}, u32[]{:S(2)}) copy-start(bf16[8192]{0:T(1024)(128)(2,1)} %param.21) | copy-start | bytes 49156
  14.7 6.7 %copy-start.19 = (bf16[4,256]{1,0:T(4,128)(2,1)S(1)}, bf16[4,256]{1,0:T(4,128)(2,1)}, u32[]{:S(2)}) copy-start(bf16[4,256]{1,0:T(4,128)(2,1)} %param.22) | copy-start | bytes 6148
  14.7 6.7 %copy-start.22 = (bf16[256]{0:T(256)(128)(2,1)S(1)}, bf16[256]{0:T(256)(128)(2,1)}, u32[]{:S(2)}) copy-start(bf16[256]{0:T(256)(128)(2,1)} %param.23) | copy-start | bytes 1540
  14.7 7.3 %copy-start.18 = (s32[256]{0:T(256)S(1)}, s32[256]{0:T(256)}, u32[]{:S(2)}) copy-start(s32[256]{0:T(256)} %param.25) | copy-start | bytes 3076
  14.8 10.8 %copy-start.10 = (bf16[256,256]{1,0:T(8,128)(2,1)S(1)}, bf16[256,256]{1,0:T(8,128)(2,1)}, u32[]{:S(2)}) copy-start(bf16[256,256]{1,0:T(8,128)(2,1)} %param.15) | copy-start | bytes 393220
  43.6 5.2 %copy-start.2 = (bf16[256,8192]{0,1:T(8,128)(2,1)}, bf16[256,8192]{0,1:T(8,128)(2,1)S(1)}, u32[]{:S(2)}) copy-start(bf16[256,8192]{0,1:T(8,128)(2,1)S(1)} %multiply_convert_fusion.5) | copy-start | bytes 12582916
  48.8 2.6 copy-start.5
  51.5 4.4 %collective-permute-start.8 = (f32[64,64,128]{2,1,0:T(8,128)}, f32[64,64,128]{2,1,0:T(8,128)S(1)}, u32[]{:S(2)}, u32[]{:S(2)}) collective-permute-start(f32[64,64,128]{2,1,0:T(8,128)} %constant_dynamic-slice_fusion), channel_id=1, source_target_pairs={{0,1},{1,0},{2,3},{3,2},{4,5},{5,4},{6,7},{7,6},{8,9},{9,8},{10,11... | collective-permute-start | bytes 6291464 | tf_op jit(solution)/shard_map/ppermute | solution.py:93
  51.5 3.8 collective-permute-start.3
  55.8 103.7 %copy-start = (f32[64,64,128]{2,1,0:T(8,128)}, f32[64,64,128]{2,1,0:T(8,128)S(1)}, u32[]{:S(2)}) copy-start(f32[64,64,128]{2,1,0:T(8,128)S(1)} %collective-permute-done.8) | copy-start | bytes 6291460
  58.6 50.8 %collective-permute-start.9 = (f32[64,64,128]{2,1,0:T(8,128)S(1)}, f32[64,64,128]{2,1,0:T(8,128)S(1)}, u32[]{:S(2)}, u32[]{:S(2)}) collective-permute-start(f32[64,64,128]{2,1,0:T(8,128)S(1)} %add_select_fusion), channel_id=1, source_target_pairs={{0,2},{1,3},{2,4},{3,5},{4,6},{5,7},{6,8},{7,9},{8,10},{9,11},{10,... | collective-permute-start | bytes 6291464 | tf_op jit(solution)/shard_map/ppermute | solution.py:69
  109.4 49.9 %collective-permute-start.10 = (f32[64,64,128]{2,1,0:T(8,128)S(1)}, f32[64,64,128]{2,1,0:T(8,128)S(1)}, u32[]{:S(2)}, u32[]{:S(2)}) collective-permute-start(f32[64,64,128]{2,1,0:T(8,128)S(1)} %collective-permute-done.9), channel_id=1, source_target_pairs={{0,2},{1,3},{2,4},{3,5},{4,6},{5,7},{6,8},{7,9},{8,10},{9,11},{10,... | collective-permute-start | bytes 6291464 | tf_op jit(solution)/shard_map/ppermute | solution.py:69
  111.3 47.9 %collective-permute-start.4 = (f32[64]{0:T(128)S(1)}, f32[64]{0:T(128)S(1)}, u32[]{:S(2)}, u32[]{:S(2)}) collective-permute-start(f32[64]{0:T(128)S(1)} %get-tuple-element.63), channel_id=1, source_target_pairs={{0,2},{1,3},{2,4},{3,5},{4,6},{5,7},{6,8},{7,9},{8,10},{9,11},{10,... | collective-permute-start | bytes 776 | tf_op jit(solution)/shard_map/ppermute | solution.py:69
  159.5 48.0 %collective-permute-start.11 = (f32[64,64,128]{2,1,0:T(8,128)S(1)}, f32[64,64,128]{2,1,0:T(8,128)S(1)}, u32[]{:S(2)}, u32[]{:S(2)}) collective-permute-start(f32[64,64,128]{2,1,0:T(8,128)S(1)} %multiply_add_fusion.3), channel_id=1, source_target_pairs={{0,4},{1,5},{2,6},{3,7},{4,8},{5,9},{6,10},{7,11},{8,12},{9,13},{1... | collective-permute-start | bytes 6291464 | tf_op jit(solution)/shard_map/ppermute | solution.py:69
  161.5 44.3 %collective-permute-start.5 = (f32[64]{0:T(128)S(1)}, f32[64]{0:T(128)S(1)}, u32[]{:S(2)}, u32[]{:S(2)}) collective-permute-start(f32[64]{0:T(128)S(1)} %collective-permute-done.4), channel_id=1, source_target_pairs={{0,2},{1,3},{2,4},{3,5},{4,6},{5,7},{6,8},{7,9},{8,10},{9,11},{10,... | collective-permute-start | bytes 776 | tf_op jit(solution)/shard_map/ppermute | solution.py:69
  207.8 141.7 %copy-start.1 = (f32[64,64,128]{2,1,0:T(8,128)S(1)}, f32[64,64,128]{2,1,0:T(8,128)}, u32[]{:S(2)}) copy-start(f32[64,64,128]{2,1,0:T(8,128)} %copy-done) | copy-start | bytes 6291460
  207.8 141.7 %copy-start.6 = (f32[128,64,128]{2,1,0:T(8,128)S(1)}, f32[128,64,128]{2,1,0:T(8,128)}, u32[]{:S(2)}) copy-start(f32[128,64,128]{2,1,0:T(8,128)} %copy-done.5) | copy-start | bytes 12582916
  207.8 46.4 %collective-permute-start.12 = (f32[64,64,128]{2,1,0:T(8,128)S(1)}, f32[64,64,128]{2,1,0:T(8,128)S(1)}, u32[]{:S(2)}, u32[]{:S(2)}) collective-permute-start(f32[64,64,128]{2,1,0:T(8,128)S(1)} %multiply_add_fusion.2), channel_id=1, source_target_pairs={{0,8},{1,9},{2,10},{3,11},{4,12},{5,13},{6,14},{7,15},{8,16},{9,17... | collective-permute-start | bytes 6291464 | tf_op jit(solution)/shard_map/ppermute | solution.py:69
  211.3 41.8 %collective-permute-start.6 = (f32[64]{0:T(128)S(1)}, f32[64]{0:T(128)S(1)}, u32[]{:S(2)}, u32[]{:S(2)}) collective-permute-start(f32[64]{0:T(128)S(1)} %mul.451), channel_id=1, source_target_pairs={{0,4},{1,5},{2,6},{3,7},{4,8},{5,9},{6,10},{7,11},{8,12},{9,13},{1... | collective-permute-start | bytes 776 | tf_op jit(solution)/shard_map/ppermute | solution.py:69
  254.5 94.4 %collective-permute-start.13 = (f32[64,64,128]{2,1,0:T(8,128)S(1)}, f32[64,64,128]{2,1,0:T(8,128)S(1)}, u32[]{:S(2)}, u32[]{:S(2)}) collective-permute-start(f32[64,64,128]{2,1,0:T(8,128)S(1)} %multiply_add_fusion.1), channel_id=1, source_target_pairs={{0,16},{1,17},{2,18},{3,19},{4,20},{5,21},{6,22},{7,23},{8,24},{9,... | collective-permute-start | bytes 6291464 | tf_op jit(solution)/shard_map/ppermute | solution.py:69
  258.9 90.1 %collective-permute-start.7 = (f32[64]{0:T(128)S(1)}, f32[64]{0:T(128)S(1)}, u32[]{:S(2)}, u32[]{:S(2)}) collective-permute-start(f32[64]{0:T(128)S(1)} %mul.452), channel_id=1, source_target_pairs={{0,8},{1,9},{2,10},{3,11},{4,12},{5,13},{6,14},{7,15},{8,16},{9,17... | collective-permute-start | bytes 776 | tf_op jit(solution)/shard_map/ppermute | solution.py:69
  261.0 88.0 %copy-start.20 = (f32[64]{0:T(128)}, f32[64]{0:T(128)S(1)}, u32[]{:S(2)}) copy-start(f32[64]{0:T(128)S(1)} %broadcast_select_fusion) | copy-start | bytes 772
  348.9 0.5 copy-start.21
  349.5 1.8 copy-start.7
  351.2 13.7 %collective-permute-start.14 = (bf16[64,64,128]{2,1,0:T(8,128)(2,1)}, bf16[64,64,128]{2,1,0:T(8,128)(2,1)S(1)}, u32[]{:S(2)}, u32[]{:S(2)}) collective-permute-start(bf16[64,64,128]{2,1,0:T(8,128)(2,1)} %fusion.21), channel_id=1, source_target_pairs={{0,1},{1,0},{2,3},{3,2},{4,5},{5,4},{6,7},{7,6},{8,9},{9,8},{10,11... | collective-permute-start | bytes 3145736 | tf_op jit(solution)/shard_map/ppermute | solution.py:104
  352.5 9.3 %copy-start.17 = (bf16[8192]{0:T(1024)(128)(2,1)S(1)}, bf16[8192]{0:T(1024)(128)(2,1)}, u32[]{:S(2)}) copy-start(bf16[8192]{0:T(1024)(128)(2,1)} %param.24) | copy-start | bytes 49156
  352.5 12.1 %copy-start.8 = (f32[256,128]{1,0:T(8,128)S(1)}, f32[256,128]{1,0:T(8,128)}, u32[]{:S(2)}) copy-start(f32[256,128]{1,0:T(8,128)} %get-tuple-element.59) | copy-start | bytes 393220
  368.7 2.2 copy-start.3
  368.7 2.2 copy-start.13
  368.7 2.2 copy-start.14
  368.7 2.2 copy-start.15
  370.9 9.7 %copy-start.4 = (bf16[256,8192]{0,1:T(8,128)(2,1)S(1)}, bf16[256,8192]{0,1:T(8,128)(2,1)}, u32[]{:S(2)}) copy-start(bf16[256,8192]{0,1:T(8,128)(2,1)} %copy.49) | copy-start | bytes 12582916
  370.9 9.7 %copy-start.11 = (f32[8192]{0:T(1024)S(1)}, f32[8192]{0:T(1024)}, u32[]{:S(2)}) copy-start(f32[8192]{0:T(1024)} %mul.481) | copy-start | bytes 98308
  380.6 4.7 %copy-start.12 = (f32[8192]{0:T(1024)S(1)}, f32[8192]{0:T(1024)}, u32[]{:S(2)}) copy-start(f32[8192]{0:T(1024)} %convert_element_type.131) | copy-start | bytes 98308

commit v2 on v1

--- a/solution.py
+++ b/solution.py
@@ -69,21 +69,79 @@
     return lax.ppermute(value, axis, [(s, s + steps) for s in range(count - steps)])
 
 
-def scan_rounds(carry, axis, stride, span, count):
+def scan_round(transmit, state, axis, shift, count):
+    far_t, far_s = shifted((transmit, state), axis, shift, count)
+    return transmit * far_t, transmit[:, None, None] * far_s + state
+
+
+def scan_rounds(carry, axis, stride, span, count, far):
+    near, needed, rider = far
+    carry, rider = lax.optimization_barrier((carry, rider))
+    far[2] = rider
     transmit, state = shifted(carry, axis, stride, count)
     covered = 1
-    while covered < span - 1:
-        far_t, far_s = shifted((transmit, state), axis, stride * covered, count)
-        state = transmit[:, None, None] * far_s + state
-        transmit = transmit * far_t
+    while covered < min(span - 1, near):
+        transmit, state = scan_round(transmit, state, axis, stride * covered, count)
         covered *= 2
+    if covered < span - 1:
+
+        def rest(carried):
+            t, s = carried
+            reach = covered
+            while reach < span - 1:
+                t, s = scan_round(t, s, axis, stride * reach, count)
+                reach *= 2
+            return t, s
+
+        transmit, state = lax.cond(needed, rest, lambda carried: carried, (transmit, state))
     return state
 
 
-def device_entry(dev_transmit, dev_state, paired):
+def gather_small(value, axis):
+    count = lax.axis_size(axis)
+    if count & (count - 1):
+        return lax.all_gather(value, axis, tiled=True)
+    place = lax.axis_index(axis)
+    size = 1
+    while size < count:
+        other = lax.ppermute(value, axis, [(s, s ^ size) for s in range(count)])
+        value = jnp.where(
+            (place & size) == 0,
+            jnp.concatenate([value, other]),
+            jnp.concatenate([other, value]),
+        )
+        size *= 2
+    return value
+
+
+def long_runs(last_id, paired, tok_rows):
+    count = lax.axis_size("ctx")
+    longest = (count * tok_rows // 4 - 1) // tok_rows
+    group = 2 if paired else 1
+    near = 1
+    while near * group <= longest:
+        near *= 2
+    window = near * group
+    ids = gather_small(last_id, "ctx")
+    joined = jnp.concatenate([jnp.zeros((1,), jnp.int32), (ids[1:] == ids[:-1]).astype(jnp.int32)])
+    if window > count:
+        return near, jnp.zeros((), jnp.bool_)
+    breaks = jnp.cumsum(1 - joined)
+    ahead = jnp.concatenate([jnp.zeros((1,), jnp.int32), breaks[:-window]])
+    return near, jnp.any(breaks[window - 1 :] - ahead == 0)
+
+
+def blockwise(f, items):
+    if jax.tree.leaves(items)[0].shape[0] == 1:
+        out = f(jax.tree.map(lambda a: a[0], items))
+        return jax.tree.map(lambda a: a[None], out)
+    return lax.map(f, items)
+
+
+def device_entry(dev_transmit, dev_state, paired, far):
     count = lax.axis_size("ctx")
     if not paired:
-        return scan_rounds((dev_transmit, dev_state), "ctx", 1, count, count)
+        return scan_rounds((dev_transmit, dev_state), "ctx", 1, count, count, far)
     heads = dev_state.shape[0]
     half = heads // 2
     core = lax.axis_index("ctx") % 2
@@ -97,7 +155,7 @@
     first = core == 0
     chip_s = jnp.where(first, peer_t[:, None, None] * mine_s + other_s, mine_t[:, None, None] * other_s + mine_s)
     chip_t = mine_t * peer_t
-    entering = scan_rounds((chip_t, chip_s), "ctx", 2, count // 2, count)
+    entering = scan_rounds((chip_t, chip_s), "ctx", 2, count // 2, count, far)
     lead_t = jnp.where(first, mine_t, peer_t)
     lead_s = jnp.where(first, mine_s, other_s)
     second = lead_t[:, None, None] * entering + lead_s
@@ -108,7 +166,7 @@
     return jnp.concatenate([low, high], axis=0)
 
 
-def chain_states(block_states, transmits, paired):
+def chain_states(block_states, transmits, paired, far):
 
     def advance(carried, item):
         passing, state_now = carried
@@ -120,7 +178,7 @@
 
     start = (jnp.ones_like(transmits[0]), jnp.zeros_like(block_states[0]))
     finals, befores = lax.scan(advance, start, (transmits, block_states))
-    entering_dev = device_entry(finals[0], finals[1], paired)
+    entering_dev = device_entry(finals[0], finals[1], paired, far)
     return befores[0][:, :, None, None] * entering_dev[None] + befores[1]
 
 
@@ -168,27 +226,28 @@
     x_blocks = x_conv.reshape(block_count, GROUP, head_count, HEAD_DIM)
     b_blocks = bc_conv[:, :STATE].reshape(block_count, GROUP, STATE)
     c_blocks = bc_conv[:, STATE:].reshape(block_count, GROUP, STATE)
-    everything = (x_blocks, b_blocks, c_blocks, step_blocks, cum_decay, seg_blocks, seg_before)
-
-    def both_of(item):
-        x_group, b_group, c_group, steps_here, decay_here, segment, before = item
-        block_state, transmit = state_part(
-            x_group, b_group, steps_here, decay_here, segment, before
-        )
-        return (
-            mixing_part(x_group, b_group, c_group, steps_here, decay_here, segment),
-            block_state,
-            transmit,
-        )
-
-    y_intra, block_states, transmits = lax.map(both_of, everything)
-    entering = chain_states(block_states, transmits, paired)
+
+    def state_of(item):
+        x_group, b_group, steps_here, decay_here, segment, before = item
+        return state_part(x_group, b_group, steps_here, decay_here, segment, before)
+
+    def intra_of(item):
+        x_group, b_group, c_group, steps_here, decay_here, segment = item
+        return mixing_part(x_group, b_group, c_group, steps_here, decay_here, segment)
+
+    block_states, transmits = blockwise(
+        state_of, (x_blocks, b_blocks, step_blocks, cum_decay, seg_blocks, seg_before)
+    )
+    intra_items = (x_blocks, b_blocks, c_blocks, step_blocks, cum_decay, seg_blocks)
+    far = [*long_runs(segment_ids[tok_rows - 1 :], paired, tok_rows), intra_items]
+    entering = chain_states(block_states, transmits, paired, far)
+    y_intra = blockwise(intra_of, far[2])
 
     def enter_of(item):
         c_group, decay_here, segment, before, entering_here = item
         return entry_part(c_group, entering_here, decay_here, segment, before)
 
-    y_state = lax.map(enter_of, (c_blocks, cum_decay, seg_blocks, seg_before, entering))
+    y_state = blockwise(enter_of, (c_blocks, cum_decay, seg_blocks, seg_before, entering))
     y_blocks = y_intra + y_state
     x_heads = x_conv.reshape(tok_rows, head_count, HEAD_DIM).astype(jnp.float32)
     y_total = y_blocks.reshape(tok_rows, head_count, HEAD_DIM) + skip_d[None, :, None] * x_heads

time: 396 us -> 267 us (0.67)
  waiting for transfers between devices: 269 us -> 134 us
  local copies, waits for them, and re-layouts: 33.5 us -> 28.5 us
  matrix products: 16.3 us -> 21 us
    ppermute x9 -> x6, waiting for transfers between devices: 265 us -> 96.1 us  [shifted(): lax.ppermute(value, axis, [(s, s + steps) for s in range(count - steps)])]
    ppermute x0 -> x5, waiting for transfers between devices: none -> 34.4 us  [gather_small(): other = lax.ppermute(value, axis, [(s, s ^ size) for s in range(count)])]
    ppermute x9 -> x6, starting transfers between devices: 24.1 us -> 15.1 us  [shifted(): lax.ppermute(value, axis, [(s, s + steps) for s in range(count - steps)])]
    ppermute x0 -> x5, starting transfers between devices: none -> 7.08 us  [gather_small(): other = lax.ppermute(value, axis, [(s, s ^ size) for s in range(count)])]
    ppermute x1, starting transfers between devices: 0.49 us -> 5.78 us  [device_entry(): back = lax.ppermute(jnp.where(first, second, entering), 'ctx', swap)]
    unnamed x49 -> x35, local copies, waits for them, and re-layouts: 16.4 us -> 15 us
  transfers between devices with their start and end apart: 15 -> 17, of which waited for: 9 -> 9; matrix products, arithmetic and copies ran while one was open for 7% -> 14% of each run, Pallas kernels for 0% -> 0%
where the time goes in v2:
time: 267 us; the launch traced here: 265 us
  waiting for transfers between devices  134 us (50%)
  other arithmetic  41.2 us (15%)
  starting transfers between devices  37.6 us (14%)
  local copies, waits for them, and re-layouts  28.5 us (11%)
  matrix products  21 us (8%)
    ppermute x6, waiting for transfers between devices, shifted(): lax.ppermute(value, axis, [(s, s + steps) for s in range(count - steps)])  96.1 us
    ppermute x5, waiting for transfers between devices, gather_small(): other = lax.ppermute(value, axis, [(s, s ^ size) for s in range(count)])  34.4 us
    convert_element_type x2, other arithmetic, causal_conv(): return jax.nn.silu(summed).astype(jnp.bfloat16)  16.9 us
    ppermute x6, starting transfers between devices, shifted(): lax.ppermute(value, axis, [(s, s + steps) for s in range(count - steps)])  15.1 us
    unnamed x35, local copies, waits for them, and re-layouts  15 us
    dot_general x1, matrix products, mixing_part(): jnp.einsum('hij,jhp->ihp', mixing, x_group, preferred_element_type=jnp.fl...  10.8 us
    ppermute x3, starting transfers between devices, passed_along(): lax.ppermute(value, axis, [(source, source + steps) for source in range(l...  9.08 us
    ppermute x5, starting transfers between devices, gather_small(): other = lax.ppermute(value, axis, [(s, s ^ size) for s in range(count)])  7.08 us
  transfers between devices with their start and end apart: 17, of which 9 were waited for; matrix products, arithmetic and copies ran while one was open for 14% of the time, Pallas kernels for 0%

profile of v2, /device:TPU:9, one launch (start us, length us, event | category | flops | bytes accessed | tf_op | source)
XLA Modules:
  0.0 265.3 jit_solution(6422711393744093828)
XLA Ops:
  0.0 0.7 convert.20
  0.8 3.7 %collective-permute-start.3 = (bf16[3]{0:T(256)(128)(2,1)S(1)}, bf16[3]{0:T(256)(128)(2,1)S(1)}, u32[]{:S(2)}, u32[]{:S(2)}) collective-permute-start(bf16[3]{0:T(256)(128)(2,1)S(1)} %slice.110), channel_id=1, source_target_pairs={{0,1},{1,2},{2,3},{3,4},{4,5},{5,6},{6,7},{7,8},{8,9},{9,10},{10,1... | collective-permute-start | bytes 26 | tf_op jit(solution)/shard_map/ppermute | solution.py:21
  4.4 0.7 slice.124
  5.1 1.9 collective-permute-start.6
  7.0 0.9 slice.113
  8.0 3.5 %collective-permute-start.5 = (bf16[3,8192]{1,0:T(4,128)(2,1)S(1)}, bf16[3,8192]{1,0:T(4,128)(2,1)S(1)}, u32[]{:S(2)}, u32[]{:S(2)}) collective-permute-start(bf16[3,8192]{1,0:T(4,128)(2,1)S(1)} %slice.113), channel_id=1, source_target_pairs={{0,1},{1,2},{2,3},{3,4},{4,5},{5,6},{6,7},{7,8},{8,9},{9,10},{10,1... | collective-permute-start | bytes 147464 | tf_op jit(solution)/shard_map/ppermute | solution.py:21
  11.5 1.3 slice.109
  12.9 1.0 copy.39
  13.9 0.8 negate_multiply_fusion
  14.9 6.4 %copy.43 = bf16[256,8192]{0,1:T(8,128)(2,1)} copy(bf16[256,8192]{1,0:T(8,128)(2,1)} %param.15) | data formatting | bytes 8388608 | tf_op args[0]
  21.6 0.6 slice.111
  23.6 1.4 compare_convert_fusion.4
  25.7 1.1 copy.42
  26.8 16.7 %multiply_convert_fusion.5 = bf16[256,8192]{0,1:T(8,128)(2,1)S(1)} fusion(bf16[256,8192]{0,1:T(8,128)(2,1)} %copy.43, bf16[3,8192]{0,1:T(8,128)(2,1)S(1)} %copy.42, f32[8192]{0:T(1024)S(1)} %bitcast.73, f32[256]{0:T(256)S(1)} %get-tuple-element.77, f32[8192]{0:T(1024)S(1)} %bitcast.74, f32[256]{0:T(256)S(1)} %get-tuple-element.78, f32[8192]{0:T(1024)S(1)} %bitcast.72, ...), kind=kLoop, calls=%fused_computation.24 | loop fusion | flops 60817408 | bytes 8604672 | tf_op jit(solution)/shard_map/convert_element_type | solution.py:37
  43.5 5.2 %fusion.17 = f32[128,64,128]{2,1,0:T(8,128)S(1)} fusion(bf16[256,128,64]{0,2,1:T(8,128)(2,1)S(1)} %bitcast.66, f32[128,256]{1,0:T(8,128)S(1)} %copy.45, f32[256,128]{1,0:T(8,128)S(1)} %get-tuple-element.71, f32[128]{0:T(128)S(1)} %get-tuple-element.65), kind=kOutput, calls=%fused_computation.33 | convolution fusion | flops 546308096 | bytes 8651264 | tf_op jit(solution)/shard_map/hjn,jhp->hpn/dot_general | solution.py:56
  48.7 1.6 constant_dynamic-slice_fusion
  50.3 1.1 copy-done.5
  51.9 3.3 %collective-permute-done.4 = f32[128]{0:T(128)S(1)} collective-permute-done((f32[128]{0:T(128)S(1)}, f32[128]{0:T(128)S(1)}, u32[]{:S(2)}, u32[]{:S(2)}) %collective-permute-start.4) | collective-permute-done | bytes 544 | tf_op jit(solution)/shard_map/ppermute | solution.py:151
  55.7 2.8 %add_select_fusion = f32[64,64,128]{2,1,0:T(8,128)S(1)} fusion(f32[64,64,128]{2,1,0:T(8,128)S(1)} %collective-permute-done.7, f32[128,64,128]{2,1,0:T(8,128)} %copy-done.5, s32[]{:T(128)S(6)} %select_n.101, f32[64]{0:T(128)S(1)} %get-tuple-element.62, f32[64]{0:T(128)S(1)} %get-tuple-element.61, pred[]{:T(512)S(6)} %eq.73), kind=kLoop, calls=%fused_computation.42 | loop fusion | flops 2621440 | bytes 6291973 | tf_op jit(solution)/shard_map/jit(_where)/select_n | solution.py:156
  58.5 3.1 %collective-permute-start.15 = (f32[64,64,128]{2,1,0:T(8,128)S(1)}, f32[64,64,128]{2,1,0:T(8,128)S(1)}, u32[]{:S(2)}, u32[]{:S(2)}) collective-permute-start(f32[64,64,128]{2,1,0:T(8,128)S(1)} %add_select_fusion), channel_id=1, source_target_pairs={{0,2},{1,3},{2,4},{3,5},{4,6},{5,7},{6,8},{7,9},{8,10},{9,11},{10,... | collective-permute-start | bytes 6291464 | tf_op jit(solution)/shard_map/ppermute | solution.py:69
  61.6 47.7 %collective-permute-done.15 = f32[64,64,128]{2,1,0:T(8,128)S(1)} collective-permute-done((f32[64,64,128]{2,1,0:T(8,128)S(1)}, f32[64,64,128]{2,1,0:T(8,128)S(1)}, u32[]{:S(2)}, u32[]{:S(2)}) %collective-permute-start.15) | collective-permute-done | bytes 2097184 | tf_op jit(solution)/shard_map/ppermute | solution.py:69
  109.3 1.9 collective-permute-start.16
  111.2 3.4 %collective-permute-start.13 = (f32[64]{0:T(128)S(1)}, f32[64]{0:T(128)S(1)}, u32[]{:S(2)}, u32[]{:S(2)}) collective-permute-start(f32[64]{0:T(128)S(1)} %mul.373), channel_id=1, source_target_pairs={{0,2},{1,3},{2,4},{3,5},{4,6},{5,7},{6,8},{7,9},{8,10},{9,11},{10,... | collective-permute-start | bytes 776 | tf_op jit(solution)/shard_map/ppermute | solution.py:69
  114.6 44.5 %collective-permute-done.13 = f32[64]{0:T(128)S(1)} collective-permute-done((f32[64]{0:T(128)S(1)}, f32[64]{0:T(128)S(1)}, u32[]{:S(2)}, u32[]{:S(2)}) %collective-permute-start.13) | collective-permute-done | bytes 288 | tf_op jit(solution)/shard_map/ppermute | solution.py:69
  159.2 1.6 multiply_add_fusion.3
  160.8 1.9 collective-permute-start.17
  162.7 2.0 collective-permute-start.8
  164.7 6.4 %copy.54 = bf16[256,8192]{0,1:T(8,128)(2,1)} copy(bf16[256,8192]{1,0:T(8,128)(2,1)} %param.16) | data formatting | bytes 8388608 | tf_op args[1]
  171.3 1.4 broadcast_select_fusion.1
  172.7 2.8 %collective-permute-done.9 = s32[2]{0:T(128)S(1)} collective-permute-done((s32[2]{0:T(128)S(1)}, s32[2]{0:T(128)S(1)}, u32[]{:S(2)}, u32[]{:S(2)}) %collective-permute-start.9) | collective-permute-done | bytes 40 | tf_op jit(solution)/shard_map/ppermute | solution.py:107
  175.5 2.8 %collective-permute-start.10 = (s32[4]{0:T(128)S(1)}, s32[4]{0:T(128)S(1)}, u32[]{:S(2)}, u32[]{:S(2)}) collective-permute-start(s32[4]{0:T(128)S(1)} %broadcast_select_fusion.2), channel_id=1, source_target_pairs={{0,4},{1,5},{2,6},{3,7},{4,0},{5,1},{6,2},{7,3},{8,12},{9,13},{10,... | collective-permute-start | bytes 56 | tf_op jit(solution)/shard_map/ppermute | solution.py:107
  178.3 28.0 %collective-permute-done.10 = s32[4]{0:T(128)S(1)} collective-permute-done((s32[4]{0:T(128)S(1)}, s32[4]{0:T(128)S(1)}, u32[]{:S(2)}, u32[]{:S(2)}) %collective-permute-start.10) | collective-permute-done | bytes 48 | tf_op jit(solution)/shard_map/ppermute | solution.py:107
  206.4 2.8 %collective-permute-done.11 = s32[8]{0:T(128)S(1)} collective-permute-done((s32[8]{0:T(128)S(1)}, s32[8]{0:T(128)S(1)}, u32[]{:S(2)}, u32[]{:S(2)}) %collective-permute-start.11) | collective-permute-done | bytes 64 | tf_op jit(solution)/shard_map/ppermute | solution.py:107
  209.2 2.3 collective-permute-start.12
  211.6 0.9 collective-permute-done.12
  213.1 0.8 compare_reduce_fusion
  214.8 1.9 collective-permute-start.14
  217.0 3.9 %collective-permute-done.14 = f32[64]{0:T(128)S(1)} collective-permute-done((f32[64]{0:T(128)S(1)}, f32[64]{0:T(128)S(1)}, u32[]{:S(2)}, u32[]{:S(2)}) %collective-permute-start.14) | collective-permute-done | bytes 288 | tf_op jit(solution)/shard_map/ppermute | solution.py:69
  220.9 2.9 %collective-permute-start.18 = (f32[64]{0:T(128)S(1)}, f32[64]{0:T(128)S(1)}, u32[]{:S(2)}, u32[]{:S(2)}) collective-permute-start(f32[64]{0:T(128)S(1)} %mul.437), channel_id=1, source_target_pairs={{0,4},{1,5},{2,6},{3,7},{4,8},{5,9},{6,10},{7,11},{8,12},{9,13},{1... | collective-permute-start | bytes 776 | tf_op jit(solution)/shard_map/ppermute | solution.py:69
  223.8 2.5 multiply_add_fusion.2
  226.5 2.8 %fusion.21 = bf16[64,64,128]{2,1,0:T(8,128)(2,1)S(1)} fusion(f32[64,64,128]{2,1,0:T(8,128)S(1)} %get-tuple-element.85, f32[64,64,128]{2,1,0:T(8,128)} %copy-done, f32[128,64,128]{2,1,0:T(8,128)} %copy-done.5, s32[]{:T(128)S(6)} %select_n.101, f32[64]{0:T(128)S(1)} %get-tuple-element.60, pred[]{:T(512)S(6)} %eq.73), kind=kLoop, calls=%fused_computation.43 | loop fusion | flops 2097152 | bytes 7340293 | tf_op jit(solution)/shard_map/jit(_where)/select_n | solution.py:162
  229.4 5.8 %collective-permute-start.19 = (bf16[64,64,128]{2,1,0:T(8,128)(2,1)S(1)}, bf16[64,64,128]{2,1,0:T(8,128)(2,1)S(1)}, u32[]{:S(2)}, u32[]{:S(2)}) collective-permute-start(bf16[64,64,128]{2,1,0:T(8,128)(2,1)S(1)} %fusion.21), channel_id=1, source_target_pairs={{0,1},{1,0},{2,3},{3,2},{4,5},{5,4},{6,7},{7,6},{8,9},{9,8},{10,11... | collective-permute-start | bytes 3145736 | tf_op jit(solution)/shard_map/ppermute | solution.py:162
  235.1 10.8 %fusion = f32[128,64,256]{2,1,0:T(8,128)} fusion(f32[128,256]{1,0:T(8,128)S(1)} %copy.49, f32[128,256]{1,0:T(8,128)S(1)} %copy.47, f32[256,256]{1,0:T(8,128)S(1)} %fusion.29, pred[256,256]{1,0:T(8,128)(4,1)S(1)} %fusion.23, bf16[1,256,128,64]{1,3,2,0:T(8,128)(2,1)S(1)} %bitcast.67), kind=kOutput, calls=%fused_computation.3 | convolution fusion | flops 1115684864 | bytes 13172736 | tf_op jit(solution)/shard_map/hij,jhp->ihp/dot_general | solution.py:48
  246.0 0.8 select_convert_fusion.1
  246.9 4.8 %bitcast_add_fusion.1 = f32[256,128,64]{0,2,1:T(8,128)S(1)} fusion(f32[128,64,256]{2,1,0:T(8,128)} %fusion, f32[256,128]{0,1:T(8,128)S(1)} %copy.52, bf16[64,64,128]{2,1,0:T(8,128)(2,1)S(1)} %select_convert_fusion, bf16[64,64,128]{2,1,0:T(8,128)(2,1)S(1)} %get-tuple-element.58, bf16[256,256]{1,0:T(8,128)(2,1)S(1)} %multiply_convert_fusion.8), kind=kOutput, calls=%fused_computation.19 | convolution fusion | flops 545259520 | bytes 19070976 | tf_op jit(solution)/shard_map/in,hpn->ihp/dot_general | solution.py:64
  251.7 4.7 %multiply_reduce_fusion = (f32[256]{0:T(256)S(1)}, f32[256,8192]{0,1:T(8,128)S(1)}) fusion(bf16[256,8192]{0,1:T(8,128)(2,1)S(1)} %copy-done.4, bf16[256,8192]{0,1:T(8,128)(2,1)S(1)} %copy-done.3, f32[8192]{0:T(1024)S(1)} %mul.449, f32[256,128,64]{0,2,1:T(8,128)S(1)} %bitcast_add_fusion.1), kind=kLoop, calls=%fused_computation.21 | loop fusion | flops 23068416 | bytes 25199616 | tf_op jit(solution)/shard_map/reduce_sum | solution.py:255
  256.4 2.6 multiply_convert_fusion.4
  259.0 6.3 %copy.55 = bf16[256,8192]{1,0:T(8,128)(2,1)} copy(bf16[256,8192]{0,1:T(8,128)(2,1)} %multiply_convert_fusion.4) | data formatting | bytes 8388608 | tf_op jit(solution)/shard_map/convert_element_type | solution.py:258
  (88 shorter events, 4.1 us)
Async XLA Ops:
  0.8 20.8 %collective-permute-start.3 = (bf16[3]{0:T(256)(128)(2,1)S(1)}, bf16[3]{0:T(256)(128)(2,1)S(1)}, u32[]{:S(2)}, u32[]{:S(2)}) collective-permute-start(bf16[3]{0:T(256)(128)(2,1)S(1)} %slice.110), channel_id=1, source_target_pairs={{0,1},{1,2},{2,3},{3,4},{4,5},{5,6},{6,7},{7,8},{8,9},{9,10},{10,1... | collective-permute-start | bytes 26 | tf_op jit(solution)/shard_map/ppermute | solution.py:21
  5.1 20.3 %collective-permute-start.6 = (bf16[3,256]{1,0:T(4,128)(2,1)S(1)}, bf16[3,256]{1,0:T(4,128)(2,1)S(1)}, u32[]{:S(2)}, u32[]{:S(2)}) collective-permute-start(bf16[3,256]{1,0:T(4,128)(2,1)S(1)} %slice.124), channel_id=1, source_target_pairs={{0,1},{1,2},{2,3},{3,4},{4,5},{5,6},{6,7},{7,8},{8,9},{9,10},{10,1... | collective-permute-start | bytes 4616 | tf_op jit(solution)/shard_map/ppermute | solution.py:21
  8.0 17.7 %collective-permute-start.5 = (bf16[3,8192]{1,0:T(4,128)(2,1)S(1)}, bf16[3,8192]{1,0:T(4,128)(2,1)S(1)}, u32[]{:S(2)}, u32[]{:S(2)}) collective-permute-start(bf16[3,8192]{1,0:T(4,128)(2,1)S(1)} %slice.113), channel_id=1, source_target_pairs={{0,1},{1,2},{2,3},{3,4},{4,5},{5,6},{6,7},{7,8},{8,9},{9,10},{10,1... | collective-permute-start | bytes 147464 | tf_op jit(solution)/shard_map/ppermute | solution.py:21
  14.8 6.6 %copy-start.12 = (bf16[4,256]{1,0:T(4,128)(2,1)S(1)}, bf16[4,256]{1,0:T(4,128)(2,1)}, u32[]{:S(2)}) copy-start(bf16[4,256]{1,0:T(4,128)(2,1)} %param.24) | copy-start | bytes 6148
  14.8 6.6 %copy-start.15 = (bf16[256]{0:T(256)(128)(2,1)S(1)}, bf16[256]{0:T(256)(128)(2,1)}, u32[]{:S(2)}) copy-start(bf16[256]{0:T(256)(128)(2,1)} %param.25) | copy-start | bytes 1540
  14.8 6.6 %copy-start.7 = (bf16[4,8192]{1,0:T(4,128)(2,1)S(1)}, bf16[4,8192]{1,0:T(4,128)(2,1)}, u32[]{:S(2)}) copy-start(bf16[4,8192]{1,0:T(4,128)(2,1)} %param.22) | copy-start | bytes 196612
  14.8 6.7 %copy-start.9 = (bf16[8192]{0:T(1024)(128)(2,1)S(1)}, bf16[8192]{0:T(1024)(128)(2,1)}, u32[]{:S(2)}) copy-start(bf16[8192]{0:T(1024)(128)(2,1)} %param.23) | copy-start | bytes 49156
  14.8 7.4 %copy-start.11 = (s32[256]{0:T(256)S(1)}, s32[256]{0:T(256)}, u32[]{:S(2)}) copy-start(s32[256]{0:T(256)} %param.27) | copy-start | bytes 3076
  14.8 10.3 %copy-start.13 = (f32[128]{0:T(128)S(1)}, f32[128]{0:T(128)}, u32[]{:S(2)}) copy-start(f32[128]{0:T(128)} %param.19) | copy-start | bytes 1540
  14.9 10.6 %copy-start.8 = (bf16[256,256]{1,0:T(8,128)(2,1)S(1)}, bf16[256,256]{1,0:T(8,128)(2,1)}, u32[]{:S(2)}) copy-start(bf16[256,256]{1,0:T(8,128)(2,1)} %param.17) | copy-start | bytes 393220
  43.5 5.2 %copy-start.2 = (bf16[256,8192]{0,1:T(8,128)(2,1)}, bf16[256,8192]{0,1:T(8,128)(2,1)S(1)}, u32[]{:S(2)}) copy-start(bf16[256,8192]{0,1:T(8,128)(2,1)S(1)} %multiply_convert_fusion.5) | copy-start | bytes 12582916
  48.7 2.6 copy-start.5
  51.3 4.4 %collective-permute-start.7 = (f32[64,64,128]{2,1,0:T(8,128)}, f32[64,64,128]{2,1,0:T(8,128)S(1)}, u32[]{:S(2)}, u32[]{:S(2)}) collective-permute-start(f32[64,64,128]{2,1,0:T(8,128)} %constant_dynamic-slice_fusion), channel_id=1, source_target_pairs={{0,1},{1,0},{2,3},{3,2},{4,5},{5,4},{6,7},{7,6},{8,9},{9,8},{10,11... | collective-permute-start | bytes 6291464 | tf_op jit(solution)/shard_map/ppermute | solution.py:151
  51.4 3.8 %collective-permute-start.4 = (f32[128]{0:T(128)S(1)}, f32[128]{0:T(128)S(1)}, u32[]{:S(2)}, u32[]{:S(2)}) collective-permute-start(f32[128]{0:T(128)S(1)} %get-tuple-element.66), channel_id=1, source_target_pairs={{0,1},{1,0},{2,3},{3,2},{4,5},{5,4},{6,7},{7,6},{8,9},{9,8},{10,11... | collective-permute-start | bytes 1544 | tf_op jit(solution)/shard_map/ppermute | solution.py:151
  55.7 105.1 %copy-start = (f32[64,64,128]{2,1,0:T(8,128)}, f32[64,64,128]{2,1,0:T(8,128)S(1)}, u32[]{:S(2)}) copy-start(f32[64,64,128]{2,1,0:T(8,128)S(1)} %collective-permute-done.7) | copy-start | bytes 6291460
  58.5 50.8 %collective-permute-start.15 = (f32[64,64,128]{2,1,0:T(8,128)S(1)}, f32[64,64,128]{2,1,0:T(8,128)S(1)}, u32[]{:S(2)}, u32[]{:S(2)}) collective-permute-start(f32[64,64,128]{2,1,0:T(8,128)S(1)} %add_select_fusion), channel_id=1, source_target_pairs={{0,2},{1,3},{2,4},{3,5},{4,6},{5,7},{6,8},{7,9},{8,10},{9,11},{10,... | collective-permute-start | bytes 6291464 | tf_op jit(solution)/shard_map/ppermute | solution.py:69
  109.3 49.9 %collective-permute-start.16 = (f32[64,64,128]{2,1,0:T(8,128)S(1)}, f32[64,64,128]{2,1,0:T(8,128)S(1)}, u32[]{:S(2)}, u32[]{:S(2)}) collective-permute-start(f32[64,64,128]{2,1,0:T(8,128)S(1)} %collective-permute-done.15), channel_id=1, source_target_pairs={{0,2},{1,3},{2,4},{3,5},{4,6},{5,7},{6,8},{7,9},{8,10},{9,11},{10,... | collective-permute-start | bytes 6291464 | tf_op jit(solution)/shard_map/ppermute | solution.py:69
  111.2 47.9 %collective-permute-start.13 = (f32[64]{0:T(128)S(1)}, f32[64]{0:T(128)S(1)}, u32[]{:S(2)}, u32[]{:S(2)}) collective-permute-start(f32[64]{0:T(128)S(1)} %mul.373), channel_id=1, source_target_pairs={{0,2},{1,3},{2,4},{3,5},{4,6},{5,7},{6,8},{7,9},{8,10},{9,11},{10,... | collective-permute-start | bytes 776 | tf_op jit(solution)/shard_map/ppermute | solution.py:69
  160.8 63.0 %collective-permute-start.17 = (f32[64,64,128]{2,1,0:T(8,128)}, f32[64,64,128]{2,1,0:T(8,128)}, u32[]{:S(2)}, u32[]{:S(2)}) collective-permute-start(f32[64,64,128]{2,1,0:T(8,128)} %multiply_add_fusion.3), channel_id=1, source_target_pairs={{0,4},{1,5},{2,6},{3,7},{4,8},{5,9},{6,10},{7,11},{8,12},{9,13},{1... | collective-permute-start | bytes 6291464 | tf_op jit(solution)/shard_map/ppermute | solution.py:69
  162.7 8.6 %collective-permute-start.8 = (s32[1]{0:T(128)}, s32[1]{0:T(128)}, u32[]{:S(2)}, u32[]{:S(2)}) collective-permute-start(s32[1]{0:T(128)} %slice.109), channel_id=1, source_target_pairs={{0,1},{1,0},{2,3},{3,2},{4,5},{5,4},{6,7},{7,6},{8,9},{9,8},{10,11... | collective-permute-start | bytes 20 | tf_op jit(solution)/shard_map/ppermute | solution.py:107
  164.7 6.4 %copy-start.14 = (f32[128]{0:T(128)S(1)}, f32[128]{0:T(128)}, u32[]{:S(2)}) copy-start(f32[128]{0:T(128)} %param.21) | copy-start | bytes 1540
  164.7 6.5 %copy-start.10 = (bf16[8192]{0:T(1024)(128)(2,1)S(1)}, bf16[8192]{0:T(1024)(128)(2,1)}, u32[]{:S(2)}) copy-start(bf16[8192]{0:T(1024)(128)(2,1)} %param.26) | copy-start | bytes 49156
  172.7 2.8 %collective-permute-start.9 = (s32[2]{0:T(128)S(1)}, s32[2]{0:T(128)S(1)}, u32[]{:S(2)}, u32[]{:S(2)}) collective-permute-start(s32[2]{0:T(128)S(1)} %broadcast_select_fusion.1), channel_id=1, source_target_pairs={{0,2},{1,3},{2,0},{3,1},{4,6},{5,7},{6,4},{7,5},{8,10},{9,11},{10,... | collective-permute-start | bytes 32 | tf_op jit(solution)/shard_map/ppermute | solution.py:107
  175.5 30.7 %collective-permute-start.10 = (s32[4]{0:T(128)S(1)}, s32[4]{0:T(128)S(1)}, u32[]{:S(2)}, u32[]{:S(2)}) collective-permute-start(s32[4]{0:T(128)S(1)} %broadcast_select_fusion.2), channel_id=1, source_target_pairs={{0,4},{1,5},{2,6},{3,7},{4,0},{5,1},{6,2},{7,3},{8,12},{9,13},{10,... | collective-permute-start | bytes 56 | tf_op jit(solution)/shard_map/ppermute | solution.py:107
  206.3 2.8 %collective-permute-start.11 = (s32[8]{0:T(128)S(1)}, s32[8]{0:T(128)S(1)}, u32[]{:S(2)}, u32[]{:S(2)}) collective-permute-start(s32[8]{0:T(128)S(1)} %broadcast_select_fusion.3), channel_id=1, source_target_pairs={{0,8},{1,9},{2,10},{3,11},{4,12},{5,13},{6,14},{7,15},{8,0},{9,1},... | collective-permute-start | bytes 104 | tf_op jit(solution)/shard_map/ppermute | solution.py:107
  209.2 3.3 %collective-permute-start.12 = (s32[16]{0:T(128)S(1)}, s32[16]{0:T(128)S(1)}, u32[]{:S(2)}, u32[]{:S(2)}) collective-permute-start(s32[16]{0:T(128)S(1)} %broadcast_select_fusion.4), channel_id=1, source_target_pairs={{0,16},{1,17},{2,18},{3,19},{4,20},{5,21},{6,22},{7,23},{8,24},{9,... | collective-permute-start | bytes 200 | tf_op jit(solution)/shard_map/ppermute | solution.py:107
  214.8 6.1 %collective-permute-start.14 = (f32[64]{0:T(128)S(1)}, f32[64]{0:T(128)S(1)}, u32[]{:S(2)}, u32[]{:S(2)}) collective-permute-start(f32[64]{0:T(128)S(1)} %collective-permute-done.13), channel_id=1, source_target_pairs={{0,2},{1,3},{2,4},{3,5},{4,6},{5,7},{6,8},{7,9},{8,10},{9,11},{10,... | collective-permute-start | bytes 776 | tf_op jit(solution)/shard_map/ppermute | solution.py:69
  220.9 5.4 %collective-permute-start.18 = (f32[64]{0:T(128)S(1)}, f32[64]{0:T(128)S(1)}, u32[]{:S(2)}, u32[]{:S(2)}) collective-permute-start(f32[64]{0:T(128)S(1)} %mul.437), channel_id=1, source_target_pairs={{0,4},{1,5},{2,6},{3,7},{4,8},{5,9},{6,10},{7,11},{8,12},{9,13},{1... | collective-permute-start | bytes 776 | tf_op jit(solution)/shard_map/ppermute | solution.py:69
  226.5 8.6 %copy-start.3 = (bf16[256,8192]{0,1:T(8,128)(2,1)S(1)}, bf16[256,8192]{0,1:T(8,128)(2,1)}, u32[]{:S(2)}) copy-start(bf16[256,8192]{0,1:T(8,128)(2,1)} %copy-done.2) | copy-start | bytes 12582916
  229.3 16.6 %copy-start.1 = (f32[64,64,128]{2,1,0:T(8,128)S(1)}, f32[64,64,128]{2,1,0:T(8,128)}, u32[]{:S(2)}) copy-start(f32[64,64,128]{2,1,0:T(8,128)} %copy-done) | copy-start | bytes 6291460
  229.3 16.6 %copy-start.6 = (f32[128,64,128]{2,1,0:T(8,128)S(1)}, f32[128,64,128]{2,1,0:T(8,128)}, u32[]{:S(2)}) copy-start(f32[128,64,128]{2,1,0:T(8,128)} %copy-done.5) | copy-start | bytes 12582916
  229.4 16.6 %collective-permute-start.19 = (bf16[64,64,128]{2,1,0:T(8,128)(2,1)S(1)}, bf16[64,64,128]{2,1,0:T(8,128)(2,1)S(1)}, u32[]{:S(2)}, u32[]{:S(2)}) collective-permute-start(bf16[64,64,128]{2,1,0:T(8,128)(2,1)S(1)} %fusion.21), channel_id=1, source_target_pairs={{0,1},{1,0},{2,3},{3,2},{4,5},{5,4},{6,7},{7,6},{8,9},{9,8},{10,11... | collective-permute-start | bytes 3145736 | tf_op jit(solution)/shard_map/ppermute | solution.py:162
  246.9 4.8 %copy-start.4 = (bf16[256,8192]{0,1:T(8,128)(2,1)S(1)}, bf16[256,8192]{0,1:T(8,128)(2,1)}, u32[]{:S(2)}) copy-start(bf16[256,8192]{0,1:T(8,128)(2,1)} %copy.54) | copy-start | bytes 12582916

commit v3 on v2

--- a/solution.py
+++ b/solution.py
@@ -75,10 +75,10 @@
 
 
 def scan_rounds(carry, axis, stride, span, count, far):
-    near, needed, rider = far
-    carry, rider = lax.optimization_barrier((carry, rider))
-    far[2] = rider
+    near, needed, rider, work = far
+    carry, rider, needed = lax.optimization_barrier((carry, rider, needed))
     transmit, state = shifted(carry, axis, stride, count)
+    (transmit, state), far[2] = lax.optimization_barrier(((transmit, state), work(rider)))
     covered = 1
     while covered < min(span - 1, near):
         transmit, state = scan_round(transmit, state, axis, stride * covered, count)
@@ -239,9 +239,13 @@
         state_of, (x_blocks, b_blocks, step_blocks, cum_decay, seg_blocks, seg_before)
     )
     intra_items = (x_blocks, b_blocks, c_blocks, step_blocks, cum_decay, seg_blocks)
-    far = [*long_runs(segment_ids[tok_rows - 1 :], paired, tok_rows), intra_items]
+    far = [
+        *long_runs(segment_ids[tok_rows - 1 :], paired, tok_rows),
+        intra_items,
+        functools.partial(blockwise, intra_of),
+    ]
     entering = chain_states(block_states, transmits, paired, far)
-    y_intra = blockwise(intra_of, far[2])
+    y_intra = far[2]
 
     def enter_of(item):
         c_group, decay_here, segment, before, entering_here = item

time: 267 us -> 276 us (1.034)
  other arithmetic: 41.2 us -> 58.6 us
  waiting for transfers between devices: 134 us -> 127 us
    ppermute x5, waiting for transfers between devices: 34.4 us -> 8 us  [gather_small(): other = lax.ppermute(value, axis, [(s, s ^ size) for s in range(count)])]
    ppermute x6, waiting for transfers between devices: 96.1 us -> 119 us  [shifted(): lax.ppermute(value, axis, [(s, s + steps) for s in range(count - steps)])]
    add x0 -> x1, other arithmetic: none -> 12.2 us  [local(): y_blocks = y_intra + y_state]
    ppermute x2, waiting for transfers between devices: 3.75 us -> 0.01 us  [device_entry(): other_t, other_s = lax.ppermute((dev_transmit, give), 'ctx', swap)]
    ppermute x2, starting transfers between devices: 0.51 us -> 4.04 us  [device_entry(): other_t, other_s = lax.ppermute((dev_transmit, give), 'ctx', swap)]
  transfers between devices with their start and end apart: 17 -> 17, of which waited for: 9 -> 8; matrix products, arithmetic and copies ran while one was open for 14% -> 15% of each run, Pallas kernels for 0% -> 0%
where the time goes in v3:
time: 276 us; the launch traced here: 275 us
  waiting for transfers between devices  127 us (46%)
  other arithmetic  58.6 us (21%)
  starting transfers between devices  36 us (13%)
  local copies, waits for them, and re-layouts  29 us (11%)
  matrix products  22.3 us (8%)
    ppermute x6, waiting for transfers between devices, shifted(): lax.ppermute(value, axis, [(s, s + steps) for s in range(count - steps)])  119 us
    convert_element_type x2, other arithmetic, causal_conv(): return jax.nn.silu(summed).astype(jnp.bfloat16)  16.9 us
    unnamed x35, local copies, waits for them, and re-layouts  14.8 us
    ppermute x6, starting transfers between devices, shifted(): lax.ppermute(value, axis, [(s, s + steps) for s in range(count - steps)])  12.7 us
    dot_general x1, matrix products, mixing_part(): jnp.einsum('hij,jhp->ihp', mixing, x_group, preferred_element_type=jnp.fl...  12.5 us
    add x1, other arithmetic, local(): y_blocks = y_intra + y_state  12.2 us
    ppermute x3, starting transfers between devices, passed_along(): lax.ppermute(value, axis, [(source, source + steps) for source in range(l...  9.08 us
    ppermute x5, waiting for transfers between devices, gather_small(): other = lax.ppermute(value, axis, [(s, s ^ size) for s in range(count)])  8 us
  transfers between devices with their start and end apart: 17, of which 8 were waited for; matrix products, arithmetic and copies ran while one was open for 15% of the time, Pallas kernels for 0%

profile of v3, /device:TPU:9, one launch (start us, length us, event | category | flops | bytes accessed | tf_op | source)
XLA Modules:
  0.0 274.9 jit_solution(14554727167110936423)
XLA Ops:
  0.8 3.7 %collective-permute-start.3 = (bf16[3]{0:T(256)(128)(2,1)S(1)}, bf16[3]{0:T(256)(128)(2,1)S(1)}, u32[]{:S(2)}, u32[]{:S(2)}) collective-permute-start(bf16[3]{0:T(256)(128)(2,1)S(1)} %slice.110), channel_id=1, source_target_pairs={{0,1},{1,2},{2,3},{3,4},{4,5},{5,6},{6,7},{7,8},{8,9},{9,10},{10,1... | collective-permute-start | bytes 26 | tf_op jit(solution)/shard_map/ppermute | solution.py:21
  4.4 0.7 slice.124
  5.1 1.9 collective-permute-start.6
  7.0 0.9 slice.113
  8.0 3.5 %collective-permute-start.5 = (bf16[3,8192]{1,0:T(4,128)(2,1)S(1)}, bf16[3,8192]{1,0:T(4,128)(2,1)S(1)}, u32[]{:S(2)}, u32[]{:S(2)}) collective-permute-start(bf16[3,8192]{1,0:T(4,128)(2,1)S(1)} %slice.113), channel_id=1, source_target_pairs={{0,1},{1,2},{2,3},{3,4},{4,5},{5,6},{6,7},{7,8},{8,9},{9,10},{10,1... | collective-permute-start | bytes 147464 | tf_op jit(solution)/shard_map/ppermute | solution.py:21
  11.5 1.3 slice.109
  12.8 1.0 copy.39
  13.8 0.8 negate_multiply_fusion
  14.8 6.4 %copy.43 = bf16[256,8192]{0,1:T(8,128)(2,1)} copy(bf16[256,8192]{1,0:T(8,128)(2,1)} %param.15) | data formatting | bytes 8388608 | tf_op args[0]
  23.4 1.3 compare_convert_fusion.4
  25.4 1.1 copy.42
  26.5 16.7 %multiply_convert_fusion.5 = bf16[256,8192]{0,1:T(8,128)(2,1)S(1)} fusion(bf16[256,8192]{0,1:T(8,128)(2,1)} %copy.43, bf16[3,8192]{0,1:T(8,128)(2,1)S(1)} %copy.42, f32[8192]{0:T(1024)S(1)} %bitcast.79, f32[256]{0:T(256)S(1)} %get-tuple-element.85, f32[8192]{0:T(1024)S(1)} %bitcast.80, f32[256]{0:T(256)S(1)} %get-tuple-element.86, f32[8192]{0:T(1024)S(1)} %bitcast.78, ...), kind=kLoop, calls=%fused_computation.24 | loop fusion | flops 60817408 | bytes 8604672 | tf_op jit(solution)/shard_map/convert_element_type | solution.py:37
  43.2 5.2 %fusion.20 = f32[128,64,128]{2,1,0:T(8,128)S(1)} fusion(bf16[256,128,64]{0,2,1:T(8,128)(2,1)S(1)} %bitcast.72, f32[128,256]{1,0:T(8,128)S(1)} %copy.45, f32[256,128]{1,0:T(8,128)S(1)} %get-tuple-element.79, f32[128]{0:T(128)S(1)} %get-tuple-element.73), kind=kOutput, calls=%fused_computation.34 | convolution fusion | flops 546308096 | bytes 8651264 | tf_op jit(solution)/shard_map/hjn,jhp->hpn/dot_general | solution.py:56
  48.4 1.6 constant_dynamic-slice_fusion
  50.0 1.0 copy-done.3
  51.5 3.4 %collective-permute-done.8 = s32[1]{0:T(128)} collective-permute-done((s32[1]{0:T(128)}, s32[1]{0:T(128)}, u32[]{:S(2)}, u32[]{:S(2)}) %collective-permute-start.8) | collective-permute-done | bytes 36 | tf_op jit(solution)/shard_map/ppermute | solution.py:107
  55.0 1.3 broadcast_select_fusion.1
  56.3 1.2 collective-permute-start.9
  57.5 1.2 collective-permute-done.9
  58.8 1.2 collective-permute-start.10
  60.0 1.2 collective-permute-done.10
  61.4 2.2 collective-permute-done.11
  63.7 2.3 collective-permute-start.12
  66.0 4.0 %collective-permute-start.4 = (f32[128]{0:T(128)S(1)}, f32[128]{0:T(128)S(1)}, u32[]{:S(2)}, u32[]{:S(2)}) collective-permute-start(f32[128]{0:T(128)S(1)} %get-tuple-element.74), channel_id=1, source_target_pairs={{0,1},{1,0},{2,3},{3,2},{4,5},{5,4},{6,7},{7,6},{8,9},{9,8},{10,11... | collective-permute-start | bytes 1544 | tf_op jit(solution)/shard_map/ppermute | solution.py:151
  70.7 0.7 compare_reduce_fusion
  71.5 4.1 %add_select_fusion = f32[64,64,128]{2,1,0:T(8,128)} fusion(f32[64,64,128]{2,1,0:T(8,128)S(1)} %collective-permute-done.7, f32[128,64,128]{2,1,0:T(8,128)} %copy-done.3, s32[]{:T(128)S(6)} %select_n.101, f32[64]{0:T(128)S(1)} %get-tuple-element.72, f32[64]{0:T(128)S(1)} %get-tuple-element.71, pred[]{:T(512)S(6)} %eq.73), kind=kLoop, calls=%fused_computation.44 | loop fusion | flops 2621440 | bytes 6291973 | tf_op jit(solution)/shard_map/jit(_where)/select_n | solution.py:156
  75.9 3.1 %collective-permute-start.14 = (f32[64,64,128]{2,1,0:T(8,128)}, f32[64,64,128]{2,1,0:T(8,128)S(1)}, u32[]{:S(2)}, u32[]{:S(2)}) collective-permute-start(f32[64,64,128]{2,1,0:T(8,128)} %add_select_fusion), channel_id=1, source_target_pairs={{0,2},{1,3},{2,4},{3,5},{4,6},{5,7},{6,8},{7,9},{8,10},{9,11},{10,... | collective-permute-start | bytes 6291464 | tf_op jit(solution)/shard_map/ppermute | solution.py:69
  79.0 1.9 collective-permute-start.13
  81.2 12.5 %fusion.17 = f32[1,256,128,64]{1,3,2,0:T(8,128)} fusion(f32[128,256]{1,0:T(8,128)S(1)} %copy.50, f32[128,256]{1,0:T(8,128)S(1)} %copy.48, f32[256,256]{1,0:T(8,128)S(1)} %fusion.33, pred[256,256]{1,0:T(8,128)(4,1)S(1)} %fusion.27, bf16[1,256,128,64]{1,3,2,0:T(8,128)(2,1)} %bitcast.73), kind=kOutput, calls=%fused_computation.33 | convolution fusion | flops 1115684864 | bytes 13172736 | tf_op jit(solution)/shard_map/hij,jhp->ihp/dot_general | solution.py:48
  93.7 31.4 %collective-permute-done.13 = f32[64]{0:T(128)S(1)} collective-permute-done((f32[64]{0:T(128)S(1)}, f32[64]{0:T(128)S(1)}, u32[]{:S(2)}, u32[]{:S(2)}) %collective-permute-start.13) | collective-permute-done | bytes 288 | tf_op jit(solution)/shard_map/ppermute | solution.py:69
  125.1 1.9 collective-permute-start.16
  127.0 46.1 %collective-permute-done.16 = f32[64,64,128]{2,1,0:T(8,128)S(1)} collective-permute-done((f32[64,64,128]{2,1,0:T(8,128)S(1)}, f32[64,64,128]{2,1,0:T(8,128)S(1)}, u32[]{:S(2)}, u32[]{:S(2)}) %collective-permute-start.16) | collective-permute-done | bytes 2097184 | tf_op jit(solution)/shard_map/ppermute | solution.py:69
  173.3 1.9 collective-permute-start.17
  175.3 1.9 collective-permute-start.15
  177.8 39.9 %collective-permute-done.15 = f32[64]{0:T(128)S(1)} collective-permute-done((f32[64]{0:T(128)S(1)}, f32[64]{0:T(128)S(1)}, u32[]{:S(2)}, u32[]{:S(2)}) %collective-permute-start.15) | collective-permute-done | bytes 288 | tf_op jit(solution)/shard_map/ppermute | solution.py:69
  217.7 1.9 collective-permute-start.18
  219.6 2.5 multiply_add_fusion.2
  222.1 1.2 collective-permute-done.18
  223.3 3.7 %fusion.25 = bf16[64,64,128]{2,1,0:T(8,128)(2,1)} fusion(f32[64,64,128]{2,1,0:T(8,128)S(1)} %get-tuple-element.93, f32[64,64,128]{2,1,0:T(8,128)} %copy-done, f32[128,64,128]{2,1,0:T(8,128)} %copy-done.3, s32[]{:T(128)S(6)} %select_n.101, f32[64]{0:T(128)S(1)} %get-tuple-element.70, pred[]{:T(512)S(6)} %eq.73), kind=kLoop, calls=%fused_computation.45 | loop fusion | flops 2097152 | bytes 7340293 | tf_op jit(solution)/shard_map/jit(_where)/select_n | solution.py:162
  227.0 4.8 %collective-permute-start.19 = (bf16[64,64,128]{2,1,0:T(8,128)(2,1)}, bf16[64,64,128]{2,1,0:T(8,128)(2,1)S(1)}, u32[]{:S(2)}, u32[]{:S(2)}) collective-permute-start(bf16[64,64,128]{2,1,0:T(8,128)(2,1)} %fusion.25), channel_id=1, source_target_pairs={{0,1},{1,0},{2,3},{3,2},{4,5},{5,4},{6,7},{7,6},{8,9},{9,8},{10,11... | collective-permute-start | bytes 3145736 | tf_op jit(solution)/shard_map/ppermute | solution.py:162
  231.7 6.4 %copy.54 = bf16[256,8192]{0,1:T(8,128)(2,1)} copy(bf16[256,8192]{1,0:T(8,128)(2,1)} %param.16) | data formatting | bytes 8388608 | tf_op args[1]
  238.2 0.7 mul.449
  239.6 2.8 %select_convert_fusion.1 = (bf16[64,64,128]{2,1,0:T(8,128)(2,1)S(1)}, bf16[64,64,128]{2,1,0:T(8,128)(2,1)S(1)}) fusion(bf16[64,64,128]{2,1,0:T(8,128)(2,1)S(1)} %collective-permute-done.19, pred[]{:T(512)S(6)} %eq.73, f32[64,64,128]{2,1,0:T(8,128)S(1)} %get-tuple-element.93, f32[64,64,128]{2,1,0:T(8,128)} %copy-done, f32[128,64,128]{2,1,0:T(8,128)} %copy-done.3, ...), kind=kLoop, calls=%fused_computation.40 | loop fusion | flops 2621440 | bytes 9437445 | tf_op jit(solution)/shard_map/convert.11
  242.6 4.5 %fusion.21 = f32[256,128,64]{0,2,1:T(8,128)} fusion(bf16[64,64,128]{2,1,0:T(8,128)(2,1)S(1)} %select_convert_fusion, bf16[64,64,128]{2,1,0:T(8,128)(2,1)S(1)} %get-tuple-element.68, bf16[256,256]{1,0:T(8,128)(2,1)S(1)} %multiply_convert_fusion.10), kind=kOutput, calls=%fused_computation.35 | convolution fusion | flops 541065216 | bytes 10551296 | tf_op jit(solution)/shard_map/in,hpn->ihp/dot_general | solution.py:64
  247.0 12.2 %bitcast_add_fusion.1 = f32[1,256,128,64]{1,3,2,0:T(8,128)} fusion(f32[1,256,128,64]{1,3,2,0:T(8,128)} %fusion.17, f32[256,128,64]{0,2,1:T(8,128)} %fusion.21, f32[256,128]{0,1:T(8,128)S(1)} %copy.52), kind=kLoop, calls=%fused_computation.19 | loop fusion | flops 4194304 | bytes 25296896 | tf_op jit(solution)/shard_map/add | solution.py:255
  259.2 6.8 %multiply_reduce_fusion = (f32[256]{0:T(256)S(1)}, f32[256,8192]{0,1:T(8,128)S(1)}) fusion(bf16[256,8192]{0,1:T(8,128)(2,1)} %copy.54, bf16[256,8192]{0,1:T(8,128)(2,1)S(1)} %copy-done.2, f32[8192]{0:T(1024)S(1)} %copy-done.7, f32[1,256,128,64]{1,3,2,0:T(8,128)} %bitcast_add_fusion.1), kind=kLoop, calls=%fused_computation.21 | loop fusion | flops 23068416 | bytes 25199616 | tf_op jit(solution)/shard_map/reduce_sum | solution.py:259
  266.0 2.6 multiply_convert_fusion.4
  268.6 6.3 %copy.55 = bf16[256,8192]{1,0:T(8,128)(2,1)} copy(bf16[256,8192]{0,1:T(8,128)(2,1)} %multiply_convert_fusion.4) | data formatting | bytes 8388608 | tf_op jit(solution)/shard_map/convert_element_type | solution.py:262
  (89 shorter events, 5.7 us)
Async XLA Ops:
  0.8 20.7 %collective-permute-start.3 = (bf16[3]{0:T(256)(128)(2,1)S(1)}, bf16[3]{0:T(256)(128)(2,1)S(1)}, u32[]{:S(2)}, u32[]{:S(2)}) collective-permute-start(bf16[3]{0:T(256)(128)(2,1)S(1)} %slice.110), channel_id=1, source_target_pairs={{0,1},{1,2},{2,3},{3,4},{4,5},{5,6},{6,7},{7,8},{8,9},{9,10},{10,1... | collective-permute-start | bytes 26 | tf_op jit(solution)/shard_map/ppermute | solution.py:21
  5.1 20.0 %collective-permute-start.6 = (bf16[3,256]{1,0:T(4,128)(2,1)S(1)}, bf16[3,256]{1,0:T(4,128)(2,1)S(1)}, u32[]{:S(2)}, u32[]{:S(2)}) collective-permute-start(bf16[3,256]{1,0:T(4,128)(2,1)S(1)} %slice.124), channel_id=1, source_target_pairs={{0,1},{1,2},{2,3},{3,4},{4,5},{5,6},{6,7},{7,8},{8,9},{9,10},{10,1... | collective-permute-start | bytes 4616 | tf_op jit(solution)/shard_map/ppermute | solution.py:21
  8.0 17.4 %collective-permute-start.5 = (bf16[3,8192]{1,0:T(4,128)(2,1)S(1)}, bf16[3,8192]{1,0:T(4,128)(2,1)S(1)}, u32[]{:S(2)}, u32[]{:S(2)}) collective-permute-start(bf16[3,8192]{1,0:T(4,128)(2,1)S(1)} %slice.113), channel_id=1, source_target_pairs={{0,1},{1,2},{2,3},{3,4},{4,5},{5,6},{6,7},{7,8},{8,9},{9,10},{10,1... | collective-permute-start | bytes 147464 | tf_op jit(solution)/shard_map/ppermute | solution.py:21
  14.7 6.6 %copy-start.12 = (bf16[4,256]{1,0:T(4,128)(2,1)S(1)}, bf16[4,256]{1,0:T(4,128)(2,1)}, u32[]{:S(2)}) copy-start(bf16[4,256]{1,0:T(4,128)(2,1)} %param.24) | copy-start | bytes 6148
  14.7 6.6 %copy-start.15 = (bf16[256]{0:T(256)(128)(2,1)S(1)}, bf16[256]{0:T(256)(128)(2,1)}, u32[]{:S(2)}) copy-start(bf16[256]{0:T(256)(128)(2,1)} %param.25) | copy-start | bytes 1540
  14.7 6.6 %copy-start.5 = (bf16[4,8192]{1,0:T(4,128)(2,1)S(1)}, bf16[4,8192]{1,0:T(4,128)(2,1)}, u32[]{:S(2)}) copy-start(bf16[4,8192]{1,0:T(4,128)(2,1)} %param.22) | copy-start | bytes 196612
  14.7 6.7 %copy-start.9 = (bf16[8192]{0:T(1024)(128)(2,1)S(1)}, bf16[8192]{0:T(1024)(128)(2,1)}, u32[]{:S(2)}) copy-start(bf16[8192]{0:T(1024)(128)(2,1)} %param.23) | copy-start | bytes 49156
  14.8 7.4 %copy-start.11 = (s32[256]{0:T(256)S(1)}, s32[256]{0:T(256)}, u32[]{:S(2)}) copy-start(s32[256]{0:T(256)} %param.27) | copy-start | bytes 3076
  14.8 10.1 %copy-start.13 = (f32[128]{0:T(128)S(1)}, f32[128]{0:T(128)}, u32[]{:S(2)}) copy-start(f32[128]{0:T(128)} %param.19) | copy-start | bytes 1540
  14.8 10.3 %copy-start.6 = (bf16[256,256]{1,0:T(8,128)(2,1)S(1)}, bf16[256,256]{1,0:T(8,128)(2,1)}, u32[]{:S(2)}) copy-start(bf16[256,256]{1,0:T(8,128)(2,1)} %param.17) | copy-start | bytes 393220
  43.2 5.2 %copy-start.1 = (bf16[256,8192]{0,1:T(8,128)(2,1)}, bf16[256,8192]{0,1:T(8,128)(2,1)S(1)}, u32[]{:S(2)}) copy-start(bf16[256,8192]{0,1:T(8,128)(2,1)S(1)} %multiply_convert_fusion.5) | copy-start | bytes 12582916
  48.4 2.6 copy-start.3
  51.0 20.5 %collective-permute-start.7 = (f32[64,64,128]{2,1,0:T(8,128)}, f32[64,64,128]{2,1,0:T(8,128)S(1)}, u32[]{:S(2)}, u32[]{:S(2)}) collective-permute-start(f32[64,64,128]{2,1,0:T(8,128)} %constant_dynamic-slice_fusion), channel_id=1, source_target_pairs={{0,1},{1,0},{2,3},{3,2},{4,5},{5,4},{6,7},{7,6},{8,9},{9,8},{10,11... | collective-permute-start | bytes 6291464 | tf_op jit(solution)/shard_map/ppermute | solution.py:151
  51.0 4.0 %collective-permute-start.8 = (s32[1]{0:T(128)}, s32[1]{0:T(128)}, u32[]{:S(2)}, u32[]{:S(2)}) collective-permute-start(s32[1]{0:T(128)} %slice.109), channel_id=1, source_target_pairs={{0,1},{1,0},{2,3},{3,2},{4,5},{5,4},{6,7},{7,6},{8,9},{9,8},{10,11... | collective-permute-start | bytes 20 | tf_op jit(solution)/shard_map/ppermute | solution.py:107
  56.3 2.4 collective-permute-start.9
  58.8 2.4 collective-permute-start.10
  61.2 2.4 collective-permute-start.11
  63.7 6.4 %collective-permute-start.12 = (s32[16]{0:T(128)S(1)}, s32[16]{0:T(128)S(1)}, u32[]{:S(2)}, u32[]{:S(2)}) collective-permute-start(s32[16]{0:T(128)S(1)} %broadcast_select_fusion.4), channel_id=1, source_target_pairs={{0,16},{1,17},{2,18},{3,19},{4,20},{5,21},{6,22},{7,23},{8,24},{9,... | collective-permute-start | bytes 200 | tf_op jit(solution)/shard_map/ppermute | solution.py:107
  66.0 5.4 %collective-permute-start.4 = (f32[128]{0:T(128)S(1)}, f32[128]{0:T(128)S(1)}, u32[]{:S(2)}, u32[]{:S(2)}) collective-permute-start(f32[128]{0:T(128)S(1)} %get-tuple-element.74), channel_id=1, source_target_pairs={{0,1},{1,0},{2,3},{3,2},{4,5},{5,4},{6,7},{7,6},{8,9},{9,8},{10,11... | collective-permute-start | bytes 1544 | tf_op jit(solution)/shard_map/ppermute | solution.py:151
  71.5 22.2 %copy-start = (f32[64,64,128]{2,1,0:T(8,128)}, f32[64,64,128]{2,1,0:T(8,128)S(1)}, u32[]{:S(2)}) copy-start(f32[64,64,128]{2,1,0:T(8,128)S(1)} %collective-permute-done.7) | copy-start | bytes 6291460
  75.9 49.2 %collective-permute-start.14 = (f32[64,64,128]{2,1,0:T(8,128)}, f32[64,64,128]{2,1,0:T(8,128)S(1)}, u32[]{:S(2)}, u32[]{:S(2)}) collective-permute-start(f32[64,64,128]{2,1,0:T(8,128)} %add_select_fusion), channel_id=1, source_target_pairs={{0,2},{1,3},{2,4},{3,5},{4,6},{5,7},{6,8},{7,9},{8,10},{9,11},{10,... | collective-permute-start | bytes 6291464 | tf_op jit(solution)/shard_map/ppermute | solution.py:69
  79.0 46.0 %collective-permute-start.13 = (f32[64]{0:T(128)S(1)}, f32[64]{0:T(128)S(1)}, u32[]{:S(2)}, u32[]{:S(2)}) collective-permute-start(f32[64]{0:T(128)S(1)} %mul.373), channel_id=1, source_target_pairs={{0,2},{1,3},{2,4},{3,5},{4,6},{5,7},{6,8},{7,9},{8,10},{9,11},{10,... | collective-permute-start | bytes 776 | tf_op jit(solution)/shard_map/ppermute | solution.py:69
  125.1 48.0 %collective-permute-start.16 = (f32[64,64,128]{2,1,0:T(8,128)S(1)}, f32[64,64,128]{2,1,0:T(8,128)S(1)}, u32[]{:S(2)}, u32[]{:S(2)}) collective-permute-start(f32[64,64,128]{2,1,0:T(8,128)S(1)} %collective-permute-done.14), channel_id=1, source_target_pairs={{0,2},{1,3},{2,4},{3,5},{4,6},{5,7},{6,8},{7,9},{8,10},{9,11},{10,... | collective-permute-start | bytes 6291464 | tf_op jit(solution)/shard_map/ppermute | solution.py:69
  173.3 46.3 %copy-start.4 = (f32[64,64,128]{2,1,0:T(8,128)}, f32[64,64,128]{2,1,0:T(8,128)S(1)}, u32[]{:S(2)}) copy-start(f32[64,64,128]{2,1,0:T(8,128)S(1)} %multiply_add_fusion.3) | copy-start | bytes 6291460
  173.3 46.3 %collective-permute-start.17 = (f32[64,64,128]{2,1,0:T(8,128)S(1)}, f32[64,64,128]{2,1,0:T(8,128)}, u32[]{:S(2)}, u32[]{:S(2)}) collective-permute-start(f32[64,64,128]{2,1,0:T(8,128)S(1)} %multiply_add_fusion.3), channel_id=1, source_target_pairs={{0,4},{1,5},{2,6},{3,7},{4,8},{5,9},{6,10},{7,11},{8,12},{9,13},{1... | collective-permute-start | bytes 6291464 | tf_op jit(solution)/shard_map/ppermute | solution.py:69
  175.3 42.4 %collective-permute-start.15 = (f32[64]{0:T(128)S(1)}, f32[64]{0:T(128)S(1)}, u32[]{:S(2)}, u32[]{:S(2)}) collective-permute-start(f32[64]{0:T(128)S(1)} %collective-permute-done.13), channel_id=1, source_target_pairs={{0,2},{1,3},{2,4},{3,5},{4,6},{5,7},{6,8},{7,9},{8,10},{9,11},{10,... | collective-permute-start | bytes 776 | tf_op jit(solution)/shard_map/ppermute | solution.py:69
  217.7 5.6 %collective-permute-start.18 = (f32[64]{0:T(128)S(1)}, f32[64]{0:T(128)S(1)}, u32[]{:S(2)}, u32[]{:S(2)}) collective-permute-start(f32[64]{0:T(128)S(1)} %mul.437), channel_id=1, source_target_pairs={{0,4},{1,5},{2,6},{3,7},{4,8},{5,9},{6,10},{7,11},{8,12},{9,13},{1... | collective-permute-start | bytes 776 | tf_op jit(solution)/shard_map/ppermute | solution.py:69
  227.0 11.1 %copy-start.14 = (f32[128]{0:T(128)S(1)}, f32[128]{0:T(128)}, u32[]{:S(2)}) copy-start(f32[128]{0:T(128)} %param.21) | copy-start | bytes 1540
  227.0 11.9 %copy-start.10 = (bf16[8192]{0:T(1024)(128)(2,1)S(1)}, bf16[8192]{0:T(1024)(128)(2,1)}, u32[]{:S(2)}) copy-start(bf16[8192]{0:T(1024)(128)(2,1)} %param.26) | copy-start | bytes 49156
  227.0 12.6 %collective-permute-start.19 = (bf16[64,64,128]{2,1,0:T(8,128)(2,1)}, bf16[64,64,128]{2,1,0:T(8,128)(2,1)S(1)}, u32[]{:S(2)}, u32[]{:S(2)}) collective-permute-start(bf16[64,64,128]{2,1,0:T(8,128)(2,1)} %fusion.25), channel_id=1, source_target_pairs={{0,1},{1,0},{2,3},{3,2},{4,5},{5,4},{6,7},{7,6},{8,9},{9,8},{10,11... | collective-permute-start | bytes 3145736 | tf_op jit(solution)/shard_map/ppermute | solution.py:162
  247.0 12.2 %copy-start.2 = (bf16[256,8192]{0,1:T(8,128)(2,1)S(1)}, bf16[256,8192]{0,1:T(8,128)(2,1)}, u32[]{:S(2)}) copy-start(bf16[256,8192]{0,1:T(8,128)(2,1)} %copy-done.1) | copy-start | bytes 12582916
  247.0 12.2 %copy-start.7 = (f32[8192]{0:T(1024)S(1)}, f32[8192]{0:T(1024)}, u32[]{:S(2)}) copy-start(f32[8192]{0:T(1024)} %mul.449) | copy-start | bytes 98308
  259.2 6.8 %copy-start.8 = (f32[8192]{0:T(1024)S(1)}, f32[8192]{0:T(1024)}, u32[]{:S(2)}) copy-start(f32[8192]{0:T(1024)} %convert_element_type.129) | copy-start | bytes 98308

commit v4 on v2

--- a/solution.py
+++ b/solution.py
@@ -97,24 +97,30 @@
     return state
 
 
-def gather_small(value, axis):
+def gather_round(value, axis, size):
     count = lax.axis_size(axis)
     if count & (count - 1):
-        return lax.all_gather(value, axis, tiled=True)
+        return lax.all_gather(value, axis, tiled=True) if size == 1 else value
+    if size >= count:
+        return value
     place = lax.axis_index(axis)
-    size = 1
-    while size < count:
-        other = lax.ppermute(value, axis, [(s, s ^ size) for s in range(count)])
-        value = jnp.where(
-            (place & size) == 0,
-            jnp.concatenate([value, other]),
-            jnp.concatenate([other, value]),
-        )
+    other = lax.ppermute(value, axis, [(s, s ^ size) for s in range(count)])
+    return jnp.where(
+        (place & size) == 0,
+        jnp.concatenate([value, other]),
+        jnp.concatenate([other, value]),
+    )
+
+
+def gather_rounds(value, axis, first, last):
+    size = 1 << first
+    while size < (1 << last):
+        value = gather_round(value, axis, size)
         size *= 2
     return value
 
 
-def long_runs(last_id, paired, tok_rows):
+def long_runs(ids, paired, tok_rows):
     count = lax.axis_size("ctx")
     longest = (count * tok_rows // 4 - 1) // tok_rows
     group = 2 if paired else 1
@@ -122,7 +128,6 @@
     while near * group <= longest:
         near *= 2
     window = near * group
-    ids = gather_small(last_id, "ctx")
     joined = jnp.concatenate([jnp.zeros((1,), jnp.int32), (ids[1:] == ids[:-1]).astype(jnp.int32)])
     if window > count:
         return near, jnp.zeros((), jnp.bool_)
@@ -203,17 +208,27 @@
     head_count = dt_raw.shape[0]
     block_count = tok_rows // GROUP
     rim_rows = CONV - 1
-    rim_x, rim_bc, rim_mark = passed_along(
-        (
-            x_in[tok_rows - rim_rows :],
-            bc_in[tok_rows - rim_rows :],
-            segment_ids[tok_rows - rim_rows :].astype(jnp.bfloat16),
+    bc_width = bc_in.shape[1]
+    rims = passed_along(
+        jnp.concatenate(
+            [
+                x_in[tok_rows - rim_rows :],
+                bc_in[tok_rows - rim_rows :],
+                segment_ids[tok_rows - rim_rows :, None].astype(jnp.bfloat16),
+            ],
+            axis=1,
         ),
         "ctx",
         1,
     )
-    rim_segment = rim_mark.astype(jnp.int32)
+    rim_x = rims[:, :channels]
+    rim_bc = rims[:, channels : channels + bc_width]
+    rim_segment = rims[:, channels + bc_width].astype(jnp.int32)
+    ids = gather_rounds(segment_ids[tok_rows - 1 :], "ctx", 0, 2)
+    ids, rim_x = lax.optimization_barrier((ids, rim_x))
     x_conv = causal_conv(rim_x, x_in, rim_segment, segment_ids, conv_x_w, conv_x_b)
+    ids = gather_rounds(ids, "ctx", 2, 4)
+    ids, x_conv = lax.optimization_barrier((ids, x_conv))
     bc_conv = causal_conv(rim_bc, bc_in, rim_segment, segment_ids, conv_bc_w, conv_bc_b)
     step_size = jax.nn.softplus(dt_raw + dt_bias[:, None])
     log_decay = -step_size * a_rate[:, None]
@@ -239,7 +254,9 @@
         state_of, (x_blocks, b_blocks, step_blocks, cum_decay, seg_blocks, seg_before)
     )
     intra_items = (x_blocks, b_blocks, c_blocks, step_blocks, cum_decay, seg_blocks)
-    far = [*long_runs(segment_ids[tok_rows - 1 :], paired, tok_rows), intra_items]
+    ids = gather_rounds(ids, "ctx", 4, lax.axis_size("ctx").bit_length())
+    ids, block_states = lax.optimization_barrier((ids, block_states))
+    far = [*long_runs(ids, paired, tok_rows), intra_items]
     entering = chain_states(block_states, transmits, paired, far)
     y_intra = blockwise(intra_of, far[2])
 

time: 267 us -> 256 us (0.959)
  starting transfers between devices: 37.6 us -> 28 us
    ppermute x5, waiting for transfers between devices: 34.4 us -> 3.41 us  [gather_round(): other = lax.ppermute(value, axis, [(s, s ^ size) for s in range(count)])]
    ppermute x6, waiting for transfers between devices: 96.1 us -> 127 us  [shifted(): lax.ppermute(value, axis, [(s, s + steps) for s in range(count - steps)])]
    ppermute x3 -> x1, starting transfers between devices: 9.08 us -> 3.01 us  [passed_along(): lax.ppermute(value, axis, [(source, source + steps) for source in range(l...]
    unnamed x35 -> x39, local copies, waits for them, and re-layouts: 15 us -> 15 us
  transfers between devices with their start and end apart: 17 -> 15, of which waited for: 9 -> 8; matrix products, arithmetic and copies ran while one was open for 14% -> 23% of each run, Pallas kernels for 0% -> 0%
where the time goes in v4:
time: 256 us; the launch traced here: 255 us
  waiting for transfers between devices  134 us (52%)
  other arithmetic  40.8 us (16%)
  local copies, waits for them, and re-layouts  28.4 us (11%)
  starting transfers between devices  28 us (11%)
  matrix products  21.1 us (8%)
    ppermute x6, waiting for transfers between devices, shifted(): lax.ppermute(value, axis, [(s, s + steps) for s in range(count - steps)])  127 us
    convert_element_type x2, other arithmetic, causal_conv(): return jax.nn.silu(summed).astype(jnp.bfloat16)  16.9 us
    unnamed x39, local copies, waits for them, and re-layouts  15 us
    ppermute x6, starting transfers between devices, shifted(): lax.ppermute(value, axis, [(s, s + steps) for s in range(count - steps)])  13.3 us
    dot_general x1, matrix products, mixing_part(): jnp.einsum('hij,jhp->ihp', mixing, x_group, preferred_element_type=jnp.fl...  10.8 us
    convert_element_type x1, local copies, waits for them, and re-layouts, local(): (gated * scale[:, None] * norm_gain.astype(jnp.float32)).astype(jnp.bfloa...  6.31 us
    ppermute x5, starting transfers between devices, gather_round(): other = lax.ppermute(value, axis, [(s, s ^ size) for s in range(count)])  5.68 us
    dot_general x1, matrix products, state_part(): jnp.einsum('hjn,jhp->hpn', weighted, x_group, preferred_element_type=jnp....  5.28 us
  transfers between devices with their start and end apart: 15, of which 8 were waited for; matrix products, arithmetic and copies ran while one was open for 23% of the time, Pallas kernels for 0%

profile of v4, /device:TPU:9, one launch (start us, length us, event | category | flops | bytes accessed | tf_op | source)
XLA Modules:
  0.0 254.8 jit_solution(16216664113504616892)
XLA Ops:
  0.0 1.3 slice.119
  1.3 0.7 collective-permute-start.5
  1.9 0.7 convert.20
  2.6 0.9 slice.120
  3.8 0.7 slice.121
  4.5 3.0 %collective-permute-start.3 = (bf16[3,8449]{1,0:T(4,128)(2,1)S(1)}, bf16[3,8449]{1,0:T(4,128)(2,1)S(1)}, u32[]{:S(2)}, u32[]{:S(2)}) collective-permute-start(bf16[3,8449]{1,0:T(4,128)(2,1)S(1)} %pad_maximum_fusion.2), channel_id=1, source_target_pairs={{0,1},{1,2},{2,3},{3,4},{4,5},{5,6},{6,7},{7,8},{8,9},{9,10},{10,1... | collective-permute-start | bytes 152090 | tf_op jit(solution)/shard_map/ppermute | solution.py:21
  7.6 6.5 %copy.28 = bf16[256,8192]{0,1:T(8,128)(2,1)} copy(bf16[256,8192]{1,0:T(8,128)(2,1)} %param.15) | data formatting | bytes 8388608 | tf_op args[0]
  14.7 1.4 broadcast_select_fusion.1
  16.1 1.2 collective-permute-start.6
  17.4 1.2 collective-permute-done.6
  18.6 1.3 collective-permute-start.7
  19.9 1.0 copy.27
  21.0 0.6 slice.124
  23.1 1.4 compare_convert_fusion.4
  24.5 0.2 multiply_convert_fusion.8
  25.2 16.7 %multiply_convert_fusion.5 = bf16[256,8192]{0,1:T(8,128)(2,1)S(1)} fusion(bf16[256,8192]{0,1:T(8,128)(2,1)} %copy.28, bf16[3,8192]{0,1:T(8,128)(2,1)S(1)} %copy.27, f32[8192]{0:T(1024)S(1)} %bitcast.79, f32[256]{0:T(256)S(1)} %get-tuple-element.89, f32[8192]{0:T(1024)S(1)} %bitcast.80, f32[256]{0:T(256)S(1)} %get-tuple-element.90, f32[8192]{0:T(1024)S(1)} %bitcast.78, ...), kind=kLoop, calls=%fused_computation.24 | loop fusion | flops 60817408 | bytes 8604672 | tf_op jit(solution)/shard_map/convert_element_type | solution.py:37
  42.1 2.2 collective-permute-done.8
  44.4 2.3 collective-permute-start.9
  46.7 5.3 %fusion.17 = f32[1,128,64,128]{3,2,1,0:T(8,128)S(1)} fusion(bf16[256,128,64]{0,2,1:T(8,128)(2,1)S(1)} %bitcast.72, f32[128,256]{1,0:T(8,128)S(1)} %copy.30, f32[256,128]{1,0:T(8,128)S(1)} %get-tuple-element.83), kind=kOutput, calls=%fused_computation.34 | convolution fusion | flops 545259520 | bytes 8650752 | tf_op jit(solution)/shard_map/hjn,jhp->hpn/dot_general | solution.py:56
  52.1 0.3 bitcast_add_fusion.2
  52.5 2.0 copy-done
  54.5 1.5 constant_dynamic-slice_fusion
  55.9 2.3 collective-permute-start.10
  58.2 3.6 %collective-permute-done.4 = f32[128]{0:T(128)S(1)} collective-permute-done((f32[128]{0:T(128)S(1)}, f32[128]{0:T(128)S(1)}, u32[]{:S(2)}, u32[]{:S(2)}) %collective-permute-start.4) | collective-permute-done | bytes 544 | tf_op jit(solution)/shard_map/ppermute | solution.py:156
  61.9 0.3 collective-permute-done.10
  62.2 2.8 %add_select_fusion = f32[64,64,128]{2,1,0:T(8,128)S(1)} fusion(f32[64,64,128]{2,1,0:T(8,128)S(1)} %collective-permute-done.10, f32[128,64,128]{2,1,0:T(8,128)} %copy-done, s32[]{:T(128)S(6)} %select_n.101, f32[64]{0:T(128)S(1)} %get-tuple-element.74, f32[64]{0:T(128)S(1)} %get-tuple-element.73, pred[]{:T(512)S(6)} %eq.73), kind=kLoop, calls=%fused_computation.43 | loop fusion | flops 2621440 | bytes 6291973 | tf_op jit(solution)/shard_map/jit(_where)/select_n | solution.py:161
  65.0 3.1 %collective-permute-start.13 = (f32[64,64,128]{2,1,0:T(8,128)S(1)}, f32[64,64,128]{2,1,0:T(8,128)S(1)}, u32[]{:S(2)}, u32[]{:S(2)}) collective-permute-start(f32[64,64,128]{2,1,0:T(8,128)S(1)} %add_select_fusion), channel_id=1, source_target_pairs={{0,2},{1,3},{2,4},{3,5},{4,6},{5,7},{6,8},{7,9},{8,10},{9,11},{10,... | collective-permute-start | bytes 6291464 | tf_op jit(solution)/shard_map/ppermute | solution.py:69
  68.1 47.4 %collective-permute-done.13 = f32[64,64,128]{2,1,0:T(8,128)S(1)} collective-permute-done((f32[64,64,128]{2,1,0:T(8,128)S(1)}, f32[64,64,128]{2,1,0:T(8,128)S(1)}, u32[]{:S(2)}, u32[]{:S(2)}) %collective-permute-start.13) | collective-permute-done | bytes 2097184 | tf_op jit(solution)/shard_map/ppermute | solution.py:69
  115.5 1.9 collective-permute-start.14
  117.4 2.4 collective-permute-start.11
  119.8 45.3 %collective-permute-done.11 = f32[64]{0:T(128)S(1)} collective-permute-done((f32[64]{0:T(128)S(1)}, f32[64]{0:T(128)S(1)}, u32[]{:S(2)}, u32[]{:S(2)}) %collective-permute-start.11) | collective-permute-done | bytes 288 | tf_op jit(solution)/shard_map/ppermute | solution.py:69
  165.1 1.6 multiply_add_fusion.3
  166.7 2.0 collective-permute-start.15
  168.8 6.4 %copy.39 = bf16[256,8192]{0,1:T(8,128)(2,1)} copy(bf16[256,8192]{1,0:T(8,128)(2,1)} %param.16) | data formatting | bytes 8388608 | tf_op args[1]
  175.9 0.7 compare_reduce_fusion
  177.5 1.9 collective-permute-start.12
  179.7 33.3 %collective-permute-done.12 = f32[64]{0:T(128)S(1)} collective-permute-done((f32[64]{0:T(128)S(1)}, f32[64]{0:T(128)S(1)}, u32[]{:S(2)}, u32[]{:S(2)}) %collective-permute-start.12) | collective-permute-done | bytes 288 | tf_op jit(solution)/shard_map/ppermute | solution.py:69
  213.0 1.9 collective-permute-start.16
  214.9 2.5 multiply_add_fusion.2
  217.4 0.8 collective-permute-done.16
  218.2 2.8 %fusion.21 = bf16[64,64,128]{2,1,0:T(8,128)(2,1)S(1)} fusion(f32[64,64,128]{2,1,0:T(8,128)S(1)} %get-tuple-element.97, f32[64,64,128]{2,1,0:T(8,128)} %copy-done.2, f32[128,64,128]{2,1,0:T(8,128)} %copy-done, s32[]{:T(128)S(6)} %select_n.101, f32[64]{0:T(128)S(1)} %get-tuple-element.72, pred[]{:T(512)S(6)} %eq.73), kind=kLoop, calls=%fused_computation.44 | loop fusion | flops 2097152 | bytes 7340293 | tf_op jit(solution)/shard_map/jit(_where)/select_n | solution.py:167
  221.0 3.7 %collective-permute-start.17 = (bf16[64,64,128]{2,1,0:T(8,128)(2,1)S(1)}, bf16[64,64,128]{2,1,0:T(8,128)(2,1)S(1)}, u32[]{:S(2)}, u32[]{:S(2)}) collective-permute-start(bf16[64,64,128]{2,1,0:T(8,128)(2,1)S(1)} %fusion.21), channel_id=1, source_target_pairs={{0,1},{1,0},{2,3},{3,2},{4,5},{5,4},{6,7},{7,6},{8,9},{9,8},{10,11... | collective-permute-start | bytes 3145736 | tf_op jit(solution)/shard_map/ppermute | solution.py:167
  224.7 10.8 %fusion = f32[128,64,256]{2,1,0:T(8,128)} fusion(f32[128,256]{1,0:T(8,128)S(1)} %copy.34, f32[128,256]{1,0:T(8,128)S(1)} %copy.32, f32[256,256]{1,0:T(8,128)S(1)} %fusion.29, pred[256,256]{1,0:T(8,128)(4,1)S(1)} %fusion.23, bf16[1,256,128,64]{1,3,2,0:T(8,128)(2,1)S(1)} %bitcast.73), kind=kOutput, calls=%fused_computation.3 | convolution fusion | flops 1115684864 | bytes 13172736 | tf_op jit(solution)/shard_map/hij,jhp->ihp/dot_general | solution.py:48
  235.5 0.8 select_convert_fusion.1
  236.4 4.8 %bitcast_add_fusion.1 = f32[256,128,64]{0,2,1:T(8,128)S(1)} fusion(f32[128,64,256]{2,1,0:T(8,128)} %fusion, f32[256,128]{0,1:T(8,128)S(1)} %copy.37, bf16[64,64,128]{2,1,0:T(8,128)(2,1)S(1)} %select_convert_fusion, bf16[64,64,128]{2,1,0:T(8,128)(2,1)S(1)} %get-tuple-element.70, bf16[256,256]{1,0:T(8,128)(2,1)S(1)} %multiply_convert_fusion.8), kind=kOutput, calls=%fused_computation.19 | convolution fusion | flops 545259520 | bytes 19070976 | tf_op jit(solution)/shard_map/in,hpn->ihp/dot_general | solution.py:64
  241.2 4.7 %multiply_reduce_fusion = (f32[256]{0:T(256)S(1)}, f32[256,8192]{0,1:T(8,128)S(1)}) fusion(bf16[256,8192]{0,1:T(8,128)(2,1)S(1)} %copy-done.6, bf16[256,8192]{0,1:T(8,128)(2,1)S(1)} %copy-done.5, f32[8192]{0:T(1024)S(1)} %mul.449, f32[256,128,64]{0,2,1:T(8,128)S(1)} %bitcast_add_fusion.1), kind=kLoop, calls=%fused_computation.21 | loop fusion | flops 23068416 | bytes 25199616 | tf_op jit(solution)/shard_map/reduce_sum | solution.py:272
  245.9 2.6 %multiply_convert_fusion.4 = bf16[256,8192]{0,1:T(8,128)(2,1)} fusion(f32[256,8192]{0,1:T(8,128)S(1)} %get-tuple-element.69, f32[8192]{0:T(1024)S(1)} %convert_element_type.137, f32[256]{0:T(256)S(1)} %add_rsqrt_fusion), kind=kLoop, calls=%fused_computation.20 | loop fusion | flops 6291456 | bytes 12616704 | tf_op jit(solution)/shard_map/convert_element_type | solution.py:275
  248.5 6.3 %copy.40 = bf16[256,8192]{1,0:T(8,128)(2,1)} copy(bf16[256,8192]{0,1:T(8,128)(2,1)} %multiply_convert_fusion.4) | data formatting | bytes 8388608 | tf_op jit(solution)/shard_map/convert_element_type | solution.py:275
  (94 shorter events, 3.3 us)
Async XLA Ops:
  1.3 13.5 %collective-permute-start.5 = (s32[1]{0:T(128)}, s32[1]{0:T(128)}, u32[]{:S(2)}, u32[]{:S(2)}) collective-permute-start(s32[1]{0:T(128)} %slice.119), channel_id=1, source_target_pairs={{0,1},{1,0},{2,3},{3,2},{4,5},{5,4},{6,7},{7,6},{8,9},{9,8},{10,11... | collective-permute-start | bytes 20 | tf_op jit(solution)/shard_map/ppermute | solution.py:107
  4.5 14.1 %collective-permute-start.3 = (bf16[3,8449]{1,0:T(4,128)(2,1)S(1)}, bf16[3,8449]{1,0:T(4,128)(2,1)S(1)}, u32[]{:S(2)}, u32[]{:S(2)}) collective-permute-start(bf16[3,8449]{1,0:T(4,128)(2,1)S(1)} %pad_maximum_fusion.2), channel_id=1, source_target_pairs={{0,1},{1,2},{2,3},{3,4},{4,5},{5,6},{6,7},{7,8},{8,9},{9,10},{10,1... | collective-permute-start | bytes 152090 | tf_op jit(solution)/shard_map/ppermute | solution.py:21
  7.5 6.6 %copy-start.9 = (f32[128,256]{1,0:T(8,128)S(1)}, f32[128,256]{1,0:T(8,128)}, u32[]{:S(2)}) copy-start(f32[128,256]{1,0:T(8,128)} %param.18) | copy-start | bytes 393220
  7.5 6.7 %copy-start.14 = (f32[128]{0:T(128)S(1)}, f32[128]{0:T(128)}, u32[]{:S(2)}) copy-start(f32[128]{0:T(128)} %param.19) | copy-start | bytes 1540
  7.5 6.7 %copy-start.15 = (f32[128]{0:T(128)S(1)}, f32[128]{0:T(128)}, u32[]{:S(2)}) copy-start(f32[128]{0:T(128)} %param.20) | copy-start | bytes 1540
  7.5 7.0 %copy-start.7 = (bf16[4,8192]{1,0:T(4,128)(2,1)S(1)}, bf16[4,8192]{1,0:T(4,128)(2,1)}, u32[]{:S(2)}) copy-start(bf16[4,8192]{1,0:T(4,128)(2,1)} %param.22) | copy-start | bytes 196612
  7.6 7.1 %copy-start.10 = (bf16[8192]{0:T(1024)(128)(2,1)S(1)}, bf16[8192]{0:T(1024)(128)(2,1)}, u32[]{:S(2)}) copy-start(bf16[8192]{0:T(1024)(128)(2,1)} %param.23) | copy-start | bytes 49156
  7.6 7.1 %copy-start.13 = (bf16[4,256]{1,0:T(4,128)(2,1)S(1)}, bf16[4,256]{1,0:T(4,128)(2,1)}, u32[]{:S(2)}) copy-start(bf16[4,256]{1,0:T(4,128)(2,1)} %param.24) | copy-start | bytes 6148
  7.6 7.1 %copy-start.17 = (bf16[256]{0:T(256)(128)(2,1)S(1)}, bf16[256]{0:T(256)(128)(2,1)}, u32[]{:S(2)}) copy-start(bf16[256]{0:T(256)(128)(2,1)} %param.25) | copy-start | bytes 1540
  7.6 14.1 %copy-start.12 = (s32[256]{0:T(256)S(1)}, s32[256]{0:T(256)}, u32[]{:S(2)}) copy-start(s32[256]{0:T(256)} %param.27) | copy-start | bytes 3076
  7.6 16.9 %copy-start.8 = (bf16[256,256]{1,0:T(8,128)(2,1)S(1)}, bf16[256,256]{1,0:T(8,128)(2,1)}, u32[]{:S(2)}) copy-start(bf16[256,256]{1,0:T(8,128)(2,1)} %param.17) | copy-start | bytes 393220
  16.1 2.4 collective-permute-start.6
  18.6 23.2 %collective-permute-start.7 = (s32[4]{0:T(128)S(1)}, s32[4]{0:T(128)S(1)}, u32[]{:S(2)}, u32[]{:S(2)}) collective-permute-start(s32[4]{0:T(128)S(1)} %broadcast_select_fusion.2), channel_id=1, source_target_pairs={{0,4},{1,5},{2,6},{3,7},{4,0},{5,1},{6,2},{7,3},{8,12},{9,13},{10,... | collective-permute-start | bytes 56 | tf_op jit(solution)/shard_map/ppermute | solution.py:107
  41.8 10.2 %copy-start.4 = (bf16[256,8192]{0,1:T(8,128)(2,1)}, bf16[256,8192]{0,1:T(8,128)(2,1)S(1)}, u32[]{:S(2)}) copy-start(bf16[256,8192]{0,1:T(8,128)(2,1)S(1)} %multiply_convert_fusion.5) | copy-start | bytes 12582916
  41.9 2.4 collective-permute-start.8
  44.4 7.6 %collective-permute-start.9 = (s32[16]{0:T(128)S(1)}, s32[16]{0:T(128)S(1)}, u32[]{:S(2)}, u32[]{:S(2)}) collective-permute-start(s32[16]{0:T(128)S(1)} %broadcast_select_fusion.4), channel_id=1, source_target_pairs={{0,16},{1,17},{2,18},{3,19},{4,20},{5,21},{6,22},{7,23},{8,24},{9,... | collective-permute-start | bytes 200 | tf_op jit(solution)/shard_map/ppermute | solution.py:107
  52.5 2.0 copy-start
  55.9 6.3 %collective-permute-start.10 = (f32[64,64,128]{2,1,0:T(8,128)}, f32[64,64,128]{2,1,0:T(8,128)S(1)}, u32[]{:S(2)}, u32[]{:S(2)}) collective-permute-start(f32[64,64,128]{2,1,0:T(8,128)} %constant_dynamic-slice_fusion), channel_id=1, source_target_pairs={{0,1},{1,0},{2,3},{3,2},{4,5},{5,4},{6,7},{7,6},{8,9},{9,8},{10,11... | collective-permute-start | bytes 6291464 | tf_op jit(solution)/shard_map/ppermute | solution.py:156
  58.2 3.6 %collective-permute-start.4 = (f32[128]{0:T(128)S(1)}, f32[128]{0:T(128)S(1)}, u32[]{:S(2)}, u32[]{:S(2)}) collective-permute-start(f32[128]{0:T(128)S(1)} %get-tuple-element.78), channel_id=1, source_target_pairs={{0,1},{1,0},{2,3},{3,2},{4,5},{5,4},{6,7},{7,6},{8,9},{9,8},{10,11... | collective-permute-start | bytes 1544 | tf_op jit(solution)/shard_map/ppermute | solution.py:156
  62.2 104.5 %copy-start.2 = (f32[64,64,128]{2,1,0:T(8,128)}, f32[64,64,128]{2,1,0:T(8,128)S(1)}, u32[]{:S(2)}) copy-start(f32[64,64,128]{2,1,0:T(8,128)S(1)} %collective-permute-done.10) | copy-start | bytes 6291460
  65.0 50.5 %collective-permute-start.13 = (f32[64,64,128]{2,1,0:T(8,128)S(1)}, f32[64,64,128]{2,1,0:T(8,128)S(1)}, u32[]{:S(2)}, u32[]{:S(2)}) collective-permute-start(f32[64,64,128]{2,1,0:T(8,128)S(1)} %add_select_fusion), channel_id=1, source_target_pairs={{0,2},{1,3},{2,4},{3,5},{4,6},{5,7},{6,8},{7,9},{8,10},{9,11},{10,... | collective-permute-start | bytes 6291464 | tf_op jit(solution)/shard_map/ppermute | solution.py:69
  115.5 49.6 %collective-permute-start.14 = (f32[64,64,128]{2,1,0:T(8,128)S(1)}, f32[64,64,128]{2,1,0:T(8,128)S(1)}, u32[]{:S(2)}, u32[]{:S(2)}) collective-permute-start(f32[64,64,128]{2,1,0:T(8,128)S(1)} %collective-permute-done.13), channel_id=1, source_target_pairs={{0,2},{1,3},{2,4},{3,5},{4,6},{5,7},{6,8},{7,9},{8,10},{9,11},{10,... | collective-permute-start | bytes 6291464 | tf_op jit(solution)/shard_map/ppermute | solution.py:69
  117.4 47.7 %collective-permute-start.11 = (f32[64]{0:T(128)S(1)}, f32[64]{0:T(128)S(1)}, u32[]{:S(2)}, u32[]{:S(2)}) collective-permute-start(f32[64]{0:T(128)S(1)} %mul.373), channel_id=1, source_target_pairs={{0,2},{1,3},{2,4},{3,5},{4,6},{5,7},{6,8},{7,9},{8,10},{9,11},{10,... | collective-permute-start | bytes 776 | tf_op jit(solution)/shard_map/ppermute | solution.py:69
  166.7 8.4 %copy-start.16 = (f32[128]{0:T(128)S(1)}, f32[128]{0:T(128)}, u32[]{:S(2)}) copy-start(f32[128]{0:T(128)} %param.21) | copy-start | bytes 1540
  166.7 8.6 %copy-start.11 = (bf16[8192]{0:T(1024)(128)(2,1)S(1)}, bf16[8192]{0:T(1024)(128)(2,1)}, u32[]{:S(2)}) copy-start(bf16[8192]{0:T(1024)(128)(2,1)} %param.26) | copy-start | bytes 49156
  166.7 48.2 %collective-permute-start.15 = (f32[64,64,128]{2,1,0:T(8,128)}, f32[64,64,128]{2,1,0:T(8,128)}, u32[]{:S(2)}, u32[]{:S(2)}) collective-permute-start(f32[64,64,128]{2,1,0:T(8,128)} %multiply_add_fusion.3), channel_id=1, source_target_pairs={{0,4},{1,5},{2,6},{3,7},{4,8},{5,9},{6,10},{7,11},{8,12},{9,13},{1... | collective-permute-start | bytes 6291464 | tf_op jit(solution)/shard_map/ppermute | solution.py:69
  177.5 35.5 %collective-permute-start.12 = (f32[64]{0:T(128)S(1)}, f32[64]{0:T(128)S(1)}, u32[]{:S(2)}, u32[]{:S(2)}) collective-permute-start(f32[64]{0:T(128)S(1)} %collective-permute-done.11), channel_id=1, source_target_pairs={{0,2},{1,3},{2,4},{3,5},{4,6},{5,7},{6,8},{7,9},{8,10},{9,11},{10,... | collective-permute-start | bytes 776 | tf_op jit(solution)/shard_map/ppermute | solution.py:69
  213.0 5.2 %collective-permute-start.16 = (f32[64]{0:T(128)S(1)}, f32[64]{0:T(128)S(1)}, u32[]{:S(2)}, u32[]{:S(2)}) collective-permute-start(f32[64]{0:T(128)S(1)} %mul.437), channel_id=1, source_target_pairs={{0,4},{1,5},{2,6},{3,7},{4,8},{5,9},{6,10},{7,11},{8,12},{9,13},{1... | collective-permute-start | bytes 776 | tf_op jit(solution)/shard_map/ppermute | solution.py:69
  218.2 6.5 %copy-start.5 = (bf16[256,8192]{0,1:T(8,128)(2,1)S(1)}, bf16[256,8192]{0,1:T(8,128)(2,1)}, u32[]{:S(2)}) copy-start(bf16[256,8192]{0,1:T(8,128)(2,1)} %copy-done.4) | copy-start | bytes 12582916
  221.0 14.5 %copy-start.1 = (f32[128,64,128]{2,1,0:T(8,128)S(1)}, f32[128,64,128]{2,1,0:T(8,128)}, u32[]{:S(2)}) copy-start(f32[128,64,128]{2,1,0:T(8,128)} %copy-done) | copy-start | bytes 12582916
  221.0 14.5 %copy-start.3 = (f32[64,64,128]{2,1,0:T(8,128)S(1)}, f32[64,64,128]{2,1,0:T(8,128)}, u32[]{:S(2)}) copy-start(f32[64,64,128]{2,1,0:T(8,128)} %copy-done.2) | copy-start | bytes 6291460
  221.0 14.5 %collective-permute-start.17 = (bf16[64,64,128]{2,1,0:T(8,128)(2,1)S(1)}, bf16[64,64,128]{2,1,0:T(8,128)(2,1)S(1)}, u32[]{:S(2)}, u32[]{:S(2)}) collective-permute-start(bf16[64,64,128]{2,1,0:T(8,128)(2,1)S(1)} %fusion.21), channel_id=1, source_target_pairs={{0,1},{1,0},{2,3},{3,2},{4,5},{5,4},{6,7},{7,6},{8,9},{9,8},{10,11... | collective-permute-start | bytes 3145736 | tf_op jit(solution)/shard_map/ppermute | solution.py:167
  236.4 4.8 %copy-start.6 = (bf16[256,8192]{0,1:T(8,128)(2,1)S(1)}, bf16[256,8192]{0,1:T(8,128)(2,1)}, u32[]{:S(2)}) copy-start(bf16[256,8192]{0,1:T(8,128)(2,1)} %copy.39) | copy-start | bytes 12582916

commit v5 on v4

--- a/solution.py
+++ b/solution.py
@@ -226,21 +226,25 @@
     rim_segment = rims[:, channels + bc_width].astype(jnp.int32)
     ids = gather_rounds(segment_ids[tok_rows - 1 :], "ctx", 0, 2)
     ids, rim_x = lax.optimization_barrier((ids, rim_x))
-    x_conv = causal_conv(rim_x, x_in, rim_segment, segment_ids, conv_x_w, conv_x_b)
-    ids = gather_rounds(ids, "ctx", 2, 4)
-    ids, x_conv = lax.optimization_barrier((ids, x_conv))
+    pieces = 2 if head_count % 4 == 0 else 1
+
+    def pick(a, axis, piece):
+        if pieces == 1:
+            return a
+        lead, rest = a.shape[:axis], a.shape[axis + 1 :]
+        split = a.reshape(lead + (2, pieces, a.shape[axis] // (2 * pieces)) + rest)
+        taken = lax.index_in_dim(split, piece, axis + 1, keepdims=False)
+        return taken.reshape(lead + (a.shape[axis] // pieces,) + rest)
+
     bc_conv = causal_conv(rim_bc, bc_in, rim_segment, segment_ids, conv_bc_w, conv_bc_b)
     step_size = jax.nn.softplus(dt_raw + dt_bias[:, None])
     log_decay = -step_size * a_rate[:, None]
-    cum_decay = jnp.transpose(
-        jnp.cumsum(log_decay.reshape(head_count, block_count, GROUP), axis=2), (1, 0, 2)
-    )
-    step_blocks = jnp.transpose(step_size.reshape(head_count, block_count, GROUP), (1, 0, 2))
     seg_blocks = segment_ids.reshape(block_count, GROUP)
     seg_before = jnp.concatenate([rim_segment[rim_rows - 1 :], seg_blocks[:-1, -1]])
-    x_blocks = x_conv.reshape(block_count, GROUP, head_count, HEAD_DIM)
     b_blocks = bc_conv[:, :STATE].reshape(block_count, GROUP, STATE)
     c_blocks = bc_conv[:, STATE:].reshape(block_count, GROUP, STATE)
+    part_heads = head_count // pieces
+    part_channels = channels // pieces
 
     def state_of(item):
         x_group, b_group, steps_here, decay_here, segment, before = item
@@ -250,29 +254,64 @@
         x_group, b_group, c_group, steps_here, decay_here, segment = item
         return mixing_part(x_group, b_group, c_group, steps_here, decay_here, segment)
 
-    block_states, transmits = blockwise(
-        state_of, (x_blocks, b_blocks, step_blocks, cum_decay, seg_blocks, seg_before)
-    )
-    intra_items = (x_blocks, b_blocks, c_blocks, step_blocks, cum_decay, seg_blocks)
-    ids = gather_rounds(ids, "ctx", 4, lax.axis_size("ctx").bit_length())
-    ids, block_states = lax.optimization_barrier((ids, block_states))
-    far = [*long_runs(ids, paired, tok_rows), intra_items]
-    entering = chain_states(block_states, transmits, paired, far)
-    y_intra = blockwise(intra_of, far[2])
-
     def enter_of(item):
         c_group, decay_here, segment, before, entering_here = item
         return entry_part(c_group, entering_here, decay_here, segment, before)
 
-    y_state = blockwise(enter_of, (c_blocks, cum_decay, seg_blocks, seg_before, entering))
-    y_blocks = y_intra + y_state
-    x_heads = x_conv.reshape(tok_rows, head_count, HEAD_DIM).astype(jnp.float32)
-    y_total = y_blocks.reshape(tok_rows, head_count, HEAD_DIM) + skip_d[None, :, None] * x_heads
-    gated = y_total.reshape(tok_rows, channels) * jax.nn.silu(gate_z.astype(jnp.float32))
-    local_sq = jnp.sum(gated * gated, axis=1)
+    gated_parts = []
+    square_parts = []
+    for piece in range(pieces):
+        x_conv = causal_conv(
+            pick(rim_x, 1, piece),
+            pick(x_in, 1, piece),
+            rim_segment,
+            segment_ids,
+            pick(conv_x_w, 1, piece),
+            pick(conv_x_b, 0, piece),
+        )
+        if piece == 0:
+            ids = gather_rounds(ids, "ctx", 2, 4)
+            ids, x_conv = lax.optimization_barrier((ids, x_conv))
+        steps = pick(step_size, 0, piece)
+        decays = pick(log_decay, 0, piece)
+        cum_decay = jnp.transpose(
+            jnp.cumsum(decays.reshape(part_heads, block_count, GROUP), axis=2), (1, 0, 2)
+        )
+        step_blocks = jnp.transpose(steps.reshape(part_heads, block_count, GROUP), (1, 0, 2))
+        x_blocks = x_conv.reshape(block_count, GROUP, part_heads, HEAD_DIM)
+        block_states, transmits = blockwise(
+            state_of, (x_blocks, b_blocks, step_blocks, cum_decay, seg_blocks, seg_before)
+        )
+        if piece == 0:
+            ids = gather_rounds(ids, "ctx", 4, lax.axis_size("ctx").bit_length())
+            ids, block_states = lax.optimization_barrier((ids, block_states))
+            near, needed = long_runs(ids, paired, tok_rows)
+        intra_items = (x_blocks, b_blocks, c_blocks, step_blocks, cum_decay, seg_blocks)
+        far = [near, needed, intra_items]
+        entering = chain_states(block_states, transmits, paired, far)
+        y_intra = blockwise(intra_of, far[2])
+        y_state = blockwise(enter_of, (c_blocks, cum_decay, seg_blocks, seg_before, entering))
+        y_blocks = y_intra + y_state
+        x_heads = x_conv.reshape(tok_rows, part_heads, HEAD_DIM).astype(jnp.float32)
+        skip = pick(skip_d, 0, piece)
+        y_total = y_blocks.reshape(tok_rows, part_heads, HEAD_DIM) + skip[None, :, None] * x_heads
+        gate = pick(gate_z, 1, piece).astype(jnp.float32)
+        gated = y_total.reshape(tok_rows, part_channels) * jax.nn.silu(gate)
+        gated_parts.append(gated)
+        square_parts.append(jnp.sum(gated * gated, axis=1))
+    local_sq = square_parts[0]
+    for more in square_parts[1:]:
+        local_sq = local_sq + more
     total_sq = lax.psum(local_sq, "tp")
     scale = lax.rsqrt(total_sq / INNER + epsilon)
-    return (gated * scale[:, None] * norm_gain.astype(jnp.float32)).astype(jnp.bfloat16)
+    outs = [
+        (gated * scale[:, None] * pick(norm_gain, 0, piece).astype(jnp.float32)).astype(jnp.bfloat16)
+        for piece, gated in enumerate(gated_parts)
+    ]
+    if pieces == 1:
+        return outs[0]
+    joined = jnp.stack([o.reshape(tok_rows, 2, part_channels // 2) for o in outs], axis=2)
+    return joined.reshape(tok_rows, channels)
 
 
 def cores_paired(mesh):

time: 256 us -> 359 us (1.40); the launches traced: 255 us -> 354 us
  local copies, waits for them, and re-layouts: 28.4 us -> 115 us
  waiting for transfers between devices: 134 us -> 105 us
  other arithmetic: 40.8 us -> 69.6 us
  starting transfers between devices: 28 us -> 41.6 us
    unnamed x39 -> x95, local copies, waits for them, and re-layouts: 15 us -> 40.6 us
    ppermute x6 -> x12, waiting for transfers between devices: 127 us -> 101 us  [shifted(): lax.ppermute(value, axis, [(s, s + steps) for s in range(count - steps)])]
    slice x0 -> x10, local copies, waits for them, and re-layouts: none -> 20.5 us  [the longest x8 20.2 us: pick(): taken = lax.index_in_dim(split, piece, axis + 1, keepdims=False)]
    another operation x3 -> x13, local copies, waits for them, and re-layouts: 0.02 us -> 17.4 us  [the longest x1 11.3 us: local(): jnp.stack([o.reshape(tok_rows, 2, part_channels // 2) for o in outs], axi...]
    reshape x0 -> x8, local copies, waits for them, and re-layouts: none -> 17.2 us  [the longest x6 9.38 us: pick(): split = a.reshape(lead + (2, pieces, a.shape[axis] // (2 * pieces)) + rest)]
    ppermute x6 -> x12, starting transfers between devices: 13.3 us -> 28.2 us  [shifted(): lax.ppermute(value, axis, [(s, s + steps) for s in range(count - steps)])]
    another operation x8 -> x13, other arithmetic: 1.9 us -> 11.1 us
    mul x4 -> x6, local copies, waits for them, and re-layouts: 0.34 us -> 4.39 us  [local(): skip[None, :, None] * x_heads]
  transfers between devices with their start and end apart: 15 -> 24, of which waited for: 8 -> 7; matrix products, arithmetic and copies ran while one was open for 23% -> 41% of each run, Pallas kernels for 0% -> 0%
where the time goes in v5:
time: 359 us; the launch traced here: 354 us
  local copies, waits for them, and re-layouts  115 us (32%)
  waiting for transfers between devices  105 us (29%)
  other arithmetic  69.6 us (19%)
  starting transfers between devices  41.6 us (12%)
  matrix products  20.4 us (6%)
    ppermute x12, waiting for transfers between devices, shifted(): lax.ppermute(value, axis, [(s, s + steps) for s in range(count - steps)])  101 us
    unnamed x95, local copies, waits for them, and re-layouts  40.6 us
    ppermute x12, starting transfers between devices, shifted(): lax.ppermute(value, axis, [(s, s + steps) for s in range(count - steps)])  28.2 us
    slice x8, local copies, waits for them, and re-layouts, pick(): taken = lax.index_in_dim(split, piece, axis + 1, keepdims=False)  20.2 us
    convert_element_type x3, other arithmetic, causal_conv(): return jax.nn.silu(summed).astype(jnp.bfloat16)  16.8 us
    dot_general x2, matrix products, mixing_part(): jnp.einsum('hij,jhp->ihp', mixing, x_group, preferred_element_type=jnp.fl...  13.2 us
    another operation x1, local copies, waits for them, and re-layouts, local(): jnp.stack([o.reshape(tok_rows, 2, part_channels // 2) for o in outs], axi...  11.3 us
    reshape x6, local copies, waits for them, and re-layouts, pick(): split = a.reshape(lead + (2, pieces, a.shape[axis] // (2 * pieces)) + rest)  9.38 us
  transfers between devices with their start and end apart: 24, of which 7 were waited for; matrix products, arithmetic and copies ran while one was open for 41% of the time, Pallas kernels for 0%

profile of v5, /device:TPU:9, one launch (start us, length us, event | category | flops | bytes accessed | tf_op | source)
XLA Modules:
  0.0 354.1 jit_solution(16689596537467846427)
XLA Ops:
  2.5 3.7 %collective-permute-start.6 = (bf16[3,8449]{1,0:T(4,128)(2,1)S(1)}, bf16[3,8449]{1,0:T(4,128)(2,1)S(1)}, u32[]{:S(2)}, u32[]{:S(2)}) collective-permute-start(bf16[3,8449]{1,0:T(4,128)(2,1)S(1)} %pad_maximum_fusion.4), channel_id=1, source_target_pairs={{0,1},{1,2},{2,3},{3,4},{4,5},{5,6},{6,7},{7,8},{8,9},{9,10},{10,1... | collective-permute-start | bytes 152090 | tf_op jit(solution)/shard_map/ppermute | solution.py:21
  11.8 7.8 %reshape.555 = bf16[256,2,2,2048]{3,2,1,0:T(2,128)(2,1)} reshape(bf16[256,8192]{1,0:T(8,128)(2,1)} %param.17) | data formatting | bytes 8388608 | tf_op jit(solution)/shard_map/reshape | solution.py:235
  23.9 11.7 %fusion.73 = (bf16[256,2,1,2048]{3,2,1,0:T(2,128)(2,1)}, bf16[256,2,1,2048]{3,2,1,0:T(2,128)(2,1)}) fusion(bf16[256,2,2,2048]{3,2,1,0:T(2,128)(2,1)} %reshape.555), kind=kLoop, calls=%fused_computation.186 | loop fusion | bytes 8388608 | tf_op jit(solution)/shard_map/slice | solution.py:236
  35.6 8.9 %copy.117 = bf16[256,2,1,2048]{0,3,1,2:T(8,128)(2,1)S(1)} copy(bf16[256,2,1,2048]{3,2,1,0:T(2,128)(2,1)} %get-tuple-element.148) | data formatting | bytes 4194304
  45.2 10.5 %copy.115 = bf16[256,2,1,2048]{0,3,1,2:T(8,128)(2,1)} copy(bf16[256,2,1,2048]{3,2,1,0:T(2,128)(2,1)} %get-tuple-element.147) | data formatting | bytes 4194304
  55.7 6.4 %copy.99 = bf16[256,8192]{0,1:T(8,128)(2,1)} copy(bf16[256,8192]{1,0:T(8,128)(2,1)} %param.18) | data formatting | bytes 8388608 | tf_op args[1]
  62.0 4.5 %fusion.72 = (bf16[256,2,1,2048]{0,3,2,1:T(8,128)(2,1)}, bf16[256,2,1,2048]{0,3,2,1:T(8,128)(2,1)}) fusion(bf16[256,2,2,2048]{0,3,2,1:T(8,128)(2,1)} %bitcast.167), kind=kLoop, calls=%fused_computation.185 | loop fusion | bytes 8388608 | tf_op jit(solution)/shard_map/slice | solution.py:236
  66.5 3.9 %copy.119 = bf16[256,2,1,2048]{3,0,2,1:T(8,128)(2,1)} copy(bf16[256,2,1,2048]{0,3,2,1:T(8,128)(2,1)} %get-tuple-element.146) | data formatting | bytes 4194304
  70.4 4.2 %copy.110 = f32[256,2,1,2048]{0,3,1,2:T(8,128)} copy(bf16[256,2,1,2048]{3,0,2,1:T(8,128)(2,1)} %copy.119) | data formatting | bytes 6291456 | tf_op jit(solution)/shard_map/convert_element_type | solution.py:298
  91.3 7.9 %multiply_convert_fusion.10 = bf16[256,4096]{0,1:T(8,128)(2,1)S(1)} fusion(bf16[256,4096]{0,1:T(8,128)(2,1)S(1)} %bitcast.168, bf16[3,4096]{0,1:T(8,128)(2,1)S(1)} %bitcast.176, f32[4096]{0:T(1024)} %bitcast.196, f32[4096]{0:T(1024)} %bitcast.197, f32[4096]{0:T(1024)} %bitcast.198, f32[4096]{0:T(1024)} %bitcast.199, f32[4096]{0:T(1024)} %bitcast.203, ...), kind=kLoop, calls=%fused_computation.45 | loop fusion | flops 30408704 | bytes 4303872 | tf_op jit(solution)/shard_map/convert_element_type | solution.py:37
  99.2 2.7 fusion.34
  107.1 2.2 copy.95
  109.3 8.6 %multiply_convert_fusion.11 = bf16[256,4096]{0,1:T(8,128)(2,1)S(1)} fusion(bf16[256,4096]{0,1:T(8,128)(2,1)S(1)} %bitcast.169, bf16[3,4096]{0,1:T(8,128)(2,1)} %bitcast.177, f32[4096]{0:T(1024)} %bitcast.193, f32[256]{0:T(256)} %copy-done.32, f32[4096]{0:T(1024)} %bitcast.194, f32[256]{0:T(256)} %copy-done.33, f32[4096]{0:T(1024)} %bitcast.195, ...), kind=kLoop, calls=%fused_computation.50 | loop fusion | flops 30408704 | bytes 4303872 | tf_op jit(solution)/shard_map/convert_element_type | solution.py:37
  118.9 2.2 collective-permute-done.11
  121.2 2.3 collective-permute-start.12
  123.5 2.7 fusion.35
  132.1 4.0 %copy.118 = bf16[256,2,1,2048]{3,0,2,1:T(8,128)(2,1)} copy(bf16[256,2,1,2048]{0,3,2,1:T(8,128)(2,1)} %get-tuple-element.145) | data formatting | bytes 4194304
  136.1 4.1 %copy.101 = f32[256,2,1,2048]{0,3,1,2:T(8,128)} copy(bf16[256,2,1,2048]{3,0,2,1:T(8,128)(2,1)} %copy.118) | data formatting | bytes 6291456 | tf_op jit(solution)/shard_map/convert_element_type | solution.py:298
  150.4 2.8 add_select_fusion
  153.2 2.2 collective-permute-start.25
  155.5 2.5 add_select_fusion.1
  158.0 3.0 collective-permute-start.16
  164.2 3.1 collective-permute-start.23
  168.4 13.5 %collective-permute-done.25 = f32[32,64,128]{2,1,0:T(8,128)} collective-permute-done((f32[32,64,128]{2,1,0:T(8,128)}, f32[32,64,128]{2,1,0:T(8,128)}, u32[]{:S(2)}, u32[]{:S(2)}) %collective-permute-start.25) | collective-permute-done | bytes 1048608 | tf_op jit(solution)/shard_map/ppermute | solution.py:69
  182.0 1.9 collective-permute-start.26
  183.9 20.6 %collective-permute-done.16 = f32[32,64,128]{2,1,0:T(8,128)} collective-permute-done((f32[32,64,128]{2,1,0:T(8,128)}, f32[32,64,128]{2,1,0:T(8,128)}, u32[]{:S(2)}, u32[]{:S(2)}) %collective-permute-start.16) | collective-permute-done | bytes 1048608 | tf_op jit(solution)/shard_map/ppermute | solution.py:69
  204.4 1.9 collective-permute-start.17
  206.4 7.2 %fusion.1 = f32[64,64,256]{2,1,0:T(8,128)} fusion(f32[64,256]{1,0:T(8,128)} %bitcast.189, f32[64,256]{1,0:T(8,128)S(1)} %bitcast.205, f32[256,256]{1,0:T(8,128)S(1)} %fusion.50, pred[256,256]{1,0:T(8,128)(4,1)S(1)} %fusion.46, bf16[1,256,64,64]{1,3,2,0:T(8,128)(2,1)} %bitcast.175), kind=kOutput, calls=%fused_computation.7 | convolution fusion | flops 557842432 | bytes 6750208 | tf_op jit(solution)/shard_map/hij,jhp->ihp/dot_general | solution.py:48
  213.6 2.5 collective-permute-start.14
  216.5 2.2 collective-permute-start.24
  218.7 8.1 %collective-permute-done.26 = f32[32,64,128]{2,1,0:T(8,128)S(1)} collective-permute-done((f32[32,64,128]{2,1,0:T(8,128)}, f32[32,64,128]{2,1,0:T(8,128)S(1)}, u32[]{:S(2)}, u32[]{:S(2)}) %collective-permute-start.26) | collective-permute-done | bytes 1048608 | tf_op jit(solution)/shard_map/ppermute | solution.py:69
  228.2 1.9 collective-permute-start.27
  230.2 31.6 %collective-permute-done.14 = f32[32]{0:T(128)S(1)} collective-permute-done((f32[32]{0:T(128)S(1)}, f32[32]{0:T(128)S(1)}, u32[]{:S(2)}, u32[]{:S(2)}) %collective-permute-start.14) | collective-permute-done | bytes 160 | tf_op jit(solution)/shard_map/ppermute | solution.py:69
  261.7 2.4 multiply_add_fusion.7
  264.2 1.9 collective-permute-start.18
  266.1 6.0 %fusion = f32[64,64,256]{2,1,0:T(8,128)} fusion(f32[64,256]{1,0:T(8,128)S(1)} %bitcast.188, f32[64,256]{1,0:T(8,128)S(1)} %bitcast.204, f32[256,256]{1,0:T(8,128)S(1)} %fusion.56, pred[256,256]{1,0:T(8,128)(4,1)S(1)} %fusion.47, bf16[1,256,64,64]{1,3,2,0:T(8,128)(2,1)S(1)} %bitcast.173), kind=kOutput, calls=%fused_computation.6 | convolution fusion | flops 557842432 | bytes 6750208 | tf_op jit(solution)/shard_map/hij,jhp->ihp/dot_general | solution.py:48
  274.0 3.5 collective-permute-start.28
  277.5 27.5 %collective-permute-done.15 = f32[32]{0:T(128)S(1)} collective-permute-done((f32[32]{0:T(128)S(1)}, f32[32]{0:T(128)S(1)}, u32[]{:S(2)}, u32[]{:S(2)}) %collective-permute-start.15) | collective-permute-done | bytes 160 | tf_op jit(solution)/shard_map/ppermute | solution.py:69
  305.0 2.0 collective-permute-start.19
  307.3 2.6 fusion.44
  310.7 2.7 multiply_add_fusion.6
  313.5 1.9 fusion.42
  320.6 2.2 multiply_reduce_fusion
  328.2 2.2 multiply_reduce_fusion.1
  330.5 2.2 multiply_convert_fusion.9
  332.7 2.4 pad_maximum_fusion
  335.0 11.3 %copy.111 = bf16[256,2,2,2048]{3,2,1,0:T(2,128)(2,1)} copy(bf16[256,2,2,2048]{0,3,1,2:T(8,128)(2,1)} %pad_maximum_fusion) | data formatting | bytes 8388608 | tf_op jit(solution)/shard_map/stack | solution.py:313
  346.3 7.8 %reshape.576 = bf16[256,8192]{1,0:T(8,128)(2,1)} reshape(bf16[256,2,2,2048]{3,2,1,0:T(2,128)(2,1)} %copy.111) | data formatting | bytes 8388608 | tf_op jit(solution)/shard_map/reshape | solution.py:314
  (218 shorter events, 69.4 us)
Async XLA Ops:
  2.5 77.0 %collective-permute-start.6 = (bf16[3,8449]{1,0:T(4,128)(2,1)S(1)}, bf16[3,8449]{1,0:T(4,128)(2,1)S(1)}, u32[]{:S(2)}, u32[]{:S(2)}) collective-permute-start(bf16[3,8449]{1,0:T(4,128)(2,1)S(1)} %pad_maximum_fusion.4), channel_id=1, source_target_pairs={{0,1},{1,2},{2,3},{3,4},{4,5},{5,6},{6,7},{7,8},{8,9},{9,10},{10,1... | collective-permute-start | bytes 152090 | tf_op jit(solution)/shard_map/ppermute | solution.py:21
  7.6 67.7 %collective-permute-start.8 = (s32[1]{0:T(128)}, s32[1]{0:T(128)}, u32[]{:S(2)}, u32[]{:S(2)}) collective-permute-start(s32[1]{0:T(128)} %slice.222), channel_id=1, source_target_pairs={{0,1},{1,0},{2,3},{3,2},{4,5},{5,4},{6,7},{7,6},{8,9},{9,8},{10,11... | collective-permute-start | bytes 20 | tf_op jit(solution)/shard_map/ppermute | solution.py:107
  11.8 11.3 %copy-start.26 = (bf16[4,8192]{1,0:T(4,128)(2,1)S(1)}, bf16[4,8192]{1,0:T(4,128)(2,1)}, u32[]{:S(2)}) copy-start(bf16[4,8192]{1,0:T(4,128)(2,1)} %param.24) | copy-start | bytes 196612
  35.6 8.9 %copy-start.30 = (bf16[8192]{0:T(1024)(128)(2,1)S(1)}, bf16[8192]{0:T(1024)(128)(2,1)}, u32[]{:S(2)}) copy-start(bf16[8192]{0:T(1024)(128)(2,1)} %param.25) | copy-start | bytes 49156
  35.6 9.6 %copy-start.35 = (bf16[4,256]{1,0:T(4,128)(2,1)S(1)}, bf16[4,256]{1,0:T(4,128)(2,1)}, u32[]{:S(2)}) copy-start(bf16[4,256]{1,0:T(4,128)(2,1)} %param.26) | copy-start | bytes 6148
  35.6 9.6 %copy-start.41 = (bf16[256]{0:T(256)(128)(2,1)S(1)}, bf16[256]{0:T(256)(128)(2,1)}, u32[]{:S(2)}) copy-start(bf16[256]{0:T(256)(128)(2,1)} %param.27) | copy-start | bytes 1540
  70.4 4.2 %copy-start.39 = (f32[128]{0:T(128)S(1)}, f32[128]{0:T(128)}, u32[]{:S(2)}) copy-start(f32[128]{0:T(128)} %param.23) | copy-start | bytes 1540
  70.4 9.8 %copy-start.28 = (s32[256]{0:T(256)S(1)}, s32[256]{0:T(256)}, u32[]{:S(2)}) copy-start(s32[256]{0:T(256)} %param.29) | copy-start | bytes 3076
  70.4 14.3 %copy-start.19 = (bf16[256,256]{1,0:T(8,128)(2,1)S(1)}, bf16[256,256]{1,0:T(8,128)(2,1)}, u32[]{:S(2)}) copy-start(bf16[256,256]{1,0:T(8,128)(2,1)} %param.19) | copy-start | bytes 393220
  76.6 2.4 collective-permute-start.9
  85.0 16.9 %copy-start.20 = (f32[256,128]{1,0:T(8,128)}, f32[256,128]{1,0:T(8,128)S(1)}, u32[]{:S(2)}) copy-start(f32[256,128]{1,0:T(8,128)S(1)} %get-tuple-element.155) | copy-start | bytes 393220
  99.2 5.0 %copy-start.11 = (bf16[256,4096]{0,1:T(8,128)(2,1)}, bf16[256,4096]{0,1:T(8,128)(2,1)S(1)}, u32[]{:S(2)}) copy-start(bf16[256,4096]{0,1:T(8,128)(2,1)S(1)} %multiply_convert_fusion.10) | copy-start | bytes 6291460
  99.2 10.1 %copy-start.5 = (bf16[256,2,1,2048]{0,3,1,2:T(8,128)(2,1)S(1)}, bf16[256,2,1,2048]{0,3,1,2:T(8,128)(2,1)}, u32[]{:S(2)}) copy-start(bf16[256,2,1,2048]{0,3,1,2:T(8,128)(2,1)} %copy.115) | copy-start | bytes 6291460
  104.2 46.2 %collective-permute-start.22 = (f32[32,64,128]{2,1,0:T(8,128)}, f32[32,64,128]{2,1,0:T(8,128)S(1)}, u32[]{:S(2)}, u32[]{:S(2)}) collective-permute-start(f32[32,64,128]{2,1,0:T(8,128)} %constant_dynamic-slice_fusion), channel_id=1, source_target_pairs={{0,1},{1,0},{2,3},{3,2},{4,5},{5,4},{6,7},{7,6},{8,9},{9,8},{10,11... | collective-permute-start | bytes 3145736 | tf_op jit(solution)/shard_map/ppermute | solution.py:156
  105.9 12.1 %collective-permute-start.10 = (s32[4]{0:T(128)}, s32[4]{0:T(128)}, u32[]{:S(2)}, u32[]{:S(2)}) collective-permute-start(s32[4]{0:T(128)} %broadcast_select_fusion.3), channel_id=1, source_target_pairs={{0,4},{1,5},{2,6},{3,7},{4,0},{5,1},{6,2},{7,3},{8,12},{9,13},{10,... | collective-permute-start | bytes 56 | tf_op jit(solution)/shard_map/ppermute | solution.py:107
  109.3 14.2 %copy-start.21 = (f32[256,128]{1,0:T(8,128)S(1)}, f32[256,128]{1,0:T(8,128)}, u32[]{:S(2)}) copy-start(f32[256,128]{1,0:T(8,128)} %copy-done.20) | copy-start | bytes 393220
  109.3 14.2 %copy-start.27 = (f32[64,256]{1,0:T(8,128)S(1)}, f32[64,256]{1,0:T(8,128)}, u32[]{:S(2)}) copy-start(f32[64,256]{1,0:T(8,128)} %get-tuple-element.179) | copy-start | bytes 196612
  109.3 17.6 %copy-start.38 = (f32[64]{0:T(128)S(1)}, f32[64]{0:T(128)}, u32[]{:S(2)}) copy-start(f32[64]{0:T(128)} %get-tuple-element.132) | copy-start | bytes 772
  117.9 9.2 %copy-start.8 = (bf16[256,4096]{0,1:T(8,128)(2,1)}, bf16[256,4096]{0,1:T(8,128)(2,1)S(1)}, u32[]{:S(2)}) copy-start(bf16[256,4096]{0,1:T(8,128)(2,1)S(1)} %multiply_convert_fusion.11) | copy-start | bytes 6291460
  118.7 2.4 collective-permute-start.11
  121.2 5.0 %collective-permute-start.12 = (s32[16]{0:T(128)S(1)}, s32[16]{0:T(128)S(1)}, u32[]{:S(2)}, u32[]{:S(2)}) collective-permute-start(s32[16]{0:T(128)S(1)} %broadcast_select_fusion.5), channel_id=1, source_target_pairs={{0,16},{1,17},{2,18},{3,19},{4,20},{5,21},{6,22},{7,23},{8,24},{9,... | collective-permute-start | bytes 200 | tf_op jit(solution)/shard_map/ppermute | solution.py:107
  126.2 3.7 %copy-start.34 = (f32[2,2,32]{2,1,0:T(2,128)S(1)}, f32[2,2,32]{2,1,0:T(2,128)}, u32[]{:S(2)}) copy-start(f32[2,2,32]{2,1,0:T(2,128)} %reshape.564) | copy-start | bytes 1540
  128.2 27.3 %collective-permute-start.13 = (f32[32,64,128]{2,1,0:T(8,128)}, f32[32,64,128]{2,1,0:T(8,128)}, u32[]{:S(2)}, u32[]{:S(2)}) collective-permute-start(f32[32,64,128]{2,1,0:T(8,128)} %constant_dynamic-slice_fusion.1), channel_id=1, source_target_pairs={{0,1},{1,0},{2,3},{3,2},{4,5},{5,4},{6,7},{7,6},{8,9},{9,8},{10,11... | collective-permute-start | bytes 3145736 | tf_op jit(solution)/shard_map/ppermute | solution.py:156
  143.1 17.9 %copy-start.40 = (s32[32]{0:T(128)S(1)}, s32[32]{0:T(128)}, u32[]{:S(2)}) copy-start(s32[32]{0:T(128)} %broadcast_select_fusion.6) | copy-start | bytes 388
  145.3 1.5 collective-permute-start.21
  146.2 21.2 %copy-start.17 = (f32[1,64,256]{2,0,1:T(1,128)S(1)}, f32[1,64,256]{2,0,1:T(1,128)}, u32[]{:S(2)}) copy-start(f32[1,64,256]{2,0,1:T(1,128)} %reduce_window_sum.59) | copy-start | bytes 196612
  146.2 2.4 collective-permute-start.7
  150.4 63.2 %copy-start.3 = (f32[32,64,128]{2,1,0:T(8,128)}, f32[32,64,128]{2,1,0:T(8,128)S(1)}, u32[]{:S(2)}) copy-start(f32[32,64,128]{2,1,0:T(8,128)S(1)} %collective-permute-done.22) | copy-start | bytes 3145732
  153.2 28.7 %collective-permute-start.25 = (f32[32,64,128]{2,1,0:T(8,128)}, f32[32,64,128]{2,1,0:T(8,128)}, u32[]{:S(2)}, u32[]{:S(2)}) collective-permute-start(f32[32,64,128]{2,1,0:T(8,128)} %add_select_fusion), channel_id=1, source_target_pairs={{0,2},{1,3},{2,4},{3,5},{4,6},{5,7},{6,8},{7,9},{8,10},{9,11},{10,... | collective-permute-start | bytes 3145736 | tf_op jit(solution)/shard_map/ppermute | solution.py:69
  158.0 46.5 %collective-permute-start.16 = (f32[32,64,128]{2,1,0:T(8,128)}, f32[32,64,128]{2,1,0:T(8,128)}, u32[]{:S(2)}, u32[]{:S(2)}) collective-permute-start(f32[32,64,128]{2,1,0:T(8,128)} %add_select_fusion.1), channel_id=1, source_target_pairs={{0,2},{1,3},{2,4},{3,5},{4,6},{5,7},{6,8},{7,9},{8,10},{9,11},{10,... | collective-permute-start | bytes 3145736 | tf_op jit(solution)/shard_map/ppermute | solution.py:69
  164.2 52.3 %collective-permute-start.23 = (f32[32]{0:T(128)}, f32[32]{0:T(128)S(1)}, u32[]{:S(2)}, u32[]{:S(2)}) collective-permute-start(f32[32]{0:T(128)} %mul.690), channel_id=1, source_target_pairs={{0,2},{1,3},{2,4},{3,5},{4,6},{5,7},{6,8},{7,9},{8,10},{9,11},{10,... | collective-permute-start | bytes 392 | tf_op jit(solution)/shard_map/ppermute | solution.py:69
  182.0 44.8 %collective-permute-start.26 = (f32[32,64,128]{2,1,0:T(8,128)}, f32[32,64,128]{2,1,0:T(8,128)S(1)}, u32[]{:S(2)}, u32[]{:S(2)}) collective-permute-start(f32[32,64,128]{2,1,0:T(8,128)} %collective-permute-done.25), channel_id=1, source_target_pairs={{0,2},{1,3},{2,4},{3,5},{4,6},{5,7},{6,8},{7,9},{8,10},{9,11},{10,... | collective-permute-start | bytes 3145736 | tf_op jit(solution)/shard_map/ppermute | solution.py:69
  204.4 57.3 %collective-permute-start.17 = (f32[32,64,128]{2,1,0:T(8,128)}, f32[32,64,128]{2,1,0:T(8,128)S(1)}, u32[]{:S(2)}, u32[]{:S(2)}) collective-permute-start(f32[32,64,128]{2,1,0:T(8,128)} %collective-permute-done.16), channel_id=1, source_target_pairs={{0,2},{1,3},{2,4},{3,5},{4,6},{5,7},{6,8},{7,9},{8,10},{9,11},{10,... | collective-permute-start | bytes 3145736 | tf_op jit(solution)/shard_map/ppermute | solution.py:69
  206.4 7.3 %copy-start.42 = (f32[32]{0:T(128)S(1)}, f32[32]{0:T(128)}, u32[]{:S(2)}) copy-start(f32[32]{0:T(128)} %mul.614) | copy-start | bytes 388
  206.4 9.8 %copy-start.29 = (s32[256]{0:T(256)S(1)}, s32[256]{0:T(256)}, u32[]{:S(2)}) copy-start(s32[256]{0:T(256)} %param.29) | copy-start | bytes 3076
  213.6 52.5 %copy-start.9 = (bf16[256,4096]{0,1:T(8,128)(2,1)S(1)}, bf16[256,4096]{0,1:T(8,128)(2,1)}, u32[]{:S(2)}) copy-start(bf16[256,4096]{0,1:T(8,128)(2,1)} %copy-done.8) | copy-start | bytes 6291460
  213.6 52.5 %copy-start.18 = (f32[2,1,32,256]{3,2,1,0:T(8,128)S(1)}, f32[2,1,32,256]{3,2,1,0:T(8,128)}, u32[]{:S(2)}) copy-start(f32[2,1,32,256]{3,2,1,0:T(8,128)} %get-tuple-element.151) | copy-start | bytes 196612
  213.6 48.1 %collective-permute-start.14 = (f32[32]{0:T(128)S(1)}, f32[32]{0:T(128)S(1)}, u32[]{:S(2)}, u32[]{:S(2)}) collective-permute-start(f32[32]{0:T(128)S(1)} %copy-done.42), channel_id=1, source_target_pairs={{0,2},{1,3},{2,4},{3,5},{4,6},{5,7},{6,8},{7,9},{8,10},{9,11},{10,... | collective-permute-start | bytes 392 | tf_op jit(solution)/shard_map/ppermute | solution.py:69
  216.5 57.5 %collective-permute-start.24 = (f32[32]{0:T(128)S(1)}, f32[32]{0:T(128)S(1)}, u32[]{:S(2)}, u32[]{:S(2)}) collective-permute-start(f32[32]{0:T(128)S(1)} %collective-permute-done.23), channel_id=1, source_target_pairs={{0,2},{1,3},{2,4},{3,5},{4,6},{5,7},{6,8},{7,9},{8,10},{9,11},{10,... | collective-permute-start | bytes 392 | tf_op jit(solution)/shard_map/ppermute | solution.py:69
  228.2 78.8 %collective-permute-start.27 = (f32[32,64,128]{2,1,0:T(8,128)S(1)}, f32[32,64,128]{2,1,0:T(8,128)S(1)}, u32[]{:S(2)}, u32[]{:S(2)}) collective-permute-start(f32[32,64,128]{2,1,0:T(8,128)S(1)} %multiply_add_fusion.5), channel_id=1, source_target_pairs={{0,4},{1,5},{2,6},{3,7},{4,8},{5,9},{6,10},{7,11},{8,12},{9,13},{1... | collective-permute-start | bytes 3145736 | tf_op jit(solution)/shard_map/ppermute | solution.py:69
  264.2 46.5 %collective-permute-start.18 = (f32[32,64,128]{2,1,0:T(8,128)}, f32[32,64,128]{2,1,0:T(8,128)}, u32[]{:S(2)}, u32[]{:S(2)}) collective-permute-start(f32[32,64,128]{2,1,0:T(8,128)} %multiply_add_fusion.7), channel_id=1, source_target_pairs={{0,4},{1,5},{2,6},{3,7},{4,8},{5,9},{6,10},{7,11},{8,12},{9,13},{1... | collective-permute-start | bytes 3145736 | tf_op jit(solution)/shard_map/ppermute | solution.py:69
  272.1 32.9 %collective-permute-start.15 = (f32[32]{0:T(128)S(1)}, f32[32]{0:T(128)S(1)}, u32[]{:S(2)}, u32[]{:S(2)}) collective-permute-start(f32[32]{0:T(128)S(1)} %collective-permute-done.14), channel_id=1, source_target_pairs={{0,2},{1,3},{2,4},{3,5},{4,6},{5,7},{6,8},{7,9},{8,10},{9,11},{10,... | collective-permute-start | bytes 392 | tf_op jit(solution)/shard_map/ppermute | solution.py:69
  274.0 33.2 %collective-permute-start.28 = (f32[32]{0:T(128)S(1)}, f32[32]{0:T(128)S(1)}, u32[]{:S(2)}, u32[]{:S(2)}) collective-permute-start(f32[32]{0:T(128)S(1)} %mul.718), channel_id=1, source_target_pairs={{0,4},{1,5},{2,6},{3,7},{4,8},{5,9},{6,10},{7,11},{8,12},{9,13},{1... | collective-permute-start | bytes 392 | tf_op jit(solution)/shard_map/ppermute | solution.py:69
  305.0 8.4 %collective-permute-start.19 = (f32[32]{0:T(128)S(1)}, f32[32]{0:T(128)S(1)}, u32[]{:S(2)}, u32[]{:S(2)}) collective-permute-start(f32[32]{0:T(128)S(1)} %mul.670), channel_id=1, source_target_pairs={{0,4},{1,5},{2,6},{3,7},{4,8},{5,9},{6,10},{7,11},{8,12},{9,13},{1... | collective-permute-start | bytes 392 | tf_op jit(solution)/shard_map/ppermute | solution.py:69
  309.9 5.6 %collective-permute-start.29 = (bf16[32,64,128]{2,1,0:T(8,128)(2,1)}, bf16[32,64,128]{2,1,0:T(8,128)(2,1)}, u32[]{:S(2)}, u32[]{:S(2)}) collective-permute-start(bf16[32,64,128]{2,1,0:T(8,128)(2,1)} %fusion.44), channel_id=1, source_target_pairs={{0,1},{1,0},{2,3},{3,2},{4,5},{5,4},{6,7},{7,6},{8,9},{9,8},{10,11... | collective-permute-start | bytes 1572872 | tf_op jit(solution)/shard_map/ppermute | solution.py:167
  313.4 4.3 %copy-start.13 = (f32[64,64,256]{2,1,0:T(8,128)S(1)}, f32[64,64,256]{2,1,0:T(8,128)}, u32[]{:S(2)}) copy-start(f32[64,64,256]{2,1,0:T(8,128)} %fusion.1) | copy-start | bytes 12582916
  313.4 4.3 %copy-start.16 = (f32[256,64]{0,1:T(8,128)S(1)}, f32[256,64]{0,1:T(8,128)}, u32[]{:S(2)}) copy-start(f32[256,64]{0,1:T(8,128)} %get-tuple-element.181) | copy-start | bytes 196612
  315.4 7.5 %collective-permute-start.20 = (bf16[32,64,128]{2,1,0:T(8,128)(2,1)S(1)}, bf16[32,64,128]{2,1,0:T(8,128)(2,1)S(1)}, u32[]{:S(2)}, u32[]{:S(2)}) collective-permute-start(bf16[32,64,128]{2,1,0:T(8,128)(2,1)S(1)} %fusion.42), channel_id=1, source_target_pairs={{0,1},{1,0},{2,3},{3,2},{4,5},{5,4},{6,7},{7,6},{8,9},{9,8},{10,11... | collective-permute-start | bytes 1572872 | tf_op jit(solution)/shard_map/ppermute | solution.py:167
  (19 other events, 43.3 us)

commit v6 on v5

--- a/solution.py
+++ b/solution.py
@@ -231,10 +231,8 @@
     def pick(a, axis, piece):
         if pieces == 1:
             return a
-        lead, rest = a.shape[:axis], a.shape[axis + 1 :]
-        split = a.reshape(lead + (2, pieces, a.shape[axis] // (2 * pieces)) + rest)
-        taken = lax.index_in_dim(split, piece, axis + 1, keepdims=False)
-        return taken.reshape(lead + (a.shape[axis] // pieces,) + rest)
+        size = a.shape[axis] // pieces
+        return lax.slice_in_dim(a, piece * size, (piece + 1) * size, axis=axis)
 
     bc_conv = causal_conv(rim_bc, bc_in, rim_segment, segment_ids, conv_bc_w, conv_bc_b)
     step_size = jax.nn.softplus(dt_raw + dt_bias[:, None])
@@ -310,8 +308,7 @@
     ]
     if pieces == 1:
         return outs[0]
-    joined = jnp.stack([o.reshape(tok_rows, 2, part_channels // 2) for o in outs], axis=2)
-    return joined.reshape(tok_rows, channels)
+    return jnp.concatenate(outs, axis=1)
 
 
 def cores_paired(mesh):

time: 359 us -> 290 us (0.81)
  local copies, waits for them, and re-layouts: 115 us -> 46.5 us
    unnamed x95 -> x114, local copies, waits for them, and re-layouts: 40.6 us -> 20 us
    reshape x8 -> x2, local copies, waits for them, and re-layouts: 17.2 us -> 0.04 us  [the longest x6 9.38 us: pick(): split = a.reshape(lead + (2, pieces, a.shape[axis] // (2 * pieces)) + rest)]
    another operation x13, local copies, waits for them, and re-layouts: 17.4 us -> 2.11 us  [the longest x1 11.3 us: local(): jnp.stack([o.reshape(tok_rows, 2, part_channels // 2) for o in outs], axi...]
    slice x9 -> x8, local copies, waits for them, and re-layouts: 20.4 us -> 10.8 us  [the longest x7 10.7 us: pick(): return lax.slice_in_dim(a, piece * size, (piece + 1) * size, axis=axis)]
    convert_element_type x2 -> x0, local copies, waits for them, and re-layouts: 8.29 us -> none  [local(): gate = pick(gate_z, 1, piece).astype(jnp.float32)]
    concatenate x0 -> x1, local copies, waits for them, and re-layouts: none -> 6.31 us  [local(): return jnp.concatenate(outs, axis=1)]
  transfers between devices with their start and end apart: 24 -> 24, of which waited for: 7 -> 7; matrix products, arithmetic and copies ran while one was open for 41% -> 39% of each run, Pallas kernels for 0% -> 0%
where the time goes in v6:
time: 290 us; the launch traced here: 286 us
  waiting for transfers between devices  105 us (36%)
  other arithmetic  69.8 us (24%)
  local copies, waits for them, and re-layouts  46.5 us (16%)
  starting transfers between devices  41.6 us (14%)
  matrix products  20.3 us (7%)
  between operations  2.92 us (1%)
    ppermute x12, waiting for transfers between devices, shifted(): lax.ppermute(value, axis, [(s, s + steps) for s in range(count - steps)])  102 us
    ppermute x12, starting transfers between devices, shifted(): lax.ppermute(value, axis, [(s, s + steps) for s in range(count - steps)])  28.6 us
    unnamed x114, local copies, waits for them, and re-layouts  20 us
    convert_element_type x3, other arithmetic, causal_conv(): return jax.nn.silu(summed).astype(jnp.bfloat16)  16.4 us
    dot_general x2, matrix products, mixing_part(): jnp.einsum('hij,jhp->ihp', mixing, x_group, preferred_element_type=jnp.fl...  13.1 us
    slice x7, local copies, waits for them, and re-layouts, pick(): return lax.slice_in_dim(a, piece * size, (piece + 1) * size, axis=axis)  10.7 us
    another operation x12, other arithmetic  8.03 us
    add x4, other arithmetic, scan_round(): return (transmit * far_t, transmit[:, None, None] * far_s + state)  6.7 us
  transfers between devices with their start and end apart: 24, of which 7 were waited for; matrix products, arithmetic and copies ran while one was open for 39% of the time, Pallas kernels for 0%

profile of v6, /device:TPU:9, one launch (start us, length us, event | category | flops | bytes accessed | tf_op | source)
XLA Modules:
  0.0 286.4 jit_solution(17908434181141419830)
XLA Ops:
  4.6 3.0 %collective-permute-start.6 = (bf16[3,8449]{1,0:T(4,128)(2,1)S(1)}, bf16[3,8449]{1,0:T(4,128)(2,1)S(1)}, u32[]{:S(2)}, u32[]{:S(2)}) collective-permute-start(bf16[3,8449]{1,0:T(4,128)(2,1)S(1)} %pad_maximum_fusion.4), channel_id=1, source_target_pairs={{0,1},{1,2},{2,3},{3,4},{4,5},{5,6},{6,7},{7,8},{8,9},{9,10},{10,1... | collective-permute-start | bytes 152090 | tf_op jit(solution)/shard_map/ppermute | solution.py:21
  7.6 1.7 negate_multiply_fusion
  11.2 4.8 %fusion.71 = (bf16[256,4096]{1,0:T(8,128)(2,1)}, bf16[256,4096]{1,0:T(8,128)(2,1)}) fusion(bf16[256,8192]{1,0:T(8,128)(2,1)} %param.17), kind=kLoop, calls=%fused_computation.184 | loop fusion | bytes 8388608 | tf_op jit(solution)/shard_map/slice | solution.py:235
  17.6 3.3 %copy.45 = bf16[256,4096]{0,1:T(8,128)(2,1)S(1)} copy(bf16[256,4096]{1,0:T(8,128)(2,1)} %get-tuple-element.145) | data formatting | bytes 4194304
  20.9 4.1 %copy.46 = bf16[256,4096]{0,1:T(8,128)(2,1)} copy(bf16[256,4096]{1,0:T(8,128)(2,1)} %get-tuple-element.146) | data formatting | bytes 4194304
  32.0 1.8 compare_convert_fusion.4
  41.0 1.6 slice_bitcast_fusion.1
  42.7 9.3 %multiply_convert_fusion.10 = bf16[256,4096]{0,1:T(8,128)(2,1)S(1)} fusion(bf16[256,4096]{0,1:T(8,128)(2,1)} %copy.46, bf16[3,4096]{0,1:T(8,128)(2,1)S(1)} %copy.39, f32[4096]{0:T(1024)} %bitcast.136, f32[4096]{0:T(1024)} %bitcast.137, f32[4096]{0:T(1024)} %bitcast.134, f32[4096]{0:T(1024)} %bitcast.135, f32[4096]{0:T(1024)} %get-tuple-element.171, ...), kind=kLoop, calls=%fused_computation.45 | loop fusion | flops 30408704 | bytes 4303872 | tf_op jit(solution)/shard_map/convert_element_type | solution.py:37
  52.1 2.7 fusion.34
  56.8 6.8 %multiply_convert_fusion.11 = bf16[256,4096]{0,1:T(8,128)(2,1)S(1)} fusion(bf16[256,4096]{0,1:T(8,128)(2,1)S(1)} %copy.45, bf16[3,4096]{0,1:T(8,128)(2,1)S(1)} %copy-done.15, f32[4096]{0:T(1024)S(1)} %bitcast.131, f32[256]{0:T(256)S(1)} %copy-done.40, f32[4096]{0:T(1024)S(1)} %bitcast.132, f32[256]{0:T(256)S(1)} %copy-done.42, f32[4096]{0:T(1024)S(1)} %bitcast.133, ...), kind=kLoop, calls=%fused_computation.50 | loop fusion | flops 30408704 | bytes 4303872 | tf_op jit(solution)/shard_map/convert_element_type | solution.py:37
  64.7 2.2 collective-permute-done.11
  67.0 2.3 collective-permute-start.12
  69.3 2.7 fusion.35
  75.4 2.5 fusion.70
  80.2 4.1 %copy.47 = bf16[256,4096]{0,1:T(8,128)(2,1)} copy(bf16[256,4096]{1,0:T(8,128)(2,1)} %get-tuple-element.143) | data formatting | bytes 4194304
  84.3 4.1 %copy.48 = bf16[256,4096]{0,1:T(8,128)(2,1)} copy(bf16[256,4096]{1,0:T(8,128)(2,1)} %get-tuple-element.144) | data formatting | bytes 4194304
  96.6 2.9 %add_select_fusion = f32[32,64,128]{2,1,0:T(8,128)} fusion(f32[32,64,128]{2,1,0:T(8,128)S(1)} %collective-permute-done.22, f32[64,64,128]{2,1,0:T(8,128)} %copy-done.10, s32[]{:T(128)S(6)} %select_n.138, f32[32]{0:T(128)S(1)} %get-tuple-element.136, f32[32]{0:T(128)S(1)} %get-tuple-element.135, pred[]{:T(512)S(6)} %eq.102), kind=kLoop, calls=%fused_computation.81 | loop fusion | flops 1310720 | bytes 3145989 | tf_op jit(solution)/shard_map/jit(_where)/select_n | solution.py:161
  99.5 3.3 %collective-permute-start.25 = (f32[32,64,128]{2,1,0:T(8,128)}, f32[32,64,128]{2,1,0:T(8,128)}, u32[]{:S(2)}, u32[]{:S(2)}) collective-permute-start(f32[32,64,128]{2,1,0:T(8,128)} %add_select_fusion), channel_id=1, source_target_pairs={{0,2},{1,3},{2,4},{3,5},{4,6},{5,7},{6,8},{7,9},{8,10},{9,11},{10,... | collective-permute-start | bytes 3145736 | tf_op jit(solution)/shard_map/ppermute | solution.py:69
  102.8 2.5 add_select_fusion.1
  105.3 2.1 collective-permute-start.16
  109.3 3.1 %collective-permute-start.23 = (f32[32]{0:T(128)}, f32[32]{0:T(128)S(1)}, u32[]{:S(2)}, u32[]{:S(2)}) collective-permute-start(f32[32]{0:T(128)} %mul.717), channel_id=1, source_target_pairs={{0,2},{1,3},{2,4},{3,5},{4,6},{5,7},{6,8},{7,9},{8,10},{9,11},{10,... | collective-permute-start | bytes 392 | tf_op jit(solution)/shard_map/ppermute | solution.py:69
  113.5 14.3 %collective-permute-done.25 = f32[32,64,128]{2,1,0:T(8,128)} collective-permute-done((f32[32,64,128]{2,1,0:T(8,128)}, f32[32,64,128]{2,1,0:T(8,128)}, u32[]{:S(2)}, u32[]{:S(2)}) %collective-permute-start.25) | collective-permute-done | bytes 1048608 | tf_op jit(solution)/shard_map/ppermute | solution.py:69
  127.8 1.9 collective-permute-start.26
  129.7 20.6 %collective-permute-done.16 = f32[32,64,128]{2,1,0:T(8,128)} collective-permute-done((f32[32,64,128]{2,1,0:T(8,128)}, f32[32,64,128]{2,1,0:T(8,128)}, u32[]{:S(2)}, u32[]{:S(2)}) %collective-permute-start.16) | collective-permute-done | bytes 1048608 | tf_op jit(solution)/shard_map/ppermute | solution.py:69
  150.2 1.9 collective-permute-start.17
  152.2 7.2 %fusion.1 = f32[64,64,256]{2,1,0:T(8,128)} fusion(f32[64,256]{1,0:T(8,128)} %bitcast.141, f32[64,256]{1,0:T(8,128)S(1)} %bitcast.139, f32[256,256]{1,0:T(8,128)S(1)} %fusion.50, pred[256,256]{1,0:T(8,128)(4,1)S(1)} %fusion.46, bf16[1,256,64,64]{1,3,2,0:T(8,128)(2,1)} %bitcast.121), kind=kOutput, calls=%fused_computation.7 | convolution fusion | flops 557842432 | bytes 6750208 | tf_op jit(solution)/shard_map/hij,jhp->ihp/dot_general | solution.py:48
  159.4 2.5 collective-permute-start.14
  162.3 2.2 collective-permute-start.24
  164.5 8.1 %collective-permute-done.26 = f32[32,64,128]{2,1,0:T(8,128)S(1)} collective-permute-done((f32[32,64,128]{2,1,0:T(8,128)}, f32[32,64,128]{2,1,0:T(8,128)S(1)}, u32[]{:S(2)}, u32[]{:S(2)}) %collective-permute-start.26) | collective-permute-done | bytes 1048608 | tf_op jit(solution)/shard_map/ppermute | solution.py:69
  174.0 1.9 collective-permute-start.27
  176.0 31.6 %collective-permute-done.14 = f32[32]{0:T(128)S(1)} collective-permute-done((f32[32]{0:T(128)S(1)}, f32[32]{0:T(128)S(1)}, u32[]{:S(2)}, u32[]{:S(2)}) %collective-permute-start.14) | collective-permute-done | bytes 160 | tf_op jit(solution)/shard_map/ppermute | solution.py:69
  207.5 2.4 multiply_add_fusion.7
  210.0 1.9 collective-permute-start.18
  211.9 5.9 %fusion = f32[64,64,256]{2,1,0:T(8,128)} fusion(f32[64,256]{1,0:T(8,128)S(1)} %bitcast.140, f32[64,256]{1,0:T(8,128)S(1)} %bitcast.138, f32[256,256]{1,0:T(8,128)S(1)} %fusion.55, pred[256,256]{1,0:T(8,128)(4,1)S(1)} %fusion.47, bf16[1,256,64,64]{1,3,2,0:T(8,128)(2,1)S(1)} %bitcast.119), kind=kOutput, calls=%fused_computation.6 | convolution fusion | flops 557842432 | bytes 6750208 | tf_op jit(solution)/shard_map/hij,jhp->ihp/dot_general | solution.py:48
  217.8 1.9 collective-permute-start.15
  219.8 3.7 %collective-permute-start.28 = (f32[32]{0:T(128)S(1)}, f32[32]{0:T(128)S(1)}, u32[]{:S(2)}, u32[]{:S(2)}) collective-permute-start(f32[32]{0:T(128)S(1)} %mul.753), channel_id=1, source_target_pairs={{0,4},{1,5},{2,6},{3,7},{4,8},{5,9},{6,10},{7,11},{8,12},{9,13},{1... | collective-permute-start | bytes 392 | tf_op jit(solution)/shard_map/ppermute | solution.py:69
  223.5 27.3 %collective-permute-done.15 = f32[32]{0:T(128)S(1)} collective-permute-done((f32[32]{0:T(128)S(1)}, f32[32]{0:T(128)S(1)}, u32[]{:S(2)}, u32[]{:S(2)}) %collective-permute-start.15) | collective-permute-done | bytes 160 | tf_op jit(solution)/shard_map/ppermute | solution.py:69
  250.8 2.0 collective-permute-start.19
  253.1 2.6 fusion.44
  257.0 2.7 multiply_add_fusion.6
  259.7 1.9 fusion.42
  262.2 1.6 select_convert_fusion.1
  266.2 2.3 multiply_reduce_fusion
  268.6 1.7 select_convert_fusion.3
  273.3 2.3 multiply_reduce_fusion.1
  275.7 2.2 multiply_convert_fusion.9
  277.8 2.3 pad_maximum_fusion
  280.1 6.3 %copy.42 = bf16[256,8192]{1,0:T(8,128)(2,1)} copy(bf16[256,8192]{0,1:T(8,128)(2,1)} %pad_maximum_fusion) | data formatting | bytes 8388608 | tf_op jit(solution)/shard_map/concatenate | solution.py:311
  (227 shorter events, 49.1 us)
Async XLA Ops:
  1.3 23.7 %collective-permute-start.8 = (s32[1]{0:T(128)}, s32[1]{0:T(128)}, u32[]{:S(2)}, u32[]{:S(2)}) collective-permute-start(s32[1]{0:T(128)} %slice.214), channel_id=1, source_target_pairs={{0,1},{1,0},{2,3},{3,2},{4,5},{5,4},{6,7},{7,6},{8,9},{9,8},{10,11... | collective-permute-start | bytes 20 | tf_op jit(solution)/shard_map/ppermute | solution.py:107
  4.6 24.8 %collective-permute-start.6 = (bf16[3,8449]{1,0:T(4,128)(2,1)S(1)}, bf16[3,8449]{1,0:T(4,128)(2,1)S(1)}, u32[]{:S(2)}, u32[]{:S(2)}) collective-permute-start(bf16[3,8449]{1,0:T(4,128)(2,1)S(1)} %pad_maximum_fusion.4), channel_id=1, source_target_pairs={{0,1},{1,2},{2,3},{3,4},{4,5},{5,6},{6,7},{7,8},{8,9},{9,10},{10,1... | collective-permute-start | bytes 152090 | tf_op jit(solution)/shard_map/ppermute | solution.py:21
  11.1 4.8 %copy-start.52 = (bf16[256]{0:T(256)(128)(2,1)S(1)}, bf16[256]{0:T(256)(128)(2,1)}, u32[]{:S(2)}) copy-start(bf16[256]{0:T(256)(128)(2,1)} %param.27) | copy-start | bytes 1540
  11.1 4.8 %copy-start.43 = (bf16[4,256]{1,0:T(4,128)(2,1)S(1)}, bf16[4,256]{1,0:T(4,128)(2,1)}, u32[]{:S(2)}) copy-start(bf16[4,256]{1,0:T(4,128)(2,1)} %param.26) | copy-start | bytes 6148
  11.1 4.8 %copy-start.36 = (bf16[8192]{0:T(1024)(128)(2,1)S(1)}, bf16[8192]{0:T(1024)(128)(2,1)}, u32[]{:S(2)}) copy-start(bf16[8192]{0:T(1024)(128)(2,1)} %param.25) | copy-start | bytes 49156
  11.1 5.4 %copy-start.23 = (bf16[4,8192]{1,0:T(4,128)(2,1)S(1)}, bf16[4,8192]{1,0:T(4,128)(2,1)}, u32[]{:S(2)}) copy-start(bf16[4,8192]{1,0:T(4,128)(2,1)} %param.24) | copy-start | bytes 196612
  17.6 11.9 %copy-start.34 = (s32[256]{0:T(256)S(1)}, s32[256]{0:T(256)}, u32[]{:S(2)}) copy-start(s32[256]{0:T(256)} %param.29) | copy-start | bytes 3076
  17.6 17.4 %copy-start.24 = (bf16[256,256]{1,0:T(8,128)(2,1)S(1)}, bf16[256,256]{1,0:T(8,128)(2,1)}, u32[]{:S(2)}) copy-start(bf16[256,256]{1,0:T(8,128)(2,1)} %param.19) | copy-start | bytes 393220
  26.4 2.4 collective-permute-start.9
  33.8 29.9 %collective-permute-start.10 = (s32[4]{0:T(128)}, s32[4]{0:T(128)}, u32[]{:S(2)}, u32[]{:S(2)}) collective-permute-start(s32[4]{0:T(128)} %broadcast_select_fusion.3), channel_id=1, source_target_pairs={{0,4},{1,5},{2,6},{3,7},{4,0},{5,1},{6,2},{7,3},{8,12},{9,13},{10,... | collective-permute-start | bytes 56 | tf_op jit(solution)/shard_map/ppermute | solution.py:107
  41.0 11.1 %copy-start.25 = (f32[256,128]{1,0:T(8,128)S(1)}, f32[256,128]{1,0:T(8,128)}, u32[]{:S(2)}) copy-start(f32[256,128]{1,0:T(8,128)} %get-tuple-element.157) | copy-start | bytes 393220
  41.0 11.1 %copy-start.51 = (f32[64]{0:T(128)S(1)}, f32[64]{0:T(128)}, u32[]{:S(2)}) copy-start(f32[64]{0:T(128)} %get-tuple-element.139) | copy-start | bytes 772
  52.0 4.8 %copy-start.6 = (bf16[256,4096]{0,1:T(8,128)(2,1)}, bf16[256,4096]{0,1:T(8,128)(2,1)S(1)}, u32[]{:S(2)}) copy-start(bf16[256,4096]{0,1:T(8,128)(2,1)S(1)} %multiply_convert_fusion.10) | copy-start | bytes 6291460
  52.0 4.8 %copy-start.15 = (bf16[3,4096]{0,1:T(8,128)(2,1)S(1)}, bf16[3,4096]{0,1:T(8,128)(2,1)}, u32[]{:S(2)}) copy-start(bf16[3,4096]{0,1:T(8,128)(2,1)} %copy.31) | copy-start | bytes 73732
  52.0 4.8 %copy-start.29 = (f32[1,4096]{1,0:T(1,128)S(1)}, f32[1,4096]{1,0:T(1,128)}, u32[]{:S(2)}) copy-start(f32[1,4096]{1,0:T(1,128)} %get-tuple-element.158) | copy-start | bytes 49156
  54.8 17.2 %copy-start.10 = (f32[64,64,128]{2,1,0:T(8,128)}, f32[64,64,128]{2,1,0:T(8,128)S(1)}, u32[]{:S(2)}) copy-start(f32[64,64,128]{2,1,0:T(8,128)S(1)} %fusion.34) | copy-start | bytes 6291460
  55.9 40.7 %collective-permute-start.22 = (f32[32,64,128]{2,1,0:T(8,128)}, f32[32,64,128]{2,1,0:T(8,128)S(1)}, u32[]{:S(2)}, u32[]{:S(2)}) collective-permute-start(f32[32,64,128]{2,1,0:T(8,128)} %constant_dynamic-slice_fusion), channel_id=1, source_target_pairs={{0,1},{1,0},{2,3},{3,2},{4,5},{5,4},{6,7},{7,6},{8,9},{9,8},{10,11... | collective-permute-start | bytes 3145736 | tf_op jit(solution)/shard_map/ppermute | solution.py:156
  56.8 15.8 %copy-start.48 = (f32[64]{0:T(128)S(1)}, f32[64]{0:T(128)}, u32[]{:S(2)}) copy-start(f32[64]{0:T(128)} %get-tuple-element.130) | copy-start | bytes 772
  63.7 9.2 %copy-start.3 = (bf16[256,4096]{0,1:T(8,128)(2,1)}, bf16[256,4096]{0,1:T(8,128)(2,1)S(1)}, u32[]{:S(2)}) copy-start(bf16[256,4096]{0,1:T(8,128)(2,1)S(1)} %multiply_convert_fusion.11) | copy-start | bytes 6291460
  64.5 2.4 collective-permute-start.11
  67.0 5.0 %collective-permute-start.12 = (s32[16]{0:T(128)S(1)}, s32[16]{0:T(128)S(1)}, u32[]{:S(2)}, u32[]{:S(2)}) collective-permute-start(s32[16]{0:T(128)S(1)} %broadcast_select_fusion.5), channel_id=1, source_target_pairs={{0,16},{1,17},{2,18},{3,19},{4,20},{5,21},{6,22},{7,23},{8,24},{9,... | collective-permute-start | bytes 200 | tf_op jit(solution)/shard_map/ppermute | solution.py:107
  73.9 5.3 %copy-start.49 = (f32[128]{0:T(128)S(1)}, f32[128]{0:T(128)}, u32[]{:S(2)}) copy-start(f32[128]{0:T(128)} %param.23) | copy-start | bytes 1540
  73.9 28.9 %collective-permute-start.13 = (f32[32,64,128]{2,1,0:T(8,128)}, f32[32,64,128]{2,1,0:T(8,128)}, u32[]{:S(2)}, u32[]{:S(2)}) collective-permute-start(f32[32,64,128]{2,1,0:T(8,128)} %constant_dynamic-slice_fusion.1), channel_id=1, source_target_pairs={{0,1},{1,0},{2,3},{3,2},{4,5},{5,4},{6,7},{7,6},{8,9},{9,8},{10,11... | collective-permute-start | bytes 3145736 | tf_op jit(solution)/shard_map/ppermute | solution.py:156
  88.4 24.9 %copy-start.16 = (bf16[1,256,128]{2,1,0:T(8,128)(2,1)S(1)}, bf16[1,256,128]{2,1,0:T(8,128)(2,1)}, u32[]{:S(2)}) copy-start(bf16[1,256,128]{2,1,0:T(8,128)(2,1)} %get-tuple-element.112) | copy-start | bytes 196612
  88.4 24.9 %copy-start.17 = (bf16[1,256,128]{2,1,0:T(8,128)(2,1)S(1)}, bf16[1,256,128]{2,1,0:T(8,128)(2,1)}, u32[]{:S(2)}) copy-start(bf16[1,256,128]{2,1,0:T(8,128)(2,1)} %get-tuple-element.113) | copy-start | bytes 196612
  88.4 19.0 %copy-start.50 = (s32[32]{0:T(128)S(1)}, s32[32]{0:T(128)}, u32[]{:S(2)}) copy-start(s32[32]{0:T(128)} %broadcast_select_fusion.6) | copy-start | bytes 388
  91.3 1.7 collective-permute-start.21
  92.9 1.9 collective-permute-start.7
  96.6 62.8 %copy-start.1 = (f32[32,64,128]{2,1,0:T(8,128)}, f32[32,64,128]{2,1,0:T(8,128)S(1)}, u32[]{:S(2)}) copy-start(f32[32,64,128]{2,1,0:T(8,128)S(1)} %collective-permute-done.22) | copy-start | bytes 3145732
  99.5 28.3 %collective-permute-start.25 = (f32[32,64,128]{2,1,0:T(8,128)}, f32[32,64,128]{2,1,0:T(8,128)}, u32[]{:S(2)}, u32[]{:S(2)}) collective-permute-start(f32[32,64,128]{2,1,0:T(8,128)} %add_select_fusion), channel_id=1, source_target_pairs={{0,2},{1,3},{2,4},{3,5},{4,6},{5,7},{6,8},{7,9},{8,10},{9,11},{10,... | collective-permute-start | bytes 3145736 | tf_op jit(solution)/shard_map/ppermute | solution.py:69
  105.3 45.0 %collective-permute-start.16 = (f32[32,64,128]{2,1,0:T(8,128)}, f32[32,64,128]{2,1,0:T(8,128)}, u32[]{:S(2)}, u32[]{:S(2)}) collective-permute-start(f32[32,64,128]{2,1,0:T(8,128)} %add_select_fusion.1), channel_id=1, source_target_pairs={{0,2},{1,3},{2,4},{3,5},{4,6},{5,7},{6,8},{7,9},{8,10},{9,11},{10,... | collective-permute-start | bytes 3145736 | tf_op jit(solution)/shard_map/ppermute | solution.py:69
  109.3 53.0 %collective-permute-start.23 = (f32[32]{0:T(128)}, f32[32]{0:T(128)S(1)}, u32[]{:S(2)}, u32[]{:S(2)}) collective-permute-start(f32[32]{0:T(128)} %mul.717), channel_id=1, source_target_pairs={{0,2},{1,3},{2,4},{3,5},{4,6},{5,7},{6,8},{7,9},{8,10},{9,11},{10,... | collective-permute-start | bytes 392 | tf_op jit(solution)/shard_map/ppermute | solution.py:69
  127.8 44.8 %collective-permute-start.26 = (f32[32,64,128]{2,1,0:T(8,128)}, f32[32,64,128]{2,1,0:T(8,128)S(1)}, u32[]{:S(2)}, u32[]{:S(2)}) collective-permute-start(f32[32,64,128]{2,1,0:T(8,128)} %collective-permute-done.25), channel_id=1, source_target_pairs={{0,2},{1,3},{2,4},{3,5},{4,6},{5,7},{6,8},{7,9},{8,10},{9,11},{10,... | collective-permute-start | bytes 3145736 | tf_op jit(solution)/shard_map/ppermute | solution.py:69
  150.2 57.3 %collective-permute-start.17 = (f32[32,64,128]{2,1,0:T(8,128)}, f32[32,64,128]{2,1,0:T(8,128)S(1)}, u32[]{:S(2)}, u32[]{:S(2)}) collective-permute-start(f32[32,64,128]{2,1,0:T(8,128)} %collective-permute-done.16), channel_id=1, source_target_pairs={{0,2},{1,3},{2,4},{3,5},{4,6},{5,7},{6,8},{7,9},{8,10},{9,11},{10,... | collective-permute-start | bytes 3145736 | tf_op jit(solution)/shard_map/ppermute | solution.py:69
  152.2 7.3 %copy-start.53 = (f32[32]{0:T(128)S(1)}, f32[32]{0:T(128)}, u32[]{:S(2)}) copy-start(f32[32]{0:T(128)} %mul.634) | copy-start | bytes 388
  152.2 9.8 %copy-start.35 = (s32[256]{0:T(256)S(1)}, s32[256]{0:T(256)}, u32[]{:S(2)}) copy-start(s32[256]{0:T(256)} %param.29) | copy-start | bytes 3076
  152.2 10.1 %copy-start.22 = (f32[1,64,256]{2,0,1:T(1,128)S(1)}, f32[1,64,256]{2,0,1:T(1,128)}, u32[]{:S(2)}) copy-start(f32[1,64,256]{2,0,1:T(1,128)} %reduce_window_sum.49) | copy-start | bytes 196612
  159.4 52.5 %copy-start.4 = (bf16[256,4096]{0,1:T(8,128)(2,1)S(1)}, bf16[256,4096]{0,1:T(8,128)(2,1)}, u32[]{:S(2)}) copy-start(bf16[256,4096]{0,1:T(8,128)(2,1)} %copy-done.3) | copy-start | bytes 6291460
  159.4 52.5 %copy-start.33 = (f32[1,64,256]{2,1,0:T(8,128)S(1)}, f32[1,64,256]{2,1,0:T(8,128)}, u32[]{:S(2)}) copy-start(f32[1,64,256]{2,1,0:T(8,128)} %get-tuple-element.107) | copy-start | bytes 196612
  159.4 48.1 %collective-permute-start.14 = (f32[32]{0:T(128)S(1)}, f32[32]{0:T(128)S(1)}, u32[]{:S(2)}, u32[]{:S(2)}) collective-permute-start(f32[32]{0:T(128)S(1)} %copy-done.53), channel_id=1, source_target_pairs={{0,2},{1,3},{2,4},{3,5},{4,6},{5,7},{6,8},{7,9},{8,10},{9,11},{10,... | collective-permute-start | bytes 392 | tf_op jit(solution)/shard_map/ppermute | solution.py:69
  162.3 57.4 %collective-permute-start.24 = (f32[32]{0:T(128)S(1)}, f32[32]{0:T(128)S(1)}, u32[]{:S(2)}, u32[]{:S(2)}) collective-permute-start(f32[32]{0:T(128)S(1)} %collective-permute-done.23), channel_id=1, source_target_pairs={{0,2},{1,3},{2,4},{3,5},{4,6},{5,7},{6,8},{7,9},{8,10},{9,11},{10,... | collective-permute-start | bytes 392 | tf_op jit(solution)/shard_map/ppermute | solution.py:69
  174.0 78.8 %collective-permute-start.27 = (f32[32,64,128]{2,1,0:T(8,128)S(1)}, f32[32,64,128]{2,1,0:T(8,128)S(1)}, u32[]{:S(2)}, u32[]{:S(2)}) collective-permute-start(f32[32,64,128]{2,1,0:T(8,128)S(1)} %multiply_add_fusion.5), channel_id=1, source_target_pairs={{0,4},{1,5},{2,6},{3,7},{4,8},{5,9},{6,10},{7,11},{8,12},{9,13},{1... | collective-permute-start | bytes 3145736 | tf_op jit(solution)/shard_map/ppermute | solution.py:69
  210.0 47.0 %collective-permute-start.18 = (f32[32,64,128]{2,1,0:T(8,128)}, f32[32,64,128]{2,1,0:T(8,128)}, u32[]{:S(2)}, u32[]{:S(2)}) collective-permute-start(f32[32,64,128]{2,1,0:T(8,128)} %multiply_add_fusion.7), channel_id=1, source_target_pairs={{0,4},{1,5},{2,6},{3,7},{4,8},{5,9},{6,10},{7,11},{8,12},{9,13},{1... | collective-permute-start | bytes 3145736 | tf_op jit(solution)/shard_map/ppermute | solution.py:69
  217.8 33.0 %collective-permute-start.15 = (f32[32]{0:T(128)S(1)}, f32[32]{0:T(128)S(1)}, u32[]{:S(2)}, u32[]{:S(2)}) collective-permute-start(f32[32]{0:T(128)S(1)} %collective-permute-done.14), channel_id=1, source_target_pairs={{0,2},{1,3},{2,4},{3,5},{4,6},{5,7},{6,8},{7,9},{8,10},{9,11},{10,... | collective-permute-start | bytes 392 | tf_op jit(solution)/shard_map/ppermute | solution.py:69
  219.8 33.3 %collective-permute-start.28 = (f32[32]{0:T(128)S(1)}, f32[32]{0:T(128)S(1)}, u32[]{:S(2)}, u32[]{:S(2)}) collective-permute-start(f32[32]{0:T(128)S(1)} %mul.753), channel_id=1, source_target_pairs={{0,4},{1,5},{2,6},{3,7},{4,8},{5,9},{6,10},{7,11},{8,12},{9,13},{1... | collective-permute-start | bytes 392 | tf_op jit(solution)/shard_map/ppermute | solution.py:69
  250.8 8.9 %collective-permute-start.19 = (f32[32]{0:T(128)S(1)}, f32[32]{0:T(128)S(1)}, u32[]{:S(2)}, u32[]{:S(2)}) collective-permute-start(f32[32]{0:T(128)S(1)} %mul.698), channel_id=1, source_target_pairs={{0,4},{1,5},{2,6},{3,7},{4,8},{5,9},{6,10},{7,11},{8,12},{9,13},{1... | collective-permute-start | bytes 392 | tf_op jit(solution)/shard_map/ppermute | solution.py:69
  255.7 6.1 %collective-permute-start.29 = (bf16[32,64,128]{2,1,0:T(8,128)(2,1)}, bf16[32,64,128]{2,1,0:T(8,128)(2,1)}, u32[]{:S(2)}, u32[]{:S(2)}) collective-permute-start(bf16[32,64,128]{2,1,0:T(8,128)(2,1)} %fusion.44), channel_id=1, source_target_pairs={{0,1},{1,0},{2,3},{3,2},{4,5},{5,4},{6,7},{7,6},{8,9},{9,8},{10,11... | collective-permute-start | bytes 1572872 | tf_op jit(solution)/shard_map/ppermute | solution.py:167
  261.7 6.9 %collective-permute-start.20 = (bf16[32,64,128]{2,1,0:T(8,128)(2,1)S(1)}, bf16[32,64,128]{2,1,0:T(8,128)(2,1)S(1)}, u32[]{:S(2)}, u32[]{:S(2)}) collective-permute-start(bf16[32,64,128]{2,1,0:T(8,128)(2,1)S(1)} %fusion.42), channel_id=1, source_target_pairs={{0,1},{1,0},{2,3},{3,2},{4,5},{5,4},{6,7},{7,6},{8,9},{9,8},{10,11... | collective-permute-start | bytes 1572872 | tf_op jit(solution)/shard_map/ppermute | solution.py:167
  (30 other events, 91.5 us)

commit v7 on v4

--- a/solution.py
+++ b/solution.py
@@ -3,6 +3,8 @@
 import jax
 import jax.numpy as jnp
 from jax import lax
+from jax.experimental import pallas as pl
+from jax.experimental.pallas import tpu as pltpu
 from jax.sharding import PartitionSpec as P
 
 HEAD_DIM = 64
@@ -35,6 +37,48 @@
             * visible[:, None]
         )
     return jax.nn.silu(summed).astype(jnp.bfloat16)
+
+
+def conv_rows_kernel(rim_ref, x_ref, w_ref, b_ref, vis_ref, o_ref):
+    rows = x_ref.shape[0]
+    here = x_ref[...].astype(jnp.float32)
+    rim = jnp.concatenate(
+        [rim_ref[...].astype(jnp.float32), jnp.zeros((rows - rim_ref.shape[0],) + here.shape[1:], jnp.float32)]
+    )
+    row = lax.broadcasted_iota(jnp.int32, here.shape, 0)
+    summed = b_ref[...].astype(jnp.float32) + w_ref[CONV - 1 : CONV, :].astype(jnp.float32) * here
+    for offset in range(CONV - 1):
+        lag = CONV - 1 - offset
+        early = pltpu.roll(rim, rows - offset, 0) if offset else rim
+        seen = jnp.where(row < lag, early, pltpu.roll(here, lag, 0))
+        summed = summed + w_ref[offset : offset + 1, :].astype(jnp.float32) * seen * vis_ref[offset]
+    o_ref[...] = jax.nn.silu(summed).astype(o_ref.dtype)
+
+
+def conv_rows(rim_vals, values, rim_segment, segment, weight, offset_bias):
+    rows, width = values.shape
+    ext_segment = jnp.concatenate([rim_segment, segment], axis=0)
+    vis = jnp.stack(
+        [(ext_segment[k : k + rows] == segment).astype(jnp.float32) for k in range(CONV - 1)]
+    )[:, :, None]
+    rim8 = jnp.concatenate([rim_vals, jnp.zeros((8 - rim_vals.shape[0], width), rim_vals.dtype)])
+    tile = min(width, 1024)
+    return pl.pallas_call(
+        conv_rows_kernel,
+        out_shape=jax.ShapeDtypeStruct((rows, width), jnp.bfloat16),
+        grid=(width // tile,),
+        in_specs=[
+            pl.BlockSpec((8, tile), lambda j: (0, j)),
+            pl.BlockSpec((rows, tile), lambda j: (0, j)),
+            pl.BlockSpec((CONV, tile), lambda j: (0, j)),
+            pl.BlockSpec((1, tile), lambda j: (0, j)),
+            pl.BlockSpec((CONV - 1, rows, 1), lambda j: (0, 0, 0)),
+        ],
+        out_specs=pl.BlockSpec((rows, tile), lambda j: (0, j)),
+        cost_estimate=pl.CostEstimate(
+            flops=20 * rows * width, transcendentals=rows * width, bytes_accessed=4 * rows * width
+        ),
+    )(rim8, values, weight, offset_bias.reshape(1, width), vis)
 
 
 def mixing_part(x_group, b_group, c_group, step_size, cum_decay, segment):
@@ -226,7 +270,7 @@
     rim_segment = rims[:, channels + bc_width].astype(jnp.int32)
     ids = gather_rounds(segment_ids[tok_rows - 1 :], "ctx", 0, 2)
     ids, rim_x = lax.optimization_barrier((ids, rim_x))
-    x_conv = causal_conv(rim_x, x_in, rim_segment, segment_ids, conv_x_w, conv_x_b)
+    x_conv = conv_rows(rim_x, x_in, rim_segment, segment_ids, conv_x_w, conv_x_b)
     ids = gather_rounds(ids, "ctx", 2, 4)
     ids, x_conv = lax.optimization_barrier((ids, x_conv))
     bc_conv = causal_conv(rim_bc, bc_in, rim_segment, segment_ids, conv_bc_w, conv_bc_b)

time: 256 us -> 264 us (1.031)
  Pallas kernels: 0 us -> 10.4 us
  other arithmetic: 40.8 us -> 33.1 us
  waiting for transfers between devices: 134 us -> 140 us
    convert_element_type x2 -> x1, other arithmetic: 16.9 us -> 1.4 us  [causal_conv(): return jax.nn.silu(summed).astype(jnp.bfloat16)]
    unnamed x39 -> x17, local copies, waits for them, and re-layouts: 15 us -> 3 us
    pallas_call x0 -> x1, Pallas kernels: none -> 10.4 us  [conv_rows(): pl.pallas_call(conv_rows_kernel, out_shape=jax.ShapeDtypeStruct((rows, wi...]
    reshape x0 -> x2, local copies, waits for them, and re-layouts: none -> 10.2 us  [the longest x1 8.88 us: local(): y_blocks.reshape(tok_rows, head_count, HEAD_DIM)]
    convert_element_type x1 -> x0, local copies, waits for them, and re-layouts: 6.31 us -> none  [local(): (gated * scale[:, None] * norm_gain.astype(jnp.float32)).astype(jnp.bfloa...]
    ppermute x6, waiting for transfers between devices: 127 us -> 133 us  [shifted(): lax.ppermute(value, axis, [(s, s + steps) for s in range(count - steps)])]
    optimization_barrier x1, local copies, waits for them, and re-layouts: 1.05 us -> 6.37 us  [local(): ids, x_conv = lax.optimization_barrier((ids, x_conv))]
    reduce_sum x1, other arithmetic: 4.7 us -> 8.07 us  [local(): local_sq = jnp.sum(gated * gated, axis=1)]
  transfers between devices with their start and end apart: 15 -> 15, of which waited for: 8 -> 8; matrix products, arithmetic and copies ran while one was open for 23% -> 14% of each run, Pallas kernels for 0% -> 4%
where the time goes in v7:
time: 264 us; the launch traced here: 263 us
  waiting for transfers between devices  140 us (53%)
  other arithmetic  33.1 us (13%)
  starting transfers between devices  28 us (11%)
  local copies, waits for them, and re-layouts  27.2 us (10%)
  matrix products  21.9 us (8%)
  Pallas kernels  10.4 us (4%)
    ppermute x6, waiting for transfers between devices, shifted(): lax.ppermute(value, axis, [(s, s + steps) for s in range(count - steps)])  133 us
    ppermute x6, starting transfers between devices, shifted(): lax.ppermute(value, axis, [(s, s + steps) for s in range(count - steps)])  13.3 us
    pallas_call x1, Pallas kernels, conv_rows(): pl.pallas_call(conv_rows_kernel, out_shape=jax.ShapeDtypeStruct((rows, wi...  10.4 us
    reshape x1, local copies, waits for them, and re-layouts, local(): y_blocks.reshape(tok_rows, head_count, HEAD_DIM)  8.88 us
    dot_general x1, matrix products, mixing_part(): jnp.einsum('hij,jhp->ihp', mixing, x_group, preferred_element_type=jnp.fl...  8.81 us
    dot_general x1, matrix products, state_part(): jnp.einsum('hjn,jhp->hpn', weighted, x_group, preferred_element_type=jnp....  8.34 us
    reduce_sum x1, other arithmetic, local(): local_sq = jnp.sum(gated * gated, axis=1)  8.07 us
    optimization_barrier x1, local copies, waits for them, and re-layouts, local(): ids, x_conv = lax.optimization_barrier((ids, x_conv))  6.37 us
  transfers between devices with their start and end apart: 15, of which 8 were waited for; matrix products, arithmetic and copies ran while one was open for 14% of the time, Pallas kernels for 4%

profile of v7, /device:TPU:9, one launch (start us, length us, event | category | flops | bytes accessed | tf_op | source)
XLA Modules:
  0.0 263.2 jit_solution(5002526385435459709)
XLA Ops:
  0.0 1.3 slice.98
  2.6 0.9 slice.99
  3.7 0.7 slice.100
  4.5 3.0 %collective-permute-start.3 = (bf16[3,8449]{1,0:T(4,128)(2,1)S(1)}, bf16[3,8449]{1,0:T(4,128)(2,1)S(1)}, u32[]{:S(2)}, u32[]{:S(2)}) collective-permute-start(bf16[3,8449]{1,0:T(4,128)(2,1)S(1)} %pad_maximum_fusion.1), channel_id=1, source_target_pairs={{0,1},{1,2},{2,3},{3,4},{4,5},{5,6},{6,7},{7,8},{8,9},{9,10},{10,1... | collective-permute-start | bytes 152090 | tf_op jit(solution)/shard_map/ppermute | solution.py:23
  7.5 1.0 copy.23
  8.5 0.8 negate_multiply_fusion
  9.4 1.3 reshape.198.b_ref
  10.8 0.8 slice_convert_fusion.5
  12.3 1.3 broadcast_select_fusion.1
  13.6 1.2 collective-permute-start.6
  14.8 1.2 collective-permute-done.6
  16.1 1.3 collective-permute-start.7
  18.1 0.8 pad_add_fusion
  20.0 2.0 compare_convert_fusion.4
  22.0 0.9 copy.27.vis_ref
  23.0 1.4 multiply_convert_fusion.7
  24.5 0.8 fusion.35
  26.1 10.4 %shard_map.127 = bf16[256,8192]{1,0:T(8,128)(2,1)} custom-call(bf16[8,8192]{1,0:T(8,128)(2,1)} %concatenate.76.rim_ref, bf16[256,8192]{1,0:T(8,128)(2,1)} %x_ref.1, bf16[4,8192]{1,0:T(4,128)(2,1)} %w_ref.1, bf16[1,8192]{1,0:T(2,128)(2,1)} %reshape.198.b_ref, f32[3,256,1]{2,1,0:T(8,128)} %copy.27.vis_ref), custom_call_target="tpu_custom_call" | custom-call | flops 41943040 | bytes 8388608 | tf_op jit(solution)/shard_map/pallas_call | solution.py:66
  36.8 2.2 collective-permute-done.8
  39.1 6.4 %copy.28 = bf16[256,8192]{0,1:T(8,128)(2,1)} copy(bf16[256,8192]{1,0:T(8,128)(2,1)} %shard_map.127) | data formatting | bytes 8388608 | tf_op jit(solution)/shard_map/optimization_barrier | solution.py:275
  45.4 2.3 collective-permute-start.9
  47.7 8.3 %fusion.15 = f32[1,128,64,128]{3,2,1,0:T(8,128)S(1)} fusion(bf16[256,128,64]{0,2,1:T(8,128)(2,1)} %bitcast.70, f32[128,256]{1,0:T(8,128)S(1)} %copy.29, f32[256,128]{1,0:T(8,128)S(1)} %get-tuple-element.83), kind=kOutput, calls=%fused_computation.25 | convolution fusion | flops 545259520 | bytes 8650752 | tf_op jit(solution)/shard_map/hjn,jhp->hpn/dot_general | solution.py:100
  56.5 2.0 copy-done
  58.5 1.5 constant_dynamic-slice_fusion
  60.0 2.3 collective-permute-start.10
  62.3 3.6 %collective-permute-done.4 = f32[128]{0:T(128)S(1)} collective-permute-done((f32[128]{0:T(128)S(1)}, f32[128]{0:T(128)S(1)}, u32[]{:S(2)}, u32[]{:S(2)}) %collective-permute-start.4) | collective-permute-done | bytes 544 | tf_op jit(solution)/shard_map/ppermute | solution.py:200
  66.3 2.8 %add_select_fusion = f32[64,64,128]{2,1,0:T(8,128)S(1)} fusion(f32[64,64,128]{2,1,0:T(8,128)S(1)} %collective-permute-done.10, f32[128,64,128]{2,1,0:T(8,128)} %copy-done, s32[]{:T(128)S(6)} %select_n.101, f32[64]{0:T(128)S(1)} %get-tuple-element.74, f32[64]{0:T(128)S(1)} %get-tuple-element.73, pred[]{:T(512)S(6)} %eq.73), kind=kLoop, calls=%fused_computation.34 | loop fusion | flops 2621440 | bytes 6291973 | tf_op jit(solution)/shard_map/jit(_where)/select_n | solution.py:205
  69.1 3.3 %collective-permute-start.13 = (f32[64,64,128]{2,1,0:T(8,128)S(1)}, f32[64,64,128]{2,1,0:T(8,128)S(1)}, u32[]{:S(2)}, u32[]{:S(2)}) collective-permute-start(f32[64,64,128]{2,1,0:T(8,128)S(1)} %add_select_fusion), channel_id=1, source_target_pairs={{0,2},{1,3},{2,4},{3,5},{4,6},{5,7},{6,8},{7,9},{8,10},{9,11},{10,... | collective-permute-start | bytes 6291464 | tf_op jit(solution)/shard_map/ppermute | solution.py:113
  72.3 47.4 %collective-permute-done.13 = f32[64,64,128]{2,1,0:T(8,128)S(1)} collective-permute-done((f32[64,64,128]{2,1,0:T(8,128)S(1)}, f32[64,64,128]{2,1,0:T(8,128)S(1)}, u32[]{:S(2)}, u32[]{:S(2)}) %collective-permute-start.13) | collective-permute-done | bytes 2097184 | tf_op jit(solution)/shard_map/ppermute | solution.py:113
  119.8 1.9 collective-permute-start.14
  121.7 2.4 collective-permute-start.11
  124.1 45.3 %collective-permute-done.11 = f32[64]{0:T(128)S(1)} collective-permute-done((f32[64]{0:T(128)S(1)}, f32[64]{0:T(128)S(1)}, u32[]{:S(2)}, u32[]{:S(2)}) %collective-permute-start.11) | collective-permute-done | bytes 288 | tf_op jit(solution)/shard_map/ppermute | solution.py:113
  169.4 1.6 multiply_add_fusion.3
  171.0 1.9 collective-permute-start.15
  173.7 0.8 compare_reduce_fusion
  175.5 1.9 collective-permute-start.12
  177.6 39.5 %collective-permute-done.12 = f32[64]{0:T(128)S(1)} collective-permute-done((f32[64]{0:T(128)S(1)}, f32[64]{0:T(128)S(1)}, u32[]{:S(2)}, u32[]{:S(2)}) %collective-permute-start.12) | collective-permute-done | bytes 288 | tf_op jit(solution)/shard_map/ppermute | solution.py:113
  217.1 1.9 collective-permute-start.16
  219.0 2.5 multiply_add_fusion.2
  221.5 0.8 collective-permute-done.16
  222.3 2.8 %fusion.19 = bf16[64,64,128]{2,1,0:T(8,128)(2,1)S(1)} fusion(f32[64,64,128]{2,1,0:T(8,128)S(1)} %get-tuple-element.93, f32[64,64,128]{2,1,0:T(8,128)} %copy-done.2, f32[128,64,128]{2,1,0:T(8,128)} %copy-done, s32[]{:T(128)S(6)} %select_n.101, f32[64]{0:T(128)S(1)} %get-tuple-element.72, pred[]{:T(512)S(6)} %eq.73), kind=kLoop, calls=%fused_computation.35 | loop fusion | flops 2097152 | bytes 7340293 | tf_op jit(solution)/shard_map/jit(_where)/select_n | solution.py:211
  225.1 3.7 %collective-permute-start.17 = (bf16[64,64,128]{2,1,0:T(8,128)(2,1)S(1)}, bf16[64,64,128]{2,1,0:T(8,128)(2,1)S(1)}, u32[]{:S(2)}, u32[]{:S(2)}) collective-permute-start(bf16[64,64,128]{2,1,0:T(8,128)(2,1)S(1)} %fusion.19), channel_id=1, source_target_pairs={{0,1},{1,0},{2,3},{3,2},{4,5},{5,4},{6,7},{7,6},{8,9},{9,8},{10,11... | collective-permute-start | bytes 3145736 | tf_op jit(solution)/shard_map/ppermute | solution.py:211
  228.8 8.8 %fusion = f32[128,64,256]{2,1,0:T(8,128)S(1)} fusion(f32[128,256]{1,0:T(8,128)S(1)} %copy.34, f32[128,256]{1,0:T(8,128)S(1)} %copy.32, f32[256,256]{1,0:T(8,128)S(1)} %fusion.27, pred[256,256]{1,0:T(8,128)(4,1)S(1)} %fusion.21, bf16[1,256,128,64]{1,3,2,0:T(8,128)(2,1)S(1)} %bitcast.71), kind=kOutput, calls=%fused_computation.3 | convolution fusion | flops 1115684864 | bytes 13172736 | tf_op jit(solution)/shard_map/hij,jhp->ihp/dot_general | solution.py:92
  237.7 0.7 select_convert_fusion.1
  238.5 4.5 %bitcast_add_fusion = f32[256,128,64]{0,2,1:T(8,128)} fusion(f32[128,64,256]{2,1,0:T(8,128)S(1)} %fusion, f32[256,128]{0,1:T(8,128)S(1)} %copy.37, bf16[64,64,128]{2,1,0:T(8,128)(2,1)S(1)} %select_convert_fusion, bf16[64,64,128]{2,1,0:T(8,128)(2,1)S(1)} %get-tuple-element.70, bf16[256,256]{1,0:T(8,128)(2,1)S(1)} %multiply_convert_fusion.7), kind=kOutput, calls=%fused_computation.18 | convolution fusion | flops 545259520 | bytes 19070976 | tf_op jit(solution)/shard_map/in,hpn->ihp/dot_general | solution.py:108
  243.0 8.9 %copy.39 = f32[256,8192]{1,0:T(8,128)} copy(f32[256,8192]{0,1:T(8,128)} %bitcast.69) | data formatting | bytes 16777216 | tf_op jit(solution)/shard_map/reshape | solution.py:314
  251.9 8.1 %multiply_reduce_fusion = (f32[256]{0:T(256)S(1)}, f32[256,8192]{1,0:T(8,128)S(1)}) fusion(bf16[256,8192]{1,0:T(8,128)(2,1)} %param.16, f32[256,8192]{1,0:T(8,128)} %copy.39, bf16[256,8192]{1,0:T(8,128)(2,1)} %shard_map.127, f32[8192]{0:T(1024)S(1)} %mul.347), kind=kLoop, calls=%fused_computation.20 | loop fusion | flops 23068416 | bytes 25199616 | tf_op jit(solution)/shard_map/reduce_sum | solution.py:316
  260.0 3.2 %multiply_convert_fusion.4 = bf16[256,8192]{1,0:T(8,128)(2,1)} fusion(f32[256,8192]{1,0:T(8,128)S(1)} %get-tuple-element.69, f32[8192]{0:T(1024)S(1)} %convert_element_type.105, f32[256]{0:T(256)S(1)} %add_rsqrt_fusion), kind=kLoop, calls=%fused_computation.19 | loop fusion | flops 6291456 | bytes 12616704 | tf_op jit(solution)/shard_map/convert_element_type | solution.py:319
  (74 shorter events, 6.7 us)
Async XLA Ops:
  1.3 11.1 %collective-permute-start.5 = (s32[1]{0:T(128)}, s32[1]{0:T(128)}, u32[]{:S(2)}, u32[]{:S(2)}) collective-permute-start(s32[1]{0:T(128)} %slice.98), channel_id=1, source_target_pairs={{0,1},{1,0},{2,3},{3,2},{4,5},{5,4},{6,7},{7,6},{8,9},{9,8},{10,11... | collective-permute-start | bytes 20 | tf_op jit(solution)/shard_map/ppermute | solution.py:151
  4.5 11.6 %collective-permute-start.3 = (bf16[3,8449]{1,0:T(4,128)(2,1)S(1)}, bf16[3,8449]{1,0:T(4,128)(2,1)S(1)}, u32[]{:S(2)}, u32[]{:S(2)}) collective-permute-start(bf16[3,8449]{1,0:T(4,128)(2,1)S(1)} %pad_maximum_fusion.1), channel_id=1, source_target_pairs={{0,1},{1,2},{2,3},{3,4},{4,5},{5,6},{6,7},{7,8},{8,9},{9,10},{10,1... | collective-permute-start | bytes 152090 | tf_op jit(solution)/shard_map/ppermute | solution.py:23
  13.6 2.4 collective-permute-start.6
  16.1 20.4 %collective-permute-start.7 = (s32[4]{0:T(128)S(1)}, s32[4]{0:T(128)S(1)}, u32[]{:S(2)}, u32[]{:S(2)}) collective-permute-start(s32[4]{0:T(128)S(1)} %broadcast_select_fusion.2), channel_id=1, source_target_pairs={{0,4},{1,5},{2,6},{3,7},{4,0},{5,1},{6,2},{7,3},{8,12},{9,13},{10,... | collective-permute-start | bytes 56 | tf_op jit(solution)/shard_map/ppermute | solution.py:151
  36.6 2.4 collective-permute-start.8
  45.4 10.7 %collective-permute-start.9 = (s32[16]{0:T(128)S(1)}, s32[16]{0:T(128)S(1)}, u32[]{:S(2)}, u32[]{:S(2)}) collective-permute-start(s32[16]{0:T(128)S(1)} %broadcast_select_fusion.4), channel_id=1, source_target_pairs={{0,16},{1,17},{2,18},{3,19},{4,20},{5,21},{6,22},{7,23},{8,24},{9,... | collective-permute-start | bytes 200 | tf_op jit(solution)/shard_map/ppermute | solution.py:151
  56.5 2.0 copy-start
  60.0 6.3 %collective-permute-start.10 = (f32[64,64,128]{2,1,0:T(8,128)}, f32[64,64,128]{2,1,0:T(8,128)S(1)}, u32[]{:S(2)}, u32[]{:S(2)}) collective-permute-start(f32[64,64,128]{2,1,0:T(8,128)} %constant_dynamic-slice_fusion), channel_id=1, source_target_pairs={{0,1},{1,0},{2,3},{3,2},{4,5},{5,4},{6,7},{7,6},{8,9},{9,8},{10,11... | collective-permute-start | bytes 6291464 | tf_op jit(solution)/shard_map/ppermute | solution.py:200
  62.3 3.6 %collective-permute-start.4 = (f32[128]{0:T(128)S(1)}, f32[128]{0:T(128)S(1)}, u32[]{:S(2)}, u32[]{:S(2)}) collective-permute-start(f32[128]{0:T(128)S(1)} %get-tuple-element.78), channel_id=1, source_target_pairs={{0,1},{1,0},{2,3},{3,2},{4,5},{5,4},{6,7},{7,6},{8,9},{9,8},{10,11... | collective-permute-start | bytes 1544 | tf_op jit(solution)/shard_map/ppermute | solution.py:200
  66.3 104.7 %copy-start.2 = (f32[64,64,128]{2,1,0:T(8,128)}, f32[64,64,128]{2,1,0:T(8,128)S(1)}, u32[]{:S(2)}) copy-start(f32[64,64,128]{2,1,0:T(8,128)S(1)} %collective-permute-done.10) | copy-start | bytes 6291460
  69.1 103.8 %copy-start.7 = (f32[128]{0:T(128)S(1)}, f32[128]{0:T(128)}, u32[]{:S(2)}) copy-start(f32[128]{0:T(128)} %param.21) | copy-start | bytes 1540
  69.1 104.0 %copy-start.5 = (bf16[8192]{0:T(1024)(128)(2,1)S(1)}, bf16[8192]{0:T(1024)(128)(2,1)}, u32[]{:S(2)}) copy-start(bf16[8192]{0:T(1024)(128)(2,1)} %param.26) | copy-start | bytes 49156
  69.1 106.1 %copy-start.6 = (s32[256]{0:T(256)S(1)}, s32[256]{0:T(256)}, u32[]{:S(2)}) copy-start(s32[256]{0:T(256)} %param.27) | copy-start | bytes 3076
  69.1 50.7 %collective-permute-start.13 = (f32[64,64,128]{2,1,0:T(8,128)S(1)}, f32[64,64,128]{2,1,0:T(8,128)S(1)}, u32[]{:S(2)}, u32[]{:S(2)}) collective-permute-start(f32[64,64,128]{2,1,0:T(8,128)S(1)} %add_select_fusion), channel_id=1, source_target_pairs={{0,2},{1,3},{2,4},{3,5},{4,6},{5,7},{6,8},{7,9},{8,10},{9,11},{10,... | collective-permute-start | bytes 6291464 | tf_op jit(solution)/shard_map/ppermute | solution.py:113
  119.8 49.6 %collective-permute-start.14 = (f32[64,64,128]{2,1,0:T(8,128)S(1)}, f32[64,64,128]{2,1,0:T(8,128)S(1)}, u32[]{:S(2)}, u32[]{:S(2)}) collective-permute-start(f32[64,64,128]{2,1,0:T(8,128)S(1)} %collective-permute-done.13), channel_id=1, source_target_pairs={{0,2},{1,3},{2,4},{3,5},{4,6},{5,7},{6,8},{7,9},{8,10},{9,11},{10,... | collective-permute-start | bytes 6291464 | tf_op jit(solution)/shard_map/ppermute | solution.py:113
  121.7 47.7 %collective-permute-start.11 = (f32[64]{0:T(128)S(1)}, f32[64]{0:T(128)S(1)}, u32[]{:S(2)}, u32[]{:S(2)}) collective-permute-start(f32[64]{0:T(128)S(1)} %mul.294), channel_id=1, source_target_pairs={{0,2},{1,3},{2,4},{3,5},{4,6},{5,7},{6,8},{7,9},{8,10},{9,11},{10,... | collective-permute-start | bytes 776 | tf_op jit(solution)/shard_map/ppermute | solution.py:113
  171.0 48.1 %collective-permute-start.15 = (f32[64,64,128]{2,1,0:T(8,128)}, f32[64,64,128]{2,1,0:T(8,128)}, u32[]{:S(2)}, u32[]{:S(2)}) collective-permute-start(f32[64,64,128]{2,1,0:T(8,128)} %multiply_add_fusion.3), channel_id=1, source_target_pairs={{0,4},{1,5},{2,6},{3,7},{4,8},{5,9},{6,10},{7,11},{8,12},{9,13},{1... | collective-permute-start | bytes 6291464 | tf_op jit(solution)/shard_map/ppermute | solution.py:113
  175.5 41.6 %collective-permute-start.12 = (f32[64]{0:T(128)S(1)}, f32[64]{0:T(128)S(1)}, u32[]{:S(2)}, u32[]{:S(2)}) collective-permute-start(f32[64]{0:T(128)S(1)} %collective-permute-done.11), channel_id=1, source_target_pairs={{0,2},{1,3},{2,4},{3,5},{4,6},{5,7},{6,8},{7,9},{8,10},{9,11},{10,... | collective-permute-start | bytes 776 | tf_op jit(solution)/shard_map/ppermute | solution.py:113
  217.1 5.2 %collective-permute-start.16 = (f32[64]{0:T(128)S(1)}, f32[64]{0:T(128)S(1)}, u32[]{:S(2)}, u32[]{:S(2)}) collective-permute-start(f32[64]{0:T(128)S(1)} %mul.335), channel_id=1, source_target_pairs={{0,4},{1,5},{2,6},{3,7},{4,8},{5,9},{6,10},{7,11},{8,12},{9,13},{1... | collective-permute-start | bytes 776 | tf_op jit(solution)/shard_map/ppermute | solution.py:113
  222.3 6.5 %copy-start.4 = (bf16[256,8192]{0,1:T(8,128)(2,1)S(1)}, bf16[256,8192]{0,1:T(8,128)(2,1)}, u32[]{:S(2)}) copy-start(bf16[256,8192]{0,1:T(8,128)(2,1)} %copy.28) | copy-start | bytes 12582916
  225.1 12.6 %copy-start.1 = (f32[128,64,128]{2,1,0:T(8,128)S(1)}, f32[128,64,128]{2,1,0:T(8,128)}, u32[]{:S(2)}) copy-start(f32[128,64,128]{2,1,0:T(8,128)} %copy-done) | copy-start | bytes 12582916
  225.1 12.6 %copy-start.3 = (f32[64,64,128]{2,1,0:T(8,128)S(1)}, f32[64,64,128]{2,1,0:T(8,128)}, u32[]{:S(2)}) copy-start(f32[64,64,128]{2,1,0:T(8,128)} %copy-done.2) | copy-start | bytes 6291460
  225.1 12.5 %collective-permute-start.17 = (bf16[64,64,128]{2,1,0:T(8,128)(2,1)S(1)}, bf16[64,64,128]{2,1,0:T(8,128)(2,1)S(1)}, u32[]{:S(2)}, u32[]{:S(2)}) collective-permute-start(bf16[64,64,128]{2,1,0:T(8,128)(2,1)S(1)} %fusion.19), channel_id=1, source_target_pairs={{0,1},{1,0},{2,3},{3,2},{4,5},{5,4},{6,7},{7,6},{8,9},{9,8},{10,11... | collective-permute-start | bytes 3145736 | tf_op jit(solution)/shard_map/ppermute | solution.py:211

commit v8 on v7

--- a/solution.py
+++ b/solution.py
@@ -52,7 +52,7 @@
         early = pltpu.roll(rim, rows - offset, 0) if offset else rim
         seen = jnp.where(row < lag, early, pltpu.roll(here, lag, 0))
         summed = summed + w_ref[offset : offset + 1, :].astype(jnp.float32) * seen * vis_ref[offset]
-    o_ref[...] = jax.nn.silu(summed).astype(o_ref.dtype)
+    o_ref[...] = jnp.transpose(jax.nn.silu(summed)).astype(o_ref.dtype)
 
 
 def conv_rows(rim_vals, values, rim_segment, segment, weight, offset_bias):
@@ -65,7 +65,7 @@
     tile = min(width, 1024)
     return pl.pallas_call(
         conv_rows_kernel,
-        out_shape=jax.ShapeDtypeStruct((rows, width), jnp.bfloat16),
+        out_shape=jax.ShapeDtypeStruct((width, rows), jnp.bfloat16),
         grid=(width // tile,),
         in_specs=[
             pl.BlockSpec((8, tile), lambda j: (0, j)),
@@ -74,11 +74,11 @@
             pl.BlockSpec((1, tile), lambda j: (0, j)),
             pl.BlockSpec((CONV - 1, rows, 1), lambda j: (0, 0, 0)),
         ],
-        out_specs=pl.BlockSpec((rows, tile), lambda j: (0, j)),
+        out_specs=pl.BlockSpec((tile, rows), lambda j: (j, 0)),
         cost_estimate=pl.CostEstimate(
             flops=20 * rows * width, transcendentals=rows * width, bytes_accessed=4 * rows * width
         ),
-    )(rim8, values, weight, offset_bias.reshape(1, width), vis)
+    )(rim8, values, weight, offset_bias.reshape(1, width), vis).T
 
 
 def mixing_part(x_group, b_group, c_group, step_size, cum_decay, segment):

time: 264 us -> 254 us (0.962)
  waiting for transfers between devices: 140 us -> 134 us
  other arithmetic: 33.1 us -> 29.4 us
    reshape x1 -> x0, local copies, waits for them, and re-layouts: 8.88 us -> none  [local(): y_blocks.reshape(tok_rows, head_count, HEAD_DIM)]
    optimization_barrier x1 -> x0, local copies, waits for them, and re-layouts: 6.37 us -> none  [local(): ids, x_conv = lax.optimization_barrier((ids, x_conv))]
    unnamed x17 -> x20, local copies, waits for them, and re-layouts: 3 us -> 9.35 us
    ppermute x6, waiting for transfers between devices: 133 us -> 127 us  [shifted(): lax.ppermute(value, axis, [(s, s + steps) for s in range(count - steps)])]
    convert_element_type x0 -> x1, local copies, waits for them, and re-layouts: none -> 6.31 us  [local(): (gated * scale[:, None] * norm_gain.astype(jnp.float32)).astype(jnp.bfloa...]
    reduce_sum x1, other arithmetic: 8.07 us -> 4.7 us  [local(): local_sq = jnp.sum(gated * gated, axis=1)]
  transfers between devices with their start and end apart: 15 -> 15, of which waited for: 8 -> 8; matrix products, arithmetic and copies ran while one was open for 14% -> 18% of each run, Pallas kernels for 4% -> 4%
where the time goes in v8:
time: 254 us; the launch traced here: 253 us
  waiting for transfers between devices  134 us (53%)
  other arithmetic  29.4 us (12%)
  starting transfers between devices  28 us (11%)
  local copies, waits for them, and re-layouts  24.6 us (10%)
  matrix products  24.1 us (9%)
  Pallas kernels  10.8 us (4%)
    ppermute x6, waiting for transfers between devices, shifted(): lax.ppermute(value, axis, [(s, s + steps) for s in range(count - steps)])  127 us
    ppermute x6, starting transfers between devices, shifted(): lax.ppermute(value, axis, [(s, s + steps) for s in range(count - steps)])  13.3 us
    pallas_call x1, Pallas kernels, conv_rows(): pl.pallas_call(conv_rows_kernel, out_shape=jax.ShapeDtypeStruct((width, r...  10.8 us
    dot_general x1, matrix products, mixing_part(): jnp.einsum('hij,jhp->ihp', mixing, x_group, preferred_element_type=jnp.fl...  10.8 us
    unnamed x20, local copies, waits for them, and re-layouts  9.35 us
    dot_general x1, matrix products, state_part(): jnp.einsum('hjn,jhp->hpn', weighted, x_group, preferred_element_type=jnp....  8.34 us
    convert_element_type x1, local copies, waits for them, and re-layouts, local(): (gated * scale[:, None] * norm_gain.astype(jnp.float32)).astype(jnp.bfloa...  6.31 us
    ppermute x5, starting transfers between devices, gather_round(): other = lax.ppermute(value, axis, [(s, s ^ size) for s in range(count)])  5.68 us
  transfers between devices with their start and end apart: 15, of which 8 were waited for; matrix products, arithmetic and copies ran while one was open for 18% of the time, Pallas kernels for 4%

profile of v8, /device:TPU:9, one launch (start us, length us, event | category | flops | bytes accessed | tf_op | source)
XLA Modules:
  0.0 253.1 jit_solution(12757038381757881523)
XLA Ops:
  0.0 1.3 slice.98
  2.6 0.9 slice.99
  3.7 0.7 slice.100
  4.5 3.0 %collective-permute-start.3 = (bf16[3,8449]{1,0:T(4,128)(2,1)S(1)}, bf16[3,8449]{1,0:T(4,128)(2,1)S(1)}, u32[]{:S(2)}, u32[]{:S(2)}) collective-permute-start(bf16[3,8449]{1,0:T(4,128)(2,1)S(1)} %pad_maximum_fusion.1), channel_id=1, source_target_pairs={{0,1},{1,2},{2,3},{3,4},{4,5},{5,6},{6,7},{7,8},{8,9},{9,10},{10,1... | collective-permute-start | bytes 152090 | tf_op jit(solution)/shard_map/ppermute | solution.py:23
  7.5 1.0 copy.22
  8.5 0.8 negate_multiply_fusion
  9.4 1.3 reshape.198.b_ref
  10.8 0.8 slice_convert_fusion.5
  12.3 1.4 broadcast_select_fusion.1
  13.7 1.2 collective-permute-start.6
  14.9 1.2 collective-permute-done.6
  16.2 1.3 collective-permute-start.7
  18.2 0.8 pad_add_fusion
  20.2 2.0 compare_convert_fusion.4
  22.3 0.9 copy.26.vis_ref
  23.2 1.4 multiply_convert_fusion.7
  24.8 0.8 fusion.35
  26.3 10.8 %shard_map.127 = bf16[8192,256]{1,0:T(8,128)(2,1)} custom-call(bf16[8,8192]{1,0:T(8,128)(2,1)} %concatenate.76.rim_ref, bf16[256,8192]{1,0:T(8,128)(2,1)} %x_ref.1, bf16[4,8192]{1,0:T(4,128)(2,1)} %w_ref.1, bf16[1,8192]{1,0:T(2,128)(2,1)} %reshape.198.b_ref, f32[3,256,1]{2,1,0:T(8,128)} %copy.26.vis_ref), custom_call_target="tpu_custom_call" | custom-call | flops 41943040 | bytes 8388608 | tf_op jit(solution)/shard_map/pallas_call | solution.py:66
  37.4 2.2 collective-permute-done.8
  39.7 2.3 collective-permute-start.9
  42.0 8.3 %fusion.15 = f32[1,128,64,128]{3,2,1,0:T(8,128)S(1)} fusion(bf16[256,128,64]{0,2,1:T(8,128)(2,1)} %bitcast.74, f32[128,256]{1,0:T(8,128)S(1)} %copy.27, f32[256,128]{1,0:T(8,128)S(1)} %get-tuple-element.83), kind=kOutput, calls=%fused_computation.26 | convolution fusion | flops 545259520 | bytes 8650752 | tf_op jit(solution)/shard_map/hjn,jhp->hpn/dot_general | solution.py:100
  50.8 2.0 copy-done
  52.7 1.5 constant_dynamic-slice_fusion
  54.2 2.3 collective-permute-start.10
  56.5 3.6 %collective-permute-done.4 = f32[128]{0:T(128)S(1)} collective-permute-done((f32[128]{0:T(128)S(1)}, f32[128]{0:T(128)S(1)}, u32[]{:S(2)}, u32[]{:S(2)}) %collective-permute-start.4) | collective-permute-done | bytes 544 | tf_op jit(solution)/shard_map/ppermute | solution.py:200
  60.5 2.8 %add_select_fusion = f32[64,64,128]{2,1,0:T(8,128)S(1)} fusion(f32[64,64,128]{2,1,0:T(8,128)S(1)} %collective-permute-done.10, f32[128,64,128]{2,1,0:T(8,128)} %copy-done, s32[]{:T(128)S(6)} %select_n.101, f32[64]{0:T(128)S(1)} %get-tuple-element.74, f32[64]{0:T(128)S(1)} %get-tuple-element.73, pred[]{:T(512)S(6)} %eq.73), kind=kLoop, calls=%fused_computation.35 | loop fusion | flops 2621440 | bytes 6291973 | tf_op jit(solution)/shard_map/jit(_where)/select_n | solution.py:205
  63.3 3.1 %collective-permute-start.13 = (f32[64,64,128]{2,1,0:T(8,128)S(1)}, f32[64,64,128]{2,1,0:T(8,128)S(1)}, u32[]{:S(2)}, u32[]{:S(2)}) collective-permute-start(f32[64,64,128]{2,1,0:T(8,128)S(1)} %add_select_fusion), channel_id=1, source_target_pairs={{0,2},{1,3},{2,4},{3,5},{4,6},{5,7},{6,8},{7,9},{8,10},{9,11},{10,... | collective-permute-start | bytes 6291464 | tf_op jit(solution)/shard_map/ppermute | solution.py:113
  66.4 47.4 %collective-permute-done.13 = f32[64,64,128]{2,1,0:T(8,128)S(1)} collective-permute-done((f32[64,64,128]{2,1,0:T(8,128)S(1)}, f32[64,64,128]{2,1,0:T(8,128)S(1)}, u32[]{:S(2)}, u32[]{:S(2)}) %collective-permute-start.13) | collective-permute-done | bytes 2097184 | tf_op jit(solution)/shard_map/ppermute | solution.py:113
  113.8 1.9 collective-permute-start.14
  115.7 2.4 collective-permute-start.11
  118.1 45.3 %collective-permute-done.11 = f32[64]{0:T(128)S(1)} collective-permute-done((f32[64]{0:T(128)S(1)}, f32[64]{0:T(128)S(1)}, u32[]{:S(2)}, u32[]{:S(2)}) %collective-permute-start.11) | collective-permute-done | bytes 288 | tf_op jit(solution)/shard_map/ppermute | solution.py:113
  163.4 1.6 multiply_add_fusion.3
  165.0 2.1 collective-permute-start.15
  167.1 6.4 %copy.36 = bf16[256,8192]{0,1:T(8,128)(2,1)} copy(bf16[256,8192]{1,0:T(8,128)(2,1)} %param.16) | data formatting | bytes 8388608 | tf_op args[1]
  174.2 0.8 compare_reduce_fusion
  176.0 1.9 collective-permute-start.12
  178.2 33.1 %collective-permute-done.12 = f32[64]{0:T(128)S(1)} collective-permute-done((f32[64]{0:T(128)S(1)}, f32[64]{0:T(128)S(1)}, u32[]{:S(2)}, u32[]{:S(2)}) %collective-permute-start.12) | collective-permute-done | bytes 288 | tf_op jit(solution)/shard_map/ppermute | solution.py:113
  211.3 1.9 collective-permute-start.16
  213.2 2.5 multiply_add_fusion.2
  215.7 0.8 collective-permute-done.16
  216.5 2.8 %fusion.19 = bf16[64,64,128]{2,1,0:T(8,128)(2,1)S(1)} fusion(f32[64,64,128]{2,1,0:T(8,128)S(1)} %get-tuple-element.93, f32[64,64,128]{2,1,0:T(8,128)} %copy-done.2, f32[128,64,128]{2,1,0:T(8,128)} %copy-done, s32[]{:T(128)S(6)} %select_n.101, f32[64]{0:T(128)S(1)} %get-tuple-element.72, pred[]{:T(512)S(6)} %eq.73), kind=kLoop, calls=%fused_computation.36 | loop fusion | flops 2097152 | bytes 7340293 | tf_op jit(solution)/shard_map/jit(_where)/select_n | solution.py:211
  219.3 3.7 %collective-permute-start.17 = (bf16[64,64,128]{2,1,0:T(8,128)(2,1)S(1)}, bf16[64,64,128]{2,1,0:T(8,128)(2,1)S(1)}, u32[]{:S(2)}, u32[]{:S(2)}) collective-permute-start(bf16[64,64,128]{2,1,0:T(8,128)(2,1)S(1)} %fusion.19), channel_id=1, source_target_pairs={{0,1},{1,0},{2,3},{3,2},{4,5},{5,4},{6,7},{7,6},{8,9},{9,8},{10,11... | collective-permute-start | bytes 3145736 | tf_op jit(solution)/shard_map/ppermute | solution.py:211
  223.0 10.8 %fusion = f32[128,64,256]{2,1,0:T(8,128)} fusion(f32[128,256]{1,0:T(8,128)S(1)} %copy.31, f32[128,256]{1,0:T(8,128)S(1)} %copy.29, f32[256,256]{1,0:T(8,128)S(1)} %fusion.27, pred[256,256]{1,0:T(8,128)(4,1)S(1)} %fusion.21, bf16[1,256,128,64]{1,3,2,0:T(8,128)(2,1)S(1)} %bitcast.75), kind=kOutput, calls=%fused_computation.3 | convolution fusion | flops 1115684864 | bytes 13172736 | tf_op jit(solution)/shard_map/hij,jhp->ihp/dot_general | solution.py:92
  233.8 0.8 select_convert_fusion.1
  234.7 4.8 %bitcast_add_fusion.1 = f32[256,128,64]{0,2,1:T(8,128)S(1)} fusion(f32[128,64,256]{2,1,0:T(8,128)} %fusion, f32[256,128]{0,1:T(8,128)S(1)} %copy.34, bf16[64,64,128]{2,1,0:T(8,128)(2,1)S(1)} %select_convert_fusion, bf16[64,64,128]{2,1,0:T(8,128)(2,1)S(1)} %get-tuple-element.70, bf16[256,256]{1,0:T(8,128)(2,1)S(1)} %multiply_convert_fusion.7), kind=kOutput, calls=%fused_computation.19 | convolution fusion | flops 545259520 | bytes 19070976 | tf_op jit(solution)/shard_map/in,hpn->ihp/dot_general | solution.py:108
  239.5 4.7 %multiply_reduce_fusion = (f32[256]{0:T(256)S(1)}, f32[256,8192]{0,1:T(8,128)S(1)}) fusion(bf16[256,8192]{0,1:T(8,128)(2,1)S(1)} %copy-done.5, bf16[256,8192]{0,1:T(8,128)(2,1)S(1)} %bitcast.76, f32[8192]{0:T(1024)S(1)} %mul.347, f32[256,128,64]{0,2,1:T(8,128)S(1)} %bitcast_add_fusion.1), kind=kLoop, calls=%fused_computation.21 | loop fusion | flops 23068416 | bytes 25199616 | tf_op jit(solution)/shard_map/reduce_sum | solution.py:316
  244.2 2.6 %multiply_convert_fusion.4 = bf16[256,8192]{0,1:T(8,128)(2,1)} fusion(f32[256,8192]{0,1:T(8,128)S(1)} %get-tuple-element.69, f32[8192]{0:T(1024)S(1)} %convert_element_type.105, f32[256]{0:T(256)S(1)} %add_rsqrt_fusion), kind=kLoop, calls=%fused_computation.20 | loop fusion | flops 6291456 | bytes 12616704 | tf_op jit(solution)/shard_map/convert_element_type | solution.py:319
  246.8 6.3 %copy.37 = bf16[256,8192]{1,0:T(8,128)(2,1)} copy(bf16[256,8192]{0,1:T(8,128)(2,1)} %multiply_convert_fusion.4) | data formatting | bytes 8388608 | tf_op jit(solution)/shard_map/convert_element_type | solution.py:319
  (76 shorter events, 6.7 us)
Async XLA Ops:
  1.3 11.1 %collective-permute-start.5 = (s32[1]{0:T(128)}, s32[1]{0:T(128)}, u32[]{:S(2)}, u32[]{:S(2)}) collective-permute-start(s32[1]{0:T(128)} %slice.98), channel_id=1, source_target_pairs={{0,1},{1,0},{2,3},{3,2},{4,5},{5,4},{6,7},{7,6},{8,9},{9,8},{10,11... | collective-permute-start | bytes 20 | tf_op jit(solution)/shard_map/ppermute | solution.py:151
  4.5 11.7 %collective-permute-start.3 = (bf16[3,8449]{1,0:T(4,128)(2,1)S(1)}, bf16[3,8449]{1,0:T(4,128)(2,1)S(1)}, u32[]{:S(2)}, u32[]{:S(2)}) collective-permute-start(bf16[3,8449]{1,0:T(4,128)(2,1)S(1)} %pad_maximum_fusion.1), channel_id=1, source_target_pairs={{0,1},{1,2},{2,3},{3,4},{4,5},{5,6},{6,7},{7,8},{8,9},{9,10},{10,1... | collective-permute-start | bytes 152090 | tf_op jit(solution)/shard_map/ppermute | solution.py:23
  13.7 2.4 collective-permute-start.6
  16.2 20.9 %collective-permute-start.7 = (s32[4]{0:T(128)S(1)}, s32[4]{0:T(128)S(1)}, u32[]{:S(2)}, u32[]{:S(2)}) collective-permute-start(s32[4]{0:T(128)S(1)} %broadcast_select_fusion.2), channel_id=1, source_target_pairs={{0,4},{1,5},{2,6},{3,7},{4,0},{5,1},{6,2},{7,3},{8,12},{9,13},{10,... | collective-permute-start | bytes 56 | tf_op jit(solution)/shard_map/ppermute | solution.py:151
  37.2 2.4 collective-permute-start.8
  39.7 10.7 %collective-permute-start.9 = (s32[16]{0:T(128)S(1)}, s32[16]{0:T(128)S(1)}, u32[]{:S(2)}, u32[]{:S(2)}) collective-permute-start(s32[16]{0:T(128)S(1)} %broadcast_select_fusion.4), channel_id=1, source_target_pairs={{0,16},{1,17},{2,18},{3,19},{4,20},{5,21},{6,22},{7,23},{8,24},{9,... | collective-permute-start | bytes 200 | tf_op jit(solution)/shard_map/ppermute | solution.py:151
  50.8 2.0 copy-start
  54.2 6.3 %collective-permute-start.10 = (f32[64,64,128]{2,1,0:T(8,128)}, f32[64,64,128]{2,1,0:T(8,128)S(1)}, u32[]{:S(2)}, u32[]{:S(2)}) collective-permute-start(f32[64,64,128]{2,1,0:T(8,128)} %constant_dynamic-slice_fusion), channel_id=1, source_target_pairs={{0,1},{1,0},{2,3},{3,2},{4,5},{5,4},{6,7},{7,6},{8,9},{9,8},{10,11... | collective-permute-start | bytes 6291464 | tf_op jit(solution)/shard_map/ppermute | solution.py:200
  56.5 3.6 %collective-permute-start.4 = (f32[128]{0:T(128)S(1)}, f32[128]{0:T(128)S(1)}, u32[]{:S(2)}, u32[]{:S(2)}) collective-permute-start(f32[128]{0:T(128)S(1)} %get-tuple-element.78), channel_id=1, source_target_pairs={{0,1},{1,0},{2,3},{3,2},{4,5},{5,4},{6,7},{7,6},{8,9},{9,8},{10,11... | collective-permute-start | bytes 1544 | tf_op jit(solution)/shard_map/ppermute | solution.py:200
  60.5 104.5 %copy-start.2 = (f32[64,64,128]{2,1,0:T(8,128)}, f32[64,64,128]{2,1,0:T(8,128)S(1)}, u32[]{:S(2)}) copy-start(f32[64,64,128]{2,1,0:T(8,128)S(1)} %collective-permute-done.10) | copy-start | bytes 6291460
  63.3 50.5 %collective-permute-start.13 = (f32[64,64,128]{2,1,0:T(8,128)S(1)}, f32[64,64,128]{2,1,0:T(8,128)S(1)}, u32[]{:S(2)}, u32[]{:S(2)}) collective-permute-start(f32[64,64,128]{2,1,0:T(8,128)S(1)} %add_select_fusion), channel_id=1, source_target_pairs={{0,2},{1,3},{2,4},{3,5},{4,6},{5,7},{6,8},{7,9},{8,10},{9,11},{10,... | collective-permute-start | bytes 6291464 | tf_op jit(solution)/shard_map/ppermute | solution.py:113
  113.8 49.6 %collective-permute-start.14 = (f32[64,64,128]{2,1,0:T(8,128)S(1)}, f32[64,64,128]{2,1,0:T(8,128)S(1)}, u32[]{:S(2)}, u32[]{:S(2)}) collective-permute-start(f32[64,64,128]{2,1,0:T(8,128)S(1)} %collective-permute-done.13), channel_id=1, source_target_pairs={{0,2},{1,3},{2,4},{3,5},{4,6},{5,7},{6,8},{7,9},{8,10},{9,11},{10,... | collective-permute-start | bytes 6291464 | tf_op jit(solution)/shard_map/ppermute | solution.py:113
  115.7 47.7 %collective-permute-start.11 = (f32[64]{0:T(128)S(1)}, f32[64]{0:T(128)S(1)}, u32[]{:S(2)}, u32[]{:S(2)}) collective-permute-start(f32[64]{0:T(128)S(1)} %mul.294), channel_id=1, source_target_pairs={{0,2},{1,3},{2,4},{3,5},{4,6},{5,7},{6,8},{7,9},{8,10},{9,11},{10,... | collective-permute-start | bytes 776 | tf_op jit(solution)/shard_map/ppermute | solution.py:113
  165.0 8.4 %copy-start.8 = (f32[128]{0:T(128)S(1)}, f32[128]{0:T(128)}, u32[]{:S(2)}) copy-start(f32[128]{0:T(128)} %param.21) | copy-start | bytes 1540
  165.0 8.6 %copy-start.6 = (bf16[8192]{0:T(1024)(128)(2,1)S(1)}, bf16[8192]{0:T(1024)(128)(2,1)}, u32[]{:S(2)}) copy-start(bf16[8192]{0:T(1024)(128)(2,1)} %param.26) | copy-start | bytes 49156
  165.0 10.7 %copy-start.7 = (s32[256]{0:T(256)S(1)}, s32[256]{0:T(256)}, u32[]{:S(2)}) copy-start(s32[256]{0:T(256)} %param.27) | copy-start | bytes 3076
  165.0 48.2 %collective-permute-start.15 = (f32[64,64,128]{2,1,0:T(8,128)}, f32[64,64,128]{2,1,0:T(8,128)}, u32[]{:S(2)}, u32[]{:S(2)}) collective-permute-start(f32[64,64,128]{2,1,0:T(8,128)} %multiply_add_fusion.3), channel_id=1, source_target_pairs={{0,4},{1,5},{2,6},{3,7},{4,8},{5,9},{6,10},{7,11},{8,12},{9,13},{1... | collective-permute-start | bytes 6291464 | tf_op jit(solution)/shard_map/ppermute | solution.py:113
  176.0 35.3 %collective-permute-start.12 = (f32[64]{0:T(128)S(1)}, f32[64]{0:T(128)S(1)}, u32[]{:S(2)}, u32[]{:S(2)}) collective-permute-start(f32[64]{0:T(128)S(1)} %collective-permute-done.11), channel_id=1, source_target_pairs={{0,2},{1,3},{2,4},{3,5},{4,6},{5,7},{6,8},{7,9},{8,10},{9,11},{10,... | collective-permute-start | bytes 776 | tf_op jit(solution)/shard_map/ppermute | solution.py:113
  211.3 5.2 %collective-permute-start.16 = (f32[64]{0:T(128)S(1)}, f32[64]{0:T(128)S(1)}, u32[]{:S(2)}, u32[]{:S(2)}) collective-permute-start(f32[64]{0:T(128)S(1)} %mul.335), channel_id=1, source_target_pairs={{0,4},{1,5},{2,6},{3,7},{4,8},{5,9},{6,10},{7,11},{8,12},{9,13},{1... | collective-permute-start | bytes 776 | tf_op jit(solution)/shard_map/ppermute | solution.py:113
  216.5 6.5 %copy-start.4 = (bf16[8192,256]{1,0:T(8,128)(2,1)S(1)}, bf16[8192,256]{1,0:T(8,128)(2,1)}, u32[]{:S(2)}) copy-start(bf16[8192,256]{1,0:T(8,128)(2,1)} %shard_map.127) | copy-start | bytes 12582916
  219.3 14.5 %copy-start.1 = (f32[128,64,128]{2,1,0:T(8,128)S(1)}, f32[128,64,128]{2,1,0:T(8,128)}, u32[]{:S(2)}) copy-start(f32[128,64,128]{2,1,0:T(8,128)} %copy-done) | copy-start | bytes 12582916
  219.3 14.5 %copy-start.3 = (f32[64,64,128]{2,1,0:T(8,128)S(1)}, f32[64,64,128]{2,1,0:T(8,128)}, u32[]{:S(2)}) copy-start(f32[64,64,128]{2,1,0:T(8,128)} %copy-done.2) | copy-start | bytes 6291460
  219.3 14.5 %collective-permute-start.17 = (bf16[64,64,128]{2,1,0:T(8,128)(2,1)S(1)}, bf16[64,64,128]{2,1,0:T(8,128)(2,1)S(1)}, u32[]{:S(2)}, u32[]{:S(2)}) collective-permute-start(bf16[64,64,128]{2,1,0:T(8,128)(2,1)S(1)} %fusion.19), channel_id=1, source_target_pairs={{0,1},{1,0},{2,3},{3,2},{4,5},{5,4},{6,7},{7,6},{8,9},{9,8},{10,11... | collective-permute-start | bytes 3145736 | tf_op jit(solution)/shard_map/ppermute | solution.py:211
  234.7 4.8 %copy-start.5 = (bf16[256,8192]{0,1:T(8,128)(2,1)S(1)}, bf16[256,8192]{0,1:T(8,128)(2,1)}, u32[]{:S(2)}) copy-start(bf16[256,8192]{0,1:T(8,128)(2,1)} %copy.36) | copy-start | bytes 12582916

commit v9 on v8

--- a/solution.py
+++ b/solution.py
@@ -79,6 +79,27 @@
             flops=20 * rows * width, transcendentals=rows * width, bytes_accessed=4 * rows * width
         ),
     )(rim8, values, weight, offset_bias.reshape(1, width), vis).T
+
+
+def scale_rows_kernel(g_ref, s_ref, n_ref, o_ref):
+    o_ref[...] = jnp.transpose(g_ref[...] * s_ref[...] * n_ref[...]).astype(o_ref.dtype)
+
+
+def scale_rows(gated, scale, gain):
+    rows, width = gated.shape
+    tile = min(width, 1024)
+    return pl.pallas_call(
+        scale_rows_kernel,
+        out_shape=jax.ShapeDtypeStruct((rows, width), jnp.bfloat16),
+        grid=(width // tile,),
+        in_specs=[
+            pl.BlockSpec((tile, rows), lambda j: (j, 0)),
+            pl.BlockSpec((1, rows), lambda j: (0, 0)),
+            pl.BlockSpec((tile, 1), lambda j: (j, 0)),
+        ],
+        out_specs=pl.BlockSpec((rows, tile), lambda j: (0, j)),
+        cost_estimate=pl.CostEstimate(flops=2 * rows * width, transcendentals=0, bytes_accessed=6 * rows * width),
+    )(gated.T, scale[None, :], gain.astype(jnp.float32)[:, None])
 
 
 def mixing_part(x_group, b_group, c_group, step_size, cum_decay, segment):
@@ -316,7 +337,7 @@
     local_sq = jnp.sum(gated * gated, axis=1)
     total_sq = lax.psum(local_sq, "tp")
     scale = lax.rsqrt(total_sq / INNER + epsilon)
-    return (gated * scale[:, None] * norm_gain.astype(jnp.float32)).astype(jnp.bfloat16)
+    return scale_rows(gated, scale, norm_gain)
 
 
 def cores_paired(mesh):

time: 254 us -> 252 us (level)
  Pallas kernels: 10.8 us -> 20.3 us
  matrix products: 24.1 us -> 18.6 us
  waiting for transfers between devices: 134 us -> 131 us
  local copies, waits for them, and re-layouts: 24.6 us -> 21.9 us
    pallas_call x0 -> x1, Pallas kernels: none -> 9.48 us  [scale_rows(): pl.pallas_call(scale_rows_kernel, out_shape=jax.ShapeDtypeStruct((rows, w...]
    convert_element_type x1 -> x0, local copies, waits for them, and re-layouts: 6.31 us -> none  [local(): (gated * scale[:, None] * norm_gain.astype(jnp.float32)).astype(jnp.bfloa...]
    dot_general x1, matrix products: 4.78 us -> 1.26 us  [entry_part(): jnp.einsum('in,hpn->ihp', c_group, packed, preferred_element_type=jnp.flo...]
    broadcast_in_dim x0 -> x1, local copies, waits for them, and re-layouts: none -> 2.65 us  [scale_rows(): gain.astype(jnp.float32)[:, None]]
    convert_element_type x2 -> x0, other arithmetic: 2.59 us -> none  [the longest x1 2.58 us: local(): (gated * scale[:, None] * norm_gain.astype(jnp.float32)).astype(jnp.bfloa...]
  transfers between devices with their start and end apart: 15 -> 15, of which waited for: 8 -> 8; matrix products, arithmetic and copies ran while one was open for 18% -> 19% of each run, Pallas kernels for 4% -> 4%
where the time goes in v9:
time: 252 us; the launch traced here: 251 us
  waiting for transfers between devices  131 us (52%)
  other arithmetic  28.3 us (11%)
  starting transfers between devices  28 us (11%)
  local copies, waits for them, and re-layouts  21.9 us (9%)
  Pallas kernels  20.3 us (8%)
  matrix products  18.6 us (7%)
    ppermute x6, waiting for transfers between devices, shifted(): lax.ppermute(value, axis, [(s, s + steps) for s in range(count - steps)])  124 us
    ppermute x6, starting transfers between devices, shifted(): lax.ppermute(value, axis, [(s, s + steps) for s in range(count - steps)])  13.3 us
    pallas_call x1, Pallas kernels, conv_rows(): pl.pallas_call(conv_rows_kernel, out_shape=jax.ShapeDtypeStruct((width, r...  10.8 us
    unnamed x20, local copies, waits for them, and re-layouts  10.3 us
    pallas_call x1, Pallas kernels, scale_rows(): pl.pallas_call(scale_rows_kernel, out_shape=jax.ShapeDtypeStruct((rows, w...  9.48 us
    dot_general x1, matrix products, mixing_part(): jnp.einsum('hij,jhp->ihp', mixing, x_group, preferred_element_type=jnp.fl...  8.86 us
    dot_general x1, matrix products, state_part(): jnp.einsum('hjn,jhp->hpn', weighted, x_group, preferred_element_type=jnp....  8.34 us
    reduce_sum x1, other arithmetic, local(): local_sq = jnp.sum(gated * gated, axis=1)  5.72 us
  transfers between devices with their start and end apart: 15, of which 8 were waited for; matrix products, arithmetic and copies ran while one was open for 19% of the time, Pallas kernels for 4%

profile of v9, /device:TPU:9, one launch (start us, length us, event | category | flops | bytes accessed | tf_op | source)
XLA Modules:
  0.0 250.7 jit_solution(4324217724903116772)
XLA Ops:
  0.0 1.3 slice.98
  2.6 0.9 slice.99
  4.5 3.0 %collective-permute-start.3 = (bf16[3,8449]{1,0:T(4,128)(2,1)S(1)}, bf16[3,8449]{1,0:T(4,128)(2,1)S(1)}, u32[]{:S(2)}, u32[]{:S(2)}) collective-permute-start(bf16[3,8449]{1,0:T(4,128)(2,1)S(1)} %pad_maximum_fusion.1), channel_id=1, source_target_pairs={{0,1},{1,2},{2,3},{3,4},{4,5},{5,6},{6,7},{7,8},{8,9},{9,10},{10,1... | collective-permute-start | bytes 152090 | tf_op jit(solution)/shard_map/ppermute | solution.py:23
  7.5 1.0 copy.21
  8.5 0.8 negate_multiply_fusion
  9.4 1.3 reshape.210.b_ref
  10.8 0.8 slice_convert_fusion.5
  12.3 1.4 broadcast_select_fusion.1
  13.7 1.2 collective-permute-start.6
  14.9 1.2 collective-permute-done.6
  16.2 1.3 collective-permute-start.7
  18.2 0.8 pad_add_fusion
  20.2 2.0 compare_convert_fusion.4
  22.3 0.9 copy.25.vis_ref
  23.2 1.5 multiply_convert_fusion.6
  24.9 0.8 fusion.35
  26.4 10.8 %shard_map.127 = bf16[8192,256]{1,0:T(8,128)(2,1)} custom-call(bf16[8,8192]{1,0:T(8,128)(2,1)} %concatenate.76.rim_ref, bf16[256,8192]{1,0:T(8,128)(2,1)} %x_ref.1, bf16[4,8192]{1,0:T(4,128)(2,1)} %w_ref.1, bf16[1,8192]{1,0:T(2,128)(2,1)} %reshape.210.b_ref, f32[3,256,1]{2,1,0:T(8,128)} %copy.25.vis_ref), custom_call_target="tpu_custom_call" | custom-call | flops 41943040 | bytes 8388608 | tf_op jit(solution)/shard_map/pallas_call | solution.py:66
  37.5 2.2 collective-permute-done.8
  39.8 2.3 collective-permute-start.9
  42.1 8.3 %fusion.15 = f32[1,128,64,128]{3,2,1,0:T(8,128)S(1)} fusion(bf16[256,128,64]{0,2,1:T(8,128)(2,1)} %bitcast.78, f32[128,256]{1,0:T(8,128)S(1)} %copy.26, f32[256,128]{1,0:T(8,128)S(1)} %get-tuple-element.83), kind=kOutput, calls=%fused_computation.25 | convolution fusion | flops 545259520 | bytes 8650752 | tf_op jit(solution)/shard_map/hjn,jhp->hpn/dot_general | solution.py:121
  50.9 2.0 copy-done
  52.8 1.5 constant_dynamic-slice_fusion
  54.3 2.3 collective-permute-start.10
  56.6 3.6 %collective-permute-done.4 = f32[128]{0:T(128)S(1)} collective-permute-done((f32[128]{0:T(128)S(1)}, f32[128]{0:T(128)S(1)}, u32[]{:S(2)}, u32[]{:S(2)}) %collective-permute-start.4) | collective-permute-done | bytes 544 | tf_op jit(solution)/shard_map/ppermute | solution.py:221
  60.6 2.8 %add_select_fusion = f32[64,64,128]{2,1,0:T(8,128)S(1)} fusion(f32[64,64,128]{2,1,0:T(8,128)S(1)} %collective-permute-done.10, f32[128,64,128]{2,1,0:T(8,128)} %copy-done, s32[]{:T(128)S(6)} %select_n.101, f32[64]{0:T(128)S(1)} %get-tuple-element.74, f32[64]{0:T(128)S(1)} %get-tuple-element.73, pred[]{:T(512)S(6)} %eq.73), kind=kLoop, calls=%fused_computation.34 | loop fusion | flops 2621440 | bytes 6291973 | tf_op jit(solution)/shard_map/jit(_where)/select_n | solution.py:226
  63.4 3.1 %collective-permute-start.13 = (f32[64,64,128]{2,1,0:T(8,128)S(1)}, f32[64,64,128]{2,1,0:T(8,128)S(1)}, u32[]{:S(2)}, u32[]{:S(2)}) collective-permute-start(f32[64,64,128]{2,1,0:T(8,128)S(1)} %add_select_fusion), channel_id=1, source_target_pairs={{0,2},{1,3},{2,4},{3,5},{4,6},{5,7},{6,8},{7,9},{8,10},{9,11},{10,... | collective-permute-start | bytes 6291464 | tf_op jit(solution)/shard_map/ppermute | solution.py:134
  66.5 47.4 %collective-permute-done.13 = f32[64,64,128]{2,1,0:T(8,128)S(1)} collective-permute-done((f32[64,64,128]{2,1,0:T(8,128)S(1)}, f32[64,64,128]{2,1,0:T(8,128)S(1)}, u32[]{:S(2)}, u32[]{:S(2)}) %collective-permute-start.13) | collective-permute-done | bytes 2097184 | tf_op jit(solution)/shard_map/ppermute | solution.py:134
  113.9 1.9 collective-permute-start.14
  115.8 2.4 collective-permute-start.11
  118.2 45.3 %collective-permute-done.11 = f32[64]{0:T(128)S(1)} collective-permute-done((f32[64]{0:T(128)S(1)}, f32[64]{0:T(128)S(1)}, u32[]{:S(2)}, u32[]{:S(2)}) %collective-permute-start.11) | collective-permute-done | bytes 288 | tf_op jit(solution)/shard_map/ppermute | solution.py:134
  163.5 1.6 multiply_add_fusion.3
  165.1 2.0 collective-permute-start.15
  167.1 6.4 %copy.35 = bf16[256,8192]{0,1:T(8,128)(2,1)} copy(bf16[256,8192]{1,0:T(8,128)(2,1)} %param.16) | data formatting | bytes 8388608 | tf_op args[1]
  173.7 2.6 %copy.36.n_ref = f32[8192,1]{1,0:T(8,128)} copy(f32[8192,1]{0,1:T(1,128)S(1)} %bitcast.84) | data formatting | bytes 65536 | tf_op jit(solution)/shard_map/broadcast_in_dim | solution.py:102
  176.9 0.7 compare_reduce_fusion
  178.6 1.9 collective-permute-start.12
  180.7 30.6 %collective-permute-done.12 = f32[64]{0:T(128)S(1)} collective-permute-done((f32[64]{0:T(128)S(1)}, f32[64]{0:T(128)S(1)}, u32[]{:S(2)}, u32[]{:S(2)}) %collective-permute-start.12) | collective-permute-done | bytes 288 | tf_op jit(solution)/shard_map/ppermute | solution.py:134
  211.3 1.9 collective-permute-start.16
  213.3 2.5 multiply_add_fusion.2
  215.8 0.8 collective-permute-done.16
  216.5 2.8 %fusion.19 = bf16[64,64,128]{2,1,0:T(8,128)(2,1)S(1)} fusion(f32[64,64,128]{2,1,0:T(8,128)S(1)} %get-tuple-element.93, f32[64,64,128]{2,1,0:T(8,128)} %copy-done.2, f32[128,64,128]{2,1,0:T(8,128)} %copy-done, s32[]{:T(128)S(6)} %select_n.101, f32[64]{0:T(128)S(1)} %get-tuple-element.72, pred[]{:T(512)S(6)} %eq.73), kind=kLoop, calls=%fused_computation.35 | loop fusion | flops 2097152 | bytes 7340293 | tf_op jit(solution)/shard_map/jit(_where)/select_n | solution.py:232
  219.3 3.7 %collective-permute-start.17 = (bf16[64,64,128]{2,1,0:T(8,128)(2,1)S(1)}, bf16[64,64,128]{2,1,0:T(8,128)(2,1)S(1)}, u32[]{:S(2)}, u32[]{:S(2)}) collective-permute-start(bf16[64,64,128]{2,1,0:T(8,128)(2,1)S(1)} %fusion.19), channel_id=1, source_target_pairs={{0,1},{1,0},{2,3},{3,2},{4,5},{5,4},{6,7},{7,6},{8,9},{9,8},{10,11... | collective-permute-start | bytes 3145736 | tf_op jit(solution)/shard_map/ppermute | solution.py:232
  223.0 8.9 %fusion = f32[128,64,256]{2,1,0:T(8,128)S(1)} fusion(f32[128,256]{1,0:T(8,128)S(1)} %copy.30, f32[128,256]{1,0:T(8,128)S(1)} %copy.28, f32[256,256]{1,0:T(8,128)S(1)} %fusion.27, pred[256,256]{1,0:T(8,128)(4,1)S(1)} %fusion.21, bf16[1,256,128,64]{1,3,2,0:T(8,128)(2,1)S(1)} %bitcast.79), kind=kOutput, calls=%fused_computation.3 | convolution fusion | flops 1115684864 | bytes 13172736 | tf_op jit(solution)/shard_map/hij,jhp->ihp/dot_general | solution.py:113
  231.9 0.7 select_convert_fusion.1
  232.8 1.3 bitcast_add_fusion.1
  234.1 0.9 copy-done.5
  235.0 5.7 %multiply_reduce_fusion = (f32[256]{0:T(256)S(1)}, f32[256,8192]{0,1:T(8,128)}) fusion(bf16[256,8192]{0,1:T(8,128)(2,1)S(1)} %copy-done.5, bf16[256,8192]{0,1:T(8,128)(2,1)S(1)} %bitcast.80, f32[8192]{0:T(1024)S(1)} %mul.331, f32[256,128,64]{0,2,1:T(8,128)S(1)} %bitcast_add_fusion.1), kind=kLoop, calls=%fused_computation.20 | loop fusion | flops 23068416 | bytes 25199616 | tf_op jit(solution)/shard_map/reduce_sum | solution.py:337
  241.3 9.5 %shard_map.128 = bf16[256,8192]{1,0:T(8,128)(2,1)} custom-call(f32[8192,256]{1,0:T(8,128)} %bitcast.77, f32[1,256]{1,0:T(1,128)} %bitcast.88, f32[8192,1]{1,0:T(8,128)} %copy.36.n_ref), custom_call_target="tpu_custom_call" | custom-call | flops 4194304 | bytes 12582912 | tf_op jit(solution)/shard_map/pallas_call | solution.py:91
  (76 shorter events, 7.9 us)
Async XLA Ops:
  1.3 11.1 %collective-permute-start.5 = (s32[1]{0:T(128)}, s32[1]{0:T(128)}, u32[]{:S(2)}, u32[]{:S(2)}) collective-permute-start(s32[1]{0:T(128)} %slice.98), channel_id=1, source_target_pairs={{0,1},{1,0},{2,3},{3,2},{4,5},{5,4},{6,7},{7,6},{8,9},{9,8},{10,11... | collective-permute-start | bytes 20 | tf_op jit(solution)/shard_map/ppermute | solution.py:172
  4.5 11.7 %collective-permute-start.3 = (bf16[3,8449]{1,0:T(4,128)(2,1)S(1)}, bf16[3,8449]{1,0:T(4,128)(2,1)S(1)}, u32[]{:S(2)}, u32[]{:S(2)}) collective-permute-start(bf16[3,8449]{1,0:T(4,128)(2,1)S(1)} %pad_maximum_fusion.1), channel_id=1, source_target_pairs={{0,1},{1,2},{2,3},{3,4},{4,5},{5,6},{6,7},{7,8},{8,9},{9,10},{10,1... | collective-permute-start | bytes 152090 | tf_op jit(solution)/shard_map/ppermute | solution.py:23
  13.7 2.4 collective-permute-start.6
  16.2 21.0 %collective-permute-start.7 = (s32[4]{0:T(128)S(1)}, s32[4]{0:T(128)S(1)}, u32[]{:S(2)}, u32[]{:S(2)}) collective-permute-start(s32[4]{0:T(128)S(1)} %broadcast_select_fusion.2), channel_id=1, source_target_pairs={{0,4},{1,5},{2,6},{3,7},{4,0},{5,1},{6,2},{7,3},{8,12},{9,13},{10,... | collective-permute-start | bytes 56 | tf_op jit(solution)/shard_map/ppermute | solution.py:172
  37.3 2.4 collective-permute-start.8
  39.8 10.7 %collective-permute-start.9 = (s32[16]{0:T(128)S(1)}, s32[16]{0:T(128)S(1)}, u32[]{:S(2)}, u32[]{:S(2)}) collective-permute-start(s32[16]{0:T(128)S(1)} %broadcast_select_fusion.4), channel_id=1, source_target_pairs={{0,16},{1,17},{2,18},{3,19},{4,20},{5,21},{6,22},{7,23},{8,24},{9,... | collective-permute-start | bytes 200 | tf_op jit(solution)/shard_map/ppermute | solution.py:172
  50.9 2.0 copy-start
  54.3 6.3 %collective-permute-start.10 = (f32[64,64,128]{2,1,0:T(8,128)}, f32[64,64,128]{2,1,0:T(8,128)S(1)}, u32[]{:S(2)}, u32[]{:S(2)}) collective-permute-start(f32[64,64,128]{2,1,0:T(8,128)} %constant_dynamic-slice_fusion), channel_id=1, source_target_pairs={{0,1},{1,0},{2,3},{3,2},{4,5},{5,4},{6,7},{7,6},{8,9},{9,8},{10,11... | collective-permute-start | bytes 6291464 | tf_op jit(solution)/shard_map/ppermute | solution.py:221
  56.6 3.6 %collective-permute-start.4 = (f32[128]{0:T(128)S(1)}, f32[128]{0:T(128)S(1)}, u32[]{:S(2)}, u32[]{:S(2)}) collective-permute-start(f32[128]{0:T(128)S(1)} %get-tuple-element.78), channel_id=1, source_target_pairs={{0,1},{1,0},{2,3},{3,2},{4,5},{5,4},{6,7},{7,6},{8,9},{9,8},{10,11... | collective-permute-start | bytes 1544 | tf_op jit(solution)/shard_map/ppermute | solution.py:221
  60.6 104.5 %copy-start.2 = (f32[64,64,128]{2,1,0:T(8,128)}, f32[64,64,128]{2,1,0:T(8,128)S(1)}, u32[]{:S(2)}) copy-start(f32[64,64,128]{2,1,0:T(8,128)S(1)} %collective-permute-done.10) | copy-start | bytes 6291460
  63.4 50.5 %collective-permute-start.13 = (f32[64,64,128]{2,1,0:T(8,128)S(1)}, f32[64,64,128]{2,1,0:T(8,128)S(1)}, u32[]{:S(2)}, u32[]{:S(2)}) collective-permute-start(f32[64,64,128]{2,1,0:T(8,128)S(1)} %add_select_fusion), channel_id=1, source_target_pairs={{0,2},{1,3},{2,4},{3,5},{4,6},{5,7},{6,8},{7,9},{8,10},{9,11},{10,... | collective-permute-start | bytes 6291464 | tf_op jit(solution)/shard_map/ppermute | solution.py:134
  113.9 49.6 %collective-permute-start.14 = (f32[64,64,128]{2,1,0:T(8,128)S(1)}, f32[64,64,128]{2,1,0:T(8,128)S(1)}, u32[]{:S(2)}, u32[]{:S(2)}) collective-permute-start(f32[64,64,128]{2,1,0:T(8,128)S(1)} %collective-permute-done.13), channel_id=1, source_target_pairs={{0,2},{1,3},{2,4},{3,5},{4,6},{5,7},{6,8},{7,9},{8,10},{9,11},{10,... | collective-permute-start | bytes 6291464 | tf_op jit(solution)/shard_map/ppermute | solution.py:134
  115.8 47.7 %collective-permute-start.11 = (f32[64]{0:T(128)S(1)}, f32[64]{0:T(128)S(1)}, u32[]{:S(2)}, u32[]{:S(2)}) collective-permute-start(f32[64]{0:T(128)S(1)} %mul.278), channel_id=1, source_target_pairs={{0,2},{1,3},{2,4},{3,5},{4,6},{5,7},{6,8},{7,9},{8,10},{9,11},{10,... | collective-permute-start | bytes 776 | tf_op jit(solution)/shard_map/ppermute | solution.py:134
  165.1 8.4 %copy-start.8 = (f32[128]{0:T(128)S(1)}, f32[128]{0:T(128)}, u32[]{:S(2)}) copy-start(f32[128]{0:T(128)} %param.21) | copy-start | bytes 1540
  165.1 8.6 %copy-start.6 = (bf16[8192]{0:T(1024)(128)(2,1)S(1)}, bf16[8192]{0:T(1024)(128)(2,1)}, u32[]{:S(2)}) copy-start(bf16[8192]{0:T(1024)(128)(2,1)} %param.26) | copy-start | bytes 49156
  165.1 48.2 %collective-permute-start.15 = (f32[64,64,128]{2,1,0:T(8,128)}, f32[64,64,128]{2,1,0:T(8,128)}, u32[]{:S(2)}, u32[]{:S(2)}) collective-permute-start(f32[64,64,128]{2,1,0:T(8,128)} %multiply_add_fusion.3), channel_id=1, source_target_pairs={{0,4},{1,5},{2,6},{3,7},{4,8},{5,9},{6,10},{7,11},{8,12},{9,13},{1... | collective-permute-start | bytes 6291464 | tf_op jit(solution)/shard_map/ppermute | solution.py:134
  173.5 4.8 %copy-start.7 = (s32[256]{0:T(256)S(1)}, s32[256]{0:T(256)}, u32[]{:S(2)}) copy-start(s32[256]{0:T(256)} %param.27) | copy-start | bytes 3076
  178.6 32.7 %collective-permute-start.12 = (f32[64]{0:T(128)S(1)}, f32[64]{0:T(128)S(1)}, u32[]{:S(2)}, u32[]{:S(2)}) collective-permute-start(f32[64]{0:T(128)S(1)} %collective-permute-done.11), channel_id=1, source_target_pairs={{0,2},{1,3},{2,4},{3,5},{4,6},{5,7},{6,8},{7,9},{8,10},{9,11},{10,... | collective-permute-start | bytes 776 | tf_op jit(solution)/shard_map/ppermute | solution.py:134
  211.3 5.2 %collective-permute-start.16 = (f32[64]{0:T(128)S(1)}, f32[64]{0:T(128)S(1)}, u32[]{:S(2)}, u32[]{:S(2)}) collective-permute-start(f32[64]{0:T(128)S(1)} %mul.319), channel_id=1, source_target_pairs={{0,4},{1,5},{2,6},{3,7},{4,8},{5,9},{6,10},{7,11},{8,12},{9,13},{1... | collective-permute-start | bytes 776 | tf_op jit(solution)/shard_map/ppermute | solution.py:134
  216.5 6.5 %copy-start.4 = (bf16[8192,256]{1,0:T(8,128)(2,1)S(1)}, bf16[8192,256]{1,0:T(8,128)(2,1)}, u32[]{:S(2)}) copy-start(bf16[8192,256]{1,0:T(8,128)(2,1)} %shard_map.127) | copy-start | bytes 12582916
  219.3 12.6 %copy-start.1 = (f32[128,64,128]{2,1,0:T(8,128)S(1)}, f32[128,64,128]{2,1,0:T(8,128)}, u32[]{:S(2)}) copy-start(f32[128,64,128]{2,1,0:T(8,128)} %copy-done) | copy-start | bytes 12582916
  219.3 12.6 %copy-start.3 = (f32[64,64,128]{2,1,0:T(8,128)S(1)}, f32[64,64,128]{2,1,0:T(8,128)}, u32[]{:S(2)}) copy-start(f32[64,64,128]{2,1,0:T(8,128)} %copy-done.2) | copy-start | bytes 6291460
  219.3 12.6 %collective-permute-start.17 = (bf16[64,64,128]{2,1,0:T(8,128)(2,1)S(1)}, bf16[64,64,128]{2,1,0:T(8,128)(2,1)S(1)}, u32[]{:S(2)}, u32[]{:S(2)}) collective-permute-start(bf16[64,64,128]{2,1,0:T(8,128)(2,1)S(1)} %fusion.19), channel_id=1, source_target_pairs={{0,1},{1,0},{2,3},{3,2},{4,5},{5,4},{6,7},{7,6},{8,9},{9,8},{10,11... | collective-permute-start | bytes 3145736 | tf_op jit(solution)/shard_map/ppermute | solution.py:232
  232.8 2.2 copy-start.5

commit v10 on v9

--- a/solution.py
+++ b/solution.py
@@ -140,10 +140,10 @@
 
 
 def scan_rounds(carry, axis, stride, span, count, far):
-    near, needed, rider = far
+    near, needed, rider, work = far
     carry, rider = lax.optimization_barrier((carry, rider))
-    far[2] = rider
     transmit, state = shifted(carry, axis, stride, count)
+    (transmit, state), far[2] = lax.optimization_barrier(((transmit, state), work(rider)))
     covered = 1
     while covered < min(span - 1, near):
         transmit, state = scan_round(transmit, state, axis, stride * covered, count)
@@ -321,9 +321,9 @@
     intra_items = (x_blocks, b_blocks, c_blocks, step_blocks, cum_decay, seg_blocks)
     ids = gather_rounds(ids, "ctx", 4, lax.axis_size("ctx").bit_length())
     ids, block_states = lax.optimization_barrier((ids, block_states))
-    far = [*long_runs(ids, paired, tok_rows), intra_items]
+    far = [*long_runs(ids, paired, tok_rows), intra_items, functools.partial(blockwise, intra_of)]
     entering = chain_states(block_states, transmits, paired, far)
-    y_intra = blockwise(intra_of, far[2])
+    y_intra = far[2]
 
     def enter_of(item):
         c_group, decay_here, segment, before, entering_here = item

time: 252 us -> 275 us (1.091)
  other arithmetic: 28.3 us -> 48.3 us
  matrix products: 18.6 us -> 25.4 us
    add x0 -> x1, other arithmetic: none -> 12.1 us  [local(): y_blocks = y_intra + y_state]
    reduce_sum x1, other arithmetic: 5.72 us -> 10.6 us  [local(): local_sq = jnp.sum(gated * gated, axis=1)]
    dot_general x1, matrix products: 8.86 us -> 12.4 us  [mixing_part(): jnp.einsum('hij,jhp->ihp', mixing, x_group, preferred_element_type=jnp.fl...]
    dot_general x1, matrix products: 1.26 us -> 4.48 us  [entry_part(): jnp.einsum('in,hpn->ihp', c_group, packed, preferred_element_type=jnp.flo...]
    unnamed x20 -> x18, local copies, waits for them, and re-layouts: 10.3 us -> 9.34 us
where the time goes in v10:
time: 275 us; the launch traced here: 274 us
  waiting for transfers between devices  129 us (47%)
  other arithmetic  48.3 us (18%)
  starting transfers between devices  27.5 us (10%)
  matrix products  25.4 us (9%)
  local copies, waits for them, and re-layouts  21.5 us (8%)
  Pallas kernels  20.3 us (7%)
    ppermute x6, waiting for transfers between devices, shifted(): lax.ppermute(value, axis, [(s, s + steps) for s in range(count - steps)])  121 us
    ppermute x6, starting transfers between devices, shifted(): lax.ppermute(value, axis, [(s, s + steps) for s in range(count - steps)])  12.9 us
    dot_general x1, matrix products, mixing_part(): jnp.einsum('hij,jhp->ihp', mixing, x_group, preferred_element_type=jnp.fl...  12.4 us
    add x1, other arithmetic, local(): y_blocks = y_intra + y_state  12.1 us
    pallas_call x1, Pallas kernels, conv_rows(): pl.pallas_call(conv_rows_kernel, out_shape=jax.ShapeDtypeStruct((width, r...  10.8 us
    reduce_sum x1, other arithmetic, local(): local_sq = jnp.sum(gated * gated, axis=1)  10.6 us
    pallas_call x1, Pallas kernels, scale_rows(): pl.pallas_call(scale_rows_kernel, out_shape=jax.ShapeDtypeStruct((rows, w...  9.48 us
    unnamed x18, local copies, waits for them, and re-layouts  9.34 us
  transfers between devices with their start and end apart: 15, of which 8 were waited for; matrix products, arithmetic and copies ran while one was open for 19% of the time, Pallas kernels for 4%

profile of v10, /device:TPU:9, one launch (start us, length us, event | category | flops | bytes accessed | tf_op | source)
XLA Modules:
  0.0 273.9 jit_solution(11207050085885645983)
XLA Ops:
  0.0 1.3 slice.98
  2.6 0.9 slice.99
  4.5 3.0 %collective-permute-start.3 = (bf16[3,8449]{1,0:T(4,128)(2,1)S(1)}, bf16[3,8449]{1,0:T(4,128)(2,1)S(1)}, u32[]{:S(2)}, u32[]{:S(2)}) collective-permute-start(bf16[3,8449]{1,0:T(4,128)(2,1)S(1)} %pad_maximum_fusion.1), channel_id=1, source_target_pairs={{0,1},{1,2},{2,3},{3,4},{4,5},{5,6},{6,7},{7,8},{8,9},{9,10},{10,1... | collective-permute-start | bytes 152090 | tf_op jit(solution)/shard_map/ppermute | solution.py:23
  7.5 1.0 copy.21
  8.5 0.8 negate_multiply_fusion
  9.4 1.3 reshape.208.b_ref
  10.8 0.8 slice_convert_fusion.5
  12.3 1.3 broadcast_select_fusion.1
  13.6 1.2 collective-permute-start.6
  14.8 1.2 collective-permute-done.6
  16.1 1.3 collective-permute-start.7
  18.1 0.8 pad_add_fusion
  20.0 2.0 compare_convert_fusion.4
  22.0 0.9 copy.25.vis_ref
  23.0 1.5 multiply_convert_fusion.8
  24.6 0.8 fusion.39
  26.2 10.8 %shard_map.127 = bf16[8192,256]{1,0:T(8,128)(2,1)} custom-call(bf16[8,8192]{1,0:T(8,128)(2,1)} %concatenate.76.rim_ref, bf16[256,8192]{1,0:T(8,128)(2,1)} %x_ref.1, bf16[4,8192]{1,0:T(4,128)(2,1)} %w_ref.1, bf16[1,8192]{1,0:T(2,128)(2,1)} %reshape.208.b_ref, f32[3,256,1]{2,1,0:T(8,128)} %copy.25.vis_ref), custom_call_target="tpu_custom_call" | custom-call | flops 41943040 | bytes 8388608 | tf_op jit(solution)/shard_map/pallas_call | solution.py:66
  37.2 2.2 collective-permute-done.8
  39.5 2.3 collective-permute-start.9
  41.8 8.3 %fusion.18 = f32[1,128,64,128]{3,2,1,0:T(8,128)S(1)} fusion(bf16[256,128,64]{0,2,1:T(8,128)(2,1)} %bitcast.84, f32[128,256]{1,0:T(8,128)S(1)} %copy.26, f32[256,128]{1,0:T(8,128)S(1)} %get-tuple-element.89), kind=kOutput, calls=%fused_computation.26 | convolution fusion | flops 545259520 | bytes 8650752 | tf_op jit(solution)/shard_map/hjn,jhp->hpn/dot_general | solution.py:121
  50.6 2.0 copy-done
  52.6 1.5 constant_dynamic-slice_fusion
  54.1 2.3 collective-permute-start.10
  56.4 3.6 %collective-permute-done.4 = f32[128]{0:T(128)S(1)} collective-permute-done((f32[128]{0:T(128)S(1)}, f32[128]{0:T(128)S(1)}, u32[]{:S(2)}, u32[]{:S(2)}) %collective-permute-start.4) | collective-permute-done | bytes 544 | tf_op jit(solution)/shard_map/ppermute | solution.py:221
  60.3 4.1 %add_select_fusion = f32[64,64,128]{2,1,0:T(8,128)} fusion(f32[64,64,128]{2,1,0:T(8,128)S(1)} %collective-permute-done.10, f32[128,64,128]{2,1,0:T(8,128)} %copy-done, s32[]{:T(128)S(6)} %select_n.101, f32[64]{0:T(128)S(1)} %get-tuple-element.82, f32[64]{0:T(128)S(1)} %get-tuple-element.81, pred[]{:T(512)S(6)} %eq.73), kind=kLoop, calls=%fused_computation.36 | loop fusion | flops 2621440 | bytes 6291973 | tf_op jit(solution)/shard_map/jit(_where)/select_n | solution.py:226
  64.8 3.1 %collective-permute-start.12 = (f32[64,64,128]{2,1,0:T(8,128)}, f32[64,64,128]{2,1,0:T(8,128)S(1)}, u32[]{:S(2)}, u32[]{:S(2)}) collective-permute-start(f32[64,64,128]{2,1,0:T(8,128)} %add_select_fusion), channel_id=1, source_target_pairs={{0,2},{1,3},{2,4},{3,5},{4,6},{5,7},{6,8},{7,9},{8,10},{9,11},{10,... | collective-permute-start | bytes 6291464 | tf_op jit(solution)/shard_map/ppermute | solution.py:134
  67.9 2.1 collective-permute-start.11
  70.2 12.4 %fusion.15 = f32[1,256,128,64]{1,3,2,0:T(8,128)} fusion(f32[128,256]{1,0:T(8,128)S(1)} %copy.30, f32[128,256]{1,0:T(8,128)S(1)} %copy.28, f32[256,256]{1,0:T(8,128)S(1)} %fusion.31, pred[256,256]{1,0:T(8,128)(4,1)S(1)} %fusion.25, bf16[1,256,128,64]{1,3,2,0:T(8,128)(2,1)} %bitcast.85), kind=kOutput, calls=%fused_computation.25 | convolution fusion | flops 1115684864 | bytes 13172736 | tf_op jit(solution)/shard_map/hij,jhp->ihp/dot_general | solution.py:113
  82.6 32.9 %collective-permute-done.11 = f32[64]{0:T(128)S(1)} collective-permute-done((f32[64]{0:T(128)S(1)}, f32[64]{0:T(128)S(1)}, u32[]{:S(2)}, u32[]{:S(2)}) %collective-permute-start.11) | collective-permute-done | bytes 288 | tf_op jit(solution)/shard_map/ppermute | solution.py:134
  115.5 1.9 collective-permute-start.14
  117.4 47.6 %collective-permute-done.14 = f32[64,64,128]{2,1,0:T(8,128)S(1)} collective-permute-done((f32[64,64,128]{2,1,0:T(8,128)S(1)}, f32[64,64,128]{2,1,0:T(8,128)S(1)}, u32[]{:S(2)}, u32[]{:S(2)}) %collective-permute-start.14) | collective-permute-done | bytes 2097184 | tf_op jit(solution)/shard_map/ppermute | solution.py:134
  165.3 1.9 collective-permute-start.15
  167.8 1.9 collective-permute-start.13
  169.7 0.8 compare_reduce_fusion
  171.2 40.1 %collective-permute-done.13 = f32[64]{0:T(128)S(1)} collective-permute-done((f32[64]{0:T(128)S(1)}, f32[64]{0:T(128)S(1)}, u32[]{:S(2)}, u32[]{:S(2)}) %collective-permute-start.13) | collective-permute-done | bytes 288 | tf_op jit(solution)/shard_map/ppermute | solution.py:134
  211.2 1.9 collective-permute-start.16
  213.2 2.5 multiply_add_fusion.2
  215.7 0.7 collective-permute-done.16
  216.4 3.6 %fusion.23 = bf16[64,64,128]{2,1,0:T(8,128)(2,1)} fusion(f32[64,64,128]{2,1,0:T(8,128)S(1)} %get-tuple-element.99, f32[64,64,128]{2,1,0:T(8,128)} %copy-done.1, f32[128,64,128]{2,1,0:T(8,128)} %copy-done, s32[]{:T(128)S(6)} %select_n.101, f32[64]{0:T(128)S(1)} %get-tuple-element.80, pred[]{:T(512)S(6)} %eq.73), kind=kLoop, calls=%fused_computation.37 | loop fusion | flops 2097152 | bytes 7340293 | tf_op jit(solution)/shard_map/jit(_where)/select_n | solution.py:232
  220.1 3.6 %collective-permute-start.17 = (bf16[64,64,128]{2,1,0:T(8,128)(2,1)}, bf16[64,64,128]{2,1,0:T(8,128)(2,1)S(1)}, u32[]{:S(2)}, u32[]{:S(2)}) collective-permute-start(bf16[64,64,128]{2,1,0:T(8,128)(2,1)} %fusion.23), channel_id=1, source_target_pairs={{0,1},{1,0},{2,3},{3,2},{4,5},{5,4},{6,7},{7,6},{8,9},{9,8},{10,11... | collective-permute-start | bytes 3145736 | tf_op jit(solution)/shard_map/ppermute | solution.py:232
  223.7 6.4 %copy.35 = bf16[256,8192]{0,1:T(8,128)(2,1)} copy(bf16[256,8192]{1,0:T(8,128)(2,1)} %param.16) | data formatting | bytes 8388608 | tf_op args[1]
  230.1 0.7 mul.331
  230.8 2.7 copy.36.n_ref
  233.6 2.8 %select_convert_fusion.1 = (bf16[64,64,128]{2,1,0:T(8,128)(2,1)S(1)}, bf16[64,64,128]{2,1,0:T(8,128)(2,1)S(1)}) fusion(bf16[64,64,128]{2,1,0:T(8,128)(2,1)S(1)} %collective-permute-done.17, pred[]{:T(512)S(6)} %eq.73, f32[64,64,128]{2,1,0:T(8,128)S(1)} %get-tuple-element.99, f32[64,64,128]{2,1,0:T(8,128)} %copy-done.1, f32[128,64,128]{2,1,0:T(8,128)} %copy-done, ...), kind=kLoop, calls=%fused_computation.32 | loop fusion | flops 2621440 | bytes 9437445 | tf_op jit(solution)/shard_map/convert.8
  236.6 4.5 %fusion.19 = f32[256,128,64]{0,2,1:T(8,128)} fusion(bf16[64,64,128]{2,1,0:T(8,128)(2,1)S(1)} %select_convert_fusion, bf16[64,64,128]{2,1,0:T(8,128)(2,1)S(1)} %get-tuple-element.78, bf16[256,256]{1,0:T(8,128)(2,1)S(1)} %multiply_convert_fusion.8), kind=kOutput, calls=%fused_computation.27 | convolution fusion | flops 541065216 | bytes 10551296 | tf_op jit(solution)/shard_map/in,hpn->ihp/dot_general | solution.py:129
  241.0 12.1 %bitcast_add_fusion.1 = f32[1,256,128,64]{1,3,2,0:T(8,128)} fusion(f32[1,256,128,64]{1,3,2,0:T(8,128)} %fusion.15, f32[256,128,64]{0,2,1:T(8,128)} %fusion.19, f32[256,128]{0,1:T(8,128)S(1)} %copy.33), kind=kLoop, calls=%fused_computation.19 | loop fusion | flops 4194304 | bytes 25296896 | tf_op jit(solution)/shard_map/add | solution.py:333
  253.2 10.6 %multiply_reduce_fusion = (f32[256]{0:T(256)S(1)}, f32[256,8192]{0,1:T(8,128)}) fusion(bf16[256,8192]{0,1:T(8,128)(2,1)} %copy.35, bf16[256,8192]{0,1:T(8,128)(2,1)S(1)} %bitcast.86, f32[8192]{0:T(1024)S(1)} %copy-done.4, f32[1,256,128,64]{1,3,2,0:T(8,128)} %bitcast_add_fusion.1), kind=kLoop, calls=%fused_computation.20 | loop fusion | flops 23068416 | bytes 25199616 | tf_op jit(solution)/shard_map/reduce_sum | solution.py:337
  264.4 9.5 %shard_map.128 = bf16[256,8192]{1,0:T(8,128)(2,1)} custom-call(f32[8192,256]{1,0:T(8,128)} %bitcast.83, f32[1,256]{1,0:T(1,128)} %bitcast.94, f32[8192,1]{1,0:T(8,128)} %copy.36.n_ref), custom_call_target="tpu_custom_call" | custom-call | flops 4194304 | bytes 12582912 | tf_op jit(solution)/shard_map/pallas_call | solution.py:91
  (75 shorter events, 8.1 us)
Async XLA Ops:
  1.3 11.1 %collective-permute-start.5 = (s32[1]{0:T(128)}, s32[1]{0:T(128)}, u32[]{:S(2)}, u32[]{:S(2)}) collective-permute-start(s32[1]{0:T(128)} %slice.98), channel_id=1, source_target_pairs={{0,1},{1,0},{2,3},{3,2},{4,5},{5,4},{6,7},{7,6},{8,9},{9,8},{10,11... | collective-permute-start | bytes 20 | tf_op jit(solution)/shard_map/ppermute | solution.py:172
  4.5 11.6 %collective-permute-start.3 = (bf16[3,8449]{1,0:T(4,128)(2,1)S(1)}, bf16[3,8449]{1,0:T(4,128)(2,1)S(1)}, u32[]{:S(2)}, u32[]{:S(2)}) collective-permute-start(bf16[3,8449]{1,0:T(4,128)(2,1)S(1)} %pad_maximum_fusion.1), channel_id=1, source_target_pairs={{0,1},{1,2},{2,3},{3,4},{4,5},{5,6},{6,7},{7,8},{8,9},{9,10},{10,1... | collective-permute-start | bytes 152090 | tf_op jit(solution)/shard_map/ppermute | solution.py:23
  13.6 2.4 collective-permute-start.6
  16.1 20.9 %collective-permute-start.7 = (s32[4]{0:T(128)S(1)}, s32[4]{0:T(128)S(1)}, u32[]{:S(2)}, u32[]{:S(2)}) collective-permute-start(s32[4]{0:T(128)S(1)} %broadcast_select_fusion.2), channel_id=1, source_target_pairs={{0,4},{1,5},{2,6},{3,7},{4,0},{5,1},{6,2},{7,3},{8,12},{9,13},{10,... | collective-permute-start | bytes 56 | tf_op jit(solution)/shard_map/ppermute | solution.py:172
  37.1 2.4 collective-permute-start.8
  39.5 10.7 %collective-permute-start.9 = (s32[16]{0:T(128)S(1)}, s32[16]{0:T(128)S(1)}, u32[]{:S(2)}, u32[]{:S(2)}) collective-permute-start(s32[16]{0:T(128)S(1)} %broadcast_select_fusion.4), channel_id=1, source_target_pairs={{0,16},{1,17},{2,18},{3,19},{4,20},{5,21},{6,22},{7,23},{8,24},{9,... | collective-permute-start | bytes 200 | tf_op jit(solution)/shard_map/ppermute | solution.py:172
  50.6 2.0 copy-start
  54.1 10.6 %copy-start.6 = (s32[256]{0:T(256)S(1)}, s32[256]{0:T(256)}, u32[]{:S(2)}) copy-start(s32[256]{0:T(256)} %param.27) | copy-start | bytes 3076
  54.1 6.3 %collective-permute-start.10 = (f32[64,64,128]{2,1,0:T(8,128)}, f32[64,64,128]{2,1,0:T(8,128)S(1)}, u32[]{:S(2)}, u32[]{:S(2)}) collective-permute-start(f32[64,64,128]{2,1,0:T(8,128)} %constant_dynamic-slice_fusion), channel_id=1, source_target_pairs={{0,1},{1,0},{2,3},{3,2},{4,5},{5,4},{6,7},{7,6},{8,9},{9,8},{10,11... | collective-permute-start | bytes 6291464 | tf_op jit(solution)/shard_map/ppermute | solution.py:221
  56.3 3.6 %collective-permute-start.4 = (f32[128]{0:T(128)S(1)}, f32[128]{0:T(128)S(1)}, u32[]{:S(2)}, u32[]{:S(2)}) collective-permute-start(f32[128]{0:T(128)S(1)} %get-tuple-element.84), channel_id=1, source_target_pairs={{0,1},{1,0},{2,3},{3,2},{4,5},{5,4},{6,7},{7,6},{8,9},{9,8},{10,11... | collective-permute-start | bytes 1544 | tf_op jit(solution)/shard_map/ppermute | solution.py:221
  60.3 22.3 %copy-start.1 = (f32[64,64,128]{2,1,0:T(8,128)}, f32[64,64,128]{2,1,0:T(8,128)S(1)}, u32[]{:S(2)}) copy-start(f32[64,64,128]{2,1,0:T(8,128)S(1)} %collective-permute-done.10) | copy-start | bytes 6291460
  64.8 50.7 %collective-permute-start.12 = (f32[64,64,128]{2,1,0:T(8,128)}, f32[64,64,128]{2,1,0:T(8,128)S(1)}, u32[]{:S(2)}, u32[]{:S(2)}) collective-permute-start(f32[64,64,128]{2,1,0:T(8,128)} %add_select_fusion), channel_id=1, source_target_pairs={{0,2},{1,3},{2,4},{3,5},{4,6},{5,7},{6,8},{7,9},{8,10},{9,11},{10,... | collective-permute-start | bytes 6291464 | tf_op jit(solution)/shard_map/ppermute | solution.py:134
  67.9 47.6 %collective-permute-start.11 = (f32[64]{0:T(128)S(1)}, f32[64]{0:T(128)S(1)}, u32[]{:S(2)}, u32[]{:S(2)}) collective-permute-start(f32[64]{0:T(128)S(1)} %mul.278), channel_id=1, source_target_pairs={{0,2},{1,3},{2,4},{3,5},{4,6},{5,7},{6,8},{7,9},{8,10},{9,11},{10,... | collective-permute-start | bytes 776 | tf_op jit(solution)/shard_map/ppermute | solution.py:134
  115.5 49.5 %collective-permute-start.14 = (f32[64,64,128]{2,1,0:T(8,128)S(1)}, f32[64,64,128]{2,1,0:T(8,128)S(1)}, u32[]{:S(2)}, u32[]{:S(2)}) collective-permute-start(f32[64,64,128]{2,1,0:T(8,128)S(1)} %collective-permute-done.12), channel_id=1, source_target_pairs={{0,2},{1,3},{2,4},{3,5},{4,6},{5,7},{6,8},{7,9},{8,10},{9,11},{10,... | collective-permute-start | bytes 6291464 | tf_op jit(solution)/shard_map/ppermute | solution.py:134
  165.3 47.9 %copy-start.3 = (f32[64,64,128]{2,1,0:T(8,128)}, f32[64,64,128]{2,1,0:T(8,128)S(1)}, u32[]{:S(2)}) copy-start(f32[64,64,128]{2,1,0:T(8,128)S(1)} %multiply_add_fusion.3) | copy-start | bytes 6291460
  165.3 47.9 %collective-permute-start.15 = (f32[64,64,128]{2,1,0:T(8,128)S(1)}, f32[64,64,128]{2,1,0:T(8,128)}, u32[]{:S(2)}, u32[]{:S(2)}) collective-permute-start(f32[64,64,128]{2,1,0:T(8,128)S(1)} %multiply_add_fusion.3), channel_id=1, source_target_pairs={{0,4},{1,5},{2,6},{3,7},{4,8},{5,9},{6,10},{7,11},{8,12},{9,13},{1... | collective-permute-start | bytes 6291464 | tf_op jit(solution)/shard_map/ppermute | solution.py:134
  167.8 43.5 %collective-permute-start.13 = (f32[64]{0:T(128)S(1)}, f32[64]{0:T(128)S(1)}, u32[]{:S(2)}, u32[]{:S(2)}) collective-permute-start(f32[64]{0:T(128)S(1)} %collective-permute-done.11), channel_id=1, source_target_pairs={{0,2},{1,3},{2,4},{3,5},{4,6},{5,7},{6,8},{7,9},{8,10},{9,11},{10,... | collective-permute-start | bytes 776 | tf_op jit(solution)/shard_map/ppermute | solution.py:134
  211.2 5.2 %collective-permute-start.16 = (f32[64]{0:T(128)S(1)}, f32[64]{0:T(128)S(1)}, u32[]{:S(2)}, u32[]{:S(2)}) collective-permute-start(f32[64]{0:T(128)S(1)} %mul.319), channel_id=1, source_target_pairs={{0,4},{1,5},{2,6},{3,7},{4,8},{5,9},{6,10},{7,11},{8,12},{9,13},{1... | collective-permute-start | bytes 776 | tf_op jit(solution)/shard_map/ppermute | solution.py:134
  220.0 10.0 %copy-start.7 = (f32[128]{0:T(128)S(1)}, f32[128]{0:T(128)}, u32[]{:S(2)}) copy-start(f32[128]{0:T(128)} %param.21) | copy-start | bytes 1540
  220.1 10.8 %copy-start.5 = (bf16[8192]{0:T(1024)(128)(2,1)S(1)}, bf16[8192]{0:T(1024)(128)(2,1)}, u32[]{:S(2)}) copy-start(bf16[8192]{0:T(1024)(128)(2,1)} %param.26) | copy-start | bytes 49156
  220.1 13.5 %collective-permute-start.17 = (bf16[64,64,128]{2,1,0:T(8,128)(2,1)}, bf16[64,64,128]{2,1,0:T(8,128)(2,1)S(1)}, u32[]{:S(2)}, u32[]{:S(2)}) collective-permute-start(bf16[64,64,128]{2,1,0:T(8,128)(2,1)} %fusion.23), channel_id=1, source_target_pairs={{0,1},{1,0},{2,3},{3,2},{4,5},{5,4},{6,7},{7,6},{8,9},{9,8},{10,11... | collective-permute-start | bytes 3145736 | tf_op jit(solution)/shard_map/ppermute | solution.py:232
  241.0 12.2 %copy-start.2 = (bf16[8192,256]{1,0:T(8,128)(2,1)S(1)}, bf16[8192,256]{1,0:T(8,128)(2,1)}, u32[]{:S(2)}) copy-start(bf16[8192,256]{1,0:T(8,128)(2,1)} %shard_map.127) | copy-start | bytes 12582916
  241.0 12.2 %copy-start.4 = (f32[8192]{0:T(1024)S(1)}, f32[8192]{0:T(1024)}, u32[]{:S(2)}) copy-start(f32[8192]{0:T(1024)} %mul.331) | copy-start | bytes 98308

commit v11 on v9

--- a/solution.py
+++ b/solution.py
@@ -134,8 +134,18 @@
     return lax.ppermute(value, axis, [(s, s + steps) for s in range(count - steps)])
 
 
+def shifted_pair(pair, axis, shift, count):
+    transmit, state = pair
+    heads = state.shape[0]
+    packed = jnp.concatenate(
+        [state.reshape(heads, -1), jnp.broadcast_to(transmit[:, None], (heads, 128))], axis=1
+    )
+    moved = shifted(packed, axis, shift, count)
+    return moved[:, -1], moved[:, :-128].reshape(state.shape)
+
+
 def scan_round(transmit, state, axis, shift, count):
-    far_t, far_s = shifted((transmit, state), axis, shift, count)
+    far_t, far_s = shifted_pair((transmit, state), axis, shift, count)
     return transmit * far_t, transmit[:, None, None] * far_s + state
 
 
@@ -143,7 +153,7 @@
     near, needed, rider = far
     carry, rider = lax.optimization_barrier((carry, rider))
     far[2] = rider
-    transmit, state = shifted(carry, axis, stride, count)
+    transmit, state = shifted_pair(carry, axis, stride, count)
     covered = 1
     while covered < min(span - 1, near):
         transmit, state = scan_round(transmit, state, axis, stride * covered, count)

time: 252 us -> 255 us (1.012)
  starting transfers between devices: 28 us -> 20.5 us
  local copies, waits for them, and re-layouts: 21.9 us -> 27.8 us
  waiting for transfers between devices: 131 us -> 136 us
    ppermute x6 -> x3, starting transfers between devices: 13.3 us -> 7.08 us  [shifted(): lax.ppermute(value, axis, [(s, s + steps) for s in range(count - steps)])]
    unnamed x20 -> x33, local copies, waits for them, and re-layouts: 10.3 us -> 15.7 us
    ppermute x6 -> x3, waiting for transfers between devices: 124 us -> 129 us  [shifted(): lax.ppermute(value, axis, [(s, s + steps) for s in range(count - steps)])]
  transfers between devices with their start and end apart: 15 -> 12, of which waited for: 8 -> 7; matrix products, arithmetic and copies ran while one was open for 19% -> 18% of each run, Pallas kernels for 4% -> 4%
where the time goes in v11:
time: 255 us; the launch traced here: 254 us
  waiting for transfers between devices  136 us (53%)
  local copies, waits for them, and re-layouts  27.8 us (11%)
  other arithmetic  27.4 us (11%)
  starting transfers between devices  20.5 us (8%)
  Pallas kernels  20.3 us (8%)
  matrix products  18.6 us (7%)
    ppermute x3, waiting for transfers between devices, shifted(): lax.ppermute(value, axis, [(s, s + steps) for s in range(count - steps)])  129 us
    unnamed x33, local copies, waits for them, and re-layouts  15.7 us
    pallas_call x1, Pallas kernels, conv_rows(): pl.pallas_call(conv_rows_kernel, out_shape=jax.ShapeDtypeStruct((width, r...  10.9 us
    pallas_call x1, Pallas kernels, scale_rows(): pl.pallas_call(scale_rows_kernel, out_shape=jax.ShapeDtypeStruct((rows, w...  9.48 us
    dot_general x1, matrix products, mixing_part(): jnp.einsum('hij,jhp->ihp', mixing, x_group, preferred_element_type=jnp.fl...  8.86 us
    dot_general x1, matrix products, state_part(): jnp.einsum('hjn,jhp->hpn', weighted, x_group, preferred_element_type=jnp....  8.34 us
    ppermute x3, starting transfers between devices, shifted(): lax.ppermute(value, axis, [(s, s + steps) for s in range(count - steps)])  7.08 us
    reduce_sum x1, other arithmetic, local(): local_sq = jnp.sum(gated * gated, axis=1)  5.7 us
  transfers between devices with their start and end apart: 12, of which 7 were waited for; matrix products, arithmetic and copies ran while one was open for 18% of the time, Pallas kernels for 4%

profile of v11, /device:TPU:9, one launch (start us, length us, event | category | flops | bytes accessed | tf_op | source)
XLA Modules:
  0.0 253.7 jit_solution(896754463639857493)
XLA Ops:
  0.0 1.3 slice.126
  2.0 0.7 convert.17
  2.7 0.9 slice.127
  3.8 0.7 slice.128
  4.5 3.0 %collective-permute-start.2 = (bf16[3,8449]{1,0:T(4,128)(2,1)S(1)}, bf16[3,8449]{1,0:T(4,128)(2,1)S(1)}, u32[]{:S(2)}, u32[]{:S(2)}) collective-permute-start(bf16[3,8449]{1,0:T(4,128)(2,1)S(1)} %pad_maximum_fusion.6), channel_id=1, source_target_pairs={{0,1},{1,2},{2,3},{3,4},{4,5},{5,6},{6,7},{7,8},{8,9},{9,10},{10,1... | collective-permute-start | bytes 152090 | tf_op jit(solution)/shard_map/ppermute | solution.py:23
  7.5 1.0 copy.63
  8.5 0.8 negate_multiply_fusion
  9.5 1.4 reshape.246.b_ref
  10.8 0.8 slice_convert_fusion.5
  12.4 1.3 broadcast_select_fusion.1
  13.7 1.2 collective-permute-start.5
  14.9 1.2 collective-permute-done.5
  16.2 1.3 collective-permute-start.6
  18.2 0.8 pad_add_fusion
  20.2 2.0 compare_convert_fusion.4
  22.2 0.9 copy.67.vis_ref
  23.8 0.7 concatenate.91.rim_ref
  24.5 10.9 %shard_map.127 = bf16[8192,256]{1,0:T(8,128)(2,1)} custom-call(bf16[8,8192]{1,0:T(8,128)(2,1)} %concatenate.91.rim_ref, bf16[256,8192]{1,0:T(8,128)(2,1)} %x_ref.1, bf16[4,8192]{1,0:T(4,128)(2,1)} %w_ref.1, bf16[1,8192]{1,0:T(2,128)(2,1)} %reshape.246.b_ref, f32[3,256,1]{2,1,0:T(8,128)} %copy.67.vis_ref), custom_call_target="tpu_custom_call" | custom-call | flops 41943040 | bytes 8388608 | tf_op jit(solution)/shard_map/pallas_call | solution.py:66
  35.6 2.2 collective-permute-done.7
  37.9 2.3 collective-permute-start.8
  40.2 8.3 %fusion.18 = f32[1,128,64,128]{3,2,1,0:T(8,128)S(1)} fusion(bf16[256,128,64]{0,2,1:T(8,128)(2,1)} %bitcast.130, f32[128,256]{1,0:T(8,128)S(1)} %copy.68, f32[256,128]{1,0:T(8,128)S(1)} %get-tuple-element.104), kind=kOutput, calls=%fused_computation.37 | convolution fusion | flops 545259520 | bytes 8650752 | tf_op jit(solution)/shard_map/hjn,jhp->hpn/dot_general | solution.py:121
  49.0 1.9 copy-done
  51.0 1.5 constant_dynamic-slice_fusion
  52.4 2.3 collective-permute-start.9
  54.7 3.6 %collective-permute-done.3 = f32[128]{0:T(128)S(1)} collective-permute-done((f32[128]{0:T(128)S(1)}, f32[128]{0:T(128)S(1)}, u32[]{:S(2)}, u32[]{:S(2)}) %collective-permute-start.3) | collective-permute-done | bytes 544 | tf_op jit(solution)/shard_map/ppermute | solution.py:231
  58.7 2.8 %add_select_fusion = f32[64,64,128]{2,1,0:T(8,128)S(1)} fusion(f32[64,64,128]{2,1,0:T(8,128)S(1)} %collective-permute-done.9, f32[128,64,128]{2,1,0:T(8,128)} %copy-done, s32[]{:T(128)S(6)} %select_n.101, f32[64]{0:T(128)S(1)} %get-tuple-element.91, f32[64]{0:T(128)S(1)} %get-tuple-element.90, pred[]{:T(512)S(6)} %eq.73), kind=kLoop, calls=%fused_computation.54 | loop fusion | flops 2621440 | bytes 6291973 | tf_op jit(solution)/shard_map/jit(_where)/select_n | solution.py:236
  61.5 1.2 copy.98
  62.9 3.1 %collective-permute-start.10 = (f32[64,8320]{1,0:T(8,128)S(1)}, f32[64,8320]{1,0:T(8,128)S(1)}, u32[]{:S(2)}, u32[]{:S(2)}) collective-permute-start(f32[64,8320]{1,0:T(8,128)S(1)} %pad_maximum_fusion.2), channel_id=1, source_target_pairs={{0,2},{1,3},{2,4},{3,5},{4,6},{5,7},{6,8},{7,9},{8,10},{9,11},{10,... | collective-permute-start | bytes 6389768 | tf_op jit(solution)/shard_map/ppermute | solution.py:134
  66.0 48.1 %collective-permute-done.10 = f32[64,8320]{1,0:T(8,128)S(1)} collective-permute-done((f32[64,8320]{1,0:T(8,128)S(1)}, f32[64,8320]{1,0:T(8,128)S(1)}, u32[]{:S(2)}, u32[]{:S(2)}) %collective-permute-start.10) | collective-permute-done | bytes 2129952 | tf_op jit(solution)/shard_map/ppermute | solution.py:134
  114.7 1.9 collective-permute-start.11
  116.6 48.4 %collective-permute-done.11 = f32[64,8320]{1,0:T(8,128)S(1)} collective-permute-done((f32[64,8320]{1,0:T(8,128)S(1)}, f32[64,8320]{1,0:T(8,128)S(1)}, u32[]{:S(2)}, u32[]{:S(2)}) %collective-permute-start.11) | collective-permute-done | bytes 2129952 | tf_op jit(solution)/shard_map/ppermute | solution.py:134
  165.2 2.7 %multiply_add_fusion = (f32[64,8192]{1,0:T(8,128)S(1)}, f32[8,8,64,128]{3,1,2,0:T(8,128)}, f32[8,8,64,128]{3,1,2,0:T(8,128)}) fusion(f32[64,8320]{1,0:T(8,128)S(1)} %collective-permute-done.11, f32[64]{0:T(128)S(1)} %slice_reduce_fusion.1, f32[64,8320]{1,0:T(8,128)S(1)} %collective-permute-done.10), kind=kLoop, calls=%fused_computation.53 | loop fusion | flops 1048576 | bytes 10486016 | tf_op jit(solution)/shard_map/add | solution.py:149
  167.9 1.5 pad_maximum_fusion.4
  169.4 2.0 collective-permute-start.12
  171.5 6.4 %copy.79 = bf16[256,8192]{0,1:T(8,128)(2,1)} copy(bf16[256,8192]{1,0:T(8,128)(2,1)} %param.16) | data formatting | bytes 8388608 | tf_op args[1]
  178.0 2.6 %copy.80.n_ref = f32[8192,1]{1,0:T(8,128)} copy(f32[8192,1]{0,1:T(1,128)S(1)} %bitcast.140) | data formatting | bytes 65536 | tf_op jit(solution)/shard_map/broadcast_in_dim | solution.py:102
  181.3 0.7 compare_reduce_fusion
  183.2 2.1 copy.89
  185.8 32.5 %collective-permute-done.12 = f32[64,8320]{1,0:T(8,128)S(1)} collective-permute-done((f32[64,8320]{1,0:T(8,128)}, f32[64,8320]{1,0:T(8,128)S(1)}, u32[]{:S(2)}, u32[]{:S(2)}) %collective-permute-start.12) | collective-permute-done | bytes 2129952 | tf_op jit(solution)/shard_map/ppermute | solution.py:134
  218.4 1.2 copy-done.6
  220.6 2.8 %fusion.23 = bf16[64,64,128]{2,1,0:T(8,128)(2,1)S(1)} fusion(f32[64,64,128]{2,1,0:T(8,128)S(1)} %get-tuple-element.114, f32[64,64,128]{2,1,0:T(8,128)} %copy-done.2, f32[128,64,128]{2,1,0:T(8,128)} %copy-done, s32[]{:T(128)S(6)} %select_n.101, f32[64]{0:T(128)S(1)} %get-tuple-element.89, pred[]{:T(512)S(6)} %eq.73), kind=kLoop, calls=%fused_computation.56 | loop fusion | flops 2097152 | bytes 7340293 | tf_op jit(solution)/shard_map/jit(_where)/select_n | solution.py:242
  223.5 2.5 collective-permute-start.13
  226.0 8.9 %fusion.3 = f32[128,64,256]{2,1,0:T(8,128)S(1)} fusion(f32[128,256]{1,0:T(8,128)S(1)} %copy.72, f32[128,256]{1,0:T(8,128)S(1)} %copy.70, f32[256,256]{1,0:T(8,128)S(1)} %fusion.31, pred[256,256]{1,0:T(8,128)(4,1)S(1)} %fusion.25, bf16[1,256,128,64]{1,3,2,0:T(8,128)(2,1)S(1)} %bitcast.131), kind=kOutput, calls=%fused_computation.15 | convolution fusion | flops 1115684864 | bytes 13172736 | tf_op jit(solution)/shard_map/hij,jhp->ihp/dot_general | solution.py:113
  234.9 0.8 select_convert_fusion.1
  235.7 1.3 bitcast_add_fusion.1
  237.0 0.9 copy-done.5
  237.9 5.7 %multiply_reduce_fusion = (f32[256]{0:T(256)S(1)}, f32[256,8192]{0,1:T(8,128)}) fusion(bf16[256,8192]{0,1:T(8,128)(2,1)S(1)} %copy-done.5, bf16[256,8192]{0,1:T(8,128)(2,1)S(1)} %bitcast.132, f32[8192]{0:T(1024)S(1)} %mul.349, f32[256,128,64]{0,2,1:T(8,128)S(1)} %bitcast_add_fusion.1), kind=kLoop, calls=%fused_computation.32 | loop fusion | flops 23068416 | bytes 25199616 | tf_op jit(solution)/shard_map/reduce_sum | solution.py:347
  244.2 9.5 %shard_map.128 = bf16[256,8192]{1,0:T(8,128)(2,1)} custom-call(f32[8192,256]{1,0:T(8,128)} %bitcast.128, f32[1,256]{1,0:T(1,128)} %bitcast.144, f32[8192,1]{1,0:T(8,128)} %copy.80.n_ref), custom_call_target="tpu_custom_call" | custom-call | flops 4194304 | bytes 12582912 | tf_op jit(solution)/shard_map/pallas_call | solution.py:91
  (92 shorter events, 8.8 us)
Async XLA Ops:
  0.0 23.2 %copy-start.8 = (bf16[256,256]{1,0:T(8,128)(2,1)S(1)}, bf16[256,256]{1,0:T(8,128)(2,1)}, u32[]{:S(2)}) copy-start(bf16[256,256]{1,0:T(8,128)(2,1)} %param.17) | copy-start | bytes 393220
  0.0 23.6 %copy-start.11 = (f32[128]{0:T(128)S(1)}, f32[128]{0:T(128)}, u32[]{:S(2)}) copy-start(f32[128]{0:T(128)} %param.19) | copy-start | bytes 1540
  1.3 11.1 %collective-permute-start.4 = (s32[1]{0:T(128)}, s32[1]{0:T(128)}, u32[]{:S(2)}, u32[]{:S(2)}) collective-permute-start(s32[1]{0:T(128)} %slice.126), channel_id=1, source_target_pairs={{0,1},{1,0},{2,3},{3,2},{4,5},{5,4},{6,7},{7,6},{8,9},{9,8},{10,11... | collective-permute-start | bytes 20 | tf_op jit(solution)/shard_map/ppermute | solution.py:182
  4.5 11.7 %collective-permute-start.2 = (bf16[3,8449]{1,0:T(4,128)(2,1)S(1)}, bf16[3,8449]{1,0:T(4,128)(2,1)S(1)}, u32[]{:S(2)}, u32[]{:S(2)}) collective-permute-start(bf16[3,8449]{1,0:T(4,128)(2,1)S(1)} %pad_maximum_fusion.6), channel_id=1, source_target_pairs={{0,1},{1,2},{2,3},{3,4},{4,5},{5,6},{6,7},{7,8},{8,9},{9,10},{10,1... | collective-permute-start | bytes 152090 | tf_op jit(solution)/shard_map/ppermute | solution.py:23
  13.7 2.4 collective-permute-start.5
  16.2 19.1 %collective-permute-start.6 = (s32[4]{0:T(128)S(1)}, s32[4]{0:T(128)S(1)}, u32[]{:S(2)}, u32[]{:S(2)}) collective-permute-start(s32[4]{0:T(128)S(1)} %broadcast_select_fusion.2), channel_id=1, source_target_pairs={{0,4},{1,5},{2,6},{3,7},{4,0},{5,1},{6,2},{7,3},{8,12},{9,13},{10,... | collective-permute-start | bytes 56 | tf_op jit(solution)/shard_map/ppermute | solution.py:182
  35.4 2.4 collective-permute-start.7
  37.9 10.7 %collective-permute-start.8 = (s32[16]{0:T(128)S(1)}, s32[16]{0:T(128)S(1)}, u32[]{:S(2)}, u32[]{:S(2)}) collective-permute-start(s32[16]{0:T(128)S(1)} %broadcast_select_fusion.4), channel_id=1, source_target_pairs={{0,16},{1,17},{2,18},{3,19},{4,20},{5,21},{6,22},{7,23},{8,24},{9,... | collective-permute-start | bytes 200 | tf_op jit(solution)/shard_map/ppermute | solution.py:182
  49.0 2.0 copy-start
  52.4 6.3 %collective-permute-start.9 = (f32[64,64,128]{2,1,0:T(8,128)}, f32[64,64,128]{2,1,0:T(8,128)S(1)}, u32[]{:S(2)}, u32[]{:S(2)}) collective-permute-start(f32[64,64,128]{2,1,0:T(8,128)} %constant_dynamic-slice_fusion), channel_id=1, source_target_pairs={{0,1},{1,0},{2,3},{3,2},{4,5},{5,4},{6,7},{7,6},{8,9},{9,8},{10,11... | collective-permute-start | bytes 6291464 | tf_op jit(solution)/shard_map/ppermute | solution.py:231
  54.7 3.6 %collective-permute-start.3 = (f32[128]{0:T(128)S(1)}, f32[128]{0:T(128)S(1)}, u32[]{:S(2)}, u32[]{:S(2)}) collective-permute-start(f32[128]{0:T(128)S(1)} %get-tuple-element.95), channel_id=1, source_target_pairs={{0,1},{1,0},{2,3},{3,2},{4,5},{5,4},{6,7},{7,6},{8,9},{9,8},{10,11... | collective-permute-start | bytes 1544 | tf_op jit(solution)/shard_map/ppermute | solution.py:231
  58.7 2.8 %copy-start.2 = (f32[64,64,128]{2,1,0:T(8,128)}, f32[64,64,128]{2,1,0:T(8,128)S(1)}, u32[]{:S(2)}) copy-start(f32[64,64,128]{2,1,0:T(8,128)S(1)} %collective-permute-done.9) | copy-start | bytes 6291460
  62.9 51.2 %collective-permute-start.10 = (f32[64,8320]{1,0:T(8,128)S(1)}, f32[64,8320]{1,0:T(8,128)S(1)}, u32[]{:S(2)}, u32[]{:S(2)}) collective-permute-start(f32[64,8320]{1,0:T(8,128)S(1)} %pad_maximum_fusion.2), channel_id=1, source_target_pairs={{0,2},{1,3},{2,4},{3,5},{4,6},{5,7},{6,8},{7,9},{8,10},{9,11},{10,... | collective-permute-start | bytes 6389768 | tf_op jit(solution)/shard_map/ppermute | solution.py:134
  114.7 50.3 %collective-permute-start.11 = (f32[64,8320]{1,0:T(8,128)S(1)}, f32[64,8320]{1,0:T(8,128)S(1)}, u32[]{:S(2)}, u32[]{:S(2)}) collective-permute-start(f32[64,8320]{1,0:T(8,128)S(1)} %pad_maximum_fusion.3), channel_id=1, source_target_pairs={{0,2},{1,3},{2,4},{3,5},{4,6},{5,7},{6,8},{7,9},{8,10},{9,11},{10,... | collective-permute-start | bytes 6389768 | tf_op jit(solution)/shard_map/ppermute | solution.py:134
  169.4 8.4 %copy-start.12 = (f32[128]{0:T(128)S(1)}, f32[128]{0:T(128)}, u32[]{:S(2)}) copy-start(f32[128]{0:T(128)} %param.21) | copy-start | bytes 1540
  169.4 8.6 %copy-start.9 = (bf16[8192]{0:T(1024)(128)(2,1)S(1)}, bf16[8192]{0:T(1024)(128)(2,1)}, u32[]{:S(2)}) copy-start(bf16[8192]{0:T(1024)(128)(2,1)} %param.26) | copy-start | bytes 49156
  169.4 48.8 %collective-permute-start.12 = (f32[64,8320]{1,0:T(8,128)}, f32[64,8320]{1,0:T(8,128)S(1)}, u32[]{:S(2)}, u32[]{:S(2)}) collective-permute-start(f32[64,8320]{1,0:T(8,128)} %pad_maximum_fusion.4), channel_id=1, source_target_pairs={{0,4},{1,5},{2,6},{3,7},{4,8},{5,9},{6,10},{7,11},{8,12},{9,13},{1... | collective-permute-start | bytes 6389768 | tf_op jit(solution)/shard_map/ppermute | solution.py:134
  178.0 4.8 %copy-start.10 = (s32[256]{0:T(256)S(1)}, s32[256]{0:T(256)}, u32[]{:S(2)}) copy-start(s32[256]{0:T(256)} %param.27) | copy-start | bytes 3076
  183.2 2.2 copy-start.7
  218.3 1.3 copy-start.6
  220.6 5.3 %copy-start.4 = (bf16[8192,256]{1,0:T(8,128)(2,1)S(1)}, bf16[8192,256]{1,0:T(8,128)(2,1)}, u32[]{:S(2)}) copy-start(bf16[8192,256]{1,0:T(8,128)(2,1)} %shard_map.127) | copy-start | bytes 12582916
  223.5 11.4 %copy-start.1 = (f32[128,64,128]{2,1,0:T(8,128)S(1)}, f32[128,64,128]{2,1,0:T(8,128)}, u32[]{:S(2)}) copy-start(f32[128,64,128]{2,1,0:T(8,128)} %copy-done) | copy-start | bytes 12582916
  223.5 11.4 %copy-start.3 = (f32[64,64,128]{2,1,0:T(8,128)S(1)}, f32[64,64,128]{2,1,0:T(8,128)}, u32[]{:S(2)}) copy-start(f32[64,64,128]{2,1,0:T(8,128)} %copy-done.2) | copy-start | bytes 6291460
  223.5 11.4 %collective-permute-start.13 = (bf16[64,64,128]{2,1,0:T(8,128)(2,1)S(1)}, bf16[64,64,128]{2,1,0:T(8,128)(2,1)S(1)}, u32[]{:S(2)}, u32[]{:S(2)}) collective-permute-start(bf16[64,64,128]{2,1,0:T(8,128)(2,1)S(1)} %fusion.23), channel_id=1, source_target_pairs={{0,1},{1,0},{2,3},{3,2},{4,5},{5,4},{6,7},{7,6},{8,9},{9,8},{10,11... | collective-permute-start | bytes 3145736 | tf_op jit(solution)/shard_map/ppermute | solution.py:242
  235.7 2.2 copy-start.5

commit v12 on v9

--- a/solution.py
+++ b/solution.py
@@ -160,29 +160,6 @@
 
         transmit, state = lax.cond(needed, rest, lambda carried: carried, (transmit, state))
     return state
-
-
-def gather_round(value, axis, size):
-    count = lax.axis_size(axis)
-    if count & (count - 1):
-        return lax.all_gather(value, axis, tiled=True) if size == 1 else value
-    if size >= count:
-        return value
-    place = lax.axis_index(axis)
-    other = lax.ppermute(value, axis, [(s, s ^ size) for s in range(count)])
-    return jnp.where(
-        (place & size) == 0,
-        jnp.concatenate([value, other]),
-        jnp.concatenate([other, value]),
-    )
-
-
-def gather_rounds(value, axis, first, last):
-    size = 1 << first
-    while size < (1 << last):
-        value = gather_round(value, axis, size)
-        size *= 2
-    return value
 
 
 def long_runs(ids, paired, tok_rows):
@@ -289,11 +266,7 @@
     rim_x = rims[:, :channels]
     rim_bc = rims[:, channels : channels + bc_width]
     rim_segment = rims[:, channels + bc_width].astype(jnp.int32)
-    ids = gather_rounds(segment_ids[tok_rows - 1 :], "ctx", 0, 2)
-    ids, rim_x = lax.optimization_barrier((ids, rim_x))
     x_conv = conv_rows(rim_x, x_in, rim_segment, segment_ids, conv_x_w, conv_x_b)
-    ids = gather_rounds(ids, "ctx", 2, 4)
-    ids, x_conv = lax.optimization_barrier((ids, x_conv))
     bc_conv = causal_conv(rim_bc, bc_in, rim_segment, segment_ids, conv_bc_w, conv_bc_b)
     step_size = jax.nn.softplus(dt_raw + dt_bias[:, None])
     log_decay = -step_size * a_rate[:, None]
@@ -319,7 +292,7 @@
         state_of, (x_blocks, b_blocks, step_blocks, cum_decay, seg_blocks, seg_before)
     )
     intra_items = (x_blocks, b_blocks, c_blocks, step_blocks, cum_decay, seg_blocks)
-    ids = gather_rounds(ids, "ctx", 4, lax.axis_size("ctx").bit_length())
+    ids = lax.all_gather(segment_ids[tok_rows - 1 :], "ctx", tiled=True)
     ids, block_states = lax.optimization_barrier((ids, block_states))
     far = [*long_runs(ids, paired, tok_rows), intra_items]
     entering = chain_states(block_states, transmits, paired, far)

time: 252 us -> 281 us (1.12)
  blocking collectives: 0 us -> 38 us
  waiting for transfers between devices: 131 us -> 125 us
    optimization_barrier x0 -> x1, blocking collectives: none -> 38 us  [local(): ids, block_states = lax.optimization_barrier((ids, block_states))]
    ppermute x5 -> x0, starting transfers between devices: 5.68 us -> none  [gather_round(): other = lax.ppermute(value, axis, [(s, s ^ size) for s in range(count)])]
    ppermute x5 -> x0, waiting for transfers between devices: 3.41 us -> none  [gather_round(): other = lax.ppermute(value, axis, [(s, s ^ size) for s in range(count)])]
    ppermute x6, waiting for transfers between devices: 124 us -> 121 us  [shifted(): lax.ppermute(value, axis, [(s, s + steps) for s in range(count - steps)])]
    unnamed x20 -> x22, local copies, waits for them, and re-layouts: 10.3 us -> 11.6 us
  transfers between devices with their start and end apart: 15 -> 10, of which waited for: 8 -> 7; matrix products, arithmetic and copies ran while one was open for 19% -> 10% of each run, Pallas kernels for 4% -> 0%
where the time goes in v12:
time: 281 us; the launch traced here: 280 us
  waiting for transfers between devices  125 us (44%)
  blocking collectives  38 us (14%)
  other arithmetic  28.8 us (10%)
  starting transfers between devices  25.2 us (9%)
  local copies, waits for them, and re-layouts  21.8 us (8%)
  Pallas kernels  20.3 us (7%)
  matrix products  18.5 us (7%)
    ppermute x6, waiting for transfers between devices, shifted(): lax.ppermute(value, axis, [(s, s + steps) for s in range(count - steps)])  121 us
    optimization_barrier x1, blocking collectives, local(): ids, block_states = lax.optimization_barrier((ids, block_states))  38 us
    ppermute x6, starting transfers between devices, shifted(): lax.ppermute(value, axis, [(s, s + steps) for s in range(count - steps)])  16 us
    unnamed x22, local copies, waits for them, and re-layouts  11.6 us
    pallas_call x1, Pallas kernels, conv_rows(): pl.pallas_call(conv_rows_kernel, out_shape=jax.ShapeDtypeStruct((width, r...  10.8 us
    pallas_call x1, Pallas kernels, scale_rows(): pl.pallas_call(scale_rows_kernel, out_shape=jax.ShapeDtypeStruct((rows, w...  9.48 us
    dot_general x1, matrix products, mixing_part(): jnp.einsum('hij,jhp->ihp', mixing, x_group, preferred_element_type=jnp.fl...  8.86 us
    dot_general x1, matrix products, state_part(): jnp.einsum('hjn,jhp->hpn', weighted, x_group, preferred_element_type=jnp....  8.19 us
  transfers between devices with their start and end apart: 10, of which 7 were waited for; matrix products, arithmetic and copies ran while one was open for 10% of the time, Pallas kernels for 0%

profile of v12, /device:TPU:9, one launch (start us, length us, event | category | flops | bytes accessed | tf_op | source)
XLA Modules:
  0.0 279.6 jit_solution(1208845799869957556)
XLA Ops:
  0.0 0.9 slice.99
  0.9 0.7 convert.17
  1.8 0.7 slice.100
  2.5 3.7 %collective-permute-start.3 = (bf16[3,8449]{1,0:T(4,128)(2,1)S(1)}, bf16[3,8449]{1,0:T(4,128)(2,1)S(1)}, u32[]{:S(2)}, u32[]{:S(2)}) collective-permute-start(bf16[3,8449]{1,0:T(4,128)(2,1)S(1)} %pad_maximum_fusion.1), channel_id=1, source_target_pairs={{0,1},{1,2},{2,3},{3,4},{4,5},{5,6},{6,7},{7,8},{8,9},{9,10},{10,1... | collective-permute-start | bytes 152090 | tf_op jit(solution)/shard_map/ppermute | solution.py:23
  6.2 0.8 slice_convert_fusion.5
  7.1 1.0 copy.21
  8.1 0.8 negate_multiply_fusion
  9.0 1.3 slice_dynamic-update-slice_fusion
  10.3 38.0 %all-reduce.1 = s32[32]{0:T(128)S(1)} all-reduce(s32[32]{0:T(128)S(1)} %get-tuple-element.84), channel_id=1, replica_groups=mesh['ctx'=32,'tp'=1] {'ctx'}, use_global_device_ids=true, to_apply=%add.1 | all-reduce | flops 32 | bytes 256 | tf_op jit(solution)/shard_map/optimization_barrier | solution.py:296
  48.3 0.7 convert_element_type.86
  49.0 1.3 reshape.210.b_ref
  50.9 0.8 pad_add_fusion
  52.9 2.0 compare_convert_fusion.4
  54.9 1.5 multiply_convert_fusion.6
  56.5 0.8 fusion.35
  57.4 0.9 copy.25.vis_ref
  58.4 0.7 concatenate.38.rim_ref
  59.0 10.8 %shard_map.127 = bf16[8192,256]{1,0:T(8,128)(2,1)} custom-call(bf16[8,8192]{1,0:T(8,128)(2,1)} %concatenate.38.rim_ref, bf16[256,8192]{1,0:T(8,128)(2,1)} %x_ref.1, bf16[4,8192]{1,0:T(4,128)(2,1)} %w_ref.1, bf16[1,8192]{1,0:T(2,128)(2,1)} %reshape.210.b_ref, f32[3,256,1]{2,1,0:T(8,128)} %copy.25.vis_ref), custom_call_target="tpu_custom_call" | custom-call | flops 41943040 | bytes 8388608 | tf_op jit(solution)/shard_map/pallas_call | solution.py:66
  69.8 8.2 %fusion.15 = f32[1,128,64,128]{3,2,1,0:T(8,128)} fusion(bf16[256,128,64]{0,2,1:T(8,128)(2,1)} %bitcast.82, f32[128,256]{1,0:T(8,128)S(1)} %copy.26, f32[256,128]{1,0:T(8,128)S(1)} %get-tuple-element.75), kind=kOutput, calls=%fused_computation.25 | convolution fusion | flops 545259520 | bytes 8650752 | tf_op jit(solution)/shard_map/hjn,jhp->hpn/dot_general | solution.py:121
  78.0 2.5 bitcast_add_fusion.2
  80.6 2.0 copy-done
  82.5 1.5 constant_dynamic-slice_fusion
  84.0 1.5 collective-permute-start.5
  85.5 3.6 %collective-permute-done.4 = f32[128]{0:T(128)S(1)} collective-permute-done((f32[128]{0:T(128)S(1)}, f32[128]{0:T(128)S(1)}, u32[]{:S(2)}, u32[]{:S(2)}) %collective-permute-start.4) | collective-permute-done | bytes 544 | tf_op jit(solution)/shard_map/ppermute | solution.py:198
  89.5 2.8 add_select_fusion
  92.3 3.9 %collective-permute-start.8 = (f32[64,64,128]{2,1,0:T(8,128)S(1)}, f32[64,64,128]{2,1,0:T(8,128)S(1)}, u32[]{:S(2)}, u32[]{:S(2)}) collective-permute-start(f32[64,64,128]{2,1,0:T(8,128)S(1)} %add_select_fusion), channel_id=1, source_target_pairs={{0,2},{1,3},{2,4},{3,5},{4,6},{5,7},{6,8},{7,9},{8,10},{9,11},{10,... | collective-permute-start | bytes 6291464 | tf_op jit(solution)/shard_map/ppermute | solution.py:134
  96.2 46.6 %collective-permute-done.8 = f32[64,64,128]{2,1,0:T(8,128)S(1)} collective-permute-done((f32[64,64,128]{2,1,0:T(8,128)S(1)}, f32[64,64,128]{2,1,0:T(8,128)S(1)}, u32[]{:S(2)}, u32[]{:S(2)}) %collective-permute-start.8) | collective-permute-done | bytes 2097184 | tf_op jit(solution)/shard_map/ppermute | solution.py:134
  142.8 2.1 collective-permute-start.9
  144.9 4.0 %collective-permute-start.6 = (f32[64]{0:T(128)S(1)}, f32[64]{0:T(128)S(1)}, u32[]{:S(2)}, u32[]{:S(2)}) collective-permute-start(f32[64]{0:T(128)S(1)} %mul.278), channel_id=1, source_target_pairs={{0,2},{1,3},{2,4},{3,5},{4,6},{5,7},{6,8},{7,9},{8,10},{9,11},{10,... | collective-permute-start | bytes 776 | tf_op jit(solution)/shard_map/ppermute | solution.py:134
  148.9 43.5 %collective-permute-done.6 = f32[64]{0:T(128)S(1)} collective-permute-done((f32[64]{0:T(128)S(1)}, f32[64]{0:T(128)S(1)}, u32[]{:S(2)}, u32[]{:S(2)}) %collective-permute-start.6) | collective-permute-done | bytes 288 | tf_op jit(solution)/shard_map/ppermute | solution.py:134
  192.4 1.6 multiply_add_fusion.3
  194.0 2.2 collective-permute-start.10
  196.2 6.4 %copy.35 = bf16[256,8192]{0,1:T(8,128)(2,1)} copy(bf16[256,8192]{1,0:T(8,128)(2,1)} %param.16) | data formatting | bytes 8388608 | tf_op args[1]
  202.8 2.7 copy.36.n_ref
  205.9 0.7 compare_reduce_fusion
  207.7 1.9 collective-permute-start.7
  209.9 30.0 %collective-permute-done.7 = f32[64]{0:T(128)S(1)} collective-permute-done((f32[64]{0:T(128)S(1)}, f32[64]{0:T(128)S(1)}, u32[]{:S(2)}, u32[]{:S(2)}) %collective-permute-start.7) | collective-permute-done | bytes 288 | tf_op jit(solution)/shard_map/ppermute | solution.py:134
  239.9 1.9 collective-permute-start.11
  242.2 2.5 multiply_add_fusion.2
  245.0 2.8 fusion.19
  247.9 4.0 %collective-permute-start.12 = (bf16[64,64,128]{2,1,0:T(8,128)(2,1)S(1)}, bf16[64,64,128]{2,1,0:T(8,128)(2,1)S(1)}, u32[]{:S(2)}, u32[]{:S(2)}) collective-permute-start(bf16[64,64,128]{2,1,0:T(8,128)(2,1)S(1)} %fusion.19), channel_id=1, source_target_pairs={{0,1},{1,0},{2,3},{3,2},{4,5},{5,4},{6,7},{7,6},{8,9},{9,8},{10,11... | collective-permute-start | bytes 3145736 | tf_op jit(solution)/shard_map/ppermute | solution.py:209
  251.9 8.9 %fusion = f32[128,64,256]{2,1,0:T(8,128)S(1)} fusion(f32[128,256]{1,0:T(8,128)S(1)} %copy.30, f32[128,256]{1,0:T(8,128)S(1)} %copy.28, f32[256,256]{1,0:T(8,128)S(1)} %fusion.27, pred[256,256]{1,0:T(8,128)(4,1)S(1)} %fusion.21, bf16[1,256,128,64]{1,3,2,0:T(8,128)(2,1)S(1)} %bitcast.83), kind=kOutput, calls=%fused_computation.3 | convolution fusion | flops 1115684864 | bytes 13172736 | tf_op jit(solution)/shard_map/hij,jhp->ihp/dot_general | solution.py:113
  260.8 0.7 select_convert_fusion.1
  261.6 1.3 bitcast_add_fusion.1
  262.9 0.9 copy-done.5
  263.8 5.7 %multiply_reduce_fusion = (f32[256]{0:T(256)S(1)}, f32[256,8192]{0,1:T(8,128)}) fusion(bf16[256,8192]{0,1:T(8,128)(2,1)S(1)} %copy-done.5, bf16[8192,256]{1,0:T(8,128)(2,1)S(1)} %copy-done.4, f32[8192]{0:T(1024)S(1)} %mul.331, f32[256,128,64]{0,2,1:T(8,128)S(1)} %bitcast_add_fusion.1), kind=kLoop, calls=%fused_computation.20 | loop fusion | flops 23068416 | bytes 25199616 | tf_op jit(solution)/shard_map/reduce_sum | solution.py:310
  269.6 0.5 add_rsqrt_fusion
  270.1 9.5 %shard_map.128 = bf16[256,8192]{1,0:T(8,128)(2,1)} custom-call(f32[8192,256]{1,0:T(8,128)} %bitcast.81, f32[1,256]{1,0:T(1,128)} %bitcast.91, f32[8192,1]{1,0:T(8,128)} %copy.36.n_ref), custom_call_target="tpu_custom_call" | custom-call | flops 4194304 | bytes 12582912 | tf_op jit(solution)/shard_map/pallas_call | solution.py:91
  (63 shorter events, 3.9 us)
Async XLA Ops:
  2.5 47.8 %collective-permute-start.3 = (bf16[3,8449]{1,0:T(4,128)(2,1)S(1)}, bf16[3,8449]{1,0:T(4,128)(2,1)S(1)}, u32[]{:S(2)}, u32[]{:S(2)}) collective-permute-start(bf16[3,8449]{1,0:T(4,128)(2,1)S(1)} %pad_maximum_fusion.1), channel_id=1, source_target_pairs={{0,1},{1,2},{2,3},{3,4},{4,5},{5,6},{6,7},{7,8},{8,9},{9,10},{10,1... | collective-permute-start | bytes 152090 | tf_op jit(solution)/shard_map/ppermute | solution.py:23
  80.6 2.0 copy-start
  84.0 5.5 %collective-permute-start.5 = (f32[64,64,128]{2,1,0:T(8,128)}, f32[64,64,128]{2,1,0:T(8,128)S(1)}, u32[]{:S(2)}, u32[]{:S(2)}) collective-permute-start(f32[64,64,128]{2,1,0:T(8,128)} %constant_dynamic-slice_fusion), channel_id=1, source_target_pairs={{0,1},{1,0},{2,3},{3,2},{4,5},{5,4},{6,7},{7,6},{8,9},{9,8},{10,11... | collective-permute-start | bytes 6291464 | tf_op jit(solution)/shard_map/ppermute | solution.py:198
  85.5 3.6 %collective-permute-start.4 = (f32[128]{0:T(128)S(1)}, f32[128]{0:T(128)S(1)}, u32[]{:S(2)}, u32[]{:S(2)}) collective-permute-start(f32[128]{0:T(128)S(1)} %get-tuple-element.70), channel_id=1, source_target_pairs={{0,1},{1,0},{2,3},{3,2},{4,5},{5,4},{6,7},{7,6},{8,9},{9,8},{10,11... | collective-permute-start | bytes 1544 | tf_op jit(solution)/shard_map/ppermute | solution.py:198
  89.5 104.5 %copy-start.2 = (f32[64,64,128]{2,1,0:T(8,128)}, f32[64,64,128]{2,1,0:T(8,128)S(1)}, u32[]{:S(2)}) copy-start(f32[64,64,128]{2,1,0:T(8,128)S(1)} %collective-permute-done.5) | copy-start | bytes 6291460
  92.3 50.5 %collective-permute-start.8 = (f32[64,64,128]{2,1,0:T(8,128)S(1)}, f32[64,64,128]{2,1,0:T(8,128)S(1)}, u32[]{:S(2)}, u32[]{:S(2)}) collective-permute-start(f32[64,64,128]{2,1,0:T(8,128)S(1)} %add_select_fusion), channel_id=1, source_target_pairs={{0,2},{1,3},{2,4},{3,5},{4,6},{5,7},{6,8},{7,9},{8,10},{9,11},{10,... | collective-permute-start | bytes 6291464 | tf_op jit(solution)/shard_map/ppermute | solution.py:134
  142.8 49.6 %collective-permute-start.9 = (f32[64,64,128]{2,1,0:T(8,128)S(1)}, f32[64,64,128]{2,1,0:T(8,128)S(1)}, u32[]{:S(2)}, u32[]{:S(2)}) collective-permute-start(f32[64,64,128]{2,1,0:T(8,128)S(1)} %collective-permute-done.8), channel_id=1, source_target_pairs={{0,2},{1,3},{2,4},{3,5},{4,6},{5,7},{6,8},{7,9},{8,10},{9,11},{10,... | collective-permute-start | bytes 6291464 | tf_op jit(solution)/shard_map/ppermute | solution.py:134
  144.9 47.5 %collective-permute-start.6 = (f32[64]{0:T(128)S(1)}, f32[64]{0:T(128)S(1)}, u32[]{:S(2)}, u32[]{:S(2)}) collective-permute-start(f32[64]{0:T(128)S(1)} %mul.278), channel_id=1, source_target_pairs={{0,2},{1,3},{2,4},{3,5},{4,6},{5,7},{6,8},{7,9},{8,10},{9,11},{10,... | collective-permute-start | bytes 776 | tf_op jit(solution)/shard_map/ppermute | solution.py:134
  194.0 8.6 %copy-start.8 = (f32[128]{0:T(128)S(1)}, f32[128]{0:T(128)}, u32[]{:S(2)}) copy-start(f32[128]{0:T(128)} %param.21) | copy-start | bytes 1540
  194.0 8.8 %copy-start.7 = (bf16[8192]{0:T(1024)(128)(2,1)S(1)}, bf16[8192]{0:T(1024)(128)(2,1)}, u32[]{:S(2)}) copy-start(bf16[8192]{0:T(1024)(128)(2,1)} %param.26) | copy-start | bytes 49156
  194.0 48.2 %collective-permute-start.10 = (f32[64,64,128]{2,1,0:T(8,128)}, f32[64,64,128]{2,1,0:T(8,128)}, u32[]{:S(2)}, u32[]{:S(2)}) collective-permute-start(f32[64,64,128]{2,1,0:T(8,128)} %multiply_add_fusion.3), channel_id=1, source_target_pairs={{0,4},{1,5},{2,6},{3,7},{4,8},{5,9},{6,10},{7,11},{8,12},{9,13},{1... | collective-permute-start | bytes 6291464 | tf_op jit(solution)/shard_map/ppermute | solution.py:134
  202.6 4.8 %copy-start.6 = (s32[256]{0:T(256)S(1)}, s32[256]{0:T(256)}, u32[]{:S(2)}) copy-start(s32[256]{0:T(256)} %param.27) | copy-start | bytes 3076
  207.7 32.1 %collective-permute-start.7 = (f32[64]{0:T(128)S(1)}, f32[64]{0:T(128)S(1)}, u32[]{:S(2)}, u32[]{:S(2)}) collective-permute-start(f32[64]{0:T(128)S(1)} %collective-permute-done.6), channel_id=1, source_target_pairs={{0,2},{1,3},{2,4},{3,5},{4,6},{5,7},{6,8},{7,9},{8,10},{9,11},{10,... | collective-permute-start | bytes 776 | tf_op jit(solution)/shard_map/ppermute | solution.py:134
  239.9 5.2 %collective-permute-start.11 = (f32[64]{0:T(128)S(1)}, f32[64]{0:T(128)S(1)}, u32[]{:S(2)}, u32[]{:S(2)}) collective-permute-start(f32[64]{0:T(128)S(1)} %mul.319), channel_id=1, source_target_pairs={{0,4},{1,5},{2,6},{3,7},{4,8},{5,9},{6,10},{7,11},{8,12},{9,13},{1... | collective-permute-start | bytes 776 | tf_op jit(solution)/shard_map/ppermute | solution.py:134
  245.0 6.8 %copy-start.4 = (bf16[8192,256]{1,0:T(8,128)(2,1)S(1)}, bf16[8192,256]{1,0:T(8,128)(2,1)}, u32[]{:S(2)}) copy-start(bf16[8192,256]{1,0:T(8,128)(2,1)} %shard_map.127) | copy-start | bytes 12582916
  247.8 12.9 %copy-start.1 = (f32[128,64,128]{2,1,0:T(8,128)S(1)}, f32[128,64,128]{2,1,0:T(8,128)}, u32[]{:S(2)}) copy-start(f32[128,64,128]{2,1,0:T(8,128)} %copy-done) | copy-start | bytes 12582916
  247.9 12.9 %copy-start.3 = (f32[64,64,128]{2,1,0:T(8,128)S(1)}, f32[64,64,128]{2,1,0:T(8,128)}, u32[]{:S(2)}) copy-start(f32[64,64,128]{2,1,0:T(8,128)} %copy-done.2) | copy-start | bytes 6291460
  247.9 12.9 %collective-permute-start.12 = (bf16[64,64,128]{2,1,0:T(8,128)(2,1)S(1)}, bf16[64,64,128]{2,1,0:T(8,128)(2,1)S(1)}, u32[]{:S(2)}, u32[]{:S(2)}) collective-permute-start(bf16[64,64,128]{2,1,0:T(8,128)(2,1)S(1)} %fusion.19), channel_id=1, source_target_pairs={{0,1},{1,0},{2,3},{3,2},{4,5},{5,4},{6,7},{7,6},{8,9},{9,8},{10,11... | collective-permute-start | bytes 3145736 | tf_op jit(solution)/shard_map/ppermute | solution.py:209
  261.6 2.2 copy-start.5

commit v13 on v9

--- a/solution.py
+++ b/solution.py
@@ -102,15 +102,55 @@
     )(gated.T, scale[None, :], gain.astype(jnp.float32)[:, None])
 
 
+def mixing_kernel(scores_ref, seg_col_ref, seg_row_ref, cum_col_ref, cum_row_ref, step_ref, x_ref, o_ref):
+    tokens = scores_ref.shape[0]
+    row = lax.broadcasted_iota(jnp.int32, (tokens, tokens), 0)
+    col = lax.broadcasted_iota(jnp.int32, (tokens, tokens), 1)
+    visible = jnp.logical_and(row >= col, seg_col_ref[...] == seg_row_ref[...])
+    scores = scores_ref[...]
+    for k in range(cum_row_ref.shape[0]):
+        exponent = jnp.where(visible, cum_col_ref[k] - cum_row_ref[k : k + 1, :], -jnp.inf)
+        mixing = (scores * jnp.exp(exponent) * step_ref[k : k + 1, :]).astype(jnp.bfloat16)
+        rows = pl.ds(k * HEAD_DIM, HEAD_DIM)
+        o_ref[rows, :] = lax.dot_general(
+            x_ref[rows, :], mixing, (((1,), (1,)), ((), ())), preferred_element_type=jnp.float32
+        )
+
+
 def mixing_part(x_group, b_group, c_group, step_size, cum_decay, segment):
-    places = jnp.arange(segment.shape[0])
-    visible = jnp.logical_and(
-        places[:, None] >= places[None, :], segment[:, None] == segment[None, :]
-    )
+    tokens, heads, width = x_group.shape
     scores = jnp.einsum("in,jn->ij", c_group, b_group, preferred_element_type=jnp.float32)
-    exponent = jnp.where(visible[None], cum_decay[:, :, None] - cum_decay[:, None, :], -jnp.inf)
-    mixing = (scores[None] * jnp.exp(exponent) * step_size[:, None, :]).astype(jnp.bfloat16)
-    return jnp.einsum("hij,jhp->ihp", mixing, x_group, preferred_element_type=jnp.float32)
+    x_t = x_group.reshape(tokens, heads * width).T
+    per = 8 if heads % 8 == 0 else heads
+    out = pl.pallas_call(
+        mixing_kernel,
+        out_shape=jax.ShapeDtypeStruct((heads * width, tokens), jnp.float32),
+        grid=(heads // per,),
+        in_specs=[
+            pl.BlockSpec((tokens, tokens), lambda g: (0, 0)),
+            pl.BlockSpec((tokens, 1), lambda g: (0, 0)),
+            pl.BlockSpec((1, tokens), lambda g: (0, 0)),
+            pl.BlockSpec((per, tokens, 1), lambda g: (g, 0, 0)),
+            pl.BlockSpec((per, tokens), lambda g: (g, 0)),
+            pl.BlockSpec((per, tokens), lambda g: (g, 0)),
+            pl.BlockSpec((per * width, tokens), lambda g: (g, 0)),
+        ],
+        out_specs=pl.BlockSpec((per * width, tokens), lambda g: (g, 0)),
+        cost_estimate=pl.CostEstimate(
+            flops=2 * tokens * tokens * heads * width + 6 * tokens * tokens * heads,
+            transcendentals=tokens * tokens * heads,
+            bytes_accessed=6 * tokens * heads * width,
+        ),
+    )(
+        scores,
+        segment[:, None],
+        segment[None, :],
+        cum_decay[:, :, None],
+        cum_decay,
+        step_size,
+        x_t,
+    )
+    return out.T.reshape(tokens, heads, width)
 
 
 def state_part(x_group, b_group, step_size, cum_decay, segment, seg_before):

time: 252 us -> 301 us (1.19)
  Pallas kernels: 20.3 us -> 40 us
  local copies, waits for them, and re-layouts: 21.9 us -> 39.1 us
  waiting for transfers between devices: 131 us -> 141 us
  other arithmetic: 28.3 us -> 32.2 us
    pallas_call x0 -> x1, Pallas kernels: none -> 19.7 us  [mixing_part(): pl.pallas_call(mixing_kernel, out_shape=jax.ShapeDtypeStruct((heads * wid...]
    another operation x3 -> x9, local copies, waits for them, and re-layouts: 0.02 us -> 10 us  [the longest x1 8.6 us: mixing_part(): cum_decay[:, :, None]]
    ppermute x6, waiting for transfers between devices: 124 us -> 134 us  [shifted(): lax.ppermute(value, axis, [(s, s + steps) for s in range(count - steps)])]
    dot_general x1 -> x0, matrix products: 8.86 us -> none  [mixing_part(): jnp.einsum('hij,jhp->ihp', mixing, x_group, preferred_element_type=jnp.fl...]
    dot_general x1, matrix products: 1.26 us -> 7.2 us  [entry_part(): jnp.einsum('in,hpn->ihp', c_group, packed, preferred_element_type=jnp.flo...]
    add x0 -> x1, local copies, waits for them, and re-layouts: none -> 5.08 us  [local(): y_blocks = y_intra + y_state]
    unnamed x20 -> x29, local copies, waits for them, and re-layouts: 10.3 us -> 8.78 us
  transfers between devices with their start and end apart: 15 -> 15, of which waited for: 8 -> 8; matrix products, arithmetic and copies ran while one was open for 19% -> 18% of each run, Pallas kernels for 4% -> 10%
where the time goes in v13:
time: 301 us; the launch traced here: 299 us
  waiting for transfers between devices  141 us (47%)
  Pallas kernels  40 us (13%)
  local copies, waits for them, and re-layouts  39.1 us (13%)
  other arithmetic  32.2 us (11%)
  starting transfers between devices  27.8 us (9%)
  matrix products  17.3 us (6%)
    ppermute x6, waiting for transfers between devices, shifted(): lax.ppermute(value, axis, [(s, s + steps) for s in range(count - steps)])  134 us
    pallas_call x1, Pallas kernels, mixing_part(): pl.pallas_call(mixing_kernel, out_shape=jax.ShapeDtypeStruct((heads * wid...  19.7 us
    ppermute x6, starting transfers between devices, shifted(): lax.ppermute(value, axis, [(s, s + steps) for s in range(count - steps)])  13.2 us
    pallas_call x1, Pallas kernels, conv_rows(): pl.pallas_call(conv_rows_kernel, out_shape=jax.ShapeDtypeStruct((width, r...  10.8 us
    pallas_call x1, Pallas kernels, scale_rows(): pl.pallas_call(scale_rows_kernel, out_shape=jax.ShapeDtypeStruct((rows, w...  9.48 us
    unnamed x29, local copies, waits for them, and re-layouts  8.78 us
    another operation x1, local copies, waits for them, and re-layouts, mixing_part(): cum_decay[:, :, None]  8.6 us
    dot_general x1, matrix products, state_part(): jnp.einsum('hjn,jhp->hpn', weighted, x_group, preferred_element_type=jnp....  8.34 us
  transfers between devices with their start and end apart: 15, of which 8 were waited for; matrix products, arithmetic and copies ran while one was open for 18% of the time, Pallas kernels for 10%

profile of v13, /device:TPU:9, one launch (start us, length us, event | category | flops | bytes accessed | tf_op | source)
XLA Modules:
  0.0 299.5 jit_solution(5310468247853832980)
XLA Ops:
  0.0 1.3 slice.98
  2.7 0.9 slice.99
  4.5 3.0 %collective-permute-start.3 = (bf16[3,8449]{1,0:T(4,128)(2,1)S(1)}, bf16[3,8449]{1,0:T(4,128)(2,1)S(1)}, u32[]{:S(2)}, u32[]{:S(2)}) collective-permute-start(bf16[3,8449]{1,0:T(4,128)(2,1)S(1)} %pad_maximum_fusion.2), channel_id=1, source_target_pairs={{0,1},{1,2},{2,3},{3,4},{4,5},{5,6},{6,7},{7,8},{8,9},{9,10},{10,1... | collective-permute-start | bytes 152090 | tf_op jit(solution)/shard_map/ppermute | solution.py:23
  7.5 1.1 negate_multiply_fusion
  9.1 1.4 reshape.164.b_ref
  10.5 0.8 slice_convert_fusion.5
  12.1 1.4 broadcast_select_fusion.1
  13.5 1.2 collective-permute-start.6
  14.7 1.2 collective-permute-done.6
  16.0 1.3 collective-permute-start.7
  20.0 2.0 compare_convert_fusion.4
  22.1 0.9 copy.29.vis_ref
  24.4 0.8 fusion.20
  25.9 10.8 %shard_map.127 = bf16[8192,256]{1,0:T(8,128)(2,1)} custom-call(bf16[8,8192]{1,0:T(8,128)(2,1)} %concatenate.76.rim_ref, bf16[256,8192]{1,0:T(8,128)(2,1)} %x_ref.1, bf16[4,8192]{1,0:T(4,128)(2,1)} %w_ref.1, bf16[1,8192]{1,0:T(2,128)(2,1)} %reshape.164.b_ref, f32[3,256,1]{2,1,0:T(8,128)} %copy.29.vis_ref), custom_call_target="tpu_custom_call" | custom-call | flops 41943040 | bytes 8388608 | tf_op jit(solution)/shard_map/pallas_call | solution.py:66
  36.9 2.2 collective-permute-done.8
  39.2 2.3 collective-permute-start.9
  41.5 8.3 %fusion.7 = f32[1,128,64,128]{3,2,1,0:T(8,128)S(1)} fusion(bf16[256,128,64]{0,2,1:T(8,128)(2,1)} %bitcast.76, f32[128,256]{1,0:T(8,128)S(1)} %get-tuple-element.80, f32[256,128]{1,0:T(8,128)S(1)} %get-tuple-element.83), kind=kOutput, calls=%fused_computation.16 | convolution fusion | flops 545259520 | bytes 8650752 | tf_op jit(solution)/shard_map/hjn,jhp->hpn/dot_general | solution.py:161
  50.3 1.6 constant_dynamic-slice_fusion
  51.9 1.0 copy-done.1
  52.9 2.3 collective-permute-start.10
  55.5 3.3 %collective-permute-done.4 = f32[128]{0:T(128)S(1)} collective-permute-done((f32[128]{0:T(128)S(1)}, f32[128]{0:T(128)S(1)}, u32[]{:S(2)}, u32[]{:S(2)}) %collective-permute-start.4) | collective-permute-done | bytes 544 | tf_op jit(solution)/shard_map/ppermute | solution.py:261
  59.2 2.8 add_select_fusion
  62.0 3.1 %collective-permute-start.13 = (f32[64,64,128]{2,1,0:T(8,128)S(1)}, f32[64,64,128]{2,1,0:T(8,128)S(1)}, u32[]{:S(2)}, u32[]{:S(2)}) collective-permute-start(f32[64,64,128]{2,1,0:T(8,128)S(1)} %add_select_fusion), channel_id=1, source_target_pairs={{0,2},{1,3},{2,4},{3,5},{4,6},{5,7},{6,8},{7,9},{8,10},{9,11},{10,... | collective-permute-start | bytes 6291464 | tf_op jit(solution)/shard_map/ppermute | solution.py:174
  65.1 47.4 %collective-permute-done.13 = f32[64,64,128]{2,1,0:T(8,128)S(1)} collective-permute-done((f32[64,64,128]{2,1,0:T(8,128)S(1)}, f32[64,64,128]{2,1,0:T(8,128)S(1)}, u32[]{:S(2)}, u32[]{:S(2)}) %collective-permute-start.13) | collective-permute-done | bytes 2097184 | tf_op jit(solution)/shard_map/ppermute | solution.py:174
  112.5 1.9 collective-permute-start.14
  114.4 2.4 collective-permute-start.11
  116.9 45.3 %collective-permute-done.11 = f32[64]{0:T(128)S(1)} collective-permute-done((f32[64]{0:T(128)S(1)}, f32[64]{0:T(128)S(1)}, u32[]{:S(2)}, u32[]{:S(2)}) %collective-permute-start.11) | collective-permute-done | bytes 288 | tf_op jit(solution)/shard_map/ppermute | solution.py:174
  162.4 1.9 collective-permute-start.15
  164.9 1.9 collective-permute-start.12
  168.1 40.2 %collective-permute-done.12 = f32[64]{0:T(128)S(1)} collective-permute-done((f32[64]{0:T(128)S(1)}, f32[64]{0:T(128)S(1)}, u32[]{:S(2)}, u32[]{:S(2)}) %collective-permute-start.12) | collective-permute-done | bytes 288 | tf_op jit(solution)/shard_map/ppermute | solution.py:174
  208.4 1.9 collective-permute-start.16
  210.3 2.5 multiply_add_fusion.2
  213.5 3.6 %fusion.9 = bf16[64,64,128]{2,1,0:T(8,128)(2,1)} fusion(f32[64,64,128]{2,1,0:T(8,128)S(1)} %get-tuple-element.93, f32[64,64,128]{2,1,0:T(8,128)} %copy-done.3, f32[128,64,128]{2,1,0:T(8,128)} %copy-done.1, s32[]{:T(128)S(6)} %select_n.97, f32[64]{0:T(128)S(1)} %get-tuple-element.72, pred[]{:T(512)S(6)} %eq.54), kind=kLoop, calls=%fused_computation.25 | loop fusion | flops 2097152 | bytes 7340293 | tf_op jit(solution)/shard_map/jit(_where)/select_n | solution.py:272
  217.2 3.6 %collective-permute-start.17 = (bf16[64,64,128]{2,1,0:T(8,128)(2,1)}, bf16[64,64,128]{2,1,0:T(8,128)(2,1)S(1)}, u32[]{:S(2)}, u32[]{:S(2)}) collective-permute-start(bf16[64,64,128]{2,1,0:T(8,128)(2,1)} %fusion.9), channel_id=1, source_target_pairs={{0,1},{1,0},{2,3},{3,2},{4,5},{5,4},{6,7},{7,6},{8,9},{9,8},{10,11... | collective-permute-start | bytes 3145736 | tf_op jit(solution)/shard_map/ppermute | solution.py:272
  220.8 6.4 %copy.37 = bf16[256,8192]{0,1:T(8,128)(2,1)} copy(bf16[256,8192]{1,0:T(8,128)(2,1)} %param.16) | data formatting | bytes 8388608 | tf_op args[1]
  227.2 1.4 mul.307
  228.5 1.5 mul.308
  230.7 3.4 %copy.38.n_ref = f32[8192,1]{1,0:T(8,128)} copy(f32[8192,1]{0,1:T(1,128)} %bitcast.85) | data formatting | bytes 65536 | tf_op jit(solution)/shard_map/broadcast_in_dim | solution.py:102
  234.1 8.6 %copy.32.cum_col_ref = f32[128,256,1]{2,1,0:T(8,128)} copy(f32[128,256,1]{1,0,2:T(8,128)S(1)} %bitcast.80) | data formatting | bytes 262144 | tf_op jit(solution)/shard_map/broadcast_in_dim;squeeze | solution.py:148
  242.7 0.8 copy.31.seg_col_ref
  243.5 1.8 fusion.14.scores_ref
  245.3 19.7 %shard_map.128 = f32[8192,256]{1,0:T(8,128)} custom-call(f32[256,256]{1,0:T(8,128)} %fusion.14.scores_ref, s32[256,1]{1,0:T(8,128)} %copy.31.seg_col_ref, s32[1,256]{1,0:T(1,128)} %bitcast.86, f32[128,256,1]{2,1,0:T(8,128)} %copy.32.cum_col_ref, f32[128,256]{1,0:T(8,128)} %bitcast.81, f32[128,256]{1,0:T(8,128)} %bitcast.84, bf16[8192,256]{1,0:T(8,128)(2,1)} %shard_map.127), custom_call_target="tpu_custom_call" | custom-call | flops 1124073472 | bytes 12582912 | tf_op jit(solution)/shard_map/pallas_call | solution.py:125
  265.0 3.0 select_convert_fusion.1
  268.3 1.3 copy-done.2
  269.6 7.2 %copy_add_fusion = f32[256,128,64]{0,1,2:T(8,128)S(1)} fusion(f32[256,128,64]{0,2,1:T(8,128)S(1)} %bitcast.78, f32[256,128]{0,1:T(8,128)S(1)} %get-tuple-element.75, bf16[128,64,128]{2,1,0:T(8,128)(2,1)S(1)} %pad_maximum_fusion, bf16[256,256]{1,0:T(8,128)(2,1)S(1)} %multiply_convert_fusion.4), kind=kOutput, calls=%fused_computation.11 | convolution fusion | flops 541065216 | bytes 19070976 | tf_op jit(solution)/shard_map/in,hpn->ihp/dot_general | solution.py:169
  276.9 5.1 %copy.36 = f32[256,128,64]{0,2,1:T(8,128)S(1)} copy(f32[256,128,64]{0,1,2:T(8,128)S(1)} %copy_add_fusion) | data formatting | bytes 16777216 | tf_op jit(solution)/shard_map/add | solution.py:373
  282.0 7.5 %multiply_reduce_fusion = (f32[256]{0:T(256)S(1)}, f32[256,8192]{0,1:T(8,128)}) fusion(bf16[256,8192]{0,1:T(8,128)(2,1)} %copy.37, bf16[256,8192]{0,1:T(8,128)(2,1)S(1)} %bitcast.77, f32[8192]{0:T(1024)S(1)} %copy-done.8, f32[256,128,64]{0,2,1:T(8,128)S(1)} %copy.36), kind=kLoop, calls=%fused_computation.12 | loop fusion | flops 23068416 | bytes 25199616 | tf_op jit(solution)/shard_map/reduce_sum | solution.py:377
  290.0 9.5 %shard_map.129 = bf16[256,8192]{1,0:T(8,128)(2,1)} custom-call(f32[8192,256]{1,0:T(8,128)} %bitcast.79, f32[1,256]{1,0:T(1,128)} %bitcast.91, f32[8192,1]{1,0:T(8,128)} %copy.38.n_ref), custom_call_target="tpu_custom_call" | custom-call | flops 4194304 | bytes 12582912 | tf_op jit(solution)/shard_map/pallas_call | solution.py:91
  (90 shorter events, 12.2 us)
Async XLA Ops:
  0.0 23.0 %copy-start.7 = (bf16[256,256]{1,0:T(8,128)(2,1)S(1)}, bf16[256,256]{1,0:T(8,128)(2,1)}, u32[]{:S(2)}) copy-start(bf16[256,256]{1,0:T(8,128)(2,1)} %param.17) | copy-start | bytes 393220
  0.0 24.3 %copy-start.6 = (f32[128,256]{1,0:T(8,128)S(1)}, f32[128,256]{1,0:T(8,128)}, u32[]{:S(2)}) copy-start(f32[128,256]{1,0:T(8,128)} %param.18) | copy-start | bytes 393220
  0.0 24.3 %copy-start.13 = (f32[128]{0:T(128)S(1)}, f32[128]{0:T(128)}, u32[]{:S(2)}) copy-start(f32[128]{0:T(128)} %param.19) | copy-start | bytes 1540
  1.3 10.8 %collective-permute-start.5 = (s32[1]{0:T(128)}, s32[1]{0:T(128)}, u32[]{:S(2)}, u32[]{:S(2)}) collective-permute-start(s32[1]{0:T(128)} %slice.98), channel_id=1, source_target_pairs={{0,1},{1,0},{2,3},{3,2},{4,5},{5,4},{6,7},{7,6},{8,9},{9,8},{10,11... | collective-permute-start | bytes 20 | tf_op jit(solution)/shard_map/ppermute | solution.py:212
  4.5 11.4 %collective-permute-start.3 = (bf16[3,8449]{1,0:T(4,128)(2,1)S(1)}, bf16[3,8449]{1,0:T(4,128)(2,1)S(1)}, u32[]{:S(2)}, u32[]{:S(2)}) collective-permute-start(bf16[3,8449]{1,0:T(4,128)(2,1)S(1)} %pad_maximum_fusion.2), channel_id=1, source_target_pairs={{0,1},{1,2},{2,3},{3,4},{4,5},{5,6},{6,7},{7,8},{8,9},{9,10},{10,1... | collective-permute-start | bytes 152090 | tf_op jit(solution)/shard_map/ppermute | solution.py:23
  13.5 2.4 collective-permute-start.6
  16.0 20.7 %collective-permute-start.7 = (s32[4]{0:T(128)S(1)}, s32[4]{0:T(128)S(1)}, u32[]{:S(2)}, u32[]{:S(2)}) collective-permute-start(s32[4]{0:T(128)S(1)} %broadcast_select_fusion.2), channel_id=1, source_target_pairs={{0,4},{1,5},{2,6},{3,7},{4,0},{5,1},{6,2},{7,3},{8,12},{9,13},{10,... | collective-permute-start | bytes 56 | tf_op jit(solution)/shard_map/ppermute | solution.py:212
  36.7 2.4 collective-permute-start.8
  39.2 10.7 %collective-permute-start.9 = (s32[16]{0:T(128)S(1)}, s32[16]{0:T(128)S(1)}, u32[]{:S(2)}, u32[]{:S(2)}) collective-permute-start(s32[16]{0:T(128)S(1)} %broadcast_select_fusion.4), channel_id=1, source_target_pairs={{0,16},{1,17},{2,18},{3,19},{4,20},{5,21},{6,22},{7,23},{8,24},{9,... | collective-permute-start | bytes 200 | tf_op jit(solution)/shard_map/ppermute | solution.py:212
  50.3 2.6 copy-start.1
  52.9 6.3 %collective-permute-start.10 = (f32[64,64,128]{2,1,0:T(8,128)}, f32[64,64,128]{2,1,0:T(8,128)S(1)}, u32[]{:S(2)}, u32[]{:S(2)}) collective-permute-start(f32[64,64,128]{2,1,0:T(8,128)} %constant_dynamic-slice_fusion), channel_id=1, source_target_pairs={{0,1},{1,0},{2,3},{3,2},{4,5},{5,4},{6,7},{7,6},{8,9},{9,8},{10,11... | collective-permute-start | bytes 6291464 | tf_op jit(solution)/shard_map/ppermute | solution.py:261
  55.2 3.6 %collective-permute-start.4 = (f32[128]{0:T(128)S(1)}, f32[128]{0:T(128)S(1)}, u32[]{:S(2)}, u32[]{:S(2)}) collective-permute-start(f32[128]{0:T(128)S(1)} %get-tuple-element.78), channel_id=1, source_target_pairs={{0,1},{1,0},{2,3},{3,2},{4,5},{5,4},{6,7},{7,6},{8,9},{9,8},{10,11... | collective-permute-start | bytes 1544 | tf_op jit(solution)/shard_map/ppermute | solution.py:261
  55.4 178.7 %copy-start.5 = (f32[1,128,256]{2,1,0:T(8,128)}, f32[1,128,256]{2,1,0:T(8,128)S(1)}, u32[]{:S(2)}) copy-start(f32[1,128,256]{2,1,0:T(8,128)S(1)} %reduce_window_sum.31) | copy-start | bytes 393220
  58.9 154.7 %copy-start.11 = (f32[64]{0:T(128)}, f32[64]{0:T(128)S(1)}, u32[]{:S(2)}) copy-start(f32[64]{0:T(128)S(1)} %get-tuple-element.72) | copy-start | bytes 772
  59.2 2.8 copy-start.3
  62.0 50.5 %collective-permute-start.13 = (f32[64,64,128]{2,1,0:T(8,128)S(1)}, f32[64,64,128]{2,1,0:T(8,128)S(1)}, u32[]{:S(2)}, u32[]{:S(2)}) collective-permute-start(f32[64,64,128]{2,1,0:T(8,128)S(1)} %add_select_fusion), channel_id=1, source_target_pairs={{0,2},{1,3},{2,4},{3,5},{4,6},{5,7},{6,8},{7,9},{8,10},{9,11},{10,... | collective-permute-start | bytes 6291464 | tf_op jit(solution)/shard_map/ppermute | solution.py:174
  112.5 49.6 %collective-permute-start.14 = (f32[64,64,128]{2,1,0:T(8,128)S(1)}, f32[64,64,128]{2,1,0:T(8,128)S(1)}, u32[]{:S(2)}, u32[]{:S(2)}) collective-permute-start(f32[64,64,128]{2,1,0:T(8,128)S(1)} %collective-permute-done.13), channel_id=1, source_target_pairs={{0,2},{1,3},{2,4},{3,5},{4,6},{5,7},{6,8},{7,9},{8,10},{9,11},{10,... | collective-permute-start | bytes 6291464 | tf_op jit(solution)/shard_map/ppermute | solution.py:174
  114.4 47.7 %collective-permute-start.11 = (f32[64]{0:T(128)S(1)}, f32[64]{0:T(128)S(1)}, u32[]{:S(2)}, u32[]{:S(2)}) collective-permute-start(f32[64]{0:T(128)S(1)} %mul.260), channel_id=1, source_target_pairs={{0,2},{1,3},{2,4},{3,5},{4,6},{5,7},{6,8},{7,9},{8,10},{9,11},{10,... | collective-permute-start | bytes 776 | tf_op jit(solution)/shard_map/ppermute | solution.py:174
  162.4 47.9 %copy-start.4 = (f32[64,64,128]{2,1,0:T(8,128)}, f32[64,64,128]{2,1,0:T(8,128)S(1)}, u32[]{:S(2)}) copy-start(f32[64,64,128]{2,1,0:T(8,128)S(1)} %multiply_add_fusion.3) | copy-start | bytes 6291460
  162.4 47.9 %collective-permute-start.15 = (f32[64,64,128]{2,1,0:T(8,128)S(1)}, f32[64,64,128]{2,1,0:T(8,128)}, u32[]{:S(2)}, u32[]{:S(2)}) collective-permute-start(f32[64,64,128]{2,1,0:T(8,128)S(1)} %multiply_add_fusion.3), channel_id=1, source_target_pairs={{0,4},{1,5},{2,6},{3,7},{4,8},{5,9},{6,10},{7,11},{8,12},{9,13},{1... | collective-permute-start | bytes 6291464 | tf_op jit(solution)/shard_map/ppermute | solution.py:174
  164.9 43.5 %collective-permute-start.12 = (f32[64]{0:T(128)S(1)}, f32[64]{0:T(128)S(1)}, u32[]{:S(2)}, u32[]{:S(2)}) collective-permute-start(f32[64]{0:T(128)S(1)} %collective-permute-done.11), channel_id=1, source_target_pairs={{0,2},{1,3},{2,4},{3,5},{4,6},{5,7},{6,8},{7,9},{8,10},{9,11},{10,... | collective-permute-start | bytes 776 | tf_op jit(solution)/shard_map/ppermute | solution.py:174
  208.4 5.2 %collective-permute-start.16 = (f32[64]{0:T(128)S(1)}, f32[64]{0:T(128)S(1)}, u32[]{:S(2)}, u32[]{:S(2)}) collective-permute-start(f32[64]{0:T(128)S(1)} %mul.296), channel_id=1, source_target_pairs={{0,4},{1,5},{2,6},{3,7},{4,8},{5,9},{6,10},{7,11},{8,12},{9,13},{1... | collective-permute-start | bytes 776 | tf_op jit(solution)/shard_map/ppermute | solution.py:174
  217.2 12.9 %copy-start.10 = (bf16[8192]{0:T(1024)(128)(2,1)S(1)}, bf16[8192]{0:T(1024)(128)(2,1)}, u32[]{:S(2)}) copy-start(bf16[8192]{0:T(1024)(128)(2,1)} %param.26) | copy-start | bytes 49156
  217.2 47.8 %collective-permute-start.17 = (bf16[64,64,128]{2,1,0:T(8,128)(2,1)}, bf16[64,64,128]{2,1,0:T(8,128)(2,1)S(1)}, u32[]{:S(2)}, u32[]{:S(2)}) collective-permute-start(bf16[64,64,128]{2,1,0:T(8,128)(2,1)} %fusion.9), channel_id=1, source_target_pairs={{0,1},{1,0},{2,3},{3,2},{4,5},{5,4},{6,7},{7,6},{8,9},{9,8},{10,11... | collective-permute-start | bytes 3145736 | tf_op jit(solution)/shard_map/ppermute | solution.py:272
  234.1 8.6 %copy-start.9 = (s32[256]{0:T(256)S(1)}, s32[256]{0:T(256)}, u32[]{:S(2)}) copy-start(s32[256]{0:T(256)} %param.27) | copy-start | bytes 3076
  245.3 19.7 %copy-start.12 = (f32[64]{0:T(128)S(1)}, f32[64]{0:T(128)}, u32[]{:S(2)}) copy-start(f32[64]{0:T(128)} %copy-done.11) | copy-start | bytes 772
  265.0 4.6 %copy-start.2 = (f32[8192,256]{1,0:T(8,128)S(1)}, f32[8192,256]{1,0:T(8,128)}, u32[]{:S(2)}) copy-start(f32[8192,256]{1,0:T(8,128)} %shard_map.128) | copy-start | bytes 25165828
  276.8 5.1 %copy-start = (bf16[8192,256]{1,0:T(8,128)(2,1)S(1)}, bf16[8192,256]{1,0:T(8,128)(2,1)}, u32[]{:S(2)}) copy-start(bf16[8192,256]{1,0:T(8,128)(2,1)} %shard_map.127) | copy-start | bytes 12582916
  276.8 5.1 %copy-start.8 = (f32[8192]{0:T(1024)S(1)}, f32[8192]{0:T(1024)}, u32[]{:S(2)}) copy-start(f32[8192]{0:T(1024)} %mul.308) | copy-start | bytes 98308

commit v14 on v13

--- a/solution.py
+++ b/solution.py
@@ -106,20 +106,18 @@
     tokens = scores_ref.shape[0]
     row = lax.broadcasted_iota(jnp.int32, (tokens, tokens), 0)
     col = lax.broadcasted_iota(jnp.int32, (tokens, tokens), 1)
-    visible = jnp.logical_and(row >= col, seg_col_ref[...] == seg_row_ref[...])
+    visible = jnp.logical_and(col >= row, seg_col_ref[...] == seg_row_ref[...])
     scores = scores_ref[...]
     for k in range(cum_row_ref.shape[0]):
-        exponent = jnp.where(visible, cum_col_ref[k] - cum_row_ref[k : k + 1, :], -jnp.inf)
-        mixing = (scores * jnp.exp(exponent) * step_ref[k : k + 1, :]).astype(jnp.bfloat16)
+        exponent = jnp.where(visible, cum_row_ref[k : k + 1, :] - cum_col_ref[k], -jnp.inf)
+        mixing = (scores * jnp.exp(exponent) * step_ref[k]).astype(jnp.bfloat16)
         rows = pl.ds(k * HEAD_DIM, HEAD_DIM)
-        o_ref[rows, :] = lax.dot_general(
-            x_ref[rows, :], mixing, (((1,), (1,)), ((), ())), preferred_element_type=jnp.float32
-        )
+        o_ref[rows, :] = jnp.dot(x_ref[rows, :], mixing, preferred_element_type=jnp.float32)
 
 
 def mixing_part(x_group, b_group, c_group, step_size, cum_decay, segment):
     tokens, heads, width = x_group.shape
-    scores = jnp.einsum("in,jn->ij", c_group, b_group, preferred_element_type=jnp.float32)
+    scores = jnp.einsum("jn,in->ji", b_group, c_group, preferred_element_type=jnp.float32)
     x_t = x_group.reshape(tokens, heads * width).T
     per = 8 if heads % 8 == 0 else heads
     out = pl.pallas_call(
@@ -132,7 +130,7 @@
             pl.BlockSpec((1, tokens), lambda g: (0, 0)),
             pl.BlockSpec((per, tokens, 1), lambda g: (g, 0, 0)),
             pl.BlockSpec((per, tokens), lambda g: (g, 0)),
-            pl.BlockSpec((per, tokens), lambda g: (g, 0)),
+            pl.BlockSpec((per, tokens, 1), lambda g: (g, 0, 0)),
             pl.BlockSpec((per * width, tokens), lambda g: (g, 0)),
         ],
         out_specs=pl.BlockSpec((per * width, tokens), lambda g: (g, 0)),
@@ -147,7 +145,7 @@
         segment[None, :],
         cum_decay[:, :, None],
         cum_decay,
-        step_size,
+        step_size[:, :, None],
         x_t,
     )
     return out.T.reshape(tokens, heads, width)

time: 301 us -> 312 us (1.037)
  local copies, waits for them, and re-layouts: 39.1 us -> 47.6 us
  Pallas kernels: 40 us -> 44.1 us
    another operation x7 -> x9, local copies, waits for them, and re-layouts: 0.65 us -> 10.2 us  [the longest x1 9.54 us: mixing_part(): step_size[:, :, None]]
    pallas_call x1, Pallas kernels: 19.7 us -> 23.9 us  [mixing_part(): pl.pallas_call(mixing_kernel, out_shape=jax.ShapeDtypeStruct((heads * wid...]
    unnamed x29 -> x30, local copies, waits for them, and re-layouts: 8.78 us -> 9.74 us
  transfers between devices with their start and end apart: 15 -> 15, of which waited for: 8 -> 8; matrix products, arithmetic and copies ran while one was open for 18% -> 19% of each run, Pallas kernels for 10% -> 11%
where the time goes in v14:
time: 312 us; the launch traced here: 311 us
  waiting for transfers between devices  140 us (45%)
  local copies, waits for them, and re-layouts  47.6 us (15%)
  Pallas kernels  44.1 us (14%)
  other arithmetic  32.1 us (10%)
  starting transfers between devices  27.8 us (9%)
  matrix products  16.4 us (5%)
    ppermute x6, waiting for transfers between devices, shifted(): lax.ppermute(value, axis, [(s, s + steps) for s in range(count - steps)])  134 us
    pallas_call x1, Pallas kernels, mixing_part(): pl.pallas_call(mixing_kernel, out_shape=jax.ShapeDtypeStruct((heads * wid...  23.9 us
    ppermute x6, starting transfers between devices, shifted(): lax.ppermute(value, axis, [(s, s + steps) for s in range(count - steps)])  13.2 us
    pallas_call x1, Pallas kernels, conv_rows(): pl.pallas_call(conv_rows_kernel, out_shape=jax.ShapeDtypeStruct((width, r...  10.8 us
    unnamed x30, local copies, waits for them, and re-layouts  9.74 us
    another operation x1, local copies, waits for them, and re-layouts, mixing_part(): step_size[:, :, None]  9.54 us
    pallas_call x1, Pallas kernels, scale_rows(): pl.pallas_call(scale_rows_kernel, out_shape=jax.ShapeDtypeStruct((rows, w...  9.48 us
    another operation x1, local copies, waits for them, and re-layouts, mixing_part(): cum_decay[:, :, None]  8.63 us
  transfers between devices with their start and end apart: 15, of which 8 were waited for; matrix products, arithmetic and copies ran while one was open for 19% of the time, Pallas kernels for 11%

profile of v14, /device:TPU:9, one launch (start us, length us, event | category | flops | bytes accessed | tf_op | source)
XLA Modules:
  0.0 310.7 jit_solution(14420560265949611347)
XLA Ops:
  0.0 1.3 slice.98
  2.7 0.9 slice.99
  4.5 3.0 collective-permute-start.3
  7.5 1.0 copy.39
  8.5 0.8 negate_multiply_fusion
  9.5 1.3 reshape.164.b_ref
  10.9 0.8 slice_convert_fusion.5
  12.4 1.4 broadcast_select_fusion.1
  13.8 1.2 collective-permute-start.6
  15.0 1.2 collective-permute-done.6
  16.3 1.3 collective-permute-start.7
  20.4 2.1 compare_convert_fusion.4
  22.5 0.9 copy.45.vis_ref
  26.7 10.8 %shard_map.127 = bf16[8192,256]{1,0:T(8,128)(2,1)} custom-call(bf16[8,8192]{1,0:T(8,128)(2,1)} %concatenate.76.rim_ref, bf16[256,8192]{1,0:T(8,128)(2,1)} %x_ref.1, bf16[4,8192]{1,0:T(4,128)(2,1)} %w_ref.1, bf16[1,8192]{1,0:T(2,128)(2,1)} %reshape.164.b_ref, f32[3,256,1]{2,1,0:T(8,128)} %copy.45.vis_ref), custom_call_target="tpu_custom_call" | custom-call | flops 41943040 | bytes 8388608 | tf_op jit(solution)/shard_map/pallas_call | solution.py:66
  37.8 2.2 collective-permute-done.8
  40.1 2.3 collective-permute-start.9
  42.4 8.3 %fusion.7 = f32[1,128,64,128]{3,2,1,0:T(8,128)S(1)} fusion(bf16[256,128,64]{0,2,1:T(8,128)(2,1)} %bitcast.77, f32[128,256]{1,0:T(8,128)S(1)} %copy.46, f32[256,128]{1,0:T(8,128)S(1)} %get-tuple-element.83), kind=kOutput, calls=%fused_computation.16 | convolution fusion | flops 545259520 | bytes 8650752 | tf_op jit(solution)/shard_map/hjn,jhp->hpn/dot_general | solution.py:159
  51.2 1.6 constant_dynamic-slice_fusion
  52.7 1.0 copy-done.1
  53.7 2.3 collective-permute-start.10
  56.7 2.9 collective-permute-done.4
  60.0 2.8 add_select_fusion
  62.8 3.1 %collective-permute-start.13 = (f32[64,64,128]{2,1,0:T(8,128)S(1)}, f32[64,64,128]{2,1,0:T(8,128)S(1)}, u32[]{:S(2)}, u32[]{:S(2)}) collective-permute-start(f32[64,64,128]{2,1,0:T(8,128)S(1)} %add_select_fusion), channel_id=1, source_target_pairs={{0,2},{1,3},{2,4},{3,5},{4,6},{5,7},{6,8},{7,9},{8,10},{9,11},{10,... | collective-permute-start | bytes 6291464 | tf_op jit(solution)/shard_map/ppermute | solution.py:172
  65.9 47.4 %collective-permute-done.13 = f32[64,64,128]{2,1,0:T(8,128)S(1)} collective-permute-done((f32[64,64,128]{2,1,0:T(8,128)S(1)}, f32[64,64,128]{2,1,0:T(8,128)S(1)}, u32[]{:S(2)}, u32[]{:S(2)}) %collective-permute-start.13) | collective-permute-done | bytes 2097184 | tf_op jit(solution)/shard_map/ppermute | solution.py:172
  113.3 1.9 collective-permute-start.14
  115.3 2.4 collective-permute-start.11
  117.7 45.3 %collective-permute-done.11 = f32[64]{0:T(128)S(1)} collective-permute-done((f32[64]{0:T(128)S(1)}, f32[64]{0:T(128)S(1)}, u32[]{:S(2)}, u32[]{:S(2)}) %collective-permute-start.11) | collective-permute-done | bytes 288 | tf_op jit(solution)/shard_map/ppermute | solution.py:172
  163.2 1.9 collective-permute-start.15
  165.7 1.9 collective-permute-start.12
  169.0 40.2 %collective-permute-done.12 = f32[64]{0:T(128)S(1)} collective-permute-done((f32[64]{0:T(128)S(1)}, f32[64]{0:T(128)S(1)}, u32[]{:S(2)}, u32[]{:S(2)}) %collective-permute-start.12) | collective-permute-done | bytes 288 | tf_op jit(solution)/shard_map/ppermute | solution.py:172
  209.2 1.9 collective-permute-start.16
  211.1 2.5 multiply_add_fusion.2
  214.4 3.6 %fusion.9 = bf16[64,64,128]{2,1,0:T(8,128)(2,1)} fusion(f32[64,64,128]{2,1,0:T(8,128)S(1)} %get-tuple-element.93, f32[64,64,128]{2,1,0:T(8,128)} %copy-done.3, f32[128,64,128]{2,1,0:T(8,128)} %copy-done.1, s32[]{:T(128)S(6)} %select_n.97, f32[64]{0:T(128)S(1)} %get-tuple-element.72, pred[]{:T(512)S(6)} %eq.54), kind=kLoop, calls=%fused_computation.25 | loop fusion | flops 2097152 | bytes 7340293 | tf_op jit(solution)/shard_map/jit(_where)/select_n | solution.py:270
  218.0 3.6 %collective-permute-start.17 = (bf16[64,64,128]{2,1,0:T(8,128)(2,1)}, bf16[64,64,128]{2,1,0:T(8,128)(2,1)S(1)}, u32[]{:S(2)}, u32[]{:S(2)}) collective-permute-start(bf16[64,64,128]{2,1,0:T(8,128)(2,1)} %fusion.9), channel_id=1, source_target_pairs={{0,1},{1,0},{2,3},{3,2},{4,5},{5,4},{6,7},{7,6},{8,9},{9,8},{10,11... | collective-permute-start | bytes 3145736 | tf_op jit(solution)/shard_map/ppermute | solution.py:270
  221.6 6.4 %copy.57 = bf16[256,8192]{0,1:T(8,128)(2,1)} copy(bf16[256,8192]{1,0:T(8,128)(2,1)} %param.16) | data formatting | bytes 8388608 | tf_op args[1]
  228.7 2.7 copy.58.n_ref
  231.5 1.0 copy.54
  232.5 8.6 %copy.50.cum_col_ref = f32[128,256,1]{2,1,0:T(8,128)} copy(f32[128,256,1]{1,0,2:T(8,128)S(1)} %bitcast.81) | data formatting | bytes 262144 | tf_op jit(solution)/shard_map/broadcast_in_dim;squeeze | solution.py:146
  241.1 9.5 %copy.51.step_ref = f32[128,256,1]{2,1,0:T(8,128)} copy(f32[128,256,1]{0,1,2:T(8,128)} %bitcast.83) | data formatting | bytes 262144 | tf_op jit(solution)/shard_map/broadcast_in_dim;squeeze | solution.py:148
  250.7 0.8 copy.49.seg_col_ref
  251.5 0.9 fusion.16.scores_ref
  252.4 23.9 %shard_map.128 = f32[8192,256]{1,0:T(8,128)} custom-call(f32[256,256]{1,0:T(8,128)} %fusion.16.scores_ref, s32[256,1]{1,0:T(8,128)} %copy.49.seg_col_ref, s32[1,256]{1,0:T(1,128)} %bitcast.86, f32[128,256,1]{2,1,0:T(8,128)} %copy.50.cum_col_ref, f32[128,256]{1,0:T(8,128)} %bitcast.82, f32[128,256,1]{2,1,0:T(8,128)} %copy.51.step_ref, ...), custom_call_target="tpu_custom_call" | custom-call | flops 1124073472 | bytes 12582912 | tf_op jit(solution)/shard_map/pallas_call | solution.py:123
  276.2 3.0 select_convert_fusion.1
  279.5 1.3 copy-done.2
  280.9 7.2 %copy_add_fusion = f32[256,128,64]{0,1,2:T(8,128)S(1)} fusion(f32[256,128,64]{0,2,1:T(8,128)S(1)} %bitcast.79, f32[256,128]{0,1:T(8,128)S(1)} %copy.54, bf16[128,64,128]{2,1,0:T(8,128)(2,1)S(1)} %pad_maximum_fusion, bf16[256,256]{1,0:T(8,128)(2,1)S(1)} %multiply_convert_fusion.4), kind=kOutput, calls=%fused_computation.11 | convolution fusion | flops 541065216 | bytes 19070976 | tf_op jit(solution)/shard_map/in,hpn->ihp/dot_general | solution.py:167
  288.1 5.1 %copy.56 = f32[256,128,64]{0,2,1:T(8,128)S(1)} copy(f32[256,128,64]{0,1,2:T(8,128)S(1)} %copy_add_fusion) | data formatting | bytes 16777216 | tf_op jit(solution)/shard_map/add | solution.py:371
  293.2 7.5 %multiply_reduce_fusion = (f32[256]{0:T(256)S(1)}, f32[256,8192]{0,1:T(8,128)}) fusion(bf16[256,8192]{0,1:T(8,128)(2,1)} %copy.57, bf16[256,8192]{0,1:T(8,128)(2,1)S(1)} %bitcast.78, f32[8192]{0:T(1024)S(1)} %copy-done.9, f32[256,128,64]{0,2,1:T(8,128)S(1)} %copy.56), kind=kLoop, calls=%fused_computation.12 | loop fusion | flops 23068416 | bytes 25199616 | tf_op jit(solution)/shard_map/reduce_sum | solution.py:375
  301.2 9.5 %shard_map.129 = bf16[256,8192]{1,0:T(8,128)(2,1)} custom-call(f32[8192,256]{1,0:T(8,128)} %bitcast.80, f32[1,256]{1,0:T(1,128)} %bitcast.91, f32[8192,1]{1,0:T(8,128)} %copy.58.n_ref), custom_call_target="tpu_custom_call" | custom-call | flops 4194304 | bytes 12582912 | tf_op jit(solution)/shard_map/pallas_call | solution.py:91
  (93 shorter events, 13.7 us)
Async XLA Ops:
  0.0 25.1 %copy-start.8 = (bf16[256,256]{1,0:T(8,128)(2,1)S(1)}, bf16[256,256]{1,0:T(8,128)(2,1)}, u32[]{:S(2)}) copy-start(bf16[256,256]{1,0:T(8,128)(2,1)} %param.17) | copy-start | bytes 393220
  0.0 24.2 %copy-start.12 = (f32[128]{0:T(128)S(1)}, f32[128]{0:T(128)}, u32[]{:S(2)}) copy-start(f32[128]{0:T(128)} %param.19) | copy-start | bytes 1540
  1.3 11.1 %collective-permute-start.5 = (s32[1]{0:T(128)}, s32[1]{0:T(128)}, u32[]{:S(2)}, u32[]{:S(2)}) collective-permute-start(s32[1]{0:T(128)} %slice.98), channel_id=1, source_target_pairs={{0,1},{1,0},{2,3},{3,2},{4,5},{5,4},{6,7},{7,6},{8,9},{9,8},{10,11... | collective-permute-start | bytes 20 | tf_op jit(solution)/shard_map/ppermute | solution.py:210
  4.5 11.7 %collective-permute-start.3 = (bf16[3,8449]{1,0:T(4,128)(2,1)S(1)}, bf16[3,8449]{1,0:T(4,128)(2,1)S(1)}, u32[]{:S(2)}, u32[]{:S(2)}) collective-permute-start(bf16[3,8449]{1,0:T(4,128)(2,1)S(1)} %pad_maximum_fusion.2), channel_id=1, source_target_pairs={{0,1},{1,2},{2,3},{3,4},{4,5},{5,6},{6,7},{7,8},{8,9},{9,10},{10,1... | collective-permute-start | bytes 152090 | tf_op jit(solution)/shard_map/ppermute | solution.py:23
  13.8 2.4 collective-permute-start.6
  16.3 21.2 %collective-permute-start.7 = (s32[4]{0:T(128)S(1)}, s32[4]{0:T(128)S(1)}, u32[]{:S(2)}, u32[]{:S(2)}) collective-permute-start(s32[4]{0:T(128)S(1)} %broadcast_select_fusion.2), channel_id=1, source_target_pairs={{0,4},{1,5},{2,6},{3,7},{4,0},{5,1},{6,2},{7,3},{8,12},{9,13},{10,... | collective-permute-start | bytes 56 | tf_op jit(solution)/shard_map/ppermute | solution.py:210
  37.6 2.4 collective-permute-start.8
  40.1 10.7 %collective-permute-start.9 = (s32[16]{0:T(128)S(1)}, s32[16]{0:T(128)S(1)}, u32[]{:S(2)}, u32[]{:S(2)}) collective-permute-start(s32[16]{0:T(128)S(1)} %broadcast_select_fusion.4), channel_id=1, source_target_pairs={{0,16},{1,17},{2,18},{3,19},{4,20},{5,21},{6,22},{7,23},{8,24},{9,... | collective-permute-start | bytes 200 | tf_op jit(solution)/shard_map/ppermute | solution.py:210
  51.2 2.6 copy-start.1
  53.7 6.3 %collective-permute-start.10 = (f32[64,64,128]{2,1,0:T(8,128)}, f32[64,64,128]{2,1,0:T(8,128)S(1)}, u32[]{:S(2)}, u32[]{:S(2)}) collective-permute-start(f32[64,64,128]{2,1,0:T(8,128)} %constant_dynamic-slice_fusion), channel_id=1, source_target_pairs={{0,1},{1,0},{2,3},{3,2},{4,5},{5,4},{6,7},{7,6},{8,9},{9,8},{10,11... | collective-permute-start | bytes 6291464 | tf_op jit(solution)/shard_map/ppermute | solution.py:259
  56.0 3.6 %collective-permute-start.4 = (f32[128]{0:T(128)S(1)}, f32[128]{0:T(128)S(1)}, u32[]{:S(2)}, u32[]{:S(2)}) collective-permute-start(f32[128]{0:T(128)S(1)} %get-tuple-element.78), channel_id=1, source_target_pairs={{0,1},{1,0},{2,3},{3,2},{4,5},{5,4},{6,7},{7,6},{8,9},{9,8},{10,11... | collective-permute-start | bytes 1544 | tf_op jit(solution)/shard_map/ppermute | solution.py:259
  56.7 175.8 %copy-start.5 = (f32[1,128,256]{2,1,0:T(8,128)}, f32[1,128,256]{2,1,0:T(8,128)S(1)}, u32[]{:S(2)}) copy-start(f32[1,128,256]{2,1,0:T(8,128)S(1)} %reduce_window_sum.31) | copy-start | bytes 393220
  60.0 2.8 copy-start.3
  62.8 50.5 %collective-permute-start.13 = (f32[64,64,128]{2,1,0:T(8,128)S(1)}, f32[64,64,128]{2,1,0:T(8,128)S(1)}, u32[]{:S(2)}, u32[]{:S(2)}) collective-permute-start(f32[64,64,128]{2,1,0:T(8,128)S(1)} %add_select_fusion), channel_id=1, source_target_pairs={{0,2},{1,3},{2,4},{3,5},{4,6},{5,7},{6,8},{7,9},{8,10},{9,11},{10,... | collective-permute-start | bytes 6291464 | tf_op jit(solution)/shard_map/ppermute | solution.py:172
  113.3 49.6 %collective-permute-start.14 = (f32[64,64,128]{2,1,0:T(8,128)S(1)}, f32[64,64,128]{2,1,0:T(8,128)S(1)}, u32[]{:S(2)}, u32[]{:S(2)}) collective-permute-start(f32[64,64,128]{2,1,0:T(8,128)S(1)} %collective-permute-done.13), channel_id=1, source_target_pairs={{0,2},{1,3},{2,4},{3,5},{4,6},{5,7},{6,8},{7,9},{8,10},{9,11},{10,... | collective-permute-start | bytes 6291464 | tf_op jit(solution)/shard_map/ppermute | solution.py:172
  115.3 47.7 %collective-permute-start.11 = (f32[64]{0:T(128)S(1)}, f32[64]{0:T(128)S(1)}, u32[]{:S(2)}, u32[]{:S(2)}) collective-permute-start(f32[64]{0:T(128)S(1)} %mul.260), channel_id=1, source_target_pairs={{0,2},{1,3},{2,4},{3,5},{4,6},{5,7},{6,8},{7,9},{8,10},{9,11},{10,... | collective-permute-start | bytes 776 | tf_op jit(solution)/shard_map/ppermute | solution.py:172
  163.2 47.9 %copy-start.4 = (f32[64,64,128]{2,1,0:T(8,128)}, f32[64,64,128]{2,1,0:T(8,128)S(1)}, u32[]{:S(2)}) copy-start(f32[64,64,128]{2,1,0:T(8,128)S(1)} %multiply_add_fusion.3) | copy-start | bytes 6291460
  163.2 47.9 %collective-permute-start.15 = (f32[64,64,128]{2,1,0:T(8,128)S(1)}, f32[64,64,128]{2,1,0:T(8,128)}, u32[]{:S(2)}, u32[]{:S(2)}) collective-permute-start(f32[64,64,128]{2,1,0:T(8,128)S(1)} %multiply_add_fusion.3), channel_id=1, source_target_pairs={{0,4},{1,5},{2,6},{3,7},{4,8},{5,9},{6,10},{7,11},{8,12},{9,13},{1... | collective-permute-start | bytes 6291464 | tf_op jit(solution)/shard_map/ppermute | solution.py:172
  165.7 43.5 %collective-permute-start.12 = (f32[64]{0:T(128)S(1)}, f32[64]{0:T(128)S(1)}, u32[]{:S(2)}, u32[]{:S(2)}) collective-permute-start(f32[64]{0:T(128)S(1)} %collective-permute-done.11), channel_id=1, source_target_pairs={{0,2},{1,3},{2,4},{3,5},{4,6},{5,7},{6,8},{7,9},{8,10},{9,11},{10,... | collective-permute-start | bytes 776 | tf_op jit(solution)/shard_map/ppermute | solution.py:172
  209.2 5.2 %collective-permute-start.16 = (f32[64]{0:T(128)S(1)}, f32[64]{0:T(128)S(1)}, u32[]{:S(2)}, u32[]{:S(2)}) collective-permute-start(f32[64]{0:T(128)S(1)} %mul.296), channel_id=1, source_target_pairs={{0,4},{1,5},{2,6},{3,7},{4,8},{5,9},{6,10},{7,11},{8,12},{9,13},{1... | collective-permute-start | bytes 776 | tf_op jit(solution)/shard_map/ppermute | solution.py:172
  218.0 10.0 %copy-start.13 = (f32[128]{0:T(128)S(1)}, f32[128]{0:T(128)}, u32[]{:S(2)}) copy-start(f32[128]{0:T(128)} %param.21) | copy-start | bytes 1540
  218.0 10.8 %copy-start.11 = (bf16[8192]{0:T(1024)(128)(2,1)S(1)}, bf16[8192]{0:T(1024)(128)(2,1)}, u32[]{:S(2)}) copy-start(bf16[8192]{0:T(1024)(128)(2,1)} %param.26) | copy-start | bytes 49156
  218.0 58.2 %collective-permute-start.17 = (bf16[64,64,128]{2,1,0:T(8,128)(2,1)}, bf16[64,64,128]{2,1,0:T(8,128)(2,1)S(1)}, u32[]{:S(2)}, u32[]{:S(2)}) collective-permute-start(bf16[64,64,128]{2,1,0:T(8,128)(2,1)} %fusion.9), channel_id=1, source_target_pairs={{0,1},{1,0},{2,3},{3,2},{4,5},{5,4},{6,7},{7,6},{8,9},{9,8},{10,11... | collective-permute-start | bytes 3145736 | tf_op jit(solution)/shard_map/ppermute | solution.py:270
  241.1 9.5 %copy-start.10 = (s32[256]{0:T(256)S(1)}, s32[256]{0:T(256)}, u32[]{:S(2)}) copy-start(s32[256]{0:T(256)} %param.27) | copy-start | bytes 3076
  241.1 10.3 %copy-start.6 = (bf16[1,256,128]{2,1,0:T(8,128)(2,1)S(1)}, bf16[1,256,128]{2,1,0:T(8,128)(2,1)}, u32[]{:S(2)}) copy-start(bf16[1,256,128]{2,1,0:T(8,128)(2,1)} %get-tuple-element.60) | copy-start | bytes 196612
  241.1 10.3 %copy-start.7 = (bf16[1,256,128]{2,1,0:T(8,128)(2,1)S(1)}, bf16[1,256,128]{2,1,0:T(8,128)(2,1)}, u32[]{:S(2)}) copy-start(bf16[1,256,128]{2,1,0:T(8,128)(2,1)} %get-tuple-element.59) | copy-start | bytes 196612
  276.2 4.6 %copy-start.2 = (f32[8192,256]{1,0:T(8,128)S(1)}, f32[8192,256]{1,0:T(8,128)}, u32[]{:S(2)}) copy-start(f32[8192,256]{1,0:T(8,128)} %shard_map.128) | copy-start | bytes 25165828
  288.1 5.1 %copy-start = (bf16[8192,256]{1,0:T(8,128)(2,1)S(1)}, bf16[8192,256]{1,0:T(8,128)(2,1)}, u32[]{:S(2)}) copy-start(bf16[8192,256]{1,0:T(8,128)(2,1)} %shard_map.127) | copy-start | bytes 12582916
  288.1 5.1 %copy-start.9 = (f32[8192]{0:T(1024)S(1)}, f32[8192]{0:T(1024)}, u32[]{:S(2)}) copy-start(f32[8192]{0:T(1024)} %mul.308) | copy-start | bytes 98308

commit v15 on v9

--- a/solution.py
+++ b/solution.py
@@ -87,7 +87,7 @@
 
 def scale_rows(gated, scale, gain):
     rows, width = gated.shape
-    tile = min(width, 1024)
+    tile = min(width, 2048)
     return pl.pallas_call(
         scale_rows_kernel,
         out_shape=jax.ShapeDtypeStruct((rows, width), jnp.bfloat16),

time: 252 us -> 250 us (level)
  no operation moved by 1% of the time
where the time goes in v15:
time: 250 us; the launch traced here: 249 us
  waiting for transfers between devices  131 us (52%)
  other arithmetic  28.3 us (11%)
  starting transfers between devices  28 us (11%)
  local copies, waits for them, and re-layouts  21.9 us (9%)
  Pallas kernels  18.7 us (7%)
  matrix products  18.6 us (7%)
    ppermute x6, waiting for transfers between devices, shifted(): lax.ppermute(value, axis, [(s, s + steps) for s in range(count - steps)])  124 us
    ppermute x6, starting transfers between devices, shifted(): lax.ppermute(value, axis, [(s, s + steps) for s in range(count - steps)])  13.3 us
    pallas_call x1, Pallas kernels, conv_rows(): pl.pallas_call(conv_rows_kernel, out_shape=jax.ShapeDtypeStruct((width, r...  10.8 us
    unnamed x20, local copies, waits for them, and re-layouts  10.3 us
    dot_general x1, matrix products, mixing_part(): jnp.einsum('hij,jhp->ihp', mixing, x_group, preferred_element_type=jnp.fl...  8.86 us
    dot_general x1, matrix products, state_part(): jnp.einsum('hjn,jhp->hpn', weighted, x_group, preferred_element_type=jnp....  8.34 us
    pallas_call x1, Pallas kernels, scale_rows(): pl.pallas_call(scale_rows_kernel, out_shape=jax.ShapeDtypeStruct((rows, w...  7.87 us
    reduce_sum x1, other arithmetic, local(): local_sq = jnp.sum(gated * gated, axis=1)  5.72 us
  transfers between devices with their start and end apart: 15, of which 8 were waited for; matrix products, arithmetic and copies ran while one was open for 19% of the time, Pallas kernels for 4%

profile of v15, /device:TPU:9, one launch (start us, length us, event | category | flops | bytes accessed | tf_op | source)
XLA Modules:
  0.0 249.1 jit_solution(16709259491406586415)
XLA Ops:
  0.0 1.3 slice.98
  2.6 0.9 slice.99
  4.5 3.0 %collective-permute-start.3 = (bf16[3,8449]{1,0:T(4,128)(2,1)S(1)}, bf16[3,8449]{1,0:T(4,128)(2,1)S(1)}, u32[]{:S(2)}, u32[]{:S(2)}) collective-permute-start(bf16[3,8449]{1,0:T(4,128)(2,1)S(1)} %pad_maximum_fusion.1), channel_id=1, source_target_pairs={{0,1},{1,2},{2,3},{3,4},{4,5},{5,6},{6,7},{7,8},{8,9},{9,10},{10,1... | collective-permute-start | bytes 152090 | tf_op jit(solution)/shard_map/ppermute | solution.py:23
  7.5 1.0 copy.21
  8.5 0.8 negate_multiply_fusion
  9.4 1.3 reshape.210.b_ref
  10.8 0.8 slice_convert_fusion.5
  12.3 1.4 broadcast_select_fusion.1
  13.7 1.2 collective-permute-start.6
  14.9 1.2 collective-permute-done.6
  16.2 1.3 collective-permute-start.7
  18.2 0.8 pad_add_fusion
  20.2 2.0 compare_convert_fusion.4
  22.3 0.9 copy.25.vis_ref
  23.2 1.5 multiply_convert_fusion.6
  24.9 0.8 fusion.35
  26.4 10.8 %shard_map.127 = bf16[8192,256]{1,0:T(8,128)(2,1)} custom-call(bf16[8,8192]{1,0:T(8,128)(2,1)} %concatenate.76.rim_ref, bf16[256,8192]{1,0:T(8,128)(2,1)} %x_ref.1, bf16[4,8192]{1,0:T(4,128)(2,1)} %w_ref.1, bf16[1,8192]{1,0:T(2,128)(2,1)} %reshape.210.b_ref, f32[3,256,1]{2,1,0:T(8,128)} %copy.25.vis_ref), custom_call_target="tpu_custom_call" | custom-call | flops 41943040 | bytes 8388608 | tf_op jit(solution)/shard_map/pallas_call | solution.py:66
  37.5 2.2 collective-permute-done.8
  39.8 2.3 collective-permute-start.9
  42.1 8.3 %fusion.15 = f32[1,128,64,128]{3,2,1,0:T(8,128)S(1)} fusion(bf16[256,128,64]{0,2,1:T(8,128)(2,1)} %bitcast.78, f32[128,256]{1,0:T(8,128)S(1)} %copy.26, f32[256,128]{1,0:T(8,128)S(1)} %get-tuple-element.83), kind=kOutput, calls=%fused_computation.25 | convolution fusion | flops 545259520 | bytes 8650752 | tf_op jit(solution)/shard_map/hjn,jhp->hpn/dot_general | solution.py:121
  50.9 2.0 copy-done
  52.8 1.5 constant_dynamic-slice_fusion
  54.3 2.3 collective-permute-start.10
  56.6 3.6 %collective-permute-done.4 = f32[128]{0:T(128)S(1)} collective-permute-done((f32[128]{0:T(128)S(1)}, f32[128]{0:T(128)S(1)}, u32[]{:S(2)}, u32[]{:S(2)}) %collective-permute-start.4) | collective-permute-done | bytes 544 | tf_op jit(solution)/shard_map/ppermute | solution.py:221
  60.6 2.8 %add_select_fusion = f32[64,64,128]{2,1,0:T(8,128)S(1)} fusion(f32[64,64,128]{2,1,0:T(8,128)S(1)} %collective-permute-done.10, f32[128,64,128]{2,1,0:T(8,128)} %copy-done, s32[]{:T(128)S(6)} %select_n.101, f32[64]{0:T(128)S(1)} %get-tuple-element.74, f32[64]{0:T(128)S(1)} %get-tuple-element.73, pred[]{:T(512)S(6)} %eq.73), kind=kLoop, calls=%fused_computation.34 | loop fusion | flops 2621440 | bytes 6291973 | tf_op jit(solution)/shard_map/jit(_where)/select_n | solution.py:226
  63.4 3.1 %collective-permute-start.13 = (f32[64,64,128]{2,1,0:T(8,128)S(1)}, f32[64,64,128]{2,1,0:T(8,128)S(1)}, u32[]{:S(2)}, u32[]{:S(2)}) collective-permute-start(f32[64,64,128]{2,1,0:T(8,128)S(1)} %add_select_fusion), channel_id=1, source_target_pairs={{0,2},{1,3},{2,4},{3,5},{4,6},{5,7},{6,8},{7,9},{8,10},{9,11},{10,... | collective-permute-start | bytes 6291464 | tf_op jit(solution)/shard_map/ppermute | solution.py:134
  66.5 47.4 %collective-permute-done.13 = f32[64,64,128]{2,1,0:T(8,128)S(1)} collective-permute-done((f32[64,64,128]{2,1,0:T(8,128)S(1)}, f32[64,64,128]{2,1,0:T(8,128)S(1)}, u32[]{:S(2)}, u32[]{:S(2)}) %collective-permute-start.13) | collective-permute-done | bytes 2097184 | tf_op jit(solution)/shard_map/ppermute | solution.py:134
  113.9 1.9 collective-permute-start.14
  115.8 2.4 collective-permute-start.11
  118.2 45.3 %collective-permute-done.11 = f32[64]{0:T(128)S(1)} collective-permute-done((f32[64]{0:T(128)S(1)}, f32[64]{0:T(128)S(1)}, u32[]{:S(2)}, u32[]{:S(2)}) %collective-permute-start.11) | collective-permute-done | bytes 288 | tf_op jit(solution)/shard_map/ppermute | solution.py:134
  163.5 1.6 multiply_add_fusion.3
  165.1 2.0 collective-permute-start.15
  167.1 6.4 %copy.35 = bf16[256,8192]{0,1:T(8,128)(2,1)} copy(bf16[256,8192]{1,0:T(8,128)(2,1)} %param.16) | data formatting | bytes 8388608 | tf_op args[1]
  173.7 2.6 %copy.36.n_ref = f32[8192,1]{1,0:T(8,128)} copy(f32[8192,1]{0,1:T(1,128)S(1)} %bitcast.84) | data formatting | bytes 65536 | tf_op jit(solution)/shard_map/broadcast_in_dim | solution.py:102
  176.9 0.7 compare_reduce_fusion
  178.6 1.9 collective-permute-start.12
  180.7 30.6 %collective-permute-done.12 = f32[64]{0:T(128)S(1)} collective-permute-done((f32[64]{0:T(128)S(1)}, f32[64]{0:T(128)S(1)}, u32[]{:S(2)}, u32[]{:S(2)}) %collective-permute-start.12) | collective-permute-done | bytes 288 | tf_op jit(solution)/shard_map/ppermute | solution.py:134
  211.3 1.9 collective-permute-start.16
  213.3 2.5 multiply_add_fusion.2
  215.8 0.8 collective-permute-done.16
  216.5 2.8 %fusion.19 = bf16[64,64,128]{2,1,0:T(8,128)(2,1)S(1)} fusion(f32[64,64,128]{2,1,0:T(8,128)S(1)} %get-tuple-element.93, f32[64,64,128]{2,1,0:T(8,128)} %copy-done.2, f32[128,64,128]{2,1,0:T(8,128)} %copy-done, s32[]{:T(128)S(6)} %select_n.101, f32[64]{0:T(128)S(1)} %get-tuple-element.72, pred[]{:T(512)S(6)} %eq.73), kind=kLoop, calls=%fused_computation.35 | loop fusion | flops 2097152 | bytes 7340293 | tf_op jit(solution)/shard_map/jit(_where)/select_n | solution.py:232
  219.3 3.7 %collective-permute-start.17 = (bf16[64,64,128]{2,1,0:T(8,128)(2,1)S(1)}, bf16[64,64,128]{2,1,0:T(8,128)(2,1)S(1)}, u32[]{:S(2)}, u32[]{:S(2)}) collective-permute-start(bf16[64,64,128]{2,1,0:T(8,128)(2,1)S(1)} %fusion.19), channel_id=1, source_target_pairs={{0,1},{1,0},{2,3},{3,2},{4,5},{5,4},{6,7},{7,6},{8,9},{9,8},{10,11... | collective-permute-start | bytes 3145736 | tf_op jit(solution)/shard_map/ppermute | solution.py:232
  223.0 8.9 %fusion = f32[128,64,256]{2,1,0:T(8,128)S(1)} fusion(f32[128,256]{1,0:T(8,128)S(1)} %copy.30, f32[128,256]{1,0:T(8,128)S(1)} %copy.28, f32[256,256]{1,0:T(8,128)S(1)} %fusion.27, pred[256,256]{1,0:T(8,128)(4,1)S(1)} %fusion.21, bf16[1,256,128,64]{1,3,2,0:T(8,128)(2,1)S(1)} %bitcast.79), kind=kOutput, calls=%fused_computation.3 | convolution fusion | flops 1115684864 | bytes 13172736 | tf_op jit(solution)/shard_map/hij,jhp->ihp/dot_general | solution.py:113
  231.9 0.7 select_convert_fusion.1
  232.8 1.3 bitcast_add_fusion.1
  234.1 0.9 copy-done.5
  235.0 5.7 %multiply_reduce_fusion = (f32[256]{0:T(256)S(1)}, f32[256,8192]{0,1:T(8,128)}) fusion(bf16[256,8192]{0,1:T(8,128)(2,1)S(1)} %copy-done.5, bf16[256,8192]{0,1:T(8,128)(2,1)S(1)} %bitcast.80, f32[8192]{0:T(1024)S(1)} %mul.331, f32[256,128,64]{0,2,1:T(8,128)S(1)} %bitcast_add_fusion.1), kind=kLoop, calls=%fused_computation.20 | loop fusion | flops 23068416 | bytes 25199616 | tf_op jit(solution)/shard_map/reduce_sum | solution.py:337
  241.3 7.9 %shard_map.128 = bf16[256,8192]{1,0:T(8,128)(2,1)} custom-call(f32[8192,256]{1,0:T(8,128)} %bitcast.77, f32[1,256]{1,0:T(1,128)} %bitcast.88, f32[8192,1]{1,0:T(8,128)} %copy.36.n_ref), custom_call_target="tpu_custom_call" | custom-call | flops 4194304 | bytes 12582912 | tf_op jit(solution)/shard_map/pallas_call | solution.py:91
  (76 shorter events, 7.9 us)
Async XLA Ops:
  1.3 11.1 %collective-permute-start.5 = (s32[1]{0:T(128)}, s32[1]{0:T(128)}, u32[]{:S(2)}, u32[]{:S(2)}) collective-permute-start(s32[1]{0:T(128)} %slice.98), channel_id=1, source_target_pairs={{0,1},{1,0},{2,3},{3,2},{4,5},{5,4},{6,7},{7,6},{8,9},{9,8},{10,11... | collective-permute-start | bytes 20 | tf_op jit(solution)/shard_map/ppermute | solution.py:172
  4.5 11.7 %collective-permute-start.3 = (bf16[3,8449]{1,0:T(4,128)(2,1)S(1)}, bf16[3,8449]{1,0:T(4,128)(2,1)S(1)}, u32[]{:S(2)}, u32[]{:S(2)}) collective-permute-start(bf16[3,8449]{1,0:T(4,128)(2,1)S(1)} %pad_maximum_fusion.1), channel_id=1, source_target_pairs={{0,1},{1,2},{2,3},{3,4},{4,5},{5,6},{6,7},{7,8},{8,9},{9,10},{10,1... | collective-permute-start | bytes 152090 | tf_op jit(solution)/shard_map/ppermute | solution.py:23
  13.7 2.4 collective-permute-start.6
  16.2 21.0 %collective-permute-start.7 = (s32[4]{0:T(128)S(1)}, s32[4]{0:T(128)S(1)}, u32[]{:S(2)}, u32[]{:S(2)}) collective-permute-start(s32[4]{0:T(128)S(1)} %broadcast_select_fusion.2), channel_id=1, source_target_pairs={{0,4},{1,5},{2,6},{3,7},{4,0},{5,1},{6,2},{7,3},{8,12},{9,13},{10,... | collective-permute-start | bytes 56 | tf_op jit(solution)/shard_map/ppermute | solution.py:172
  37.3 2.4 collective-permute-start.8
  39.8 10.7 %collective-permute-start.9 = (s32[16]{0:T(128)S(1)}, s32[16]{0:T(128)S(1)}, u32[]{:S(2)}, u32[]{:S(2)}) collective-permute-start(s32[16]{0:T(128)S(1)} %broadcast_select_fusion.4), channel_id=1, source_target_pairs={{0,16},{1,17},{2,18},{3,19},{4,20},{5,21},{6,22},{7,23},{8,24},{9,... | collective-permute-start | bytes 200 | tf_op jit(solution)/shard_map/ppermute | solution.py:172
  50.9 2.0 copy-start
  54.3 6.3 %collective-permute-start.10 = (f32[64,64,128]{2,1,0:T(8,128)}, f32[64,64,128]{2,1,0:T(8,128)S(1)}, u32[]{:S(2)}, u32[]{:S(2)}) collective-permute-start(f32[64,64,128]{2,1,0:T(8,128)} %constant_dynamic-slice_fusion), channel_id=1, source_target_pairs={{0,1},{1,0},{2,3},{3,2},{4,5},{5,4},{6,7},{7,6},{8,9},{9,8},{10,11... | collective-permute-start | bytes 6291464 | tf_op jit(solution)/shard_map/ppermute | solution.py:221
  56.6 3.6 %collective-permute-start.4 = (f32[128]{0:T(128)S(1)}, f32[128]{0:T(128)S(1)}, u32[]{:S(2)}, u32[]{:S(2)}) collective-permute-start(f32[128]{0:T(128)S(1)} %get-tuple-element.78), channel_id=1, source_target_pairs={{0,1},{1,0},{2,3},{3,2},{4,5},{5,4},{6,7},{7,6},{8,9},{9,8},{10,11... | collective-permute-start | bytes 1544 | tf_op jit(solution)/shard_map/ppermute | solution.py:221
  60.6 104.5 %copy-start.2 = (f32[64,64,128]{2,1,0:T(8,128)}, f32[64,64,128]{2,1,0:T(8,128)S(1)}, u32[]{:S(2)}) copy-start(f32[64,64,128]{2,1,0:T(8,128)S(1)} %collective-permute-done.10) | copy-start | bytes 6291460
  63.4 50.5 %collective-permute-start.13 = (f32[64,64,128]{2,1,0:T(8,128)S(1)}, f32[64,64,128]{2,1,0:T(8,128)S(1)}, u32[]{:S(2)}, u32[]{:S(2)}) collective-permute-start(f32[64,64,128]{2,1,0:T(8,128)S(1)} %add_select_fusion), channel_id=1, source_target_pairs={{0,2},{1,3},{2,4},{3,5},{4,6},{5,7},{6,8},{7,9},{8,10},{9,11},{10,... | collective-permute-start | bytes 6291464 | tf_op jit(solution)/shard_map/ppermute | solution.py:134
  113.9 49.6 %collective-permute-start.14 = (f32[64,64,128]{2,1,0:T(8,128)S(1)}, f32[64,64,128]{2,1,0:T(8,128)S(1)}, u32[]{:S(2)}, u32[]{:S(2)}) collective-permute-start(f32[64,64,128]{2,1,0:T(8,128)S(1)} %collective-permute-done.13), channel_id=1, source_target_pairs={{0,2},{1,3},{2,4},{3,5},{4,6},{5,7},{6,8},{7,9},{8,10},{9,11},{10,... | collective-permute-start | bytes 6291464 | tf_op jit(solution)/shard_map/ppermute | solution.py:134
  115.8 47.7 %collective-permute-start.11 = (f32[64]{0:T(128)S(1)}, f32[64]{0:T(128)S(1)}, u32[]{:S(2)}, u32[]{:S(2)}) collective-permute-start(f32[64]{0:T(128)S(1)} %mul.278), channel_id=1, source_target_pairs={{0,2},{1,3},{2,4},{3,5},{4,6},{5,7},{6,8},{7,9},{8,10},{9,11},{10,... | collective-permute-start | bytes 776 | tf_op jit(solution)/shard_map/ppermute | solution.py:134
  165.1 8.4 %copy-start.8 = (f32[128]{0:T(128)S(1)}, f32[128]{0:T(128)}, u32[]{:S(2)}) copy-start(f32[128]{0:T(128)} %param.21) | copy-start | bytes 1540
  165.1 8.6 %copy-start.6 = (bf16[8192]{0:T(1024)(128)(2,1)S(1)}, bf16[8192]{0:T(1024)(128)(2,1)}, u32[]{:S(2)}) copy-start(bf16[8192]{0:T(1024)(128)(2,1)} %param.26) | copy-start | bytes 49156
  165.1 48.2 %collective-permute-start.15 = (f32[64,64,128]{2,1,0:T(8,128)}, f32[64,64,128]{2,1,0:T(8,128)}, u32[]{:S(2)}, u32[]{:S(2)}) collective-permute-start(f32[64,64,128]{2,1,0:T(8,128)} %multiply_add_fusion.3), channel_id=1, source_target_pairs={{0,4},{1,5},{2,6},{3,7},{4,8},{5,9},{6,10},{7,11},{8,12},{9,13},{1... | collective-permute-start | bytes 6291464 | tf_op jit(solution)/shard_map/ppermute | solution.py:134
  173.5 4.8 %copy-start.7 = (s32[256]{0:T(256)S(1)}, s32[256]{0:T(256)}, u32[]{:S(2)}) copy-start(s32[256]{0:T(256)} %param.27) | copy-start | bytes 3076
  178.6 32.7 %collective-permute-start.12 = (f32[64]{0:T(128)S(1)}, f32[64]{0:T(128)S(1)}, u32[]{:S(2)}, u32[]{:S(2)}) collective-permute-start(f32[64]{0:T(128)S(1)} %collective-permute-done.11), channel_id=1, source_target_pairs={{0,2},{1,3},{2,4},{3,5},{4,6},{5,7},{6,8},{7,9},{8,10},{9,11},{10,... | collective-permute-start | bytes 776 | tf_op jit(solution)/shard_map/ppermute | solution.py:134
  211.3 5.2 %collective-permute-start.16 = (f32[64]{0:T(128)S(1)}, f32[64]{0:T(128)S(1)}, u32[]{:S(2)}, u32[]{:S(2)}) collective-permute-start(f32[64]{0:T(128)S(1)} %mul.319), channel_id=1, source_target_pairs={{0,4},{1,5},{2,6},{3,7},{4,8},{5,9},{6,10},{7,11},{8,12},{9,13},{1... | collective-permute-start | bytes 776 | tf_op jit(solution)/shard_map/ppermute | solution.py:134
  216.5 6.5 %copy-start.4 = (bf16[8192,256]{1,0:T(8,128)(2,1)S(1)}, bf16[8192,256]{1,0:T(8,128)(2,1)}, u32[]{:S(2)}) copy-start(bf16[8192,256]{1,0:T(8,128)(2,1)} %shard_map.127) | copy-start | bytes 12582916
  219.3 12.6 %copy-start.1 = (f32[128,64,128]{2,1,0:T(8,128)S(1)}, f32[128,64,128]{2,1,0:T(8,128)}, u32[]{:S(2)}) copy-start(f32[128,64,128]{2,1,0:T(8,128)} %copy-done) | copy-start | bytes 12582916
  219.3 12.6 %copy-start.3 = (f32[64,64,128]{2,1,0:T(8,128)S(1)}, f32[64,64,128]{2,1,0:T(8,128)}, u32[]{:S(2)}) copy-start(f32[64,64,128]{2,1,0:T(8,128)} %copy-done.2) | copy-start | bytes 6291460
  219.3 12.6 %collective-permute-start.17 = (bf16[64,64,128]{2,1,0:T(8,128)(2,1)S(1)}, bf16[64,64,128]{2,1,0:T(8,128)(2,1)S(1)}, u32[]{:S(2)}, u32[]{:S(2)}) collective-permute-start(bf16[64,64,128]{2,1,0:T(8,128)(2,1)S(1)} %fusion.19), channel_id=1, source_target_pairs={{0,1},{1,0},{2,3},{3,2},{4,5},{5,4},{6,7},{7,6},{8,9},{9,8},{10,11... | collective-permute-start | bytes 3145736 | tf_op jit(solution)/shard_map/ppermute | solution.py:232
  232.8 2.2 copy-start.5

commit v16 on v15

--- a/solution.py
+++ b/solution.py
@@ -62,7 +62,7 @@
         [(ext_segment[k : k + rows] == segment).astype(jnp.float32) for k in range(CONV - 1)]
     )[:, :, None]
     rim8 = jnp.concatenate([rim_vals, jnp.zeros((8 - rim_vals.shape[0], width), rim_vals.dtype)])
-    tile = min(width, 1024)
+    tile = min(width, 2048)
     return pl.pallas_call(
         conv_rows_kernel,
         out_shape=jax.ShapeDtypeStruct((width, rows), jnp.bfloat16),

time: 250 us -> 250 us (level)
  no operation moved by 1% of the time
where the time goes in v16:
time: 250 us; the launch traced here: 249 us
  waiting for transfers between devices  131 us (52%)
  other arithmetic  28.3 us (11%)
  starting transfers between devices  28 us (11%)
  local copies, waits for them, and re-layouts  21.9 us (9%)
  matrix products  18.6 us (7%)
  Pallas kernels  18.1 us (7%)
    ppermute x6, waiting for transfers between devices, shifted(): lax.ppermute(value, axis, [(s, s + steps) for s in range(count - steps)])  124 us
    ppermute x6, starting transfers between devices, shifted(): lax.ppermute(value, axis, [(s, s + steps) for s in range(count - steps)])  13.3 us
    unnamed x20, local copies, waits for them, and re-layouts  10.3 us
    pallas_call x1, Pallas kernels, conv_rows(): pl.pallas_call(conv_rows_kernel, out_shape=jax.ShapeDtypeStruct((width, r...  10.2 us
    dot_general x1, matrix products, mixing_part(): jnp.einsum('hij,jhp->ihp', mixing, x_group, preferred_element_type=jnp.fl...  8.86 us
    dot_general x1, matrix products, state_part(): jnp.einsum('hjn,jhp->hpn', weighted, x_group, preferred_element_type=jnp....  8.34 us
    pallas_call x1, Pallas kernels, scale_rows(): pl.pallas_call(scale_rows_kernel, out_shape=jax.ShapeDtypeStruct((rows, w...  7.87 us
    reduce_sum x1, other arithmetic, local(): local_sq = jnp.sum(gated * gated, axis=1)  5.72 us
  transfers between devices with their start and end apart: 15, of which 8 were waited for; matrix products, arithmetic and copies ran while one was open for 19% of the time, Pallas kernels for 4%

profile of v16, /device:TPU:9, one launch (start us, length us, event | category | flops | bytes accessed | tf_op | source)
XLA Modules:
  0.0 248.5 jit_solution(9360432036838404285)
XLA Ops:
  0.0 1.3 slice.98
  2.6 0.9 slice.99
  4.5 3.0 %collective-permute-start.3 = (bf16[3,8449]{1,0:T(4,128)(2,1)S(1)}, bf16[3,8449]{1,0:T(4,128)(2,1)S(1)}, u32[]{:S(2)}, u32[]{:S(2)}) collective-permute-start(bf16[3,8449]{1,0:T(4,128)(2,1)S(1)} %pad_maximum_fusion.1), channel_id=1, source_target_pairs={{0,1},{1,2},{2,3},{3,4},{4,5},{5,6},{6,7},{7,8},{8,9},{9,10},{10,1... | collective-permute-start | bytes 152090 | tf_op jit(solution)/shard_map/ppermute | solution.py:23
  7.5 1.0 copy.21
  8.5 0.8 negate_multiply_fusion
  9.4 1.3 reshape.210.b_ref
  10.8 0.8 slice_convert_fusion.5
  12.3 1.4 broadcast_select_fusion.1
  13.7 1.2 collective-permute-start.6
  14.9 1.2 collective-permute-done.6
  16.2 1.3 collective-permute-start.7
  18.2 0.8 pad_add_fusion
  20.2 2.0 compare_convert_fusion.4
  22.3 0.9 copy.25.vis_ref
  23.2 1.5 multiply_convert_fusion.6
  24.9 0.8 fusion.35
  26.4 10.2 %shard_map.127 = bf16[8192,256]{1,0:T(8,128)(2,1)} custom-call(bf16[8,8192]{1,0:T(8,128)(2,1)} %concatenate.76.rim_ref, bf16[256,8192]{1,0:T(8,128)(2,1)} %x_ref.1, bf16[4,8192]{1,0:T(4,128)(2,1)} %w_ref.1, bf16[1,8192]{1,0:T(2,128)(2,1)} %reshape.210.b_ref, f32[3,256,1]{2,1,0:T(8,128)} %copy.25.vis_ref), custom_call_target="tpu_custom_call" | custom-call | flops 41943040 | bytes 8388608 | tf_op jit(solution)/shard_map/pallas_call | solution.py:66
  36.9 2.2 collective-permute-done.8
  39.2 2.3 collective-permute-start.9
  41.5 8.3 %fusion.15 = f32[1,128,64,128]{3,2,1,0:T(8,128)S(1)} fusion(bf16[256,128,64]{0,2,1:T(8,128)(2,1)} %bitcast.78, f32[128,256]{1,0:T(8,128)S(1)} %copy.26, f32[256,128]{1,0:T(8,128)S(1)} %get-tuple-element.83), kind=kOutput, calls=%fused_computation.25 | convolution fusion | flops 545259520 | bytes 8650752 | tf_op jit(solution)/shard_map/hjn,jhp->hpn/dot_general | solution.py:121
  50.3 2.0 copy-done
  52.2 1.5 constant_dynamic-slice_fusion
  53.7 2.3 collective-permute-start.10
  56.0 3.6 %collective-permute-done.4 = f32[128]{0:T(128)S(1)} collective-permute-done((f32[128]{0:T(128)S(1)}, f32[128]{0:T(128)S(1)}, u32[]{:S(2)}, u32[]{:S(2)}) %collective-permute-start.4) | collective-permute-done | bytes 544 | tf_op jit(solution)/shard_map/ppermute | solution.py:221
  60.0 2.8 %add_select_fusion = f32[64,64,128]{2,1,0:T(8,128)S(1)} fusion(f32[64,64,128]{2,1,0:T(8,128)S(1)} %collective-permute-done.10, f32[128,64,128]{2,1,0:T(8,128)} %copy-done, s32[]{:T(128)S(6)} %select_n.101, f32[64]{0:T(128)S(1)} %get-tuple-element.74, f32[64]{0:T(128)S(1)} %get-tuple-element.73, pred[]{:T(512)S(6)} %eq.73), kind=kLoop, calls=%fused_computation.34 | loop fusion | flops 2621440 | bytes 6291973 | tf_op jit(solution)/shard_map/jit(_where)/select_n | solution.py:226
  62.8 3.1 %collective-permute-start.13 = (f32[64,64,128]{2,1,0:T(8,128)S(1)}, f32[64,64,128]{2,1,0:T(8,128)S(1)}, u32[]{:S(2)}, u32[]{:S(2)}) collective-permute-start(f32[64,64,128]{2,1,0:T(8,128)S(1)} %add_select_fusion), channel_id=1, source_target_pairs={{0,2},{1,3},{2,4},{3,5},{4,6},{5,7},{6,8},{7,9},{8,10},{9,11},{10,... | collective-permute-start | bytes 6291464 | tf_op jit(solution)/shard_map/ppermute | solution.py:134
  65.9 47.4 %collective-permute-done.13 = f32[64,64,128]{2,1,0:T(8,128)S(1)} collective-permute-done((f32[64,64,128]{2,1,0:T(8,128)S(1)}, f32[64,64,128]{2,1,0:T(8,128)S(1)}, u32[]{:S(2)}, u32[]{:S(2)}) %collective-permute-start.13) | collective-permute-done | bytes 2097184 | tf_op jit(solution)/shard_map/ppermute | solution.py:134
  113.3 1.9 collective-permute-start.14
  115.2 2.4 collective-permute-start.11
  117.6 45.3 %collective-permute-done.11 = f32[64]{0:T(128)S(1)} collective-permute-done((f32[64]{0:T(128)S(1)}, f32[64]{0:T(128)S(1)}, u32[]{:S(2)}, u32[]{:S(2)}) %collective-permute-start.11) | collective-permute-done | bytes 288 | tf_op jit(solution)/shard_map/ppermute | solution.py:134
  162.9 1.6 multiply_add_fusion.3
  164.5 2.0 collective-permute-start.15
  166.5 6.4 %copy.35 = bf16[256,8192]{0,1:T(8,128)(2,1)} copy(bf16[256,8192]{1,0:T(8,128)(2,1)} %param.16) | data formatting | bytes 8388608 | tf_op args[1]
  173.1 2.6 %copy.36.n_ref = f32[8192,1]{1,0:T(8,128)} copy(f32[8192,1]{0,1:T(1,128)S(1)} %bitcast.84) | data formatting | bytes 65536 | tf_op jit(solution)/shard_map/broadcast_in_dim | solution.py:102
  176.3 0.7 compare_reduce_fusion
  178.0 1.9 collective-permute-start.12
  180.1 30.6 %collective-permute-done.12 = f32[64]{0:T(128)S(1)} collective-permute-done((f32[64]{0:T(128)S(1)}, f32[64]{0:T(128)S(1)}, u32[]{:S(2)}, u32[]{:S(2)}) %collective-permute-start.12) | collective-permute-done | bytes 288 | tf_op jit(solution)/shard_map/ppermute | solution.py:134
  210.7 1.9 collective-permute-start.16
  212.7 2.5 %multiply_add_fusion.2 = f32[64,64,128]{2,1,0:T(8,128)S(1)} fusion(f32[64,64,128]{2,1,0:T(8,128)} %multiply_add_fusion.3, f32[64,64,128]{2,1,0:T(8,128)} %collective-permute-done.15, f32[64]{0:T(128)S(1)} %mul.319), kind=kLoop, calls=%fused_computation.32 | loop fusion | flops 1048576 | bytes 6291712 | tf_op jit(solution)/shard_map/add | solution.py:139
  215.2 0.8 collective-permute-done.16
  215.9 2.8 %fusion.19 = bf16[64,64,128]{2,1,0:T(8,128)(2,1)S(1)} fusion(f32[64,64,128]{2,1,0:T(8,128)S(1)} %get-tuple-element.93, f32[64,64,128]{2,1,0:T(8,128)} %copy-done.2, f32[128,64,128]{2,1,0:T(8,128)} %copy-done, s32[]{:T(128)S(6)} %select_n.101, f32[64]{0:T(128)S(1)} %get-tuple-element.72, pred[]{:T(512)S(6)} %eq.73), kind=kLoop, calls=%fused_computation.35 | loop fusion | flops 2097152 | bytes 7340293 | tf_op jit(solution)/shard_map/jit(_where)/select_n | solution.py:232
  218.7 3.7 %collective-permute-start.17 = (bf16[64,64,128]{2,1,0:T(8,128)(2,1)S(1)}, bf16[64,64,128]{2,1,0:T(8,128)(2,1)S(1)}, u32[]{:S(2)}, u32[]{:S(2)}) collective-permute-start(bf16[64,64,128]{2,1,0:T(8,128)(2,1)S(1)} %fusion.19), channel_id=1, source_target_pairs={{0,1},{1,0},{2,3},{3,2},{4,5},{5,4},{6,7},{7,6},{8,9},{9,8},{10,11... | collective-permute-start | bytes 3145736 | tf_op jit(solution)/shard_map/ppermute | solution.py:232
  222.4 8.9 %fusion = f32[128,64,256]{2,1,0:T(8,128)S(1)} fusion(f32[128,256]{1,0:T(8,128)S(1)} %copy.30, f32[128,256]{1,0:T(8,128)S(1)} %copy.28, f32[256,256]{1,0:T(8,128)S(1)} %fusion.27, pred[256,256]{1,0:T(8,128)(4,1)S(1)} %fusion.21, bf16[1,256,128,64]{1,3,2,0:T(8,128)(2,1)S(1)} %bitcast.79), kind=kOutput, calls=%fused_computation.3 | convolution fusion | flops 1115684864 | bytes 13172736 | tf_op jit(solution)/shard_map/hij,jhp->ihp/dot_general | solution.py:113
  231.3 0.7 select_convert_fusion.1
  232.2 1.3 bitcast_add_fusion.1
  233.5 0.9 copy-done.5
  234.4 5.7 %multiply_reduce_fusion = (f32[256]{0:T(256)S(1)}, f32[256,8192]{0,1:T(8,128)}) fusion(bf16[256,8192]{0,1:T(8,128)(2,1)S(1)} %copy-done.5, bf16[256,8192]{0,1:T(8,128)(2,1)S(1)} %bitcast.80, f32[8192]{0:T(1024)S(1)} %mul.331, f32[256,128,64]{0,2,1:T(8,128)S(1)} %bitcast_add_fusion.1), kind=kLoop, calls=%fused_computation.20 | loop fusion | flops 23068416 | bytes 25199616 | tf_op jit(solution)/shard_map/reduce_sum | solution.py:337
  240.7 7.9 %shard_map.128 = bf16[256,8192]{1,0:T(8,128)(2,1)} custom-call(f32[8192,256]{1,0:T(8,128)} %bitcast.77, f32[1,256]{1,0:T(1,128)} %bitcast.88, f32[8192,1]{1,0:T(8,128)} %copy.36.n_ref), custom_call_target="tpu_custom_call" | custom-call | flops 4194304 | bytes 12582912 | tf_op jit(solution)/shard_map/pallas_call | solution.py:91
  (76 shorter events, 7.9 us)
Async XLA Ops:
  1.3 11.1 %collective-permute-start.5 = (s32[1]{0:T(128)}, s32[1]{0:T(128)}, u32[]{:S(2)}, u32[]{:S(2)}) collective-permute-start(s32[1]{0:T(128)} %slice.98), channel_id=1, source_target_pairs={{0,1},{1,0},{2,3},{3,2},{4,5},{5,4},{6,7},{7,6},{8,9},{9,8},{10,11... | collective-permute-start | bytes 20 | tf_op jit(solution)/shard_map/ppermute | solution.py:172
  4.5 11.7 %collective-permute-start.3 = (bf16[3,8449]{1,0:T(4,128)(2,1)S(1)}, bf16[3,8449]{1,0:T(4,128)(2,1)S(1)}, u32[]{:S(2)}, u32[]{:S(2)}) collective-permute-start(bf16[3,8449]{1,0:T(4,128)(2,1)S(1)} %pad_maximum_fusion.1), channel_id=1, source_target_pairs={{0,1},{1,2},{2,3},{3,4},{4,5},{5,6},{6,7},{7,8},{8,9},{9,10},{10,1... | collective-permute-start | bytes 152090 | tf_op jit(solution)/shard_map/ppermute | solution.py:23
  13.7 2.4 collective-permute-start.6
  16.2 20.4 %collective-permute-start.7 = (s32[4]{0:T(128)S(1)}, s32[4]{0:T(128)S(1)}, u32[]{:S(2)}, u32[]{:S(2)}) collective-permute-start(s32[4]{0:T(128)S(1)} %broadcast_select_fusion.2), channel_id=1, source_target_pairs={{0,4},{1,5},{2,6},{3,7},{4,0},{5,1},{6,2},{7,3},{8,12},{9,13},{10,... | collective-permute-start | bytes 56 | tf_op jit(solution)/shard_map/ppermute | solution.py:172
  36.7 2.4 collective-permute-start.8
  39.2 10.7 %collective-permute-start.9 = (s32[16]{0:T(128)S(1)}, s32[16]{0:T(128)S(1)}, u32[]{:S(2)}, u32[]{:S(2)}) collective-permute-start(s32[16]{0:T(128)S(1)} %broadcast_select_fusion.4), channel_id=1, source_target_pairs={{0,16},{1,17},{2,18},{3,19},{4,20},{5,21},{6,22},{7,23},{8,24},{9,... | collective-permute-start | bytes 200 | tf_op jit(solution)/shard_map/ppermute | solution.py:172
  50.3 2.0 copy-start
  53.7 6.3 %collective-permute-start.10 = (f32[64,64,128]{2,1,0:T(8,128)}, f32[64,64,128]{2,1,0:T(8,128)S(1)}, u32[]{:S(2)}, u32[]{:S(2)}) collective-permute-start(f32[64,64,128]{2,1,0:T(8,128)} %constant_dynamic-slice_fusion), channel_id=1, source_target_pairs={{0,1},{1,0},{2,3},{3,2},{4,5},{5,4},{6,7},{7,6},{8,9},{9,8},{10,11... | collective-permute-start | bytes 6291464 | tf_op jit(solution)/shard_map/ppermute | solution.py:221
  56.0 3.6 %collective-permute-start.4 = (f32[128]{0:T(128)S(1)}, f32[128]{0:T(128)S(1)}, u32[]{:S(2)}, u32[]{:S(2)}) collective-permute-start(f32[128]{0:T(128)S(1)} %get-tuple-element.78), channel_id=1, source_target_pairs={{0,1},{1,0},{2,3},{3,2},{4,5},{5,4},{6,7},{7,6},{8,9},{9,8},{10,11... | collective-permute-start | bytes 1544 | tf_op jit(solution)/shard_map/ppermute | solution.py:221
  60.0 104.5 %copy-start.2 = (f32[64,64,128]{2,1,0:T(8,128)}, f32[64,64,128]{2,1,0:T(8,128)S(1)}, u32[]{:S(2)}) copy-start(f32[64,64,128]{2,1,0:T(8,128)S(1)} %collective-permute-done.10) | copy-start | bytes 6291460
  62.8 50.5 %collective-permute-start.13 = (f32[64,64,128]{2,1,0:T(8,128)S(1)}, f32[64,64,128]{2,1,0:T(8,128)S(1)}, u32[]{:S(2)}, u32[]{:S(2)}) collective-permute-start(f32[64,64,128]{2,1,0:T(8,128)S(1)} %add_select_fusion), channel_id=1, source_target_pairs={{0,2},{1,3},{2,4},{3,5},{4,6},{5,7},{6,8},{7,9},{8,10},{9,11},{10,... | collective-permute-start | bytes 6291464 | tf_op jit(solution)/shard_map/ppermute | solution.py:134
  113.3 49.6 %collective-permute-start.14 = (f32[64,64,128]{2,1,0:T(8,128)S(1)}, f32[64,64,128]{2,1,0:T(8,128)S(1)}, u32[]{:S(2)}, u32[]{:S(2)}) collective-permute-start(f32[64,64,128]{2,1,0:T(8,128)S(1)} %collective-permute-done.13), channel_id=1, source_target_pairs={{0,2},{1,3},{2,4},{3,5},{4,6},{5,7},{6,8},{7,9},{8,10},{9,11},{10,... | collective-permute-start | bytes 6291464 | tf_op jit(solution)/shard_map/ppermute | solution.py:134
  115.2 47.7 %collective-permute-start.11 = (f32[64]{0:T(128)S(1)}, f32[64]{0:T(128)S(1)}, u32[]{:S(2)}, u32[]{:S(2)}) collective-permute-start(f32[64]{0:T(128)S(1)} %mul.278), channel_id=1, source_target_pairs={{0,2},{1,3},{2,4},{3,5},{4,6},{5,7},{6,8},{7,9},{8,10},{9,11},{10,... | collective-permute-start | bytes 776 | tf_op jit(solution)/shard_map/ppermute | solution.py:134
  164.5 8.4 %copy-start.8 = (f32[128]{0:T(128)S(1)}, f32[128]{0:T(128)}, u32[]{:S(2)}) copy-start(f32[128]{0:T(128)} %param.21) | copy-start | bytes 1540
  164.5 8.6 %copy-start.6 = (bf16[8192]{0:T(1024)(128)(2,1)S(1)}, bf16[8192]{0:T(1024)(128)(2,1)}, u32[]{:S(2)}) copy-start(bf16[8192]{0:T(1024)(128)(2,1)} %param.26) | copy-start | bytes 49156
  164.5 48.2 %collective-permute-start.15 = (f32[64,64,128]{2,1,0:T(8,128)}, f32[64,64,128]{2,1,0:T(8,128)}, u32[]{:S(2)}, u32[]{:S(2)}) collective-permute-start(f32[64,64,128]{2,1,0:T(8,128)} %multiply_add_fusion.3), channel_id=1, source_target_pairs={{0,4},{1,5},{2,6},{3,7},{4,8},{5,9},{6,10},{7,11},{8,12},{9,13},{1... | collective-permute-start | bytes 6291464 | tf_op jit(solution)/shard_map/ppermute | solution.py:134
  172.9 4.8 %copy-start.7 = (s32[256]{0:T(256)S(1)}, s32[256]{0:T(256)}, u32[]{:S(2)}) copy-start(s32[256]{0:T(256)} %param.27) | copy-start | bytes 3076
  178.0 32.7 %collective-permute-start.12 = (f32[64]{0:T(128)S(1)}, f32[64]{0:T(128)S(1)}, u32[]{:S(2)}, u32[]{:S(2)}) collective-permute-start(f32[64]{0:T(128)S(1)} %collective-permute-done.11), channel_id=1, source_target_pairs={{0,2},{1,3},{2,4},{3,5},{4,6},{5,7},{6,8},{7,9},{8,10},{9,11},{10,... | collective-permute-start | bytes 776 | tf_op jit(solution)/shard_map/ppermute | solution.py:134
  210.7 5.2 %collective-permute-start.16 = (f32[64]{0:T(128)S(1)}, f32[64]{0:T(128)S(1)}, u32[]{:S(2)}, u32[]{:S(2)}) collective-permute-start(f32[64]{0:T(128)S(1)} %mul.319), channel_id=1, source_target_pairs={{0,4},{1,5},{2,6},{3,7},{4,8},{5,9},{6,10},{7,11},{8,12},{9,13},{1... | collective-permute-start | bytes 776 | tf_op jit(solution)/shard_map/ppermute | solution.py:134
  215.9 6.5 %copy-start.4 = (bf16[8192,256]{1,0:T(8,128)(2,1)S(1)}, bf16[8192,256]{1,0:T(8,128)(2,1)}, u32[]{:S(2)}) copy-start(bf16[8192,256]{1,0:T(8,128)(2,1)} %shard_map.127) | copy-start | bytes 12582916
  218.7 12.6 %copy-start.1 = (f32[128,64,128]{2,1,0:T(8,128)S(1)}, f32[128,64,128]{2,1,0:T(8,128)}, u32[]{:S(2)}) copy-start(f32[128,64,128]{2,1,0:T(8,128)} %copy-done) | copy-start | bytes 12582916
  218.7 12.6 %copy-start.3 = (f32[64,64,128]{2,1,0:T(8,128)S(1)}, f32[64,64,128]{2,1,0:T(8,128)}, u32[]{:S(2)}) copy-start(f32[64,64,128]{2,1,0:T(8,128)} %copy-done.2) | copy-start | bytes 6291460
  218.7 12.6 %collective-permute-start.17 = (bf16[64,64,128]{2,1,0:T(8,128)(2,1)S(1)}, bf16[64,64,128]{2,1,0:T(8,128)(2,1)S(1)}, u32[]{:S(2)}, u32[]{:S(2)}) collective-permute-start(bf16[64,64,128]{2,1,0:T(8,128)(2,1)S(1)} %fusion.19), channel_id=1, source_target_pairs={{0,1},{1,0},{2,3},{3,2},{4,5},{5,4},{6,7},{7,6},{8,9},{9,8},{10,11... | collective-permute-start | bytes 3145736 | tf_op jit(solution)/shard_map/ppermute | solution.py:232
  232.2 2.2 copy-start.5

commit v17 on v16

--- a/solution.py
+++ b/solution.py
@@ -208,20 +208,22 @@
     return lax.map(f, items)
 
 
-def device_entry(dev_transmit, dev_state, paired, far):
+def device_entry(dev_transmit, dev_state, paired, far, split=None):
     count = lax.axis_size("ctx")
     if not paired:
         return scan_rounds((dev_transmit, dev_state), "ctx", 1, count, count, far)
-    heads = dev_state.shape[0]
-    half = heads // 2
     core = lax.axis_index("ctx") % 2
     swap = [(s, s ^ 1) for s in range(count)]
-    own_lo = core * half
-    give = lax.dynamic_slice_in_dim(dev_state, half - own_lo, half, 0)
-    other_t, other_s = lax.ppermute((dev_transmit, give), "ctx", swap)
-    mine_s = lax.dynamic_slice_in_dim(dev_state, own_lo, half, 0)
-    mine_t = lax.dynamic_slice_in_dim(dev_transmit, own_lo, half, 0)
-    peer_t = lax.dynamic_slice_in_dim(other_t, own_lo, half, 0)
+    if split is None:
+        half = dev_state.shape[0] // 2
+        own_lo = core * half
+        give_s = lax.dynamic_slice_in_dim(dev_state, half - own_lo, half, 0)
+        give_t = lax.dynamic_slice_in_dim(dev_transmit, half - own_lo, half, 0)
+        mine_s = lax.dynamic_slice_in_dim(dev_state, own_lo, half, 0)
+        mine_t = lax.dynamic_slice_in_dim(dev_transmit, own_lo, half, 0)
+    else:
+        give_s, give_t, mine_s, mine_t = split
+    peer_t, other_s = lax.ppermute((give_t, give_s), "ctx", swap)
     first = core == 0
     chip_s = jnp.where(first, peer_t[:, None, None] * mine_s + other_s, mine_t[:, None, None] * other_s + mine_s)
     chip_t = mine_t * peer_t
@@ -315,14 +317,38 @@
         x_group, b_group, c_group, steps_here, decay_here, segment = item
         return mixing_part(x_group, b_group, c_group, steps_here, decay_here, segment)
 
-    block_states, transmits = blockwise(
-        state_of, (x_blocks, b_blocks, step_blocks, cum_decay, seg_blocks, seg_before)
-    )
     intra_items = (x_blocks, b_blocks, c_blocks, step_blocks, cum_decay, seg_blocks)
     ids = gather_rounds(ids, "ctx", 4, lax.axis_size("ctx").bit_length())
-    ids, block_states = lax.optimization_barrier((ids, block_states))
-    far = [*long_runs(ids, paired, tok_rows), intra_items]
-    entering = chain_states(block_states, transmits, paired, far)
+    if paired and block_count == 1:
+        half = head_count // 2
+        core = lax.axis_index("ctx") % 2
+
+        def half_state(offset):
+            return blockwise(
+                state_of,
+                (
+                    lax.dynamic_slice_in_dim(x_blocks, offset, half, 2),
+                    b_blocks,
+                    lax.dynamic_slice_in_dim(step_blocks, offset, half, 1),
+                    lax.dynamic_slice_in_dim(cum_decay, offset, half, 1),
+                    seg_blocks,
+                    seg_before,
+                ),
+            )
+
+        give_s, give_t = half_state((1 - core) * half)
+        ids, give_s = lax.optimization_barrier((ids, give_s))
+        mine_s, mine_t = half_state(core * half)
+        far = [*long_runs(ids, paired, tok_rows), intra_items]
+        split = (give_s[0], give_t[0], mine_s[0], mine_t[0])
+        entering = device_entry(None, None, paired, far, split)[None]
+    else:
+        block_states, transmits = blockwise(
+            state_of, (x_blocks, b_blocks, step_blocks, cum_decay, seg_blocks, seg_before)
+        )
+        ids, block_states = lax.optimization_barrier((ids, block_states))
+        far = [*long_runs(ids, paired, tok_rows), intra_items]
+        entering = chain_states(block_states, transmits, paired, far)
     y_intra = blockwise(intra_of, far[2])
 
     def enter_of(item):

time: 250 us -> 260 us (1.040)
  waiting for transfers between devices: 131 us -> 141 us
  other arithmetic: 28.3 us -> 23.4 us
  matrix products: 18.6 us -> 22.8 us
    ppermute x6, waiting for transfers between devices: 124 us -> 135 us  [shifted(): lax.ppermute(value, axis, [(s, s + steps) for s in range(count - steps)])]
    unnamed x20 -> x43, local copies, waits for them, and re-layouts: 10.3 us -> 7.39 us
    select_n x1 -> x0, other arithmetic: 2.78 us -> none  [device_entry(): jnp.where(first, peer_t[:, None, None] * mine_s + other_s, mine_t[:, None...]
    mul x2, local copies, waits for them, and re-layouts: 0.15 us -> 2.88 us  [local(): skip_d[None, :, None] * x_heads]
    dot_general x1 -> x2, matrix products: 8.34 us -> 11 us  [state_part(): jnp.einsum('hjn,jhp->hpn', weighted, x_group, preferred_element_type=jnp....]
  transfers between devices with their start and end apart: 15 -> 15, of which waited for: 8 -> 8; matrix products, arithmetic and copies ran while one was open for 19% -> 14% of each run, Pallas kernels for 4% -> 4%
where the time goes in v17:
time: 260 us; the launch traced here: 259 us
  waiting for transfers between devices  141 us (54%)
  starting transfers between devices  28.4 us (11%)
  other arithmetic  23.4 us (9%)
  local copies, waits for them, and re-layouts  23.1 us (9%)
  matrix products  22.8 us (9%)
  Pallas kernels  18.1 us (7%)
    ppermute x6, waiting for transfers between devices, shifted(): lax.ppermute(value, axis, [(s, s + steps) for s in range(count - steps)])  135 us
    ppermute x6, starting transfers between devices, shifted(): lax.ppermute(value, axis, [(s, s + steps) for s in range(count - steps)])  12 us
    dot_general x2, matrix products, state_part(): jnp.einsum('hjn,jhp->hpn', weighted, x_group, preferred_element_type=jnp....  11 us
    pallas_call x1, Pallas kernels, conv_rows(): pl.pallas_call(conv_rows_kernel, out_shape=jax.ShapeDtypeStruct((width, r...  10.2 us
    dot_general x1, matrix products, mixing_part(): jnp.einsum('hij,jhp->ihp', mixing, x_group, preferred_element_type=jnp.fl...  9.48 us
    pallas_call x1, Pallas kernels, scale_rows(): pl.pallas_call(scale_rows_kernel, out_shape=jax.ShapeDtypeStruct((rows, w...  7.87 us
    unnamed x43, local copies, waits for them, and re-layouts  7.39 us
    reduce_sum x1, other arithmetic, local(): local_sq = jnp.sum(gated * gated, axis=1)  5.7 us
  transfers between devices with their start and end apart: 15, of which 8 were waited for; matrix products, arithmetic and copies ran while one was open for 14% of the time, Pallas kernels for 4%

profile of v17, /device:TPU:9, one launch (start us, length us, event | category | flops | bytes accessed | tf_op | source)
XLA Modules:
  0.0 259.0 jit_solution(11175228631761941122)
XLA Ops:
  0.0 1.0 slice.105
  1.0 0.7 convert.17
  1.9 0.7 slice.106
  2.6 3.7 %collective-permute-start.3 = (bf16[3,8449]{1,0:T(4,128)(2,1)S(1)}, bf16[3,8449]{1,0:T(4,128)(2,1)S(1)}, u32[]{:S(2)}, u32[]{:S(2)}) collective-permute-start(bf16[3,8449]{1,0:T(4,128)(2,1)S(1)} %pad_maximum_fusion.1), channel_id=1, source_target_pairs={{0,1},{1,2},{2,3},{3,4},{4,5},{5,6},{6,7},{7,8},{8,9},{9,10},{10,1... | collective-permute-start | bytes 152090 | tf_op jit(solution)/shard_map/ppermute | solution.py:23
  6.3 1.3 slice.104
  7.6 1.1 negate_multiply_fusion
  10.5 1.3 broadcast_select_fusion.2
  11.8 1.2 collective-permute-start.6
  13.0 1.2 collective-permute-done.6
  15.1 1.3 collective-permute-start.7
  16.4 1.8 compare_convert_fusion
  18.2 0.9 copy.39.vis_ref
  19.4 0.7 slice_bitcast_fusion
  20.9 10.2 %shard_map.127 = bf16[8192,256]{1,0:T(8,128)(2,1)} custom-call(bf16[8,8192]{1,0:T(8,128)(2,1)} %concatenate.74.rim_ref, bf16[256,8192]{1,0:T(8,128)(2,1)} %x_ref.1, bf16[4,8192]{1,0:T(4,128)(2,1)} %w_ref.1, bf16[1,8192]{1,0:T(2,128)(2,1)} %reshape.238.b_ref, f32[3,256,1]{2,1,0:T(8,128)} %copy.39.vis_ref), custom_call_target="tpu_custom_call" | custom-call | flops 41943040 | bytes 8388608 | tf_op jit(solution)/shard_map/pallas_call | solution.py:66
  31.3 2.2 collective-permute-done.8
  33.6 2.3 collective-permute-start.9
  35.9 5.1 %fusion.30 = f32[1,64,64,128]{3,2,1,0:T(8,128)} fusion(f32[64,256]{1,0:T(8,128)S(1)} %get-tuple-element.56, f32[256,128]{1,0:T(8,128)S(1)} %get-tuple-element.59, bf16[1,256,128,64]{1,3,2,0:T(8,128)(2,1)} %bitcast.86, s32[]{:T(128)S(6)} %select_n.106), kind=kOutput, calls=%fused_computation.44 | convolution fusion | flops 272629760 | bytes 4390916 | tf_op jit(solution)/shard_map/hjn,jhp->hpn/dot_general | solution.py:121
  41.1 3.4 %collective-permute-start.10 = (f32[64,64,128]{2,1,0:T(8,128)}, f32[64,64,128]{2,1,0:T(8,128)S(1)}, u32[]{:S(2)}, u32[]{:S(2)}) collective-permute-start(f32[64,64,128]{2,1,0:T(8,128)} %bitcast.22), channel_id=1, source_target_pairs={{0,1},{1,0},{2,3},{3,2},{4,5},{5,4},{6,7},{7,6},{8,9},{9,8},{10,11... | collective-permute-start | bytes 6291464 | tf_op jit(solution)/shard_map/ppermute | solution.py:226
  45.8 2.4 collective-permute-done.4
  48.5 5.9 %add_select_fusion = (f32[64,64,128]{2,1,0:T(8,128)S(1)}, f32[64,64,128]{2,1,0:T(8,128)}) fusion(f32[64,64,128]{2,1,0:T(8,128)S(1)} %collective-permute-done.10, f32[64]{0:T(128)S(1)} %get-tuple-element.50, f32[64]{0:T(128)S(1)} %collective-permute-done.4, pred[]{:T(512)S(6)} %eq.77, f32[64,256]{1,0:T(8,128)S(1)} %get-tuple-element.55, ...), kind=kOutput, calls=%fused_computation.39 | convolution fusion | flops 275251200 | bytes 8585733 | tf_op jit(solution)/shard_map/hjn,jhp->hpn/dot_general | solution.py:121
  54.4 1.9 collective-permute-start.13
  56.3 48.6 %collective-permute-done.13 = f32[64,64,128]{2,1,0:T(8,128)S(1)} collective-permute-done((f32[64,64,128]{2,1,0:T(8,128)S(1)}, f32[64,64,128]{2,1,0:T(8,128)S(1)}, u32[]{:S(2)}, u32[]{:S(2)}) %collective-permute-start.13) | collective-permute-done | bytes 2097184 | tf_op jit(solution)/shard_map/ppermute | solution.py:134
  104.9 1.9 collective-permute-start.14
  106.9 2.4 collective-permute-start.11
  109.3 45.3 %collective-permute-done.11 = f32[64]{0:T(128)S(1)} collective-permute-done((f32[64]{0:T(128)S(1)}, f32[64]{0:T(128)S(1)}, u32[]{:S(2)}, u32[]{:S(2)}) %collective-permute-start.11) | collective-permute-done | bytes 288 | tf_op jit(solution)/shard_map/ppermute | solution.py:134
  154.8 1.9 collective-permute-start.15
  157.3 1.9 collective-permute-start.12
  159.2 0.8 compare_reduce_fusion
  160.7 40.1 %collective-permute-done.12 = f32[64]{0:T(128)S(1)} collective-permute-done((f32[64]{0:T(128)S(1)}, f32[64]{0:T(128)S(1)}, u32[]{:S(2)}, u32[]{:S(2)}) %collective-permute-start.12) | collective-permute-done | bytes 288 | tf_op jit(solution)/shard_map/ppermute | solution.py:134
  200.8 1.9 collective-permute-start.16
  202.7 2.5 multiply_add_fusion.2
  205.2 0.7 collective-permute-done.16
  206.0 3.0 %fusion.28 = bf16[64,64,128]{2,1,0:T(8,128)(2,1)} fusion(f32[64,64,128]{2,1,0:T(8,128)S(1)} %get-tuple-element.76, f32[64,64,128]{2,1,0:T(8,128)} %get-tuple-element.75, f32[64,64,128]{2,1,0:T(8,128)} %copy-done.1, f32[64]{0:T(128)S(1)} %get-tuple-element.49, pred[]{:T(512)S(6)} %eq.77), kind=kLoop, calls=%fused_computation.42 | loop fusion | flops 2097152 | bytes 7340289 | tf_op jit(solution)/shard_map/jit(_where)/select_n | solution.py:234
  209.0 4.3 %collective-permute-start.17 = (bf16[64,64,128]{2,1,0:T(8,128)(2,1)}, bf16[64,64,128]{2,1,0:T(8,128)(2,1)S(1)}, u32[]{:S(2)}, u32[]{:S(2)}) collective-permute-start(bf16[64,64,128]{2,1,0:T(8,128)(2,1)} %fusion.28), channel_id=1, source_target_pairs={{0,1},{1,0},{2,3},{3,2},{4,5},{5,4},{6,7},{7,6},{8,9},{9,8},{10,11... | collective-permute-start | bytes 3145736 | tf_op jit(solution)/shard_map/ppermute | solution.py:234
  213.3 6.4 %copy.47 = bf16[256,8192]{0,1:T(8,128)(2,1)} copy(bf16[256,8192]{1,0:T(8,128)(2,1)} %param.16) | data formatting | bytes 8388608 | tf_op args[1]
  219.6 1.4 mul.347
  221.0 1.5 mul.348
  223.1 3.4 %copy.48.n_ref = f32[8192,1]{1,0:T(8,128)} copy(f32[8192,1]{0,1:T(1,128)} %bitcast.94) | data formatting | bytes 65536 | tf_op jit(solution)/shard_map/broadcast_in_dim | solution.py:102
  226.5 0.7 fusion.37
  227.2 1.6 copy.45
  228.9 0.7 copy.40
  229.7 1.1 fusion.39
  230.8 2.3 select_convert_fusion.1
  233.1 1.2 fusion.20
  234.4 0.9 copy-done
  235.3 9.5 %bitcast_add_fusion.1 = f32[256,128,64]{0,2,1:T(8,128)S(1)} fusion(f32[256,128,64]{0,2,1:T(8,128)S(1)} %fusion.20, f32[256,128]{0,1:T(8,128)S(1)} %copy-done.8, f32[128,256]{1,0:T(8,128)S(1)} %copy-done.5, f32[128,256]{1,0:T(8,128)S(1)} %copy-done.9, f32[256,256]{1,0:T(8,128)S(1)} %fusion.39, pred[256,256]{1,0:T(8,128)(4,1)S(1)} %fusion.33, ...), kind=kOutput, calls=%fused_computation.17 | convolution fusion | flops 1119879168 | bytes 21692416 | tf_op jit(solution)/shard_map/hij,jhp->ihp/dot_general | solution.py:113
  244.9 5.7 %multiply_reduce_fusion = (f32[256]{0:T(256)S(1)}, f32[256,8192]{0,1:T(8,128)}) fusion(bf16[256,8192]{0,1:T(8,128)(2,1)S(1)} %copy-done.2, bf16[256,8192]{0,1:T(8,128)(2,1)S(1)} %bitcast.89, f32[8192]{0:T(1024)S(1)} %copy-done.7, f32[256,128,64]{0,2,1:T(8,128)S(1)} %bitcast_add_fusion.1), kind=kLoop, calls=%fused_computation.18 | loop fusion | flops 23068416 | bytes 25199616 | tf_op jit(solution)/shard_map/reduce_sum | solution.py:363
  251.1 7.9 %shard_map.128 = bf16[256,8192]{1,0:T(8,128)(2,1)} custom-call(f32[8192,256]{1,0:T(8,128)} %bitcast.85, f32[1,256]{1,0:T(1,128)} %bitcast.98, f32[8192,1]{1,0:T(8,128)} %copy.48.n_ref), custom_call_target="tpu_custom_call" | custom-call | flops 4194304 | bytes 12582912 | tf_op jit(solution)/shard_map/pallas_call | solution.py:91
  (100 shorter events, 6.7 us)
Async XLA Ops:
  0.0 15.0 %copy-start.12 = (s32[256]{0:T(256)S(1)}, s32[256]{0:T(256)}, u32[]{:S(2)}) copy-start(s32[256]{0:T(256)} %param.27) | copy-start | bytes 3076
  0.0 19.2 %copy-start.6 = (bf16[256,256]{1,0:T(8,128)(2,1)S(1)}, bf16[256,256]{1,0:T(8,128)(2,1)}, u32[]{:S(2)}) copy-start(bf16[256,256]{1,0:T(8,128)(2,1)} %param.17) | copy-start | bytes 393220
  0.0 9.8 %copy-start.10 = (bf16[8192]{0:T(1024)(128)(2,1)S(1)}, bf16[8192]{0:T(1024)(128)(2,1)}, u32[]{:S(2)}) copy-start(bf16[8192]{0:T(1024)(128)(2,1)} %param.23) | copy-start | bytes 49156
  0.0 10.4 %copy-start.16 = (bf16[4,256]{1,0:T(4,128)(2,1)S(1)}, bf16[4,256]{1,0:T(4,128)(2,1)}, u32[]{:S(2)}) copy-start(bf16[4,256]{1,0:T(4,128)(2,1)} %param.24) | copy-start | bytes 6148
  0.0 10.4 %copy-start.20 = (bf16[256]{0:T(256)(128)(2,1)S(1)}, bf16[256]{0:T(256)(128)(2,1)}, u32[]{:S(2)}) copy-start(bf16[256]{0:T(256)(128)(2,1)} %param.25) | copy-start | bytes 1540
  2.6 11.7 %collective-permute-start.3 = (bf16[3,8449]{1,0:T(4,128)(2,1)S(1)}, bf16[3,8449]{1,0:T(4,128)(2,1)S(1)}, u32[]{:S(2)}, u32[]{:S(2)}) collective-permute-start(bf16[3,8449]{1,0:T(4,128)(2,1)S(1)} %pad_maximum_fusion.1), channel_id=1, source_target_pairs={{0,1},{1,2},{2,3},{3,4},{4,5},{5,6},{6,7},{7,8},{8,9},{9,10},{10,1... | collective-permute-start | bytes 152090 | tf_op jit(solution)/shard_map/ppermute | solution.py:23
  7.6 2.9 %collective-permute-start.5 = (s32[1]{0:T(128)}, s32[1]{0:T(128)}, u32[]{:S(2)}, u32[]{:S(2)}) collective-permute-start(s32[1]{0:T(128)} %slice.104), channel_id=1, source_target_pairs={{0,1},{1,0},{2,3},{3,2},{4,5},{5,4},{6,7},{7,6},{8,9},{9,8},{10,11... | collective-permute-start | bytes 20 | tf_op jit(solution)/shard_map/ppermute | solution.py:172
  8.7 12.2 %copy-start.4 = (f32[128,256]{1,0:T(8,128)}, f32[128,256]{1,0:T(8,128)S(1)}, u32[]{:S(2)}) copy-start(f32[128,256]{1,0:T(8,128)S(1)} %get-tuple-element.52) | copy-start | bytes 393220
  9.1 5.9 %copy-start.14 = (f32[128,2]{0,1:T(2,128)}, f32[128,2]{0,1:T(2,128)S(1)}, u32[]{:S(2)}) copy-start(f32[128,2]{0,1:T(2,128)S(1)} %slice_bitcast_fusion.3) | copy-start | bytes 3076
  11.8 2.4 collective-permute-start.6
  15.1 16.0 %collective-permute-start.7 = (s32[4]{0:T(128)S(1)}, s32[4]{0:T(128)S(1)}, u32[]{:S(2)}, u32[]{:S(2)}) collective-permute-start(s32[4]{0:T(128)S(1)} %broadcast_select_fusion.3), channel_id=1, source_target_pairs={{0,4},{1,5},{2,6},{3,7},{4,0},{5,1},{6,2},{7,3},{8,12},{9,13},{10,... | collective-permute-start | bytes 56 | tf_op jit(solution)/shard_map/ppermute | solution.py:172
  31.2 2.4 collective-permute-start.8
  33.6 7.4 %collective-permute-start.9 = (s32[16]{0:T(128)S(1)}, s32[16]{0:T(128)S(1)}, u32[]{:S(2)}, u32[]{:S(2)}) collective-permute-start(s32[16]{0:T(128)S(1)} %broadcast_select_fusion.5), channel_id=1, source_target_pairs={{0,16},{1,17},{2,18},{3,19},{4,20},{5,21},{6,22},{7,23},{8,24},{9,... | collective-permute-start | bytes 200 | tf_op jit(solution)/shard_map/ppermute | solution.py:172
  41.1 7.4 %collective-permute-start.10 = (f32[64,64,128]{2,1,0:T(8,128)}, f32[64,64,128]{2,1,0:T(8,128)S(1)}, u32[]{:S(2)}, u32[]{:S(2)}) collective-permute-start(f32[64,64,128]{2,1,0:T(8,128)} %bitcast.22), channel_id=1, source_target_pairs={{0,1},{1,0},{2,3},{3,2},{4,5},{5,4},{6,7},{7,6},{8,9},{9,8},{10,11... | collective-permute-start | bytes 6291464 | tf_op jit(solution)/shard_map/ppermute | solution.py:226
  45.8 2.5 collective-permute-start.4
  48.3 157.7 %copy-start.17 = (f32[64]{0:T(128)}, f32[64]{0:T(128)S(1)}, u32[]{:S(2)}) copy-start(f32[64]{0:T(128)S(1)} %get-tuple-element.49) | copy-start | bytes 772
  48.5 5.9 %copy-start.1 = (f32[64,64,128]{2,1,0:T(8,128)}, f32[64,64,128]{2,1,0:T(8,128)S(1)}, u32[]{:S(2)}) copy-start(f32[64,64,128]{2,1,0:T(8,128)S(1)} %collective-permute-done.10) | copy-start | bytes 6291460
  54.4 50.5 %collective-permute-start.13 = (f32[64,64,128]{2,1,0:T(8,128)S(1)}, f32[64,64,128]{2,1,0:T(8,128)S(1)}, u32[]{:S(2)}, u32[]{:S(2)}) collective-permute-start(f32[64,64,128]{2,1,0:T(8,128)S(1)} %get-tuple-element.46), channel_id=1, source_target_pairs={{0,2},{1,3},{2,4},{3,5},{4,6},{5,7},{6,8},{7,9},{8,10},{9,11},{10,... | collective-permute-start | bytes 6291464 | tf_op jit(solution)/shard_map/ppermute | solution.py:134
  104.9 49.6 %collective-permute-start.14 = (f32[64,64,128]{2,1,0:T(8,128)S(1)}, f32[64,64,128]{2,1,0:T(8,128)S(1)}, u32[]{:S(2)}, u32[]{:S(2)}) collective-permute-start(f32[64,64,128]{2,1,0:T(8,128)S(1)} %collective-permute-done.13), channel_id=1, source_target_pairs={{0,2},{1,3},{2,4},{3,5},{4,6},{5,7},{6,8},{7,9},{8,10},{9,11},{10,... | collective-permute-start | bytes 6291464 | tf_op jit(solution)/shard_map/ppermute | solution.py:134
  106.9 47.7 %collective-permute-start.11 = (f32[64]{0:T(128)S(1)}, f32[64]{0:T(128)S(1)}, u32[]{:S(2)}, u32[]{:S(2)}) collective-permute-start(f32[64]{0:T(128)S(1)} %mul.293), channel_id=1, source_target_pairs={{0,2},{1,3},{2,4},{3,5},{4,6},{5,7},{6,8},{7,9},{8,10},{9,11},{10,... | collective-permute-start | bytes 776 | tf_op jit(solution)/shard_map/ppermute | solution.py:134
  154.8 47.9 %copy-start.3 = (f32[64,64,128]{2,1,0:T(8,128)}, f32[64,64,128]{2,1,0:T(8,128)S(1)}, u32[]{:S(2)}) copy-start(f32[64,64,128]{2,1,0:T(8,128)S(1)} %multiply_add_fusion.3) | copy-start | bytes 6291460
  154.8 47.9 %collective-permute-start.15 = (f32[64,64,128]{2,1,0:T(8,128)S(1)}, f32[64,64,128]{2,1,0:T(8,128)}, u32[]{:S(2)}, u32[]{:S(2)}) collective-permute-start(f32[64,64,128]{2,1,0:T(8,128)S(1)} %multiply_add_fusion.3), channel_id=1, source_target_pairs={{0,4},{1,5},{2,6},{3,7},{4,8},{5,9},{6,10},{7,11},{8,12},{9,13},{1... | collective-permute-start | bytes 6291464 | tf_op jit(solution)/shard_map/ppermute | solution.py:134
  157.3 43.5 %collective-permute-start.12 = (f32[64]{0:T(128)S(1)}, f32[64]{0:T(128)S(1)}, u32[]{:S(2)}, u32[]{:S(2)}) collective-permute-start(f32[64]{0:T(128)S(1)} %collective-permute-done.11), channel_id=1, source_target_pairs={{0,2},{1,3},{2,4},{3,5},{4,6},{5,7},{6,8},{7,9},{8,10},{9,11},{10,... | collective-permute-start | bytes 776 | tf_op jit(solution)/shard_map/ppermute | solution.py:134
  200.8 5.2 %collective-permute-start.16 = (f32[64]{0:T(128)S(1)}, f32[64]{0:T(128)S(1)}, u32[]{:S(2)}, u32[]{:S(2)}) collective-permute-start(f32[64]{0:T(128)S(1)} %mul.336), channel_id=1, source_target_pairs={{0,4},{1,5},{2,6},{3,7},{4,8},{5,9},{6,10},{7,11},{8,12},{9,13},{1... | collective-permute-start | bytes 776 | tf_op jit(solution)/shard_map/ppermute | solution.py:134
  209.0 13.5 %copy-start.11 = (bf16[8192]{0:T(1024)(128)(2,1)S(1)}, bf16[8192]{0:T(1024)(128)(2,1)}, u32[]{:S(2)}) copy-start(bf16[8192]{0:T(1024)(128)(2,1)} %param.26) | copy-start | bytes 49156
  209.0 21.8 %collective-permute-start.17 = (bf16[64,64,128]{2,1,0:T(8,128)(2,1)}, bf16[64,64,128]{2,1,0:T(8,128)(2,1)S(1)}, u32[]{:S(2)}, u32[]{:S(2)}) collective-permute-start(bf16[64,64,128]{2,1,0:T(8,128)(2,1)} %fusion.28), channel_id=1, source_target_pairs={{0,1},{1,0},{2,3},{3,2},{4,5},{5,4},{6,7},{7,6},{8,9},{9,8},{10,11... | collective-permute-start | bytes 3145736 | tf_op jit(solution)/shard_map/ppermute | solution.py:234
  223.1 3.4 %copy-start.15 = (f32[128,2]{0,1:T(2,128)S(1)}, f32[128,2]{0,1:T(2,128)}, u32[]{:S(2)}) copy-start(f32[128,2]{0,1:T(2,128)} %copy-done.14) | copy-start | bytes 3076
  223.1 3.4 %copy-start.19 = (f32[256]{0:T(256)S(1)}, f32[256]{0:T(256)}, u32[]{:S(2)}) copy-start(f32[256]{0:T(256)} %get-tuple-element.69) | copy-start | bytes 3076
  223.1 6.5 %copy-start.13 = (s32[256]{0:T(256)S(1)}, s32[256]{0:T(256)}, u32[]{:S(2)}) copy-start(s32[256]{0:T(256)} %param.27) | copy-start | bytes 3076
  223.1 7.7 %copy-start.18 = (f32[64]{0:T(128)S(1)}, f32[64]{0:T(128)}, u32[]{:S(2)}) copy-start(f32[64]{0:T(128)} %copy-done.17) | copy-start | bytes 772
  233.1 2.2 copy-start
  233.1 2.2 copy-start.5
  233.1 2.2 copy-start.8
  233.1 2.2 copy-start.9
  235.3 9.5 %copy-start.2 = (bf16[256,8192]{0,1:T(8,128)(2,1)S(1)}, bf16[256,8192]{0,1:T(8,128)(2,1)}, u32[]{:S(2)}) copy-start(bf16[256,8192]{0,1:T(8,128)(2,1)} %copy.47) | copy-start | bytes 12582916
  235.3 9.5 %copy-start.7 = (f32[8192]{0:T(1024)S(1)}, f32[8192]{0:T(1024)}, u32[]{:S(2)}) copy-start(f32[8192]{0:T(1024)} %mul.348) | copy-start | bytes 98308

commit v18 on v16

--- a/solution.py
+++ b/solution.py
@@ -81,12 +81,13 @@
     )(rim8, values, weight, offset_bias.reshape(1, width), vis).T
 
 
-def scale_rows_kernel(g_ref, s_ref, n_ref, o_ref):
-    o_ref[...] = jnp.transpose(g_ref[...] * s_ref[...] * n_ref[...]).astype(o_ref.dtype)
-
-
-def scale_rows(gated, scale, gain):
-    rows, width = gated.shape
+def scale_rows_kernel(y_ref, z_ref, s_ref, n_ref, o_ref):
+    gated = y_ref[...] * jax.nn.silu(z_ref[...].astype(jnp.float32))
+    o_ref[...] = jnp.transpose(gated * s_ref[...] * n_ref[...]).astype(o_ref.dtype)
+
+
+def scale_rows(y_total, gate, scale, gain):
+    rows, width = y_total.shape
     tile = min(width, 2048)
     return pl.pallas_call(
         scale_rows_kernel,
@@ -94,12 +95,13 @@
         grid=(width // tile,),
         in_specs=[
             pl.BlockSpec((tile, rows), lambda j: (j, 0)),
+            pl.BlockSpec((tile, rows), lambda j: (j, 0)),
             pl.BlockSpec((1, rows), lambda j: (0, 0)),
             pl.BlockSpec((tile, 1), lambda j: (j, 0)),
         ],
         out_specs=pl.BlockSpec((rows, tile), lambda j: (0, j)),
-        cost_estimate=pl.CostEstimate(flops=2 * rows * width, transcendentals=0, bytes_accessed=6 * rows * width),
-    )(gated.T, scale[None, :], gain.astype(jnp.float32)[:, None])
+        cost_estimate=pl.CostEstimate(flops=2 * rows * width, transcendentals=0, bytes_accessed=8 * rows * width),
+    )(y_total.T, gate.T, scale[None, :], gain.astype(jnp.float32)[:, None])
 
 
 def mixing_part(x_group, b_group, c_group, step_size, cum_decay, segment):
@@ -337,7 +339,7 @@
     local_sq = jnp.sum(gated * gated, axis=1)
     total_sq = lax.psum(local_sq, "tp")
     scale = lax.rsqrt(total_sq / INNER + epsilon)
-    return scale_rows(gated, scale, norm_gain)
+    return scale_rows(y_total.reshape(tok_rows, channels), gate_z, scale, norm_gain)
 
 
 def cores_paired(mesh):

time: 250 us -> 251 us (level)
  no operation moved by 1% of the time
where the time goes in v18:
time: 251 us; the launch traced here: 250 us
  waiting for transfers between devices  131 us (52%)
  other arithmetic  28.4 us (11%)
  starting transfers between devices  28 us (11%)
  local copies, waits for them, and re-layouts  21.8 us (9%)
  Pallas kernels  19.2 us (8%)
  matrix products  18.6 us (7%)
    ppermute x6, waiting for transfers between devices, shifted(): lax.ppermute(value, axis, [(s, s + steps) for s in range(count - steps)])  124 us
    ppermute x6, starting transfers between devices, shifted(): lax.ppermute(value, axis, [(s, s + steps) for s in range(count - steps)])  13.3 us
    unnamed x20, local copies, waits for them, and re-layouts  10.3 us
    pallas_call x1, Pallas kernels, conv_rows(): pl.pallas_call(conv_rows_kernel, out_shape=jax.ShapeDtypeStruct((width, r...  10.2 us
    pallas_call x1, Pallas kernels, scale_rows(): pl.pallas_call(scale_rows_kernel, out_shape=jax.ShapeDtypeStruct((rows, w...  9.02 us
    dot_general x1, matrix products, mixing_part(): jnp.einsum('hij,jhp->ihp', mixing, x_group, preferred_element_type=jnp.fl...  8.86 us
    dot_general x1, matrix products, state_part(): jnp.einsum('hjn,jhp->hpn', weighted, x_group, preferred_element_type=jnp....  8.34 us
    reduce_sum x1, other arithmetic, local(): local_sq = jnp.sum(gated * gated, axis=1)  5.7 us
  transfers between devices with their start and end apart: 15, of which 8 were waited for; matrix products, arithmetic and copies ran while one was open for 19% of the time, Pallas kernels for 4%

profile of v18, /device:TPU:9, one launch (start us, length us, event | category | flops | bytes accessed | tf_op | source)
XLA Modules:
  0.0 249.7 jit_solution(2000314627687598923)
XLA Ops:
  0.0 1.3 slice.98
  2.6 0.9 slice.99
  4.5 3.0 %collective-permute-start.3 = (bf16[3,8449]{1,0:T(4,128)(2,1)S(1)}, bf16[3,8449]{1,0:T(4,128)(2,1)S(1)}, u32[]{:S(2)}, u32[]{:S(2)}) collective-permute-start(bf16[3,8449]{1,0:T(4,128)(2,1)S(1)} %pad_maximum_fusion.1), channel_id=1, source_target_pairs={{0,1},{1,2},{2,3},{3,4},{4,5},{5,6},{6,7},{7,8},{8,9},{9,10},{10,1... | collective-permute-start | bytes 152090 | tf_op jit(solution)/shard_map/ppermute | solution.py:23
  7.5 1.0 copy.22
  8.5 0.8 negate_multiply_fusion
  9.4 1.3 reshape.211.b_ref
  10.8 0.8 slice_convert_fusion.5
  12.3 1.4 broadcast_select_fusion.1
  13.7 1.2 collective-permute-start.6
  14.9 1.2 collective-permute-done.6
  16.2 1.3 collective-permute-start.7
  18.2 0.8 pad_add_fusion
  20.2 2.0 compare_convert_fusion.4
  22.3 0.9 copy.26.vis_ref
  23.2 1.5 multiply_convert_fusion.6
  24.8 0.8 fusion.37
  26.4 10.2 %shard_map.127 = bf16[8192,256]{1,0:T(8,128)(2,1)} custom-call(bf16[8,8192]{1,0:T(8,128)(2,1)} %concatenate.76.rim_ref, bf16[256,8192]{1,0:T(8,128)(2,1)} %x_ref.1, bf16[4,8192]{1,0:T(4,128)(2,1)} %w_ref.1, bf16[1,8192]{1,0:T(2,128)(2,1)} %reshape.211.b_ref, f32[3,256,1]{2,1,0:T(8,128)} %copy.26.vis_ref), custom_call_target="tpu_custom_call" | custom-call | flops 41943040 | bytes 8388608 | tf_op jit(solution)/shard_map/pallas_call | solution.py:66
  36.8 2.2 collective-permute-done.8
  39.1 2.3 collective-permute-start.9
  41.4 8.3 %fusion.17 = f32[1,128,64,128]{3,2,1,0:T(8,128)S(1)} fusion(bf16[256,128,64]{0,2,1:T(8,128)(2,1)} %bitcast.78, f32[128,256]{1,0:T(8,128)S(1)} %copy.27, f32[256,128]{1,0:T(8,128)S(1)} %get-tuple-element.83), kind=kOutput, calls=%fused_computation.26 | convolution fusion | flops 545259520 | bytes 8650752 | tf_op jit(solution)/shard_map/hjn,jhp->hpn/dot_general | solution.py:123
  50.2 1.9 copy-done
  52.2 1.5 constant_dynamic-slice_fusion
  53.6 2.3 collective-permute-start.10
  55.9 3.6 %collective-permute-done.4 = f32[128]{0:T(128)S(1)} collective-permute-done((f32[128]{0:T(128)S(1)}, f32[128]{0:T(128)S(1)}, u32[]{:S(2)}, u32[]{:S(2)}) %collective-permute-start.4) | collective-permute-done | bytes 544 | tf_op jit(solution)/shard_map/ppermute | solution.py:223
  59.9 2.8 %add_select_fusion = f32[64,64,128]{2,1,0:T(8,128)S(1)} fusion(f32[64,64,128]{2,1,0:T(8,128)S(1)} %collective-permute-done.10, f32[128,64,128]{2,1,0:T(8,128)} %copy-done, s32[]{:T(128)S(6)} %select_n.101, f32[64]{0:T(128)S(1)} %get-tuple-element.74, f32[64]{0:T(128)S(1)} %get-tuple-element.73, pred[]{:T(512)S(6)} %eq.73), kind=kLoop, calls=%fused_computation.35 | loop fusion | flops 2621440 | bytes 6291973 | tf_op jit(solution)/shard_map/jit(_where)/select_n | solution.py:228
  62.7 3.1 %collective-permute-start.13 = (f32[64,64,128]{2,1,0:T(8,128)S(1)}, f32[64,64,128]{2,1,0:T(8,128)S(1)}, u32[]{:S(2)}, u32[]{:S(2)}) collective-permute-start(f32[64,64,128]{2,1,0:T(8,128)S(1)} %add_select_fusion), channel_id=1, source_target_pairs={{0,2},{1,3},{2,4},{3,5},{4,6},{5,7},{6,8},{7,9},{8,10},{9,11},{10,... | collective-permute-start | bytes 6291464 | tf_op jit(solution)/shard_map/ppermute | solution.py:136
  65.8 47.4 %collective-permute-done.13 = f32[64,64,128]{2,1,0:T(8,128)S(1)} collective-permute-done((f32[64,64,128]{2,1,0:T(8,128)S(1)}, f32[64,64,128]{2,1,0:T(8,128)S(1)}, u32[]{:S(2)}, u32[]{:S(2)}) %collective-permute-start.13) | collective-permute-done | bytes 2097184 | tf_op jit(solution)/shard_map/ppermute | solution.py:136
  113.2 1.9 collective-permute-start.14
  115.2 2.4 collective-permute-start.11
  117.6 45.3 %collective-permute-done.11 = f32[64]{0:T(128)S(1)} collective-permute-done((f32[64]{0:T(128)S(1)}, f32[64]{0:T(128)S(1)}, u32[]{:S(2)}, u32[]{:S(2)}) %collective-permute-start.11) | collective-permute-done | bytes 288 | tf_op jit(solution)/shard_map/ppermute | solution.py:136
  162.8 1.6 multiply_add_fusion.3
  164.5 2.0 collective-permute-start.15
  166.5 6.4 %copy.36 = bf16[256,8192]{0,1:T(8,128)(2,1)} copy(bf16[256,8192]{1,0:T(8,128)(2,1)} %param.16) | data formatting | bytes 8388608 | tf_op args[1]
  173.1 2.6 %copy.38.n_ref = f32[8192,1]{1,0:T(8,128)} copy(f32[8192,1]{0,1:T(1,128)S(1)} %bitcast.84) | data formatting | bytes 65536 | tf_op jit(solution)/shard_map/broadcast_in_dim | solution.py:104
  176.3 0.7 compare_reduce_fusion
  178.0 1.9 collective-permute-start.12
  180.1 30.6 %collective-permute-done.12 = f32[64]{0:T(128)S(1)} collective-permute-done((f32[64]{0:T(128)S(1)}, f32[64]{0:T(128)S(1)}, u32[]{:S(2)}, u32[]{:S(2)}) %collective-permute-start.12) | collective-permute-done | bytes 288 | tf_op jit(solution)/shard_map/ppermute | solution.py:136
  210.7 1.9 collective-permute-start.16
  212.7 2.5 multiply_add_fusion.2
  215.2 0.8 collective-permute-done.16
  215.9 2.8 %fusion.21 = bf16[64,64,128]{2,1,0:T(8,128)(2,1)S(1)} fusion(f32[64,64,128]{2,1,0:T(8,128)S(1)} %get-tuple-element.93, f32[64,64,128]{2,1,0:T(8,128)} %copy-done.3, f32[128,64,128]{2,1,0:T(8,128)} %copy-done, s32[]{:T(128)S(6)} %select_n.101, f32[64]{0:T(128)S(1)} %get-tuple-element.72, pred[]{:T(512)S(6)} %eq.73), kind=kLoop, calls=%fused_computation.36 | loop fusion | flops 2097152 | bytes 7340293 | tf_op jit(solution)/shard_map/jit(_where)/select_n | solution.py:234
  218.7 3.7 %collective-permute-start.17 = (bf16[64,64,128]{2,1,0:T(8,128)(2,1)S(1)}, bf16[64,64,128]{2,1,0:T(8,128)(2,1)S(1)}, u32[]{:S(2)}, u32[]{:S(2)}) collective-permute-start(bf16[64,64,128]{2,1,0:T(8,128)(2,1)S(1)} %fusion.21), channel_id=1, source_target_pairs={{0,1},{1,0},{2,3},{3,2},{4,5},{5,4},{6,7},{7,6},{8,9},{9,8},{10,11... | collective-permute-start | bytes 3145736 | tf_op jit(solution)/shard_map/ppermute | solution.py:234
  222.4 8.9 %fusion = f32[128,64,256]{2,1,0:T(8,128)S(1)} fusion(f32[128,256]{1,0:T(8,128)S(1)} %copy.31, f32[128,256]{1,0:T(8,128)S(1)} %copy.29, f32[256,256]{1,0:T(8,128)S(1)} %fusion.29, pred[256,256]{1,0:T(8,128)(4,1)S(1)} %fusion.23, bf16[1,256,128,64]{1,3,2,0:T(8,128)(2,1)S(1)} %bitcast.79), kind=kOutput, calls=%fused_computation.3 | convolution fusion | flops 1115684864 | bytes 13172736 | tf_op jit(solution)/shard_map/hij,jhp->ihp/dot_general | solution.py:115
  231.3 0.7 select_convert_fusion.1
  232.2 1.3 bitcast_add_fusion.1
  233.5 0.9 copy-done.2
  234.4 5.7 %fusion.15 = (f32[256]{0:T(256)S(1)}, f32[256,8192]{0,1:T(8,128)}) fusion(bf16[256,8192]{0,1:T(8,128)(2,1)S(1)} %copy-done.2, bf16[256,8192]{0,1:T(8,128)(2,1)S(1)} %bitcast.80, f32[8192]{0:T(1024)S(1)} %mul.331, f32[256,128,64]{0,2,1:T(8,128)S(1)} %bitcast_add_fusion.1), kind=kLoop, calls=%fused_computation.23 | loop fusion | flops 23068416 | bytes 25199616 | tf_op jit(solution)/shard_map/reduce_sum | solution.py:339
  240.6 9.0 %shard_map.128 = bf16[256,8192]{1,0:T(8,128)(2,1)} custom-call(f32[8192,256]{1,0:T(8,128)} %bitcast.77, bf16[8192,256]{1,0:T(8,128)(2,1)} %bitcast.76, f32[1,256]{1,0:T(1,128)} %bitcast.92, f32[8192,1]{1,0:T(8,128)} %copy.38.n_ref), custom_call_target="tpu_custom_call" | custom-call | flops 4194304 | bytes 16777216 | tf_op jit(solution)/shard_map/pallas_call | solution.py:92
  (76 shorter events, 7.9 us)
Async XLA Ops:
  1.3 11.1 %collective-permute-start.5 = (s32[1]{0:T(128)}, s32[1]{0:T(128)}, u32[]{:S(2)}, u32[]{:S(2)}) collective-permute-start(s32[1]{0:T(128)} %slice.98), channel_id=1, source_target_pairs={{0,1},{1,0},{2,3},{3,2},{4,5},{5,4},{6,7},{7,6},{8,9},{9,8},{10,11... | collective-permute-start | bytes 20 | tf_op jit(solution)/shard_map/ppermute | solution.py:174
  4.5 11.7 %collective-permute-start.3 = (bf16[3,8449]{1,0:T(4,128)(2,1)S(1)}, bf16[3,8449]{1,0:T(4,128)(2,1)S(1)}, u32[]{:S(2)}, u32[]{:S(2)}) collective-permute-start(bf16[3,8449]{1,0:T(4,128)(2,1)S(1)} %pad_maximum_fusion.1), channel_id=1, source_target_pairs={{0,1},{1,2},{2,3},{3,4},{4,5},{5,6},{6,7},{7,8},{8,9},{9,10},{10,1... | collective-permute-start | bytes 152090 | tf_op jit(solution)/shard_map/ppermute | solution.py:23
  13.7 2.4 collective-permute-start.6
  16.2 20.4 %collective-permute-start.7 = (s32[4]{0:T(128)S(1)}, s32[4]{0:T(128)S(1)}, u32[]{:S(2)}, u32[]{:S(2)}) collective-permute-start(s32[4]{0:T(128)S(1)} %broadcast_select_fusion.2), channel_id=1, source_target_pairs={{0,4},{1,5},{2,6},{3,7},{4,0},{5,1},{6,2},{7,3},{8,12},{9,13},{10,... | collective-permute-start | bytes 56 | tf_op jit(solution)/shard_map/ppermute | solution.py:174
  36.7 2.4 collective-permute-start.8
  39.1 10.7 %collective-permute-start.9 = (s32[16]{0:T(128)S(1)}, s32[16]{0:T(128)S(1)}, u32[]{:S(2)}, u32[]{:S(2)}) collective-permute-start(s32[16]{0:T(128)S(1)} %broadcast_select_fusion.4), channel_id=1, source_target_pairs={{0,16},{1,17},{2,18},{3,19},{4,20},{5,21},{6,22},{7,23},{8,24},{9,... | collective-permute-start | bytes 200 | tf_op jit(solution)/shard_map/ppermute | solution.py:174
  50.2 1.9 copy-start
  53.6 6.3 %collective-permute-start.10 = (f32[64,64,128]{2,1,0:T(8,128)}, f32[64,64,128]{2,1,0:T(8,128)S(1)}, u32[]{:S(2)}, u32[]{:S(2)}) collective-permute-start(f32[64,64,128]{2,1,0:T(8,128)} %constant_dynamic-slice_fusion), channel_id=1, source_target_pairs={{0,1},{1,0},{2,3},{3,2},{4,5},{5,4},{6,7},{7,6},{8,9},{9,8},{10,11... | collective-permute-start | bytes 6291464 | tf_op jit(solution)/shard_map/ppermute | solution.py:223
  55.9 3.6 %collective-permute-start.4 = (f32[128]{0:T(128)S(1)}, f32[128]{0:T(128)S(1)}, u32[]{:S(2)}, u32[]{:S(2)}) collective-permute-start(f32[128]{0:T(128)S(1)} %get-tuple-element.78), channel_id=1, source_target_pairs={{0,1},{1,0},{2,3},{3,2},{4,5},{5,4},{6,7},{7,6},{8,9},{9,8},{10,11... | collective-permute-start | bytes 1544 | tf_op jit(solution)/shard_map/ppermute | solution.py:223
  59.9 104.5 %copy-start.3 = (f32[64,64,128]{2,1,0:T(8,128)}, f32[64,64,128]{2,1,0:T(8,128)S(1)}, u32[]{:S(2)}) copy-start(f32[64,64,128]{2,1,0:T(8,128)S(1)} %collective-permute-done.10) | copy-start | bytes 6291460
  62.7 50.5 %collective-permute-start.13 = (f32[64,64,128]{2,1,0:T(8,128)S(1)}, f32[64,64,128]{2,1,0:T(8,128)S(1)}, u32[]{:S(2)}, u32[]{:S(2)}) collective-permute-start(f32[64,64,128]{2,1,0:T(8,128)S(1)} %add_select_fusion), channel_id=1, source_target_pairs={{0,2},{1,3},{2,4},{3,5},{4,6},{5,7},{6,8},{7,9},{8,10},{9,11},{10,... | collective-permute-start | bytes 6291464 | tf_op jit(solution)/shard_map/ppermute | solution.py:136
  113.2 49.6 %collective-permute-start.14 = (f32[64,64,128]{2,1,0:T(8,128)S(1)}, f32[64,64,128]{2,1,0:T(8,128)S(1)}, u32[]{:S(2)}, u32[]{:S(2)}) collective-permute-start(f32[64,64,128]{2,1,0:T(8,128)S(1)} %collective-permute-done.13), channel_id=1, source_target_pairs={{0,2},{1,3},{2,4},{3,5},{4,6},{5,7},{6,8},{7,9},{8,10},{9,11},{10,... | collective-permute-start | bytes 6291464 | tf_op jit(solution)/shard_map/ppermute | solution.py:136
  115.2 47.7 %collective-permute-start.11 = (f32[64]{0:T(128)S(1)}, f32[64]{0:T(128)S(1)}, u32[]{:S(2)}, u32[]{:S(2)}) collective-permute-start(f32[64]{0:T(128)S(1)} %mul.278), channel_id=1, source_target_pairs={{0,2},{1,3},{2,4},{3,5},{4,6},{5,7},{6,8},{7,9},{8,10},{9,11},{10,... | collective-permute-start | bytes 776 | tf_op jit(solution)/shard_map/ppermute | solution.py:136
  164.5 8.4 %copy-start.8 = (f32[128]{0:T(128)S(1)}, f32[128]{0:T(128)}, u32[]{:S(2)}) copy-start(f32[128]{0:T(128)} %param.21) | copy-start | bytes 1540
  164.5 8.6 %copy-start.6 = (bf16[8192]{0:T(1024)(128)(2,1)S(1)}, bf16[8192]{0:T(1024)(128)(2,1)}, u32[]{:S(2)}) copy-start(bf16[8192]{0:T(1024)(128)(2,1)} %param.26) | copy-start | bytes 49156
  164.5 48.2 %collective-permute-start.15 = (f32[64,64,128]{2,1,0:T(8,128)}, f32[64,64,128]{2,1,0:T(8,128)}, u32[]{:S(2)}, u32[]{:S(2)}) collective-permute-start(f32[64,64,128]{2,1,0:T(8,128)} %multiply_add_fusion.3), channel_id=1, source_target_pairs={{0,4},{1,5},{2,6},{3,7},{4,8},{5,9},{6,10},{7,11},{8,12},{9,13},{1... | collective-permute-start | bytes 6291464 | tf_op jit(solution)/shard_map/ppermute | solution.py:136
  172.9 4.8 %copy-start.7 = (s32[256]{0:T(256)S(1)}, s32[256]{0:T(256)}, u32[]{:S(2)}) copy-start(s32[256]{0:T(256)} %param.27) | copy-start | bytes 3076
  178.0 32.7 %collective-permute-start.12 = (f32[64]{0:T(128)S(1)}, f32[64]{0:T(128)S(1)}, u32[]{:S(2)}, u32[]{:S(2)}) collective-permute-start(f32[64]{0:T(128)S(1)} %collective-permute-done.11), channel_id=1, source_target_pairs={{0,2},{1,3},{2,4},{3,5},{4,6},{5,7},{6,8},{7,9},{8,10},{9,11},{10,... | collective-permute-start | bytes 776 | tf_op jit(solution)/shard_map/ppermute | solution.py:136
  210.7 5.2 %collective-permute-start.16 = (f32[64]{0:T(128)S(1)}, f32[64]{0:T(128)S(1)}, u32[]{:S(2)}, u32[]{:S(2)}) collective-permute-start(f32[64]{0:T(128)S(1)} %mul.319), channel_id=1, source_target_pairs={{0,4},{1,5},{2,6},{3,7},{4,8},{5,9},{6,10},{7,11},{8,12},{9,13},{1... | collective-permute-start | bytes 776 | tf_op jit(solution)/shard_map/ppermute | solution.py:136
  215.9 6.5 %copy-start.5 = (bf16[8192,256]{1,0:T(8,128)(2,1)S(1)}, bf16[8192,256]{1,0:T(8,128)(2,1)}, u32[]{:S(2)}) copy-start(bf16[8192,256]{1,0:T(8,128)(2,1)} %shard_map.127) | copy-start | bytes 12582916
  218.7 12.6 %copy-start.1 = (f32[128,64,128]{2,1,0:T(8,128)S(1)}, f32[128,64,128]{2,1,0:T(8,128)}, u32[]{:S(2)}) copy-start(f32[128,64,128]{2,1,0:T(8,128)} %copy-done) | copy-start | bytes 12582916
  218.7 12.6 %copy-start.4 = (f32[64,64,128]{2,1,0:T(8,128)S(1)}, f32[64,64,128]{2,1,0:T(8,128)}, u32[]{:S(2)}) copy-start(f32[64,64,128]{2,1,0:T(8,128)} %copy-done.3) | copy-start | bytes 6291460
  218.7 12.6 %collective-permute-start.17 = (bf16[64,64,128]{2,1,0:T(8,128)(2,1)S(1)}, bf16[64,64,128]{2,1,0:T(8,128)(2,1)S(1)}, u32[]{:S(2)}, u32[]{:S(2)}) collective-permute-start(bf16[64,64,128]{2,1,0:T(8,128)(2,1)S(1)} %fusion.21), channel_id=1, source_target_pairs={{0,1},{1,0},{2,3},{3,2},{4,5},{5,4},{6,7},{7,6},{8,9},{9,8},{10,11... | collective-permute-start | bytes 3145736 | tf_op jit(solution)/shard_map/ppermute | solution.py:234
  232.2 2.2 copy-start.2

commit v19 on v16

--- a/solution.py
+++ b/solution.py
@@ -62,7 +62,7 @@
         [(ext_segment[k : k + rows] == segment).astype(jnp.float32) for k in range(CONV - 1)]
     )[:, :, None]
     rim8 = jnp.concatenate([rim_vals, jnp.zeros((8 - rim_vals.shape[0], width), rim_vals.dtype)])
-    tile = min(width, 2048)
+    tile = min(width, 4096)
     return pl.pallas_call(
         conv_rows_kernel,
         out_shape=jax.ShapeDtypeStruct((width, rows), jnp.bfloat16),
@@ -87,7 +87,7 @@
 
 def scale_rows(gated, scale, gain):
     rows, width = gated.shape
-    tile = min(width, 2048)
+    tile = min(width, 4096)
     return pl.pallas_call(
         scale_rows_kernel,
         out_shape=jax.ShapeDtypeStruct((rows, width), jnp.bfloat16),

time: 250 us -> 250 us (level)
  no operation moved by 1% of the time
where the time goes in v19:
time: 250 us; the launch traced here: 249 us
  waiting for transfers between devices  131 us (52%)
  other arithmetic  28.3 us (11%)
  starting transfers between devices  28 us (11%)
  local copies, waits for them, and re-layouts  21.9 us (9%)
  matrix products  18.6 us (7%)
  Pallas kernels  18.4 us (7%)
    ppermute x6, waiting for transfers between devices, shifted(): lax.ppermute(value, axis, [(s, s + steps) for s in range(count - steps)])  124 us
    ppermute x6, starting transfers between devices, shifted(): lax.ppermute(value, axis, [(s, s + steps) for s in range(count - steps)])  13.3 us
    pallas_call x1, Pallas kernels, conv_rows(): pl.pallas_call(conv_rows_kernel, out_shape=jax.ShapeDtypeStruct((width, r...  11 us
    unnamed x20, local copies, waits for them, and re-layouts  10.3 us
    dot_general x1, matrix products, mixing_part(): jnp.einsum('hij,jhp->ihp', mixing, x_group, preferred_element_type=jnp.fl...  8.86 us
    dot_general x1, matrix products, state_part(): jnp.einsum('hjn,jhp->hpn', weighted, x_group, preferred_element_type=jnp....  8.34 us
    pallas_call x1, Pallas kernels, scale_rows(): pl.pallas_call(scale_rows_kernel, out_shape=jax.ShapeDtypeStruct((rows, w...  7.36 us
    reduce_sum x1, other arithmetic, local(): local_sq = jnp.sum(gated * gated, axis=1)  5.72 us
  transfers between devices with their start and end apart: 15, of which 8 were waited for; matrix products, arithmetic and copies ran while one was open for 19% of the time, Pallas kernels for 4%

profile of v19, /device:TPU:9, one launch (start us, length us, event | category | flops | bytes accessed | tf_op | source)
XLA Modules:
  0.0 248.9 jit_solution(11695524927427364251)
XLA Ops:
  0.0 1.3 slice.98
  2.6 0.9 slice.99
  4.5 3.0 %collective-permute-start.3 = (bf16[3,8449]{1,0:T(4,128)(2,1)S(1)}, bf16[3,8449]{1,0:T(4,128)(2,1)S(1)}, u32[]{:S(2)}, u32[]{:S(2)}) collective-permute-start(bf16[3,8449]{1,0:T(4,128)(2,1)S(1)} %pad_maximum_fusion.1), channel_id=1, source_target_pairs={{0,1},{1,2},{2,3},{3,4},{4,5},{5,6},{6,7},{7,8},{8,9},{9,10},{10,1... | collective-permute-start | bytes 152090 | tf_op jit(solution)/shard_map/ppermute | solution.py:23
  7.5 1.0 copy.21
  8.5 0.8 negate_multiply_fusion
  9.4 1.3 reshape.210.b_ref
  10.8 0.8 slice_convert_fusion.5
  12.3 1.4 broadcast_select_fusion.1
  13.7 1.2 collective-permute-start.6
  14.9 1.2 collective-permute-done.6
  16.2 1.3 collective-permute-start.7
  18.2 0.8 pad_add_fusion
  20.2 2.0 compare_convert_fusion.4
  22.3 0.9 copy.25.vis_ref
  23.2 1.5 multiply_convert_fusion.6
  24.9 0.8 fusion.35
  26.4 11.0 %shard_map.127 = bf16[8192,256]{1,0:T(8,128)(2,1)} custom-call(bf16[8,8192]{1,0:T(8,128)(2,1)} %concatenate.76.rim_ref, bf16[256,8192]{1,0:T(8,128)(2,1)} %x_ref.1, bf16[4,8192]{1,0:T(4,128)(2,1)} %w_ref.1, bf16[1,8192]{1,0:T(2,128)(2,1)} %reshape.210.b_ref, f32[3,256,1]{2,1,0:T(8,128)} %copy.25.vis_ref), custom_call_target="tpu_custom_call" | custom-call | flops 41943040 | bytes 8388608 | tf_op jit(solution)/shard_map/pallas_call | solution.py:66
  37.7 2.2 collective-permute-done.8
  40.0 2.3 collective-permute-start.9
  42.3 8.3 %fusion.15 = f32[1,128,64,128]{3,2,1,0:T(8,128)S(1)} fusion(bf16[256,128,64]{0,2,1:T(8,128)(2,1)} %bitcast.78, f32[128,256]{1,0:T(8,128)S(1)} %copy.26, f32[256,128]{1,0:T(8,128)S(1)} %get-tuple-element.83), kind=kOutput, calls=%fused_computation.25 | convolution fusion | flops 545259520 | bytes 8650752 | tf_op jit(solution)/shard_map/hjn,jhp->hpn/dot_general | solution.py:121
  51.1 2.0 copy-done
  53.1 1.5 constant_dynamic-slice_fusion
  54.5 2.3 collective-permute-start.10
  56.8 3.6 %collective-permute-done.4 = f32[128]{0:T(128)S(1)} collective-permute-done((f32[128]{0:T(128)S(1)}, f32[128]{0:T(128)S(1)}, u32[]{:S(2)}, u32[]{:S(2)}) %collective-permute-start.4) | collective-permute-done | bytes 544 | tf_op jit(solution)/shard_map/ppermute | solution.py:221
  60.8 2.8 %add_select_fusion = f32[64,64,128]{2,1,0:T(8,128)S(1)} fusion(f32[64,64,128]{2,1,0:T(8,128)S(1)} %collective-permute-done.10, f32[128,64,128]{2,1,0:T(8,128)} %copy-done, s32[]{:T(128)S(6)} %select_n.101, f32[64]{0:T(128)S(1)} %get-tuple-element.74, f32[64]{0:T(128)S(1)} %get-tuple-element.73, pred[]{:T(512)S(6)} %eq.73), kind=kLoop, calls=%fused_computation.34 | loop fusion | flops 2621440 | bytes 6291973 | tf_op jit(solution)/shard_map/jit(_where)/select_n | solution.py:226
  63.6 3.1 %collective-permute-start.13 = (f32[64,64,128]{2,1,0:T(8,128)S(1)}, f32[64,64,128]{2,1,0:T(8,128)S(1)}, u32[]{:S(2)}, u32[]{:S(2)}) collective-permute-start(f32[64,64,128]{2,1,0:T(8,128)S(1)} %add_select_fusion), channel_id=1, source_target_pairs={{0,2},{1,3},{2,4},{3,5},{4,6},{5,7},{6,8},{7,9},{8,10},{9,11},{10,... | collective-permute-start | bytes 6291464 | tf_op jit(solution)/shard_map/ppermute | solution.py:134
  66.7 47.4 %collective-permute-done.13 = f32[64,64,128]{2,1,0:T(8,128)S(1)} collective-permute-done((f32[64,64,128]{2,1,0:T(8,128)S(1)}, f32[64,64,128]{2,1,0:T(8,128)S(1)}, u32[]{:S(2)}, u32[]{:S(2)}) %collective-permute-start.13) | collective-permute-done | bytes 2097184 | tf_op jit(solution)/shard_map/ppermute | solution.py:134
  114.1 1.9 collective-permute-start.14
  116.1 2.4 collective-permute-start.11
  118.5 45.3 %collective-permute-done.11 = f32[64]{0:T(128)S(1)} collective-permute-done((f32[64]{0:T(128)S(1)}, f32[64]{0:T(128)S(1)}, u32[]{:S(2)}, u32[]{:S(2)}) %collective-permute-start.11) | collective-permute-done | bytes 288 | tf_op jit(solution)/shard_map/ppermute | solution.py:134
  163.7 1.6 multiply_add_fusion.3
  165.3 2.0 collective-permute-start.15
  167.4 6.4 %copy.35 = bf16[256,8192]{0,1:T(8,128)(2,1)} copy(bf16[256,8192]{1,0:T(8,128)(2,1)} %param.16) | data formatting | bytes 8388608 | tf_op args[1]
  173.9 2.6 %copy.36.n_ref = f32[8192,1]{1,0:T(8,128)} copy(f32[8192,1]{0,1:T(1,128)S(1)} %bitcast.84) | data formatting | bytes 65536 | tf_op jit(solution)/shard_map/broadcast_in_dim | solution.py:102
  177.2 0.7 compare_reduce_fusion
  178.9 1.9 collective-permute-start.12
  181.0 30.6 %collective-permute-done.12 = f32[64]{0:T(128)S(1)} collective-permute-done((f32[64]{0:T(128)S(1)}, f32[64]{0:T(128)S(1)}, u32[]{:S(2)}, u32[]{:S(2)}) %collective-permute-start.12) | collective-permute-done | bytes 288 | tf_op jit(solution)/shard_map/ppermute | solution.py:134
  211.6 1.9 collective-permute-start.16
  213.5 2.5 multiply_add_fusion.2
  216.0 0.8 collective-permute-done.16
  216.8 2.8 %fusion.19 = bf16[64,64,128]{2,1,0:T(8,128)(2,1)S(1)} fusion(f32[64,64,128]{2,1,0:T(8,128)S(1)} %get-tuple-element.93, f32[64,64,128]{2,1,0:T(8,128)} %copy-done.2, f32[128,64,128]{2,1,0:T(8,128)} %copy-done, s32[]{:T(128)S(6)} %select_n.101, f32[64]{0:T(128)S(1)} %get-tuple-element.72, pred[]{:T(512)S(6)} %eq.73), kind=kLoop, calls=%fused_computation.35 | loop fusion | flops 2097152 | bytes 7340293 | tf_op jit(solution)/shard_map/jit(_where)/select_n | solution.py:232
  219.6 3.7 %collective-permute-start.17 = (bf16[64,64,128]{2,1,0:T(8,128)(2,1)S(1)}, bf16[64,64,128]{2,1,0:T(8,128)(2,1)S(1)}, u32[]{:S(2)}, u32[]{:S(2)}) collective-permute-start(bf16[64,64,128]{2,1,0:T(8,128)(2,1)S(1)} %fusion.19), channel_id=1, source_target_pairs={{0,1},{1,0},{2,3},{3,2},{4,5},{5,4},{6,7},{7,6},{8,9},{9,8},{10,11... | collective-permute-start | bytes 3145736 | tf_op jit(solution)/shard_map/ppermute | solution.py:232
  223.3 8.9 %fusion = f32[128,64,256]{2,1,0:T(8,128)S(1)} fusion(f32[128,256]{1,0:T(8,128)S(1)} %copy.30, f32[128,256]{1,0:T(8,128)S(1)} %copy.28, f32[256,256]{1,0:T(8,128)S(1)} %fusion.27, pred[256,256]{1,0:T(8,128)(4,1)S(1)} %fusion.21, bf16[1,256,128,64]{1,3,2,0:T(8,128)(2,1)S(1)} %bitcast.79), kind=kOutput, calls=%fused_computation.3 | convolution fusion | flops 1115684864 | bytes 13172736 | tf_op jit(solution)/shard_map/hij,jhp->ihp/dot_general | solution.py:113
  232.2 0.7 select_convert_fusion.1
  233.0 1.3 bitcast_add_fusion.1
  234.3 0.9 copy-done.5
  235.2 5.7 %multiply_reduce_fusion = (f32[256]{0:T(256)S(1)}, f32[256,8192]{0,1:T(8,128)}) fusion(bf16[256,8192]{0,1:T(8,128)(2,1)S(1)} %copy-done.5, bf16[256,8192]{0,1:T(8,128)(2,1)S(1)} %bitcast.80, f32[8192]{0:T(1024)S(1)} %mul.331, f32[256,128,64]{0,2,1:T(8,128)S(1)} %bitcast_add_fusion.1), kind=kLoop, calls=%fused_computation.20 | loop fusion | flops 23068416 | bytes 25199616 | tf_op jit(solution)/shard_map/reduce_sum | solution.py:337
  241.5 7.4 %shard_map.128 = bf16[256,8192]{1,0:T(8,128)(2,1)} custom-call(f32[8192,256]{1,0:T(8,128)} %bitcast.77, f32[1,256]{1,0:T(1,128)} %bitcast.88, f32[8192,1]{1,0:T(8,128)} %copy.36.n_ref), custom_call_target="tpu_custom_call" | custom-call | flops 4194304 | bytes 12582912 | tf_op jit(solution)/shard_map/pallas_call | solution.py:91
  (76 shorter events, 7.9 us)
Async XLA Ops:
  1.3 11.1 %collective-permute-start.5 = (s32[1]{0:T(128)}, s32[1]{0:T(128)}, u32[]{:S(2)}, u32[]{:S(2)}) collective-permute-start(s32[1]{0:T(128)} %slice.98), channel_id=1, source_target_pairs={{0,1},{1,0},{2,3},{3,2},{4,5},{5,4},{6,7},{7,6},{8,9},{9,8},{10,11... | collective-permute-start | bytes 20 | tf_op jit(solution)/shard_map/ppermute | solution.py:172
  4.5 11.7 %collective-permute-start.3 = (bf16[3,8449]{1,0:T(4,128)(2,1)S(1)}, bf16[3,8449]{1,0:T(4,128)(2,1)S(1)}, u32[]{:S(2)}, u32[]{:S(2)}) collective-permute-start(bf16[3,8449]{1,0:T(4,128)(2,1)S(1)} %pad_maximum_fusion.1), channel_id=1, source_target_pairs={{0,1},{1,2},{2,3},{3,4},{4,5},{5,6},{6,7},{7,8},{8,9},{9,10},{10,1... | collective-permute-start | bytes 152090 | tf_op jit(solution)/shard_map/ppermute | solution.py:23
  13.7 2.4 collective-permute-start.6
  16.2 21.3 %collective-permute-start.7 = (s32[4]{0:T(128)S(1)}, s32[4]{0:T(128)S(1)}, u32[]{:S(2)}, u32[]{:S(2)}) collective-permute-start(s32[4]{0:T(128)S(1)} %broadcast_select_fusion.2), channel_id=1, source_target_pairs={{0,4},{1,5},{2,6},{3,7},{4,0},{5,1},{6,2},{7,3},{8,12},{9,13},{10,... | collective-permute-start | bytes 56 | tf_op jit(solution)/shard_map/ppermute | solution.py:172
  37.5 2.4 collective-permute-start.8
  40.0 10.7 %collective-permute-start.9 = (s32[16]{0:T(128)S(1)}, s32[16]{0:T(128)S(1)}, u32[]{:S(2)}, u32[]{:S(2)}) collective-permute-start(s32[16]{0:T(128)S(1)} %broadcast_select_fusion.4), channel_id=1, source_target_pairs={{0,16},{1,17},{2,18},{3,19},{4,20},{5,21},{6,22},{7,23},{8,24},{9,... | collective-permute-start | bytes 200 | tf_op jit(solution)/shard_map/ppermute | solution.py:172
  51.1 2.0 copy-start
  54.5 6.3 %collective-permute-start.10 = (f32[64,64,128]{2,1,0:T(8,128)}, f32[64,64,128]{2,1,0:T(8,128)S(1)}, u32[]{:S(2)}, u32[]{:S(2)}) collective-permute-start(f32[64,64,128]{2,1,0:T(8,128)} %constant_dynamic-slice_fusion), channel_id=1, source_target_pairs={{0,1},{1,0},{2,3},{3,2},{4,5},{5,4},{6,7},{7,6},{8,9},{9,8},{10,11... | collective-permute-start | bytes 6291464 | tf_op jit(solution)/shard_map/ppermute | solution.py:221
  56.8 3.6 %collective-permute-start.4 = (f32[128]{0:T(128)S(1)}, f32[128]{0:T(128)S(1)}, u32[]{:S(2)}, u32[]{:S(2)}) collective-permute-start(f32[128]{0:T(128)S(1)} %get-tuple-element.78), channel_id=1, source_target_pairs={{0,1},{1,0},{2,3},{3,2},{4,5},{5,4},{6,7},{7,6},{8,9},{9,8},{10,11... | collective-permute-start | bytes 1544 | tf_op jit(solution)/shard_map/ppermute | solution.py:221
  60.8 104.5 %copy-start.2 = (f32[64,64,128]{2,1,0:T(8,128)}, f32[64,64,128]{2,1,0:T(8,128)S(1)}, u32[]{:S(2)}) copy-start(f32[64,64,128]{2,1,0:T(8,128)S(1)} %collective-permute-done.10) | copy-start | bytes 6291460
  63.6 50.5 %collective-permute-start.13 = (f32[64,64,128]{2,1,0:T(8,128)S(1)}, f32[64,64,128]{2,1,0:T(8,128)S(1)}, u32[]{:S(2)}, u32[]{:S(2)}) collective-permute-start(f32[64,64,128]{2,1,0:T(8,128)S(1)} %add_select_fusion), channel_id=1, source_target_pairs={{0,2},{1,3},{2,4},{3,5},{4,6},{5,7},{6,8},{7,9},{8,10},{9,11},{10,... | collective-permute-start | bytes 6291464 | tf_op jit(solution)/shard_map/ppermute | solution.py:134
  114.1 49.6 %collective-permute-start.14 = (f32[64,64,128]{2,1,0:T(8,128)S(1)}, f32[64,64,128]{2,1,0:T(8,128)S(1)}, u32[]{:S(2)}, u32[]{:S(2)}) collective-permute-start(f32[64,64,128]{2,1,0:T(8,128)S(1)} %collective-permute-done.13), channel_id=1, source_target_pairs={{0,2},{1,3},{2,4},{3,5},{4,6},{5,7},{6,8},{7,9},{8,10},{9,11},{10,... | collective-permute-start | bytes 6291464 | tf_op jit(solution)/shard_map/ppermute | solution.py:134
  116.1 47.7 %collective-permute-start.11 = (f32[64]{0:T(128)S(1)}, f32[64]{0:T(128)S(1)}, u32[]{:S(2)}, u32[]{:S(2)}) collective-permute-start(f32[64]{0:T(128)S(1)} %mul.278), channel_id=1, source_target_pairs={{0,2},{1,3},{2,4},{3,5},{4,6},{5,7},{6,8},{7,9},{8,10},{9,11},{10,... | collective-permute-start | bytes 776 | tf_op jit(solution)/shard_map/ppermute | solution.py:134
  165.3 8.4 %copy-start.8 = (f32[128]{0:T(128)S(1)}, f32[128]{0:T(128)}, u32[]{:S(2)}) copy-start(f32[128]{0:T(128)} %param.21) | copy-start | bytes 1540
  165.3 8.6 %copy-start.6 = (bf16[8192]{0:T(1024)(128)(2,1)S(1)}, bf16[8192]{0:T(1024)(128)(2,1)}, u32[]{:S(2)}) copy-start(bf16[8192]{0:T(1024)(128)(2,1)} %param.26) | copy-start | bytes 49156
  165.3 48.2 %collective-permute-start.15 = (f32[64,64,128]{2,1,0:T(8,128)}, f32[64,64,128]{2,1,0:T(8,128)}, u32[]{:S(2)}, u32[]{:S(2)}) collective-permute-start(f32[64,64,128]{2,1,0:T(8,128)} %multiply_add_fusion.3), channel_id=1, source_target_pairs={{0,4},{1,5},{2,6},{3,7},{4,8},{5,9},{6,10},{7,11},{8,12},{9,13},{1... | collective-permute-start | bytes 6291464 | tf_op jit(solution)/shard_map/ppermute | solution.py:134
  173.7 4.8 %copy-start.7 = (s32[256]{0:T(256)S(1)}, s32[256]{0:T(256)}, u32[]{:S(2)}) copy-start(s32[256]{0:T(256)} %param.27) | copy-start | bytes 3076
  178.9 32.7 %collective-permute-start.12 = (f32[64]{0:T(128)S(1)}, f32[64]{0:T(128)S(1)}, u32[]{:S(2)}, u32[]{:S(2)}) collective-permute-start(f32[64]{0:T(128)S(1)} %collective-permute-done.11), channel_id=1, source_target_pairs={{0,2},{1,3},{2,4},{3,5},{4,6},{5,7},{6,8},{7,9},{8,10},{9,11},{10,... | collective-permute-start | bytes 776 | tf_op jit(solution)/shard_map/ppermute | solution.py:134
  211.6 5.2 %collective-permute-start.16 = (f32[64]{0:T(128)S(1)}, f32[64]{0:T(128)S(1)}, u32[]{:S(2)}, u32[]{:S(2)}) collective-permute-start(f32[64]{0:T(128)S(1)} %mul.319), channel_id=1, source_target_pairs={{0,4},{1,5},{2,6},{3,7},{4,8},{5,9},{6,10},{7,11},{8,12},{9,13},{1... | collective-permute-start | bytes 776 | tf_op jit(solution)/shard_map/ppermute | solution.py:134
  216.8 6.5 %copy-start.4 = (bf16[8192,256]{1,0:T(8,128)(2,1)S(1)}, bf16[8192,256]{1,0:T(8,128)(2,1)}, u32[]{:S(2)}) copy-start(bf16[8192,256]{1,0:T(8,128)(2,1)} %shard_map.127) | copy-start | bytes 12582916
  219.6 12.6 %copy-start.1 = (f32[128,64,128]{2,1,0:T(8,128)S(1)}, f32[128,64,128]{2,1,0:T(8,128)}, u32[]{:S(2)}) copy-start(f32[128,64,128]{2,1,0:T(8,128)} %copy-done) | copy-start | bytes 12582916
  219.6 12.6 %copy-start.3 = (f32[64,64,128]{2,1,0:T(8,128)S(1)}, f32[64,64,128]{2,1,0:T(8,128)}, u32[]{:S(2)}) copy-start(f32[64,64,128]{2,1,0:T(8,128)} %copy-done.2) | copy-start | bytes 6291460
  219.6 12.6 %collective-permute-start.17 = (bf16[64,64,128]{2,1,0:T(8,128)(2,1)S(1)}, bf16[64,64,128]{2,1,0:T(8,128)(2,1)S(1)}, u32[]{:S(2)}, u32[]{:S(2)}) collective-permute-start(bf16[64,64,128]{2,1,0:T(8,128)(2,1)S(1)} %fusion.19), channel_id=1, source_target_pairs={{0,1},{1,0},{2,3},{3,2},{4,5},{5,4},{6,7},{7,6},{8,9},{9,8},{10,11... | collective-permute-start | bytes 3145736 | tf_op jit(solution)/shard_map/ppermute | solution.py:232
  233.0 2.2 copy-start.5

commit v20 on v16

--- a/solution.py
+++ b/solution.py
@@ -217,8 +217,8 @@
     core = lax.axis_index("ctx") % 2
     swap = [(s, s ^ 1) for s in range(count)]
     own_lo = core * half
-    give = lax.dynamic_slice_in_dim(dev_state, half - own_lo, half, 0)
-    other_t, other_s = lax.ppermute((dev_transmit, give), "ctx", swap)
+    other_t, other_all = lax.ppermute((dev_transmit, dev_state), "ctx", swap)
+    other_s = lax.dynamic_slice_in_dim(other_all, own_lo, half, 0)
     mine_s = lax.dynamic_slice_in_dim(dev_state, own_lo, half, 0)
     mine_t = lax.dynamic_slice_in_dim(dev_transmit, own_lo, half, 0)
     peer_t = lax.dynamic_slice_in_dim(other_t, own_lo, half, 0)

time: 250 us -> 252 us (level)
  local copies, waits for them, and re-layouts: 21.9 us -> 18.4 us
  waiting for transfers between devices: 131 us -> 134 us
  other arithmetic: 28.3 us -> 31.1 us
    ppermute x2, waiting for transfers between devices: 3.88 us -> 7.01 us  [device_entry(): other_t, other_all = lax.ppermute((dev_transmit, dev_state), 'ctx', swap)]
    unnamed x20 -> x14, local copies, waits for them, and re-layouts: 10.3 us -> 8.31 us
where the time goes in v20:
time: 252 us; the launch traced here: 251 us
  waiting for transfers between devices  134 us (53%)
  other arithmetic  31.1 us (12%)
  starting transfers between devices  28.6 us (11%)
  matrix products  18.6 us (7%)
  local copies, waits for them, and re-layouts  18.4 us (7%)
  Pallas kernels  18.1 us (7%)
    ppermute x6, waiting for transfers between devices, shifted(): lax.ppermute(value, axis, [(s, s + steps) for s in range(count - steps)])  124 us
    ppermute x6, starting transfers between devices, shifted(): lax.ppermute(value, axis, [(s, s + steps) for s in range(count - steps)])  13.3 us
    pallas_call x1, Pallas kernels, conv_rows(): pl.pallas_call(conv_rows_kernel, out_shape=jax.ShapeDtypeStruct((width, r...  10.2 us
    dot_general x1, matrix products, mixing_part(): jnp.einsum('hij,jhp->ihp', mixing, x_group, preferred_element_type=jnp.fl...  8.86 us
    dot_general x1, matrix products, state_part(): jnp.einsum('hjn,jhp->hpn', weighted, x_group, preferred_element_type=jnp....  8.34 us
    unnamed x14, local copies, waits for them, and re-layouts  8.31 us
    pallas_call x1, Pallas kernels, scale_rows(): pl.pallas_call(scale_rows_kernel, out_shape=jax.ShapeDtypeStruct((rows, w...  7.87 us
    ppermute x2, waiting for transfers between devices, device_entry(): other_t, other_all = lax.ppermute((dev_transmit, dev_state), 'ctx', swap)  7.01 us
  transfers between devices with their start and end apart: 15, of which 8 were waited for; matrix products, arithmetic and copies ran while one was open for 19% of the time, Pallas kernels for 4%

profile of v20, /device:TPU:9, one launch (start us, length us, event | category | flops | bytes accessed | tf_op | source)
XLA Modules:
  0.0 251.4 jit_solution(15226466042018585393)
XLA Ops:
  0.0 1.3 slice.98
  2.6 0.9 slice.99
  3.7 0.7 slice.100
  4.5 3.0 %collective-permute-start.3 = (bf16[3,8449]{1,0:T(4,128)(2,1)S(1)}, bf16[3,8449]{1,0:T(4,128)(2,1)S(1)}, u32[]{:S(2)}, u32[]{:S(2)}) collective-permute-start(bf16[3,8449]{1,0:T(4,128)(2,1)S(1)} %pad_maximum_fusion.1), channel_id=1, source_target_pairs={{0,1},{1,2},{2,3},{3,4},{4,5},{5,6},{6,7},{7,8},{8,9},{9,10},{10,1... | collective-permute-start | bytes 152090 | tf_op jit(solution)/shard_map/ppermute | solution.py:23
  7.5 1.0 copy.21
  8.5 0.8 negate_multiply_fusion
  9.4 1.3 reshape.210.b_ref
  10.8 0.8 slice_convert_fusion.5
  12.3 1.3 broadcast_select_fusion.1
  13.7 1.2 collective-permute-start.6
  14.9 1.2 collective-permute-done.6
  16.2 1.3 collective-permute-start.7
  18.2 0.8 pad_add_fusion
  20.2 2.0 compare_convert_fusion.4
  22.2 0.9 copy.25.vis_ref
  23.2 1.5 multiply_convert_fusion.6
  24.8 0.8 fusion.35
  26.4 10.2 %shard_map.127 = bf16[8192,256]{1,0:T(8,128)(2,1)} custom-call(bf16[8,8192]{1,0:T(8,128)(2,1)} %concatenate.76.rim_ref, bf16[256,8192]{1,0:T(8,128)(2,1)} %x_ref.1, bf16[4,8192]{1,0:T(4,128)(2,1)} %w_ref.1, bf16[1,8192]{1,0:T(2,128)(2,1)} %reshape.210.b_ref, f32[3,256,1]{2,1,0:T(8,128)} %copy.25.vis_ref), custom_call_target="tpu_custom_call" | custom-call | flops 41943040 | bytes 8388608 | tf_op jit(solution)/shard_map/pallas_call | solution.py:66
  36.9 2.2 collective-permute-done.8
  39.2 2.3 collective-permute-start.9
  41.5 8.3 %fusion.15 = f32[1,128,64,128]{3,2,1,0:T(8,128)S(1)} fusion(bf16[256,128,64]{0,2,1:T(8,128)(2,1)} %bitcast.78, f32[128,256]{1,0:T(8,128)S(1)} %copy.26, f32[256,128]{1,0:T(8,128)S(1)} %get-tuple-element.83), kind=kOutput, calls=%fused_computation.25 | convolution fusion | flops 545259520 | bytes 8650752 | tf_op jit(solution)/shard_map/hjn,jhp->hpn/dot_general | solution.py:121
  49.9 2.3 bitcast_add_fusion.2
  52.2 2.3 collective-permute-start.10
  54.5 5.7 %collective-permute-done.4 = f32[128]{0:T(128)S(1)} collective-permute-done((f32[128]{0:T(128)S(1)}, f32[128]{0:T(128)S(1)}, u32[]{:S(2)}, u32[]{:S(2)}) %collective-permute-start.4) | collective-permute-done | bytes 544 | tf_op jit(solution)/shard_map/ppermute | solution.py:220
  60.3 1.4 collective-permute-done.10
  61.6 2.7 %add_select_fusion = f32[64,64,128]{2,1,0:T(8,128)S(1)} fusion(f32[128,64,128]{2,1,0:T(8,128)} %collective-permute-done.10, s32[]{:T(128)S(6)} %select_n.99, f32[128,64,128]{2,1,0:T(8,128)} %bitcast_add_fusion.2, f32[64]{0:T(128)S(1)} %get-tuple-element.74, f32[64]{0:T(128)S(1)} %get-tuple-element.73, pred[]{:T(512)S(6)} %eq.73), kind=kLoop, calls=%fused_computation.34 | loop fusion | flops 2621440 | bytes 6291973 | tf_op jit(solution)/shard_map/jit(_where)/select_n | solution.py:226
  64.3 3.1 %collective-permute-start.13 = (f32[64,64,128]{2,1,0:T(8,128)S(1)}, f32[64,64,128]{2,1,0:T(8,128)S(1)}, u32[]{:S(2)}, u32[]{:S(2)}) collective-permute-start(f32[64,64,128]{2,1,0:T(8,128)S(1)} %add_select_fusion), channel_id=1, source_target_pairs={{0,2},{1,3},{2,4},{3,5},{4,6},{5,7},{6,8},{7,9},{8,10},{9,11},{10,... | collective-permute-start | bytes 6291464 | tf_op jit(solution)/shard_map/ppermute | solution.py:134
  67.4 47.4 %collective-permute-done.13 = f32[64,64,128]{2,1,0:T(8,128)S(1)} collective-permute-done((f32[64,64,128]{2,1,0:T(8,128)S(1)}, f32[64,64,128]{2,1,0:T(8,128)S(1)}, u32[]{:S(2)}, u32[]{:S(2)}) %collective-permute-start.13) | collective-permute-done | bytes 2097184 | tf_op jit(solution)/shard_map/ppermute | solution.py:134
  114.8 1.9 collective-permute-start.14
  116.7 2.4 collective-permute-start.11
  119.1 45.3 %collective-permute-done.11 = f32[64]{0:T(128)S(1)} collective-permute-done((f32[64]{0:T(128)S(1)}, f32[64]{0:T(128)S(1)}, u32[]{:S(2)}, u32[]{:S(2)}) %collective-permute-start.11) | collective-permute-done | bytes 288 | tf_op jit(solution)/shard_map/ppermute | solution.py:134
  164.7 2.1 collective-permute-start.15
  166.8 6.4 %copy.35 = bf16[256,8192]{0,1:T(8,128)(2,1)} copy(bf16[256,8192]{1,0:T(8,128)(2,1)} %param.16) | data formatting | bytes 8388608 | tf_op args[1]
  173.3 2.6 %copy.36.n_ref = f32[8192,1]{1,0:T(8,128)} copy(f32[8192,1]{0,1:T(1,128)S(1)} %bitcast.84) | data formatting | bytes 65536 | tf_op jit(solution)/shard_map/broadcast_in_dim | solution.py:102
  176.6 0.8 compare_reduce_fusion
  178.3 1.9 collective-permute-start.12
  180.5 30.3 %collective-permute-done.12 = f32[64]{0:T(128)S(1)} collective-permute-done((f32[64]{0:T(128)S(1)}, f32[64]{0:T(128)S(1)}, u32[]{:S(2)}, u32[]{:S(2)}) %collective-permute-start.12) | collective-permute-done | bytes 288 | tf_op jit(solution)/shard_map/ppermute | solution.py:134
  210.8 1.9 collective-permute-start.16
  212.7 2.5 multiply_add_fusion.2
  215.2 0.8 collective-permute-done.16
  216.0 2.8 %fusion.19 = bf16[64,64,128]{2,1,0:T(8,128)(2,1)S(1)} fusion(f32[64,64,128]{2,1,0:T(8,128)S(1)} %get-tuple-element.93, f32[128,64,128]{2,1,0:T(8,128)} %collective-permute-done.10, s32[]{:T(128)S(6)} %select_n.99, f32[128,64,128]{2,1,0:T(8,128)} %bitcast_add_fusion.2, f32[64]{0:T(128)S(1)} %get-tuple-element.72, pred[]{:T(512)S(6)} %eq.73), kind=kLoop, calls=%fused_computation.35 | loop fusion | flops 2097152 | bytes 7340293 | tf_op jit(solution)/shard_map/jit(_where)/select_n | solution.py:232
  218.8 4.3 %collective-permute-start.17 = (bf16[64,64,128]{2,1,0:T(8,128)(2,1)S(1)}, bf16[64,64,128]{2,1,0:T(8,128)(2,1)S(1)}, u32[]{:S(2)}, u32[]{:S(2)}) collective-permute-start(bf16[64,64,128]{2,1,0:T(8,128)(2,1)S(1)} %fusion.19), channel_id=1, source_target_pairs={{0,1},{1,0},{2,3},{3,2},{4,5},{5,4},{6,7},{7,6},{8,9},{9,8},{10,11... | collective-permute-start | bytes 3145736 | tf_op jit(solution)/shard_map/ppermute | solution.py:232
  223.1 8.9 %fusion = f32[128,64,256]{2,1,0:T(8,128)S(1)} fusion(f32[128,256]{1,0:T(8,128)S(1)} %copy.30, f32[128,256]{1,0:T(8,128)S(1)} %copy.28, f32[256,256]{1,0:T(8,128)S(1)} %fusion.27, pred[256,256]{1,0:T(8,128)(4,1)S(1)} %fusion.21, bf16[1,256,128,64]{1,3,2,0:T(8,128)(2,1)S(1)} %bitcast.79), kind=kOutput, calls=%fused_computation.3 | convolution fusion | flops 1115684864 | bytes 13172736 | tf_op jit(solution)/shard_map/hij,jhp->ihp/dot_general | solution.py:113
  232.0 2.9 %select_convert_fusion.1 = (bf16[64,64,128]{2,1,0:T(8,128)(2,1)S(1)}, bf16[64,64,128]{2,1,0:T(8,128)(2,1)S(1)}) fusion(bf16[64,64,128]{2,1,0:T(8,128)(2,1)S(1)} %collective-permute-done.17, pred[]{:T(512)S(6)} %eq.73, f32[64,64,128]{2,1,0:T(8,128)S(1)} %get-tuple-element.93, f32[128,64,128]{2,1,0:T(8,128)} %collective-permute-done.10, s32[]{:T(128)S(6)} %select_n.99, ...), kind=kLoop, calls=%fused_computation.30 | loop fusion | flops 2621440 | bytes 9437445 | tf_op jit(solution)/shard_map/convert.8
  235.0 1.3 bitcast_add_fusion.1
  236.3 0.9 copy-done.1
  237.2 5.7 %multiply_reduce_fusion = (f32[256]{0:T(256)S(1)}, f32[256,8192]{0,1:T(8,128)}) fusion(bf16[256,8192]{0,1:T(8,128)(2,1)S(1)} %copy-done.1, bf16[256,8192]{0,1:T(8,128)(2,1)S(1)} %bitcast.80, f32[8192]{0:T(1024)S(1)} %mul.331, f32[256,128,64]{0,2,1:T(8,128)S(1)} %bitcast_add_fusion.1), kind=kLoop, calls=%fused_computation.20 | loop fusion | flops 23068416 | bytes 25199616 | tf_op jit(solution)/shard_map/reduce_sum | solution.py:337
  243.5 7.9 %shard_map.128 = bf16[256,8192]{1,0:T(8,128)(2,1)} custom-call(f32[8192,256]{1,0:T(8,128)} %bitcast.77, f32[1,256]{1,0:T(1,128)} %bitcast.88, f32[8192,1]{1,0:T(8,128)} %copy.36.n_ref), custom_call_target="tpu_custom_call" | custom-call | flops 4194304 | bytes 12582912 | tf_op jit(solution)/shard_map/pallas_call | solution.py:91
  (69 shorter events, 6.9 us)
Async XLA Ops:
  1.3 11.1 %collective-permute-start.5 = (s32[1]{0:T(128)}, s32[1]{0:T(128)}, u32[]{:S(2)}, u32[]{:S(2)}) collective-permute-start(s32[1]{0:T(128)} %slice.98), channel_id=1, source_target_pairs={{0,1},{1,0},{2,3},{3,2},{4,5},{5,4},{6,7},{7,6},{8,9},{9,8},{10,11... | collective-permute-start | bytes 20 | tf_op jit(solution)/shard_map/ppermute | solution.py:172
  4.5 11.7 %collective-permute-start.3 = (bf16[3,8449]{1,0:T(4,128)(2,1)S(1)}, bf16[3,8449]{1,0:T(4,128)(2,1)S(1)}, u32[]{:S(2)}, u32[]{:S(2)}) collective-permute-start(bf16[3,8449]{1,0:T(4,128)(2,1)S(1)} %pad_maximum_fusion.1), channel_id=1, source_target_pairs={{0,1},{1,2},{2,3},{3,4},{4,5},{5,6},{6,7},{7,8},{8,9},{9,10},{10,1... | collective-permute-start | bytes 152090 | tf_op jit(solution)/shard_map/ppermute | solution.py:23
  13.7 2.4 collective-permute-start.6
  16.2 20.4 %collective-permute-start.7 = (s32[4]{0:T(128)S(1)}, s32[4]{0:T(128)S(1)}, u32[]{:S(2)}, u32[]{:S(2)}) collective-permute-start(s32[4]{0:T(128)S(1)} %broadcast_select_fusion.2), channel_id=1, source_target_pairs={{0,4},{1,5},{2,6},{3,7},{4,0},{5,1},{6,2},{7,3},{8,12},{9,13},{10,... | collective-permute-start | bytes 56 | tf_op jit(solution)/shard_map/ppermute | solution.py:172
  36.7 2.4 collective-permute-start.8
  39.2 10.7 %collective-permute-start.9 = (s32[16]{0:T(128)S(1)}, s32[16]{0:T(128)S(1)}, u32[]{:S(2)}, u32[]{:S(2)}) collective-permute-start(s32[16]{0:T(128)S(1)} %broadcast_select_fusion.4), channel_id=1, source_target_pairs={{0,16},{1,17},{2,18},{3,19},{4,20},{5,21},{6,22},{7,23},{8,24},{9,... | collective-permute-start | bytes 200 | tf_op jit(solution)/shard_map/ppermute | solution.py:172
  52.2 9.4 %collective-permute-start.10 = (f32[128,64,128]{2,1,0:T(8,128)}, f32[128,64,128]{2,1,0:T(8,128)}, u32[]{:S(2)}, u32[]{:S(2)}) collective-permute-start(f32[128,64,128]{2,1,0:T(8,128)} %bitcast_add_fusion.2), channel_id=1, source_target_pairs={{0,1},{1,0},{2,3},{3,2},{4,5},{5,4},{6,7},{7,6},{8,9},{9,8},{10,11... | collective-permute-start | bytes 12582920 | tf_op jit(solution)/shard_map/ppermute | solution.py:220
  54.5 5.7 %collective-permute-start.4 = (f32[128]{0:T(128)S(1)}, f32[128]{0:T(128)S(1)}, u32[]{:S(2)}, u32[]{:S(2)}) collective-permute-start(f32[128]{0:T(128)S(1)} %get-tuple-element.78), channel_id=1, source_target_pairs={{0,1},{1,0},{2,3},{3,2},{4,5},{5,4},{6,7},{7,6},{8,9},{9,8},{10,11... | collective-permute-start | bytes 1544 | tf_op jit(solution)/shard_map/ppermute | solution.py:220
  64.3 50.5 %collective-permute-start.13 = (f32[64,64,128]{2,1,0:T(8,128)S(1)}, f32[64,64,128]{2,1,0:T(8,128)S(1)}, u32[]{:S(2)}, u32[]{:S(2)}) collective-permute-start(f32[64,64,128]{2,1,0:T(8,128)S(1)} %add_select_fusion), channel_id=1, source_target_pairs={{0,2},{1,3},{2,4},{3,5},{4,6},{5,7},{6,8},{7,9},{8,10},{9,11},{10,... | collective-permute-start | bytes 6291464 | tf_op jit(solution)/shard_map/ppermute | solution.py:134
  114.8 49.6 %collective-permute-start.14 = (f32[64,64,128]{2,1,0:T(8,128)S(1)}, f32[64,64,128]{2,1,0:T(8,128)S(1)}, u32[]{:S(2)}, u32[]{:S(2)}) collective-permute-start(f32[64,64,128]{2,1,0:T(8,128)S(1)} %collective-permute-done.13), channel_id=1, source_target_pairs={{0,2},{1,3},{2,4},{3,5},{4,6},{5,7},{6,8},{7,9},{8,10},{9,11},{10,... | collective-permute-start | bytes 6291464 | tf_op jit(solution)/shard_map/ppermute | solution.py:134
  116.7 47.7 %collective-permute-start.11 = (f32[64]{0:T(128)S(1)}, f32[64]{0:T(128)S(1)}, u32[]{:S(2)}, u32[]{:S(2)}) collective-permute-start(f32[64]{0:T(128)S(1)} %mul.278), channel_id=1, source_target_pairs={{0,2},{1,3},{2,4},{3,5},{4,6},{5,7},{6,8},{7,9},{8,10},{9,11},{10,... | collective-permute-start | bytes 776 | tf_op jit(solution)/shard_map/ppermute | solution.py:134
  164.7 8.5 %copy-start.2 = (f32[64,64,128]{2,1,0:T(8,128)}, f32[64,64,128]{2,1,0:T(8,128)S(1)}, u32[]{:S(2)}) copy-start(f32[64,64,128]{2,1,0:T(8,128)S(1)} %multiply_add_fusion.3) | copy-start | bytes 6291460
  164.7 8.5 %copy-start.5 = (f32[128]{0:T(128)S(1)}, f32[128]{0:T(128)}, u32[]{:S(2)}) copy-start(f32[128]{0:T(128)} %param.21) | copy-start | bytes 1540
  164.7 8.6 %copy-start.3 = (bf16[8192]{0:T(1024)(128)(2,1)S(1)}, bf16[8192]{0:T(1024)(128)(2,1)}, u32[]{:S(2)}) copy-start(bf16[8192]{0:T(1024)(128)(2,1)} %param.26) | copy-start | bytes 49156
  164.7 48.0 %collective-permute-start.15 = (f32[64,64,128]{2,1,0:T(8,128)S(1)}, f32[64,64,128]{2,1,0:T(8,128)}, u32[]{:S(2)}, u32[]{:S(2)}) collective-permute-start(f32[64,64,128]{2,1,0:T(8,128)S(1)} %multiply_add_fusion.3), channel_id=1, source_target_pairs={{0,4},{1,5},{2,6},{3,7},{4,8},{5,9},{6,10},{7,11},{8,12},{9,13},{1... | collective-permute-start | bytes 6291464 | tf_op jit(solution)/shard_map/ppermute | solution.py:134
  173.2 4.9 %copy-start.4 = (s32[256]{0:T(256)S(1)}, s32[256]{0:T(256)}, u32[]{:S(2)}) copy-start(s32[256]{0:T(256)} %param.27) | copy-start | bytes 3076
  178.3 32.5 %collective-permute-start.12 = (f32[64]{0:T(128)S(1)}, f32[64]{0:T(128)S(1)}, u32[]{:S(2)}, u32[]{:S(2)}) collective-permute-start(f32[64]{0:T(128)S(1)} %collective-permute-done.11), channel_id=1, source_target_pairs={{0,2},{1,3},{2,4},{3,5},{4,6},{5,7},{6,8},{7,9},{8,10},{9,11},{10,... | collective-permute-start | bytes 776 | tf_op jit(solution)/shard_map/ppermute | solution.py:134
  210.8 5.2 %collective-permute-start.16 = (f32[64]{0:T(128)S(1)}, f32[64]{0:T(128)S(1)}, u32[]{:S(2)}, u32[]{:S(2)}) collective-permute-start(f32[64]{0:T(128)S(1)} %mul.319), channel_id=1, source_target_pairs={{0,4},{1,5},{2,6},{3,7},{4,8},{5,9},{6,10},{7,11},{8,12},{9,13},{1... | collective-permute-start | bytes 776 | tf_op jit(solution)/shard_map/ppermute | solution.py:134
  216.0 7.1 %copy-start = (bf16[8192,256]{1,0:T(8,128)(2,1)S(1)}, bf16[8192,256]{1,0:T(8,128)(2,1)}, u32[]{:S(2)}) copy-start(bf16[8192,256]{1,0:T(8,128)(2,1)} %shard_map.127) | copy-start | bytes 12582916
  218.8 13.2 %collective-permute-start.17 = (bf16[64,64,128]{2,1,0:T(8,128)(2,1)S(1)}, bf16[64,64,128]{2,1,0:T(8,128)(2,1)S(1)}, u32[]{:S(2)}, u32[]{:S(2)}) collective-permute-start(bf16[64,64,128]{2,1,0:T(8,128)(2,1)S(1)} %fusion.19), channel_id=1, source_target_pairs={{0,1},{1,0},{2,3},{3,2},{4,5},{5,4},{6,7},{7,6},{8,9},{9,8},{10,11... | collective-permute-start | bytes 3145736 | tf_op jit(solution)/shard_map/ppermute | solution.py:232
  235.0 2.2 copy-start.1

commit v21 on v16

--- a/solution.py
+++ b/solution.py
@@ -289,10 +289,8 @@
     rim_x = rims[:, :channels]
     rim_bc = rims[:, channels : channels + bc_width]
     rim_segment = rims[:, channels + bc_width].astype(jnp.int32)
-    ids = gather_rounds(segment_ids[tok_rows - 1 :], "ctx", 0, 2)
-    ids, rim_x = lax.optimization_barrier((ids, rim_x))
     x_conv = conv_rows(rim_x, x_in, rim_segment, segment_ids, conv_x_w, conv_x_b)
-    ids = gather_rounds(ids, "ctx", 2, 4)
+    ids = gather_rounds(segment_ids[tok_rows - 1 :], "ctx", 0, 3)
     ids, x_conv = lax.optimization_barrier((ids, x_conv))
     bc_conv = causal_conv(rim_bc, bc_in, rim_segment, segment_ids, conv_bc_w, conv_bc_b)
     step_size = jax.nn.softplus(dt_raw + dt_bias[:, None])
@@ -319,7 +317,7 @@
         state_of, (x_blocks, b_blocks, step_blocks, cum_decay, seg_blocks, seg_before)
     )
     intra_items = (x_blocks, b_blocks, c_blocks, step_blocks, cum_decay, seg_blocks)
-    ids = gather_rounds(ids, "ctx", 4, lax.axis_size("ctx").bit_length())
+    ids = gather_rounds(ids, "ctx", 3, lax.axis_size("ctx").bit_length())
     ids, block_states = lax.optimization_barrier((ids, block_states))
     far = [*long_runs(ids, paired, tok_rows), intra_items]
     entering = chain_states(block_states, transmits, paired, far)

time: 250 us -> 250 us (level)
    unnamed x20 -> x24, local copies, waits for them, and re-layouts: 10.3 us -> 10.3 us
  transfers between devices with their start and end apart: 15 -> 15, of which waited for: 8 -> 9; matrix products, arithmetic and copies ran while one was open for 19% -> 16% of each run, Pallas kernels for 4% -> 0%
where the time goes in v21:
time: 250 us; the launch traced here: 248 us
  waiting for transfers between devices  131 us (52%)
  starting transfers between devices  29.6 us (12%)
  other arithmetic  26.5 us (11%)
  local copies, waits for them, and re-layouts  21.9 us (9%)
  matrix products  18.6 us (7%)
  Pallas kernels  18.1 us (7%)
    ppermute x6, waiting for transfers between devices, shifted(): lax.ppermute(value, axis, [(s, s + steps) for s in range(count - steps)])  124 us
    ppermute x6, starting transfers between devices, shifted(): lax.ppermute(value, axis, [(s, s + steps) for s in range(count - steps)])  14.7 us
    unnamed x24, local copies, waits for them, and re-layouts  10.3 us
    pallas_call x1, Pallas kernels, conv_rows(): pl.pallas_call(conv_rows_kernel, out_shape=jax.ShapeDtypeStruct((width, r...  10.3 us
    dot_general x1, matrix products, mixing_part(): jnp.einsum('hij,jhp->ihp', mixing, x_group, preferred_element_type=jnp.fl...  8.86 us
    dot_general x1, matrix products, state_part(): jnp.einsum('hjn,jhp->hpn', weighted, x_group, preferred_element_type=jnp....  8.34 us
    pallas_call x1, Pallas kernels, scale_rows(): pl.pallas_call(scale_rows_kernel, out_shape=jax.ShapeDtypeStruct((rows, w...  7.87 us
    reduce_sum x1, other arithmetic, local(): local_sq = jnp.sum(gated * gated, axis=1)  5.72 us
  transfers between devices with their start and end apart: 15, of which 9 were waited for; matrix products, arithmetic and copies ran while one was open for 16% of the time, Pallas kernels for 0%

profile of v21, /device:TPU:9, one launch (start us, length us, event | category | flops | bytes accessed | tf_op | source)
XLA Modules:
  0.0 248.1 jit_solution(5490544931455782896)
XLA Ops:
  0.0 1.3 slice.98
  2.6 0.9 slice.99
  3.7 0.7 slice.100
  4.5 3.0 %collective-permute-start.3 = (bf16[3,8449]{1,0:T(4,128)(2,1)S(1)}, bf16[3,8449]{1,0:T(4,128)(2,1)S(1)}, u32[]{:S(2)}, u32[]{:S(2)}) collective-permute-start(bf16[3,8449]{1,0:T(4,128)(2,1)S(1)} %pad_maximum_fusion.1), channel_id=1, source_target_pairs={{0,1},{1,2},{2,3},{3,4},{4,5},{5,6},{6,7},{7,8},{8,9},{9,10},{10,1... | collective-permute-start | bytes 152090 | tf_op jit(solution)/shard_map/ppermute | solution.py:23
  7.5 1.0 copy.21
  8.5 0.8 negate_multiply_fusion
  9.4 1.4 reshape.210.b_ref
  10.8 0.8 slice_convert_fusion.5
  12.4 1.4 broadcast_select_fusion.1
  13.7 1.2 collective-permute-start.6
  14.9 1.2 collective-permute-done.6
  16.2 1.2 collective-permute-start.7
  17.4 1.2 collective-permute-done.7
  19.3 0.8 pad_add_fusion
  21.4 2.0 compare_convert_fusion.4
  23.4 0.9 copy.25.vis_ref
  25.1 10.3 %shard_map.127 = bf16[8192,256]{1,0:T(8,128)(2,1)} custom-call(bf16[8,8192]{1,0:T(8,128)(2,1)} %concatenate.74.rim_ref, bf16[256,8192]{1,0:T(8,128)(2,1)} %x_ref.1, bf16[4,8192]{1,0:T(4,128)(2,1)} %w_ref.1, bf16[1,8192]{1,0:T(2,128)(2,1)} %reshape.210.b_ref, f32[3,256,1]{2,1,0:T(8,128)} %copy.25.vis_ref), custom_call_target="tpu_custom_call" | custom-call | flops 41943040 | bytes 8388608 | tf_op jit(solution)/shard_map/pallas_call | solution.py:66
  36.2 8.3 %fusion.15 = f32[1,128,64,128]{3,2,1,0:T(8,128)S(1)} fusion(bf16[256,128,64]{0,2,1:T(8,128)(2,1)} %bitcast.78, f32[128,256]{1,0:T(8,128)S(1)} %copy.26, f32[256,128]{1,0:T(8,128)S(1)} %get-tuple-element.79), kind=kOutput, calls=%fused_computation.25 | convolution fusion | flops 545259520 | bytes 8650752 | tf_op jit(solution)/shard_map/hjn,jhp->hpn/dot_general | solution.py:121
  44.6 2.3 collective-permute-start.9
  47.0 1.0 collective-permute-done.9
  48.4 2.0 copy-done
  50.3 1.5 constant_dynamic-slice_fusion
  51.8 2.8 %collective-permute-start.10 = (f32[64,64,128]{2,1,0:T(8,128)}, f32[64,64,128]{2,1,0:T(8,128)S(1)}, u32[]{:S(2)}, u32[]{:S(2)}) collective-permute-start(f32[64,64,128]{2,1,0:T(8,128)} %constant_dynamic-slice_fusion), channel_id=1, source_target_pairs={{0,1},{1,0},{2,3},{3,2},{4,5},{5,4},{6,7},{7,6},{8,9},{9,8},{10,11... | collective-permute-start | bytes 6291464 | tf_op jit(solution)/shard_map/ppermute | solution.py:221
  54.6 3.6 %collective-permute-done.4 = f32[128]{0:T(128)S(1)} collective-permute-done((f32[128]{0:T(128)S(1)}, f32[128]{0:T(128)S(1)}, u32[]{:S(2)}, u32[]{:S(2)}) %collective-permute-start.4) | collective-permute-done | bytes 544 | tf_op jit(solution)/shard_map/ppermute | solution.py:221
  58.6 2.8 %add_select_fusion = f32[64,64,128]{2,1,0:T(8,128)S(1)} fusion(f32[64,64,128]{2,1,0:T(8,128)S(1)} %collective-permute-done.10, f32[128,64,128]{2,1,0:T(8,128)} %copy-done, s32[]{:T(128)S(6)} %select_n.101, f32[64]{0:T(128)S(1)} %get-tuple-element.70, f32[64]{0:T(128)S(1)} %get-tuple-element.69, pred[]{:T(512)S(6)} %eq.73), kind=kLoop, calls=%fused_computation.34 | loop fusion | flops 2621440 | bytes 6291973 | tf_op jit(solution)/shard_map/jit(_where)/select_n | solution.py:226
  61.4 3.4 %collective-permute-start.13 = (f32[64,64,128]{2,1,0:T(8,128)S(1)}, f32[64,64,128]{2,1,0:T(8,128)S(1)}, u32[]{:S(2)}, u32[]{:S(2)}) collective-permute-start(f32[64,64,128]{2,1,0:T(8,128)S(1)} %add_select_fusion), channel_id=1, source_target_pairs={{0,2},{1,3},{2,4},{3,5},{4,6},{5,7},{6,8},{7,9},{8,10},{9,11},{10,... | collective-permute-start | bytes 6291464 | tf_op jit(solution)/shard_map/ppermute | solution.py:134
  64.9 47.6 %collective-permute-done.13 = f32[64,64,128]{2,1,0:T(8,128)S(1)} collective-permute-done((f32[64,64,128]{2,1,0:T(8,128)S(1)}, f32[64,64,128]{2,1,0:T(8,128)S(1)}, u32[]{:S(2)}, u32[]{:S(2)}) %collective-permute-start.13) | collective-permute-done | bytes 2097184 | tf_op jit(solution)/shard_map/ppermute | solution.py:134
  112.5 1.9 collective-permute-start.14
  114.4 3.2 %collective-permute-start.11 = (f32[64]{0:T(128)S(1)}, f32[64]{0:T(128)S(1)}, u32[]{:S(2)}, u32[]{:S(2)}) collective-permute-start(f32[64]{0:T(128)S(1)} %mul.278), channel_id=1, source_target_pairs={{0,2},{1,3},{2,4},{3,5},{4,6},{5,7},{6,8},{7,9},{8,10},{9,11},{10,... | collective-permute-start | bytes 776 | tf_op jit(solution)/shard_map/ppermute | solution.py:134
  117.6 44.8 %collective-permute-done.11 = f32[64]{0:T(128)S(1)} collective-permute-done((f32[64]{0:T(128)S(1)}, f32[64]{0:T(128)S(1)}, u32[]{:S(2)}, u32[]{:S(2)}) %collective-permute-start.11) | collective-permute-done | bytes 288 | tf_op jit(solution)/shard_map/ppermute | solution.py:134
  162.4 1.6 multiply_add_fusion.3
  164.0 2.0 collective-permute-start.15
  166.0 6.4 %copy.35 = bf16[256,8192]{0,1:T(8,128)(2,1)} copy(bf16[256,8192]{1,0:T(8,128)(2,1)} %param.16) | data formatting | bytes 8388608 | tf_op args[1]
  172.6 2.7 %copy.36.n_ref = f32[8192,1]{1,0:T(8,128)} copy(f32[8192,1]{0,1:T(1,128)S(1)} %bitcast.84) | data formatting | bytes 65536 | tf_op jit(solution)/shard_map/broadcast_in_dim | solution.py:102
  175.8 0.7 compare_reduce_fusion
  177.4 2.2 collective-permute-start.12
  179.9 30.7 %collective-permute-done.12 = f32[64]{0:T(128)S(1)} collective-permute-done((f32[64]{0:T(128)S(1)}, f32[64]{0:T(128)S(1)}, u32[]{:S(2)}, u32[]{:S(2)}) %collective-permute-start.12) | collective-permute-done | bytes 288 | tf_op jit(solution)/shard_map/ppermute | solution.py:134
  210.6 1.9 collective-permute-start.16
  212.5 2.5 %multiply_add_fusion.2 = f32[64,64,128]{2,1,0:T(8,128)S(1)} fusion(f32[64,64,128]{2,1,0:T(8,128)} %multiply_add_fusion.3, f32[64,64,128]{2,1,0:T(8,128)} %collective-permute-done.15, f32[64]{0:T(128)S(1)} %mul.319), kind=kLoop, calls=%fused_computation.32 | loop fusion | flops 1048576 | bytes 6291712 | tf_op jit(solution)/shard_map/add | solution.py:139
  215.0 0.8 collective-permute-done.16
  215.8 2.8 %fusion.19 = bf16[64,64,128]{2,1,0:T(8,128)(2,1)S(1)} fusion(f32[64,64,128]{2,1,0:T(8,128)S(1)} %get-tuple-element.89, f32[64,64,128]{2,1,0:T(8,128)} %copy-done.2, f32[128,64,128]{2,1,0:T(8,128)} %copy-done, s32[]{:T(128)S(6)} %select_n.101, f32[64]{0:T(128)S(1)} %get-tuple-element.68, pred[]{:T(512)S(6)} %eq.73), kind=kLoop, calls=%fused_computation.35 | loop fusion | flops 2097152 | bytes 7340293 | tf_op jit(solution)/shard_map/jit(_where)/select_n | solution.py:232
  218.6 3.4 %collective-permute-start.17 = (bf16[64,64,128]{2,1,0:T(8,128)(2,1)S(1)}, bf16[64,64,128]{2,1,0:T(8,128)(2,1)S(1)}, u32[]{:S(2)}, u32[]{:S(2)}) collective-permute-start(bf16[64,64,128]{2,1,0:T(8,128)(2,1)S(1)} %fusion.19), channel_id=1, source_target_pairs={{0,1},{1,0},{2,3},{3,2},{4,5},{5,4},{6,7},{7,6},{8,9},{9,8},{10,11... | collective-permute-start | bytes 3145736 | tf_op jit(solution)/shard_map/ppermute | solution.py:232
  222.0 8.9 %fusion = f32[128,64,256]{2,1,0:T(8,128)S(1)} fusion(f32[128,256]{1,0:T(8,128)S(1)} %copy.30, f32[128,256]{1,0:T(8,128)S(1)} %copy.28, f32[256,256]{1,0:T(8,128)S(1)} %fusion.27, pred[256,256]{1,0:T(8,128)(4,1)S(1)} %fusion.21, bf16[1,256,128,64]{1,3,2,0:T(8,128)(2,1)S(1)} %bitcast.79), kind=kOutput, calls=%fused_computation.3 | convolution fusion | flops 1115684864 | bytes 13172736 | tf_op jit(solution)/shard_map/hij,jhp->ihp/dot_general | solution.py:113
  230.9 0.7 select_convert_fusion.1
  231.7 1.3 bitcast_add_fusion.1
  233.0 0.9 copy-done.5
  233.9 5.7 %multiply_reduce_fusion = (f32[256]{0:T(256)S(1)}, f32[256,8192]{0,1:T(8,128)}) fusion(bf16[256,8192]{0,1:T(8,128)(2,1)S(1)} %copy-done.5, bf16[256,8192]{0,1:T(8,128)(2,1)S(1)} %bitcast.80, f32[8192]{0:T(1024)S(1)} %mul.331, f32[256,128,64]{0,2,1:T(8,128)S(1)} %bitcast_add_fusion.1), kind=kLoop, calls=%fused_computation.20 | loop fusion | flops 23068416 | bytes 25199616 | tf_op jit(solution)/shard_map/reduce_sum | solution.py:335
  240.2 7.9 %shard_map.128 = bf16[256,8192]{1,0:T(8,128)(2,1)} custom-call(f32[8192,256]{1,0:T(8,128)} %bitcast.77, f32[1,256]{1,0:T(1,128)} %bitcast.88, f32[8192,1]{1,0:T(8,128)} %copy.36.n_ref), custom_call_target="tpu_custom_call" | custom-call | flops 4194304 | bytes 12582912 | tf_op jit(solution)/shard_map/pallas_call | solution.py:91
  (80 shorter events, 7.7 us)
Async XLA Ops:
  1.3 11.1 %collective-permute-start.5 = (s32[1]{0:T(128)}, s32[1]{0:T(128)}, u32[]{:S(2)}, u32[]{:S(2)}) collective-permute-start(s32[1]{0:T(128)} %slice.98), channel_id=1, source_target_pairs={{0,1},{1,0},{2,3},{3,2},{4,5},{5,4},{6,7},{7,6},{8,9},{9,8},{10,11... | collective-permute-start | bytes 20 | tf_op jit(solution)/shard_map/ppermute | solution.py:172
  4.5 14.2 %collective-permute-start.3 = (bf16[3,8449]{1,0:T(4,128)(2,1)S(1)}, bf16[3,8449]{1,0:T(4,128)(2,1)S(1)}, u32[]{:S(2)}, u32[]{:S(2)}) collective-permute-start(bf16[3,8449]{1,0:T(4,128)(2,1)S(1)} %pad_maximum_fusion.1), channel_id=1, source_target_pairs={{0,1},{1,2},{2,3},{3,4},{4,5},{5,6},{6,7},{7,8},{8,9},{9,10},{10,1... | collective-permute-start | bytes 152090 | tf_op jit(solution)/shard_map/ppermute | solution.py:23
  13.7 2.4 collective-permute-start.6
  16.2 2.4 collective-permute-start.7
  25.1 10.3 %copy-start.6 = (bf16[256,256]{1,0:T(8,128)(2,1)S(1)}, bf16[256,256]{1,0:T(8,128)(2,1)}, u32[]{:S(2)}) copy-start(bf16[256,256]{1,0:T(8,128)(2,1)} %param.17) | copy-start | bytes 393220
  25.1 10.7 %copy-start.9 = (f32[128]{0:T(128)S(1)}, f32[128]{0:T(128)}, u32[]{:S(2)}) copy-start(f32[128]{0:T(128)} %param.19) | copy-start | bytes 1540
  36.0 8.6 %collective-permute-start.8 = (s32[8]{0:T(128)S(1)}, s32[8]{0:T(128)S(1)}, u32[]{:S(2)}, u32[]{:S(2)}) collective-permute-start(s32[8]{0:T(128)S(1)} %broadcast_select_fusion.3), channel_id=1, source_target_pairs={{0,8},{1,9},{2,10},{3,11},{4,12},{5,13},{6,14},{7,15},{8,0},{9,1},... | collective-permute-start | bytes 104 | tf_op jit(solution)/shard_map/ppermute | solution.py:172
  44.6 3.3 %collective-permute-start.9 = (s32[16]{0:T(128)S(1)}, s32[16]{0:T(128)S(1)}, u32[]{:S(2)}, u32[]{:S(2)}) collective-permute-start(s32[16]{0:T(128)S(1)} %broadcast_select_fusion.4), channel_id=1, source_target_pairs={{0,16},{1,17},{2,18},{3,19},{4,20},{5,21},{6,22},{7,23},{8,24},{9,... | collective-permute-start | bytes 200 | tf_op jit(solution)/shard_map/ppermute | solution.py:172
  48.4 2.0 copy-start
  51.8 6.8 %collective-permute-start.10 = (f32[64,64,128]{2,1,0:T(8,128)}, f32[64,64,128]{2,1,0:T(8,128)S(1)}, u32[]{:S(2)}, u32[]{:S(2)}) collective-permute-start(f32[64,64,128]{2,1,0:T(8,128)} %constant_dynamic-slice_fusion), channel_id=1, source_target_pairs={{0,1},{1,0},{2,3},{3,2},{4,5},{5,4},{6,7},{7,6},{8,9},{9,8},{10,11... | collective-permute-start | bytes 6291464 | tf_op jit(solution)/shard_map/ppermute | solution.py:221
  54.6 3.6 %collective-permute-start.4 = (f32[128]{0:T(128)S(1)}, f32[128]{0:T(128)S(1)}, u32[]{:S(2)}, u32[]{:S(2)}) collective-permute-start(f32[128]{0:T(128)S(1)} %get-tuple-element.74), channel_id=1, source_target_pairs={{0,1},{1,0},{2,3},{3,2},{4,5},{5,4},{6,7},{7,6},{8,9},{9,8},{10,11... | collective-permute-start | bytes 1544 | tf_op jit(solution)/shard_map/ppermute | solution.py:221
  58.6 105.4 %copy-start.2 = (f32[64,64,128]{2,1,0:T(8,128)}, f32[64,64,128]{2,1,0:T(8,128)S(1)}, u32[]{:S(2)}) copy-start(f32[64,64,128]{2,1,0:T(8,128)S(1)} %collective-permute-done.10) | copy-start | bytes 6291460
  61.4 51.1 %collective-permute-start.13 = (f32[64,64,128]{2,1,0:T(8,128)S(1)}, f32[64,64,128]{2,1,0:T(8,128)S(1)}, u32[]{:S(2)}, u32[]{:S(2)}) collective-permute-start(f32[64,64,128]{2,1,0:T(8,128)S(1)} %add_select_fusion), channel_id=1, source_target_pairs={{0,2},{1,3},{2,4},{3,5},{4,6},{5,7},{6,8},{7,9},{8,10},{9,11},{10,... | collective-permute-start | bytes 6291464 | tf_op jit(solution)/shard_map/ppermute | solution.py:134
  112.5 49.9 %collective-permute-start.14 = (f32[64,64,128]{2,1,0:T(8,128)S(1)}, f32[64,64,128]{2,1,0:T(8,128)S(1)}, u32[]{:S(2)}, u32[]{:S(2)}) collective-permute-start(f32[64,64,128]{2,1,0:T(8,128)S(1)} %collective-permute-done.13), channel_id=1, source_target_pairs={{0,2},{1,3},{2,4},{3,5},{4,6},{5,7},{6,8},{7,9},{8,10},{9,11},{10,... | collective-permute-start | bytes 6291464 | tf_op jit(solution)/shard_map/ppermute | solution.py:134
  114.4 48.0 %collective-permute-start.11 = (f32[64]{0:T(128)S(1)}, f32[64]{0:T(128)S(1)}, u32[]{:S(2)}, u32[]{:S(2)}) collective-permute-start(f32[64]{0:T(128)S(1)} %mul.278), channel_id=1, source_target_pairs={{0,2},{1,3},{2,4},{3,5},{4,6},{5,7},{6,8},{7,9},{8,10},{9,11},{10,... | collective-permute-start | bytes 776 | tf_op jit(solution)/shard_map/ppermute | solution.py:134
  164.0 8.4 %copy-start.10 = (f32[128]{0:T(128)S(1)}, f32[128]{0:T(128)}, u32[]{:S(2)}) copy-start(f32[128]{0:T(128)} %param.21) | copy-start | bytes 1540
  164.0 8.6 %copy-start.7 = (bf16[8192]{0:T(1024)(128)(2,1)S(1)}, bf16[8192]{0:T(1024)(128)(2,1)}, u32[]{:S(2)}) copy-start(bf16[8192]{0:T(1024)(128)(2,1)} %param.26) | copy-start | bytes 49156
  164.0 48.5 %collective-permute-start.15 = (f32[64,64,128]{2,1,0:T(8,128)}, f32[64,64,128]{2,1,0:T(8,128)}, u32[]{:S(2)}, u32[]{:S(2)}) collective-permute-start(f32[64,64,128]{2,1,0:T(8,128)} %multiply_add_fusion.3), channel_id=1, source_target_pairs={{0,4},{1,5},{2,6},{3,7},{4,8},{5,9},{6,10},{7,11},{8,12},{9,13},{1... | collective-permute-start | bytes 6291464 | tf_op jit(solution)/shard_map/ppermute | solution.py:134
  172.4 4.7 %copy-start.8 = (s32[256]{0:T(256)S(1)}, s32[256]{0:T(256)}, u32[]{:S(2)}) copy-start(s32[256]{0:T(256)} %param.27) | copy-start | bytes 3076
  177.4 33.2 %collective-permute-start.12 = (f32[64]{0:T(128)S(1)}, f32[64]{0:T(128)S(1)}, u32[]{:S(2)}, u32[]{:S(2)}) collective-permute-start(f32[64]{0:T(128)S(1)} %collective-permute-done.11), channel_id=1, source_target_pairs={{0,2},{1,3},{2,4},{3,5},{4,6},{5,7},{6,8},{7,9},{8,10},{9,11},{10,... | collective-permute-start | bytes 776 | tf_op jit(solution)/shard_map/ppermute | solution.py:134
  210.6 5.2 %collective-permute-start.16 = (f32[64]{0:T(128)S(1)}, f32[64]{0:T(128)S(1)}, u32[]{:S(2)}, u32[]{:S(2)}) collective-permute-start(f32[64]{0:T(128)S(1)} %mul.319), channel_id=1, source_target_pairs={{0,4},{1,5},{2,6},{3,7},{4,8},{5,9},{6,10},{7,11},{8,12},{9,13},{1... | collective-permute-start | bytes 776 | tf_op jit(solution)/shard_map/ppermute | solution.py:134
  215.8 6.2 %copy-start.4 = (bf16[8192,256]{1,0:T(8,128)(2,1)S(1)}, bf16[8192,256]{1,0:T(8,128)(2,1)}, u32[]{:S(2)}) copy-start(bf16[8192,256]{1,0:T(8,128)(2,1)} %shard_map.127) | copy-start | bytes 12582916
  218.6 12.3 %copy-start.1 = (f32[128,64,128]{2,1,0:T(8,128)S(1)}, f32[128,64,128]{2,1,0:T(8,128)}, u32[]{:S(2)}) copy-start(f32[128,64,128]{2,1,0:T(8,128)} %copy-done) | copy-start | bytes 12582916
  218.6 12.3 %copy-start.3 = (f32[64,64,128]{2,1,0:T(8,128)S(1)}, f32[64,64,128]{2,1,0:T(8,128)}, u32[]{:S(2)}) copy-start(f32[64,64,128]{2,1,0:T(8,128)} %copy-done.2) | copy-start | bytes 6291460
  218.6 12.2 %collective-permute-start.17 = (bf16[64,64,128]{2,1,0:T(8,128)(2,1)S(1)}, bf16[64,64,128]{2,1,0:T(8,128)(2,1)S(1)}, u32[]{:S(2)}, u32[]{:S(2)}) collective-permute-start(bf16[64,64,128]{2,1,0:T(8,128)(2,1)S(1)} %fusion.19), channel_id=1, source_target_pairs={{0,1},{1,0},{2,3},{3,2},{4,5},{5,4},{6,7},{7,6},{8,9},{9,8},{10,11... | collective-permute-start | bytes 3145736 | tf_op jit(solution)/shard_map/ppermute | solution.py:232
  231.7 2.2 copy-start.5
